TPU v7x, 32 devices: a whole 2x2x4 slice. The times are simulated.
32 devices in a mesh: blk: 16 (over z, y, core), rep: 2 (over x).
Axes of the slice: x: 2, y: 2, z: 4, core: 2. Of those that a mesh axis runs over, the one named last changes fastest.
Arguments:
- qm_pos: float32 [3, 2048], P(None, 'blk'), may hold values from -4 to 4
- species: int32 [2048], P('blk'), may hold values from 0 to 7
- qm_count: int32 [16], P('blk'), may hold values from 64 to 128, as said below
- ghost_owner: int32 [2048, 4], P('blk'), may hold values from 0 to 15, all different within a row; in each aligned block of 128 rows (0 to 127, 128 to 255, ...) at most 64 rows name the same one
- ghost_slot: int32 [2048, 4], P('blk'), may hold values from 0 to 127
- mm_pos: float32 [3, 16384], P(None, ('blk', 'rep')), may hold values from -4 to 4
- mm_charge: float32 [16384], P(('blk', 'rep')), may hold values from -6 to 6
- species_table: bfloat16 [8, 128], replicated, may hold values from -6 to 6
- potential_gain: float32 [128], replicated, may hold values from -8 to 8
- message_weight: bfloat16 [128, 128], replicated, may hold values from -0.25 to 0.25
- hidden_weight: bfloat16 [128, 256], replicated, may hold values from -0.5 to 0.5
- energy_readout: float32 [256], replicated, may hold values from -0.375 to 0.375
- charge_readout: float32 [256], replicated, may hold values from -0.375 to 0.375
Outputs:
- atom_energy: float32 [2048], P('blk')
- qm_force: float32 [3, 2048], P(None, 'blk')
- mm_force: float32 [3, 16384], P(None, ('blk', 'rep'))
Inputs may be any that keep to these rules, and one draw needn't show every extreme that they name: `qm_count`: some block holds exactly 128 live atoms. `ghost_owner`: each row names 4 different blocks; among the rows of one device no block is named more than 64 times, and some block exactly 64 times.
All inputs are finite; a program needn't handle non-finite values.
Results may differ from a plain program's by a relative error of at most 0.0055.
Values may be sent and summed in bfloat16 or wider, within the bound.
No kernel may reach another device: no remote copies, remote signals or barrier semaphores. Data moves between devices by JAX's collectives and lax.ppermute only.
A program may use at most 64 MiB of HBM per device.

v0:
```python
import math

import jax
import jax.numpy as jnp
from jax import lax
from jax.sharding import PartitionSpec as P

SOFTEN = 0.25


def pair_parts(qm_places, mm_places):
    offset = qm_places[:, :, None] - mm_places[:, None, :]
    inverse = lax.rsqrt(jnp.sum(offset * offset, axis=0) + SOFTEN)
    return (offset, inverse)


def split_columns(stacked, limit):
    stride = math.gcd(stacked.shape[1], limit)
    shaped = stacked.reshape(stacked.shape[0], stacked.shape[1] // stride, stride)
    return jnp.transpose(shaped, (1, 0, 2))


def potential_from(qm_places, mm_stack):

    def potential_advance(running, columns):
        offset, inverse = pair_parts(qm_places, columns[:3])
        return (running + jnp.sum(inverse * columns[3][None, :], axis=1), None)

    result, _ = lax.scan(
        potential_advance,
        jnp.zeros((qm_places.shape[1],), jnp.float32),
        split_columns(mm_stack, 512),
    )
    return result


def on_device(
    qm_pos,
    species,
    qm_count,
    ghost_owner,
    ghost_slot,
    mm_pos,
    mm_charge,
    species_table,
    potential_gain,
    message_weight,
    hidden_weight,
    energy_readout,
    charge_readout,
):
    atom_rows = qm_pos.shape[1]
    blocks = lax.axis_size("blk")
    neighbours = ghost_owner.shape[1]
    channels = species_table.shape[1]
    capacity = 2 * atom_rows * neighbours // blocks
    coupling = float(mm_pos.shape[1] * blocks * lax.axis_size("rep")) ** (-0.5)
    mm_stack = jnp.concatenate([mm_pos, mm_charge[None, :]], axis=0)
    partial_sum = potential_from(qm_pos, lax.all_gather(mm_stack, "blk", axis=1, tiled=True))
    potential = lax.psum(partial_sum, "rep") * coupling
    live = (jnp.arange(atom_rows) < qm_count[0]).astype(jnp.float32)
    picks = (species[:, None] == jnp.arange(species_table.shape[0])[None, :]).astype(jnp.bfloat16)
    base = jnp.dot(picks, species_table, preferred_element_type=jnp.float32)
    start = (live[:, None] * (base + potential[:, None] * potential_gain[None, :])).astype(
        jnp.bfloat16
    )
    owners = ghost_owner.reshape(-1)
    slots = ghost_slot.reshape(-1)
    hits = (owners[:, None] == jnp.arange(blocks)[None, :]).astype(jnp.int32)
    ranks = jnp.sum((jnp.cumsum(hits, axis=0) - hits) * hits, axis=1)
    request = jnp.zeros((blocks, capacity), jnp.int32).at[owners, ranks].set(slots)
    wanted = lax.all_to_all(request, "blk", split_axis=0, concat_axis=0, tiled=True)
    outgoing = jnp.take(start, wanted, axis=0)
    arrived = lax.all_to_all(outgoing, "blk", split_axis=0, concat_axis=0, tiled=True)
    ghosts = arrived[owners, ranks]
    neighbour = jnp.sum(
        ghosts.reshape(atom_rows, neighbours, channels).astype(jnp.float32), axis=1
    ).astype(jnp.bfloat16)
    mixed = start.astype(jnp.float32) + jnp.dot(
        neighbour, message_weight, preferred_element_type=jnp.float32
    )
    before = jnp.dot(mixed.astype(jnp.bfloat16), hidden_weight, preferred_element_type=jnp.float32)
    sigma = jax.nn.sigmoid(before)
    active = before * sigma
    energy_part = live * jnp.sum(active * energy_readout[None, :], axis=1)
    charge_part = live * jnp.sum(active * charge_readout[None, :], axis=1)
    atom_energy = energy_part + charge_part * potential
    back_active = live[:, None] * (
        energy_readout[None, :] + potential[:, None] * charge_readout[None, :]
    )
    back_before = (back_active * sigma * (1.0 + before * (1.0 - sigma))).astype(jnp.bfloat16)
    back_mixed = jnp.dot(back_before, hidden_weight.T, preferred_element_type=jnp.float32)
    back_sum = jnp.dot(
        back_mixed.astype(jnp.bfloat16), message_weight.T, preferred_element_type=jnp.float32
    ).astype(jnp.bfloat16)
    outgoing_grads = (
        jnp.zeros((blocks, capacity, channels), jnp.bfloat16)
        .at[owners, ranks]
        .set(jnp.repeat(back_sum, neighbours, axis=0))
    )
    returned = lax.all_to_all(outgoing_grads, "blk", split_axis=0, concat_axis=0, tiled=True)
    picks_back = (wanted.reshape(-1)[:, None] == jnp.arange(atom_rows)[None, :]).astype(
        jnp.bfloat16
    )
    collected = jnp.einsum(
        "ra,rf->af",
        picks_back,
        returned.reshape(blocks * capacity, channels),
        preferred_element_type=jnp.float32,
    )
    back_start = back_mixed + collected
    effective = charge_part + live * jnp.sum(back_start * potential_gain[None, :], axis=1)
    qm_stack = jnp.concatenate([qm_pos, effective[None, :]], axis=0)
    portion = lax.all_gather(qm_stack, "blk", axis=1, tiled=True)
    mm_running = jnp.zeros((3, mm_pos.shape[1]), jnp.float32)

    def add_advance(running, group):
        offset, inverse = pair_parts(group[:3], mm_pos)
        weight = inverse * inverse * inverse * mm_charge[None, :]
        pull = jnp.sum(offset * weight[None], axis=2) * group[3][None, :]
        running = running - jnp.sum(offset * (weight * group[3][:, None])[None], axis=1)
        return (running, pull)

    mm_running, pulls = lax.scan(add_advance, mm_running, split_columns(portion, 512))
    block_terms = jnp.transpose(pulls, (1, 0, 2)).reshape(3, portion.shape[1])
    qm_terms = block_terms
    mm_sum, qm_terms = (mm_running, qm_terms)
    block_force = lax.psum_scatter(qm_terms, "blk", scatter_dimension=1, tiled=True)
    qm_force = lax.psum(block_force, "rep") * coupling
    return (atom_energy, qm_force, mm_sum * coupling)


def solution(mesh):
    placed = (
        P(None, "blk"),
        P("blk"),
        P("blk"),
        P("blk", None),
        P("blk", None),
        P(None, ("blk", "rep")),
        P(("blk", "rep")),
        P(),
        P(),
        P(),
        P(),
        P(),
        P(),
    )
    return jax.shard_map(
        on_device,
        mesh=mesh,
        in_specs=placed,
        out_specs=(P("blk"), P(None, "blk"), P(None, ("blk", "rep"))),
        check_vma=False,
    )
```

profile of v0, /device:TPU:0, one launch (start us, length us, event | category | flops | bytes accessed | tf_op | source)
XLA Modules:
  0.0 304.6 jit_solution(3147633748383444944)
XLA Ops:
  7.2 0.8 copy.36
  8.3 1.2 reduce-window.6
  9.8 0.8 copy.40
  11.4 70.1 %scatter_fusion = s32[16,64]{1,0:T(8,128)} fusion(s32[16,64]{1,0:T(8,128)} %broadcast_in_dim.31, s32[512]{0:T(512)S(1)} %bitcast.80, s32[512]{0:T(512)S(1)} %reshape.281), kind=kCustom, calls=%fused_computation.2 | custom fusion | bytes 10240 | tf_op jit(solution)/shard_map/scatter | solution.py:71
  81.4 7.1 %all-to-all-start = ((s32[16,1,64]{2,1,0:T(1,128)}), s32[16,1,64]{2,1,0:T(1,128)S(1)}, u32[]{:S(2)}, u32[]{:S(2)}) async-start(s32[16,1,64]{2,1,0:T(1,128)} %bitcast.8), calls=%async_computation | async-start | bytes 16384 | tf_op jit(solution)/shard_map/all_to_all | solution.py:72
  88.6 22.1 %all_gather.6 = f32[4,8192]{1,0:T(4,128)S(1)} all-gather(f32[4,512]{1,0:T(4,128)S(1)} %pad_maximum_fusion), channel_id=1, replica_groups=mesh['blk'=16,'rep'=2] {'blk'}, dimensions={1}, use_global_device_ids=true | all-gather | bytes 139264 | tf_op jit(solution)/shard_map/all_gather | solution.py:59
  110.7 5.4 %while.24 = (s32[]{:T(128)}, f32[128]{0:T(128)S(1)}, f32[3,128]{1,0:T(4,128)S(1)}, f32[16,4,512]{2,1,0:T(4,128)S(1)}, s32[]{:T(128)}, /*index=5*/s32[]{:T(128)}, s32[]{}) while((s32[]{:T(128)}, f32[128]{0:T(128)S(1)}, f32[3,128]{1,0:T(4,128)S(1)}, f32[16,4,512]{2,1,0:T(4,128)S(1)}, s32[]{:T(128)}, /*index=5*/s32[]{:T(128)}, ...), condition=%wide.region_3.4_spmd.clone, body=%wide.region_0.3_spmd.clone.sunk | while | flops 721028 | bytes 552567 | solution.py:29
  116.0 4.9 %psum.14 = f32[128]{0:T(128)S(1)} all-reduce(f32[128]{0:T(128)S(1)} %get-tuple-element.58), channel_id=1, replica_groups=mesh['blk'=16,'rep'=2] {'rep'}, use_global_device_ids=true, to_apply=%region_4.5 | all-reduce | flops 128 | bytes 1024 | tf_op jit(solution)/shard_map/psum | solution.py:60
  122.0 3.2 %gather_fusion = bf16[1024,128]{1,0:T(8,128)(2,1)S(1)} fusion(bf16[128,128]{1,0:T(8,128)(2,1)S(1)} %fusion.8, s32[1024]{0:T(1024)S(1)} %broadcast_clamp_fusion), kind=kCustom, calls=%fused_computation | custom fusion | bytes 528384 | tf_op jit(solution)/shard_map/jit(_take)/gather | solution.py:73
  125.5 12.8 %all_to_all.25 = bf16[16,64,128]{2,1,0:T(8,128)(2,1)S(1)} all-to-all(bf16[16,64,128]{2,1,0:T(8,128)(2,1)S(1)} %broadcast_select_fusion.1), channel_id=1, replica_groups=mesh['blk'=16,'rep'=2] {'blk'}, dimensions={0} | all-to-all | bytes 524288 | tf_op jit(solution)/shard_map/all_to_all | solution.py:74
  138.2 3.2 %gather_fusion.1 = bf16[512,128]{1,0:T(8,128)(2,1)S(1)} fusion(bf16[16,64,128]{2,1,0:T(8,128)(2,1)S(1)} %all_to_all.25, s32[512]{0:T(512)S(1)} %bitcast.82), kind=kCustom, calls=%fused_computation.1 | custom fusion | bytes 266240 | tf_op jit(solution)/shard_map/gather | solution.py:75
  143.2 52.6 %scatter_fusion.1 = bf16[16,64,128]{2,1,0:T(8,128)(2,1)} fusion(bf16[16,64,128]{2,1,0:T(8,128)(2,1)} %broadcast_in_dim.37, s32[512]{0:T(512)S(1)} %bitcast.81, bf16[512,128]{1,0:T(8,128)(2,1)S(1)} %bitcast.85), kind=kCustom, calls=%fused_computation.3 | custom fusion | bytes 397312 | tf_op jit(solution)/shard_map/scatter | solution.py:99
  195.9 3.5 %all-to-all-start.2 = ((bf16[16,64,128]{2,1,0:T(8,128)(2,1)}), bf16[16,64,128]{2,1,0:T(8,128)(2,1)S(1)}, u32[]{:S(2)}, u32[]{:S(2)}) async-start(bf16[16,64,128]{2,1,0:T(8,128)(2,1)} %scatter_fusion.1), calls=%async_computation.2 | async-start | bytes 524288 | tf_op jit(solution)/shard_map/all_to_all | solution.py:101
  201.4 8.1 %all-to-all-done.2 = bf16[16,64,128]{2,1,0:T(8,128)(2,1)S(1)} async-done(((bf16[16,64,128]{2,1,0:T(8,128)(2,1)}), bf16[16,64,128]{2,1,0:T(8,128)(2,1)S(1)}, u32[]{:S(2)}, u32[]{:S(2)}) %all-to-all-start.2) | async-done | bytes 262176 | tf_op jit(solution)/shard_map/all_to_all | solution.py:101
  210.0 18.8 %all_gather.7 = f32[4,2048]{1,0:T(4,128)S(1)} all-gather(f32[4,128]{1,0:T(4,128)S(1)} %pad_maximum_fusion.1), channel_id=1, replica_groups=mesh['blk'=16,'rep'=2] {'blk'}, dimensions={1}, use_global_device_ids=true | all-gather | bytes 34816 | tf_op jit(solution)/shard_map/all_gather | solution.py:114
  228.8 6.3 %while.25 = (s32[]{:T(128)}, f32[3,512]{1,0:T(4,128)S(1)}, f32[4,3,512]{2,1,0:T(4,128)S(1)}, f32[4,4,512]{2,1,0:T(4,128)S(1)}, f32[3,512]{1,0:T(4,128)S(1)}, /*index=5*/f32[512]{0:T(512)S(1)}, s32[]{:T(128)}, s32[]{:T(128)}, s32[]{}) while((s32[]{:T(128)}, f32[3,512]{1,0:T(4,128)S(1)}, f32[4,3,512]{2,1,0:T(4,128)S(1)}, ...), condition=%wide.region_18.19_spmd.clone, body=%wide.region_14.18_spmd.clone.sunk | while | flops 7341572 | bytes 6385803 | solution.py:124
  229.4 0.9 fusion.40
  231.0 0.9 fusion.40
  232.6 0.9 fusion.40
  234.2 0.9 fusion.40
  235.1 1.4 copy.46
  237.1 54.2 %reduce-scatter.4.cloned.1.call-done = f32[128,3]{1,0:T(8,128)} async-done(((f32[2048,3]{1,0:T(8,128)}), f32[128,3]{1,0:T(8,128)}) %reduce-scatter.4.cloned.1.call-update) | async-done | bytes 1552
  291.3 0.9 copy.47
  292.2 4.9 %psum.15 = f32[3,128]{1,0:T(4,128)S(1)} all-reduce(f32[3,128]{1,0:T(4,128)S(1)} %copy.47), channel_id=1, replica_groups=mesh['blk'=16,'rep'=2] {'rep'}, use_global_device_ids=true, to_apply=%region_20.21 | all-reduce | flops 384 | bytes 3072 | tf_op jit(solution)/shard_map/psum | solution.py:129
  (166 shorter events, 14.7 us)
Async XLA Ops:
  7.2 134.4 %copy-start = (bf16[128,256]{1,0:T(8,128)(2,1)S(1)}, bf16[128,256]{1,0:T(8,128)(2,1)}, u32[]{:S(2)}) copy-start(bf16[128,256]{1,0:T(8,128)(2,1)} %param.27) | copy-start | bytes 196612
  11.4 77.2 %copy-start.1 = (f32[3,512]{1,0:T(4,128)S(1)}, f32[3,512]{1,0:T(4,128)}, u32[]{:S(2)}) copy-start(f32[3,512]{1,0:T(4,128)} %param.22) | copy-start | bytes 18436
  11.4 77.2 %copy-start.3 = (f32[512]{0:T(512)S(1)}, f32[512]{0:T(512)}, u32[]{:S(2)}) copy-start(f32[512]{0:T(512)} %param.23) | copy-start | bytes 6148
  11.4 99.3 %copy-start.2 = (f32[3,128]{1,0:T(4,128)S(1)}, f32[3,128]{1,0:T(4,128)}, u32[]{:S(2)}) copy-start(f32[3,128]{1,0:T(4,128)} %param.17) | copy-start | bytes 4612
  81.4 40.5 %all-to-all-start = ((s32[16,1,64]{2,1,0:T(1,128)}), s32[16,1,64]{2,1,0:T(1,128)S(1)}, u32[]{:S(2)}, u32[]{:S(2)}) async-start(s32[16,1,64]{2,1,0:T(1,128)} %bitcast.8), calls=%async_computation | async-start | bytes 16384 | tf_op jit(solution)/shard_map/all_to_all | solution.py:72
  110.6 11.0 %copy-start.5 = (bf16[8,128]{1,0:T(8,128)(2,1)S(1)}, bf16[8,128]{1,0:T(8,128)(2,1)}, u32[]{:S(2)}) copy-start(bf16[8,128]{1,0:T(8,128)(2,1)} %param.24) | copy-start | bytes 6148
  110.7 11.0 %copy-start.8 = (s32[128]{0:T(128)S(1)}, s32[128]{0:T(128)}, u32[]{:S(2)}) copy-start(s32[128]{0:T(128)} %param.18) | copy-start | bytes 1540
  110.7 11.0 %copy-start.9 = (f32[128]{0:T(128)S(1)}, f32[128]{0:T(128)}, u32[]{:S(2)}) copy-start(f32[128]{0:T(128)} %param.25) | copy-start | bytes 1540
  125.4 16.2 %copy-start.4 = (bf16[128,128]{1,0:T(8,128)(2,1)S(1)}, bf16[128,128]{1,0:T(8,128)(2,1)}, u32[]{:S(2)}) copy-start(bf16[128,128]{1,0:T(8,128)(2,1)} %param.26) | copy-start | bytes 98308
  125.4 16.2 %copy-start.6 = (f32[256]{0:T(256)S(1)}, f32[256]{0:T(256)}, u32[]{:S(2)}) copy-start(f32[256]{0:T(256)} %param.28) | copy-start | bytes 3076
  125.5 16.2 %copy-start.7 = (f32[256]{0:T(256)S(1)}, f32[256]{0:T(256)}, u32[]{:S(2)}) copy-start(f32[256]{0:T(256)} %param.29) | copy-start | bytes 3076
  195.9 13.5 %all-to-all-start.2 = ((bf16[16,64,128]{2,1,0:T(8,128)(2,1)}), bf16[16,64,128]{2,1,0:T(8,128)(2,1)S(1)}, u32[]{:S(2)}, u32[]{:S(2)}) async-start(bf16[16,64,128]{2,1,0:T(8,128)(2,1)} %scatter_fusion.1), calls=%async_computation.2 | async-start | bytes 524288 | tf_op jit(solution)/shard_map/all_to_all | solution.py:101
  199.4 91.9 %reduce-scatter.4.cloned.1.call-start = ((), (), s32[]{:S(2)}) async-start(), calls=%async_computation.4 | async-start | bytes 1114112
Sparse Core Ops, SparseCore 0:
  236.6 54.6 reduce-scatter.3
where the time goes:
time: 308 us; the launch traced here: 305 us
  local copies, waits for them, and re-layouts  136 us (44%)
  blocking collectives  63.5 us (21%)
  waiting for transfers between devices  62.3 us (20%)
  between operations  15 us (5%)
  other arithmetic  14.6 us (5%)
  starting transfers between devices  10.7 us (3%)
    scatter x1, local copies, waits for them, and re-layouts, on_device(): jnp.zeros((blocks, capacity), jnp.int32).at[owners, ranks].set(slots)  70.1 us
    unnamed x2, waiting for transfers between devices  54.2 us
    scatter x1, local copies, waits for them, and re-layouts, on_device(): outgoing_grads = jnp.zeros((blocks, capacity, channels), jnp.bfloat16).at...  52.6 us
    all_gather x1, blocking collectives, on_device(): lax.all_gather(mm_stack, 'blk', axis=1, tiled=True)  22.1 us
    all_gather x1, blocking collectives, on_device(): portion = lax.all_gather(qm_stack, 'blk', axis=1, tiled=True)  18.8 us
    all_to_all x1, blocking collectives, on_device(): lax.all_to_all(outgoing, 'blk', split_axis=0, concat_axis=0, tiled=True)  12.8 us
    all_to_all x1, waiting for transfers between devices, on_device(): lax.all_to_all(outgoing_grads, 'blk', split_axis=0, concat_axis=0, tiled=...  8.06 us
    all_to_all x1, starting transfers between devices, on_device(): lax.all_to_all(request, 'blk', split_axis=0, concat_axis=0, tiled=True)  7.09 us
  transfers between devices with their start and end apart: 3, of which 2 were waited for; matrix products, arithmetic and copies ran while one was open for 2% of the time, Pallas kernels for 0%

commit v1 on v0

v1 whole, which is shorter than its diff:
```python
import jax
import jax.numpy as jnp
from jax import lax
from jax.sharding import PartitionSpec as P

SOFTEN = 0.25
CHUNK = 512


def gather_doubling(x, axis):
    n = lax.axis_size(axis)
    me = lax.axis_index(axis)
    step = 1
    while step < n:
        other = lax.ppermute(x, axis, [(i, i ^ step) for i in range(n)])
        low = (me // step) % 2 == 0
        x = jnp.where(low, jnp.concatenate([x, other], -1), jnp.concatenate([other, x], -1))
        step *= 2
    return x


def sum_butterfly(x, axis):
    n = lax.axis_size(axis)
    step = 1
    while step < n:
        x = x + lax.ppermute(x, axis, [(i, i ^ step) for i in range(n)])
        step *= 2
    return x


def potential_pass(qm_all, mm_pos, mm_charge):
    mm_col = [mm_pos[c][:, None] for c in range(3)]
    q_col = mm_charge[:, None]
    chunks = qm_all.shape[1] // CHUNK

    def body(block):
        d = [block[c][None, :] - mm_col[c] for c in range(3)]
        inverse = lax.rsqrt(d[0] * d[0] + d[1] * d[1] + d[2] * d[2] + SOFTEN)
        weighted = inverse * q_col
        cubed = weighted * inverse * inverse
        return jnp.stack(
            [jnp.sum(weighted, axis=0)] + [jnp.sum(d[c] * cubed, axis=0) for c in range(3)]
        )

    parts = lax.map(body, jnp.transpose(qm_all.reshape(3, chunks, CHUNK), (1, 0, 2)))
    return jnp.transpose(parts, (1, 0, 2)).reshape(4, qm_all.shape[1])


def force_pass(qm_all, effective, mm_pos):
    chunks = qm_all.shape[1] // CHUNK
    stacked = jnp.concatenate([qm_all, effective[None, :]], axis=0)
    stacked = jnp.transpose(stacked.reshape(4, chunks, CHUNK), (1, 2, 0))

    def body(running, block):
        d = [block[:, c : c + 1] - mm_pos[c][None, :] for c in range(3)]
        inverse = lax.rsqrt(d[0] * d[0] + d[1] * d[1] + d[2] * d[2] + SOFTEN)
        weight = inverse * inverse * inverse * block[:, 3:4]
        return running + jnp.stack([jnp.sum(d[c] * weight, axis=0) for c in range(3)]), None

    total, _ = lax.scan(body, jnp.zeros((3, mm_pos.shape[1]), jnp.float32), stacked)
    return total


def on_device(
    qm_pos,
    species,
    qm_count,
    ghost_owner,
    ghost_slot,
    mm_pos,
    mm_charge,
    species_table,
    potential_gain,
    message_weight,
    hidden_weight,
    energy_readout,
    charge_readout,
):
    rows = qm_pos.shape[1]
    blocks = lax.axis_size("blk")
    me = lax.axis_index("blk")
    kinds = species_table.shape[0]
    coupling = float(mm_pos.shape[1] * blocks * lax.axis_size("rep")) ** (-0.5)

    own = jnp.concatenate(
        [
            qm_pos,
            species.astype(jnp.float32)[None, :],
            jnp.broadcast_to(qm_count.astype(jnp.float32)[None, :], (1, rows)),
        ],
        axis=0,
    )
    known = gather_doubling(own, "blk")
    qm_all = known[:3]
    atoms = qm_all.shape[1]
    species_all = known[3].astype(jnp.int32)
    live_all = ((jnp.arange(atoms) % rows).astype(jnp.float32) < known[4]).astype(jnp.float32)

    partial = potential_pass(qm_all, mm_pos, mm_charge)
    total = sum_butterfly(sum_butterfly(partial, "rep"), "blk")
    potential_all = total[0] * coupling
    pull = lax.dynamic_slice_in_dim(total[1:4], me * rows, rows, axis=1)

    picks_all = (species_all[:, None] == jnp.arange(kinds)[None, :]).astype(jnp.bfloat16)
    base_all = jnp.dot(picks_all, species_table, preferred_element_type=jnp.float32)
    start_all = (
        live_all[:, None] * (base_all + potential_all[:, None] * potential_gain[None, :])
    ).astype(jnp.bfloat16)
    live = lax.dynamic_slice_in_dim(live_all, me * rows, rows)
    potential = lax.dynamic_slice_in_dim(potential_all, me * rows, rows)
    start = lax.dynamic_slice_in_dim(start_all, me * rows, rows, axis=0)

    ghost = ghost_owner * rows + ghost_slot
    columns = jnp.arange(atoms)[None, :]
    links = jnp.zeros((rows, atoms), jnp.bfloat16)
    for k in range(ghost.shape[1]):
        links = links + (ghost[:, k : k + 1] == columns).astype(jnp.bfloat16)
    neighbour = jnp.dot(links, start_all, preferred_element_type=jnp.float32).astype(jnp.bfloat16)

    mixed = start.astype(jnp.float32) + jnp.dot(
        neighbour, message_weight, preferred_element_type=jnp.float32
    )
    before = jnp.dot(mixed.astype(jnp.bfloat16), hidden_weight, preferred_element_type=jnp.float32)
    sigma = jax.nn.sigmoid(before)
    active = before * sigma
    energy_part = live * jnp.sum(active * energy_readout[None, :], axis=1)
    charge_part = live * jnp.sum(active * charge_readout[None, :], axis=1)
    atom_energy = energy_part + charge_part * potential
    back_active = live[:, None] * (
        energy_readout[None, :] + potential[:, None] * charge_readout[None, :]
    )
    back_before = (back_active * sigma * (1.0 + before * (1.0 - sigma))).astype(jnp.bfloat16)
    back_mixed = jnp.dot(back_before, hidden_weight.T, preferred_element_type=jnp.float32)
    back_sum = jnp.dot(
        back_mixed.astype(jnp.bfloat16), message_weight.T, preferred_element_type=jnp.float32
    ).astype(jnp.bfloat16)

    sent = jnp.sum(back_sum.astype(jnp.float32) * potential_gain[None, :], axis=1)
    spread = jnp.sum(links.astype(jnp.float32) * sent[:, None], axis=0) * live_all
    local = charge_part + live * jnp.sum(back_mixed * potential_gain[None, :], axis=1)
    placed = (jnp.arange(atoms) // rows == me).astype(jnp.float32)
    local_all = jnp.tile(local, atoms // rows) * placed
    effective_all = sum_butterfly(spread + local_all, "blk")
    effective = lax.dynamic_slice_in_dim(effective_all, me * rows, rows)

    qm_force = pull * (effective * coupling)[None, :]
    mm_force = force_pass(qm_all, effective_all, mm_pos) * (-coupling * mm_charge)[None, :]
    return (atom_energy, qm_force, mm_force)


def solution(mesh):
    placed = (
        P(None, "blk"),
        P("blk"),
        P("blk"),
        P("blk", None),
        P("blk", None),
        P(None, ("blk", "rep")),
        P(("blk", "rep")),
        P(),
        P(),
        P(),
        P(),
        P(),
        P(),
    )
    return jax.shard_map(
        on_device,
        mesh=mesh,
        in_specs=placed,
        out_specs=(P("blk"), P(None, "blk"), P(None, ("blk", "rep"))),
        check_vma=False,
    )
```

time: 308 us -> 63.2 us (0.21); the launches traced: 305 us -> 62.9 us
  local copies, waits for them, and re-layouts: 136 us -> 2.91 us
  blocking collectives: 63.5 us -> 0 us
  waiting for transfers between devices: 62.3 us -> 21.6 us
  starting transfers between devices: 10.7 us -> 24.1 us
  between operations: 15 us -> 1.61 us
  other arithmetic: 14.6 us -> 9.17 us
    scatter x2 -> x0, local copies, waits for them, and re-layouts: 123 us -> none  [the longest x1 70.1 us: on_device(): jnp.zeros((blocks, capacity), jnp.int32).at[owners, ranks].set(slots)]
    unnamed x2 -> x0, waiting for transfers between devices: 54.2 us -> none
    all_gather x2 -> x0, blocking collectives: 40.8 us -> none  [the longest x1 22.1 us: on_device(): lax.all_gather(mm_stack, 'blk', axis=1, tiled=True)]
    ppermute x0 -> x13, starting transfers between devices: none -> 24.1 us  [the longest x9 15.6 us: sum_butterfly(): x = x + lax.ppermute(x, axis, [(i, i ^ step) for i in range(n)])]
    ppermute x0 -> x13, waiting for transfers between devices: none -> 21.6 us  [the longest x9 15.5 us: sum_butterfly(): x = x + lax.ppermute(x, axis, [(i, i ^ step) for i in range(n)])]
    all_to_all x1 -> x0, blocking collectives: 12.8 us -> none  [on_device(): lax.all_to_all(outgoing, 'blk', split_axis=0, concat_axis=0, tiled=True)]
    all_to_all x2 -> x0, starting transfers between devices: 10.6 us -> none  [the longest x1 7.09 us: on_device(): lax.all_to_all(request, 'blk', split_axis=0, concat_axis=0, tiled=True)]
    psum x2 -> x0, blocking collectives: 9.88 us -> none  [the longest x1 4.94 us: on_device(): potential = lax.psum(partial_sum, 'rep') * coupling]
  transfers between devices with their start and end apart: 3 -> 13, of which waited for: 2 -> 13; matrix products, arithmetic and copies ran while one was open for 2% -> 0% of each run, Pallas kernels for 0% -> 0%
where the time goes in v1:
time: 63.2 us; the launch traced here: 62.9 us
  starting transfers between devices  24.1 us (38%)
  waiting for transfers between devices  21.6 us (34%)
  other arithmetic  9.17 us (15%)
  matrix products  3.3 us (5%)
  local copies, waits for them, and re-layouts  2.91 us (5%)
  between operations  1.61 us (3%)
    ppermute x9, starting transfers between devices, sum_butterfly(): x = x + lax.ppermute(x, axis, [(i, i ^ step) for i in range(n)])  15.6 us
    ppermute x9, waiting for transfers between devices, sum_butterfly(): x = x + lax.ppermute(x, axis, [(i, i ^ step) for i in range(n)])  15.5 us
    ppermute x4, starting transfers between devices, gather_doubling(): other = lax.ppermute(x, axis, [(i, i ^ step) for i in range(n)])  8.55 us
    ppermute x4, waiting for transfers between devices, gather_doubling(): other = lax.ppermute(x, axis, [(i, i ^ step) for i in range(n)])  6 us
    reduce_sum x4, other arithmetic, body(): jnp.sum(weighted, axis=0)  3.21 us
    reduce_sum x4, other arithmetic, body(): jnp.sum(d[c] * weight, axis=0)  3.03 us
    unnamed x24, local copies, waits for them, and re-layouts  2.72 us
    dot_general x1, matrix products, on_device(): jnp.dot(picks_all, species_table, preferred_element_type=jnp.float32)  1.8 us
  transfers between devices with their start and end apart: 13, of which 13 were waited for; matrix products, arithmetic and copies ran while one was open for 0% of the time, Pallas kernels for 0%

profile of v1, /device:TPU:0, one launch (start us, length us, event | category | flops | bytes accessed | tf_op | source)
XLA Modules:
  0.0 62.9 jit_solution(13475575849128367015)
XLA Ops:
  4.0 2.9 %collective-permute-start.1 = (f32[5,256]{1,0:T(8,128)S(1)}, f32[5,256]{1,0:T(8,128)S(1)}, u32[]{:S(2)}, u32[]{:S(2)}) collective-permute-start(f32[5,256]{1,0:T(8,128)S(1)} %maximum_select_fusion.3), channel_id=1, source_target_pairs={{0,4},{2,6},{4,0},{6,2},{8,12},{10,14},{12,8},{14,10},{16,20},{18,... | collective-permute-start | bytes 15368 | tf_op jit(solution)/shard_map/ppermute | solution.py:15
  6.9 1.6 %collective-permute-done.1 = f32[5,256]{1,0:T(8,128)S(1)} collective-permute-done((f32[5,256]{1,0:T(8,128)S(1)}, f32[5,256]{1,0:T(8,128)S(1)}, u32[]{:S(2)}, u32[]{:S(2)}) %collective-permute-start.1) | collective-permute-done | bytes 5152 | tf_op jit(solution)/shard_map/ppermute | solution.py:15
  8.6 2.1 %collective-permute-start.2 = (f32[5,512]{1,0:T(8,128)S(1)}, f32[5,512]{1,0:T(8,128)S(1)}, u32[]{:S(2)}, u32[]{:S(2)}) collective-permute-start(f32[5,512]{1,0:T(8,128)S(1)} %maximum_select_fusion.2), channel_id=1, source_target_pairs={{0,8},{2,10},{4,12},{6,14},{8,0},{10,2},{12,4},{14,6},{16,24},{18,... | collective-permute-start | bytes 30728 | tf_op jit(solution)/shard_map/ppermute | solution.py:15
  10.7 1.7 %collective-permute-done.2 = f32[5,512]{1,0:T(8,128)S(1)} collective-permute-done((f32[5,512]{1,0:T(8,128)S(1)}, f32[5,512]{1,0:T(8,128)S(1)}, u32[]{:S(2)}, u32[]{:S(2)}) %collective-permute-start.2) | collective-permute-done | bytes 10272 | tf_op jit(solution)/shard_map/ppermute | solution.py:15
  12.4 3.0 %collective-permute-start.3 = (f32[5,1024]{1,0:T(8,128)S(1)}, f32[5,1024]{1,0:T(8,128)S(1)}, u32[]{:S(2)}, u32[]{:S(2)}) collective-permute-start(f32[5,1024]{1,0:T(8,128)S(1)} %maximum_select_fusion.1), channel_id=1, source_target_pairs={{0,16},{2,18},{4,20},{6,22},{8,24},{10,26},{12,28},{14,30},{16,0},... | collective-permute-start | bytes 61448 | tf_op jit(solution)/shard_map/ppermute | solution.py:15
  15.5 1.8 %collective-permute-done.3 = f32[5,1024]{1,0:T(8,128)S(1)} collective-permute-done((f32[5,1024]{1,0:T(8,128)S(1)}, f32[5,1024]{1,0:T(8,128)S(1)}, u32[]{:S(2)}, u32[]{:S(2)}) %collective-permute-start.3) | collective-permute-done | bytes 20512 | tf_op jit(solution)/shard_map/ppermute | solution.py:15
  18.0 3.5 %while.21 = (s32[]{:T(128)}, f32[4,4,512]{2,1,0:T(4,128)S(1)}, f32[4,3,512]{2,1,0:T(4,128)S(1)}, f32[512,1]{0,1:T(1,128)S(1)}, f32[512,1]{0,1:T(1,128)S(1)}, /*i...) while((s32[]{:T(128)}, f32[4,4,512]{2,1,0:T(4,128)S(1)}, ...), condition=%wide.region_5.6_spmd, body=%wide.region_0.5_spmd.sunk | while | flops 4984836 | bytes 51349 | solution.py:45
  21.5 1.9 %collective-permute-start.4 = (f32[4,2048]{1,0:T(4,128)S(1)}, f32[4,2048]{1,0:T(4,128)S(1)}, u32[]{:S(2)}, u32[]{:S(2)}) collective-permute-start(f32[4,2048]{1,0:T(4,128)S(1)} %bitcast.137), channel_id=1, source_target_pairs={{0,1},{1,0},{2,3},{3,2},{4,5},{5,4},{6,7},{7,6},{8,9},{9,8},{10,11... | collective-permute-start | bytes 98312 | tf_op jit(solution)/shard_map/ppermute | solution.py:26
  23.4 2.1 %collective-permute-done.4 = f32[4,2048]{1,0:T(4,128)S(1)} collective-permute-done((f32[4,2048]{1,0:T(4,128)S(1)}, f32[4,2048]{1,0:T(4,128)S(1)}, u32[]{:S(2)}, u32[]{:S(2)}) %collective-permute-start.4) | collective-permute-done | bytes 32800 | tf_op jit(solution)/shard_map/ppermute | solution.py:26
  25.6 1.2 %collective-permute-done.5 = f32[4,2048]{1,0:T(4,128)S(1)} collective-permute-done((f32[4,2048]{1,0:T(4,128)S(1)}, f32[4,2048]{1,0:T(4,128)S(1)}, u32[]{:S(2)}, u32[]{:S(2)}) %collective-permute-start.5) | collective-permute-done | bytes 32800 | tf_op jit(solution)/shard_map/ppermute | solution.py:26
  26.8 1.9 %collective-permute-start.6 = (f32[4,2048]{1,0:T(4,128)S(1)}, f32[4,2048]{1,0:T(4,128)S(1)}, u32[]{:S(2)}, u32[]{:S(2)}) collective-permute-start(f32[4,2048]{1,0:T(4,128)S(1)} %add.135), channel_id=1, source_target_pairs={{0,4},{2,6},{4,0},{6,2},{8,12},{10,14},{12,8},{14,10},{16,20},{18,... | collective-permute-start | bytes 98312 | tf_op jit(solution)/shard_map/ppermute | solution.py:26
  28.7 2.1 %collective-permute-done.6 = f32[4,2048]{1,0:T(4,128)S(1)} collective-permute-done((f32[4,2048]{1,0:T(4,128)S(1)}, f32[4,2048]{1,0:T(4,128)S(1)}, u32[]{:S(2)}, u32[]{:S(2)}) %collective-permute-start.6) | collective-permute-done | bytes 32800 | tf_op jit(solution)/shard_map/ppermute | solution.py:26
  30.8 2.0 %collective-permute-start.7 = (f32[4,2048]{1,0:T(4,128)S(1)}, f32[4,2048]{1,0:T(4,128)S(1)}, u32[]{:S(2)}, u32[]{:S(2)}) collective-permute-start(f32[4,2048]{1,0:T(4,128)S(1)} %add.136), channel_id=1, source_target_pairs={{0,8},{2,10},{4,12},{6,14},{8,0},{10,2},{12,4},{14,6},{16,24},{18,... | collective-permute-start | bytes 98312 | tf_op jit(solution)/shard_map/ppermute | solution.py:26
  32.8 2.0 %collective-permute-done.7 = f32[4,2048]{1,0:T(4,128)S(1)} collective-permute-done((f32[4,2048]{1,0:T(4,128)S(1)}, f32[4,2048]{1,0:T(4,128)S(1)}, u32[]{:S(2)}, u32[]{:S(2)}) %collective-permute-start.7) | collective-permute-done | bytes 32800 | tf_op jit(solution)/shard_map/ppermute | solution.py:26
  34.8 3.0 %collective-permute-start.8 = (f32[4,2048]{1,0:T(4,128)S(1)}, f32[4,2048]{1,0:T(4,128)S(1)}, u32[]{:S(2)}, u32[]{:S(2)}) collective-permute-start(f32[4,2048]{1,0:T(4,128)S(1)} %add.137), channel_id=1, source_target_pairs={{0,16},{2,18},{4,20},{6,22},{8,24},{10,26},{12,28},{14,30},{16,0},... | collective-permute-start | bytes 98312 | tf_op jit(solution)/shard_map/ppermute | solution.py:26
  37.8 1.9 %collective-permute-done.8 = f32[4,2048]{1,0:T(4,128)S(1)} collective-permute-done((f32[4,2048]{1,0:T(4,128)S(1)}, f32[4,2048]{1,0:T(4,128)S(1)}, u32[]{:S(2)}, u32[]{:S(2)}) %collective-permute-start.8) | collective-permute-done | bytes 32800 | tf_op jit(solution)/shard_map/ppermute | solution.py:26
  40.4 1.8 %fusion.17 = bf16[2048,128]{1,0:T(8,128)(2,1)S(1)} fusion(bf16[8,128]{1,0:T(8,128)(2,1)S(1)} %copy-done.7, f32[128]{0:T(128)S(1)} %copy-done.11, f32[2048]{0:T(1024)S(1)} %bitcast.141, s32[2048]{0:T(1024)S(1)} %bitcast.142, f32[2048]{0:T(1024)S(1)} %get-tuple-element.120), kind=kOutput, calls=%fused_computation.39 | convolution fusion | flops 5259264 | bytes 551424 | tf_op jit(solution)/shard_map/dot_general | solution.py:105
  46.4 1.8 %collective-permute-start.10 = (f32[2048]{0:T(1024)S(1)}, f32[2048]{0:T(1024)S(1)}, u32[]{:S(2)}, u32[]{:S(2)}) collective-permute-start(f32[2048]{0:T(1024)S(1)} %add.151), channel_id=1, source_target_pairs={{0,4},{2,6},{4,0},{6,2},{8,12},{10,14},{12,8},{14,10},{16,20},{18,... | collective-permute-start | bytes 24584 | tf_op jit(solution)/shard_map/ppermute | solution.py:26
  48.2 1.8 %collective-permute-done.10 = f32[2048]{0:T(1024)S(1)} collective-permute-done((f32[2048]{0:T(1024)S(1)}, f32[2048]{0:T(1024)S(1)}, u32[]{:S(2)}, u32[]{:S(2)}) %collective-permute-start.10) | collective-permute-done | bytes 8224 | tf_op jit(solution)/shard_map/ppermute | solution.py:26
  50.0 1.9 %collective-permute-start.11 = (f32[2048]{0:T(1024)S(1)}, f32[2048]{0:T(1024)S(1)}, u32[]{:S(2)}, u32[]{:S(2)}) collective-permute-start(f32[2048]{0:T(1024)S(1)} %add.152), channel_id=1, source_target_pairs={{0,8},{2,10},{4,12},{6,14},{8,0},{10,2},{12,4},{14,6},{16,24},{18,... | collective-permute-start | bytes 24584 | tf_op jit(solution)/shard_map/ppermute | solution.py:26
  51.9 1.8 %collective-permute-done.11 = f32[2048]{0:T(1024)S(1)} collective-permute-done((f32[2048]{0:T(1024)S(1)}, f32[2048]{0:T(1024)S(1)}, u32[]{:S(2)}, u32[]{:S(2)}) %collective-permute-start.11) | collective-permute-done | bytes 8224 | tf_op jit(solution)/shard_map/ppermute | solution.py:26
  53.7 2.9 %collective-permute-start.12 = (f32[2048]{0:T(1024)S(1)}, f32[2048]{0:T(1024)S(1)}, u32[]{:S(2)}, u32[]{:S(2)}) collective-permute-start(f32[2048]{0:T(1024)S(1)} %add.153), channel_id=1, source_target_pairs={{0,16},{2,18},{4,20},{6,22},{8,24},{10,26},{12,28},{14,30},{16,0},... | collective-permute-start | bytes 24584 | tf_op jit(solution)/shard_map/ppermute | solution.py:26
  56.6 1.6 %collective-permute-done.12 = f32[2048]{0:T(1024)S(1)} collective-permute-done((f32[2048]{0:T(1024)S(1)}, f32[2048]{0:T(1024)S(1)}, u32[]{:S(2)}, u32[]{:S(2)}) %collective-permute-start.12) | collective-permute-done | bytes 8224 | tf_op jit(solution)/shard_map/ppermute | solution.py:26
  58.3 3.4 %while.22 = (s32[]{:T(128)}, f32[3,512]{1,0:T(4,128)S(1)}, f32[4,512,4]{1,2,0:T(4,128)S(1)}, f32[3,512]{1,0:T(4,128)S(1)}, s32[]{:T(128)}, /*index=5*/s32[]{:T(128)}) while((s32[]{:T(128)}, f32[3,512]{1,0:T(4,128)S(1)}, f32[4,512,4]{1,2,0:T(4,128)S(1)}, f32[3,512]{1,0:T(4,128)S(1)}, s32[]{:T(128)}, /*index=5*/s32[]{:T(128)}) %tuple.82), condition=%wide.region_15.16_spmd.clone, body=%wide.region_11.15_spmd.clone.sunk | while | flops 4723203 | bytes 84051 | solution.py:60
  (100 shorter events, 16.2 us)
Async XLA Ops:
  0.6 42.4 %copy-start = (bf16[128,256]{1,0:T(8,128)(2,1)S(1)}, bf16[128,256]{1,0:T(8,128)(2,1)}, u32[]{:S(2)}) copy-start(bf16[128,256]{1,0:T(8,128)(2,1)} %param.27) | copy-start | bytes 196612
  2.0 0.7 %copy-start.2 = (f32[3,128]{1,0:T(4,128)S(1)}, f32[3,128]{1,0:T(4,128)}, u32[]{:S(2)}) copy-start(f32[3,128]{1,0:T(4,128)} %param.17) | copy-start | bytes 4612
  2.7 1.3 %collective-permute-start = (f32[5,128]{1,0:T(8,128)S(1)}, f32[5,128]{1,0:T(8,128)S(1)}, u32[]{:S(2)}, u32[]{:S(2)}) collective-permute-start(f32[5,128]{1,0:T(8,128)S(1)} %pad_maximum_fusion), channel_id=1, source_target_pairs={{0,2},{2,0},{4,6},{6,4},{8,10},{10,8},{12,14},{14,12},{16,18},{18,... | collective-permute-start | bytes 7688 | tf_op jit(solution)/shard_map/ppermute | solution.py:15
  4.0 4.6 %collective-permute-start.1 = (f32[5,256]{1,0:T(8,128)S(1)}, f32[5,256]{1,0:T(8,128)S(1)}, u32[]{:S(2)}, u32[]{:S(2)}) collective-permute-start(f32[5,256]{1,0:T(8,128)S(1)} %maximum_select_fusion.3), channel_id=1, source_target_pairs={{0,4},{2,6},{4,0},{6,2},{8,12},{10,14},{12,8},{14,10},{16,20},{18,... | collective-permute-start | bytes 15368 | tf_op jit(solution)/shard_map/ppermute | solution.py:15
  8.6 3.8 %collective-permute-start.2 = (f32[5,512]{1,0:T(8,128)S(1)}, f32[5,512]{1,0:T(8,128)S(1)}, u32[]{:S(2)}, u32[]{:S(2)}) collective-permute-start(f32[5,512]{1,0:T(8,128)S(1)} %maximum_select_fusion.2), channel_id=1, source_target_pairs={{0,8},{2,10},{4,12},{6,14},{8,0},{10,2},{12,4},{14,6},{16,24},{18,... | collective-permute-start | bytes 30728 | tf_op jit(solution)/shard_map/ppermute | solution.py:15
  10.7 4.8 %copy-start.1 = (f32[3,512]{1,0:T(4,128)S(1)}, f32[3,512]{1,0:T(4,128)}, u32[]{:S(2)}) copy-start(f32[3,512]{1,0:T(4,128)} %param.22) | copy-start | bytes 18436
  12.4 4.9 %collective-permute-start.3 = (f32[5,1024]{1,0:T(8,128)S(1)}, f32[5,1024]{1,0:T(8,128)S(1)}, u32[]{:S(2)}, u32[]{:S(2)}) collective-permute-start(f32[5,1024]{1,0:T(8,128)S(1)} %maximum_select_fusion.1), channel_id=1, source_target_pairs={{0,16},{2,18},{4,20},{6,22},{8,24},{10,26},{12,28},{14,30},{16,0},... | collective-permute-start | bytes 61448 | tf_op jit(solution)/shard_map/ppermute | solution.py:15
  17.3 0.7 %copy-start.5 = (f32[512]{0:T(512)S(1)}, f32[512]{0:T(512)}, u32[]{:S(2)}) copy-start(f32[512]{0:T(512)} %param.23) | copy-start | bytes 6148
  21.5 4.1 %copy-start.3 = (s32[128,4]{0,1:T(4,128)S(1)}, s32[128,4]{0,1:T(4,128)}, u32[]{:S(2)}) copy-start(s32[128,4]{0,1:T(4,128)} %param.21) | copy-start | bytes 6148
  21.5 4.1 %copy-start.4 = (s32[128,4]{0,1:T(4,128)S(1)}, s32[128,4]{0,1:T(4,128)}, u32[]{:S(2)}) copy-start(s32[128,4]{0,1:T(4,128)} %param.20) | copy-start | bytes 6148
  21.5 4.0 %collective-permute-start.4 = (f32[4,2048]{1,0:T(4,128)S(1)}, f32[4,2048]{1,0:T(4,128)S(1)}, u32[]{:S(2)}, u32[]{:S(2)}) collective-permute-start(f32[4,2048]{1,0:T(4,128)S(1)} %bitcast.137), channel_id=1, source_target_pairs={{0,1},{1,0},{2,3},{3,2},{4,5},{5,4},{6,7},{7,6},{8,9},{9,8},{10,11... | collective-permute-start | bytes 98312 | tf_op jit(solution)/shard_map/ppermute | solution.py:26
  25.5 1.3 %collective-permute-start.5 = (f32[4,2048]{1,0:T(4,128)S(1)}, f32[4,2048]{1,0:T(4,128)S(1)}, u32[]{:S(2)}, u32[]{:S(2)}) collective-permute-start(f32[4,2048]{1,0:T(4,128)S(1)} %add.134), channel_id=1, source_target_pairs={{0,2},{2,0},{4,6},{6,4},{8,10},{10,8},{12,14},{14,12},{16,18},{18,... | collective-permute-start | bytes 98312 | tf_op jit(solution)/shard_map/ppermute | solution.py:26
  26.8 4.0 %collective-permute-start.6 = (f32[4,2048]{1,0:T(4,128)S(1)}, f32[4,2048]{1,0:T(4,128)S(1)}, u32[]{:S(2)}, u32[]{:S(2)}) collective-permute-start(f32[4,2048]{1,0:T(4,128)S(1)} %add.135), channel_id=1, source_target_pairs={{0,4},{2,6},{4,0},{6,2},{8,12},{10,14},{12,8},{14,10},{16,20},{18,... | collective-permute-start | bytes 98312 | tf_op jit(solution)/shard_map/ppermute | solution.py:26
  30.8 4.0 %collective-permute-start.7 = (f32[4,2048]{1,0:T(4,128)S(1)}, f32[4,2048]{1,0:T(4,128)S(1)}, u32[]{:S(2)}, u32[]{:S(2)}) collective-permute-start(f32[4,2048]{1,0:T(4,128)S(1)} %add.136), channel_id=1, source_target_pairs={{0,8},{2,10},{4,12},{6,14},{8,0},{10,2},{12,4},{14,6},{16,24},{18,... | collective-permute-start | bytes 98312 | tf_op jit(solution)/shard_map/ppermute | solution.py:26
  34.8 4.9 %collective-permute-start.8 = (f32[4,2048]{1,0:T(4,128)S(1)}, f32[4,2048]{1,0:T(4,128)S(1)}, u32[]{:S(2)}, u32[]{:S(2)}) collective-permute-start(f32[4,2048]{1,0:T(4,128)S(1)} %add.137), channel_id=1, source_target_pairs={{0,16},{2,18},{4,20},{6,22},{8,24},{10,26},{12,28},{14,30},{16,0},... | collective-permute-start | bytes 98312 | tf_op jit(solution)/shard_map/ppermute | solution.py:26
  39.7 0.7 %copy-start.7 = (bf16[8,128]{1,0:T(8,128)(2,1)S(1)}, bf16[8,128]{1,0:T(8,128)(2,1)}, u32[]{:S(2)}) copy-start(bf16[8,128]{1,0:T(8,128)(2,1)} %param.24) | copy-start | bytes 6148
  39.7 0.7 %copy-start.11 = (f32[128]{0:T(128)S(1)}, f32[128]{0:T(128)}, u32[]{:S(2)}) copy-start(f32[128]{0:T(128)} %param.25) | copy-start | bytes 1540
  40.4 1.8 %copy-start.6 = (bf16[128,128]{1,0:T(8,128)(2,1)S(1)}, bf16[128,128]{1,0:T(8,128)(2,1)}, u32[]{:S(2)}) copy-start(bf16[128,128]{1,0:T(8,128)(2,1)} %param.26) | copy-start | bytes 98308
  42.2 0.8 %copy-start.8 = (f32[256]{0:T(256)S(1)}, f32[256]{0:T(256)}, u32[]{:S(2)}) copy-start(f32[256]{0:T(256)} %param.29) | copy-start | bytes 3076
  42.2 0.8 %copy-start.9 = (f32[256]{0:T(256)S(1)}, f32[256]{0:T(256)}, u32[]{:S(2)}) copy-start(f32[256]{0:T(256)} %param.28) | copy-start | bytes 3076
  45.1 1.2 %collective-permute-start.9 = (f32[2048]{0:T(1024)S(1)}, f32[2048]{0:T(1024)S(1)}, u32[]{:S(2)}, u32[]{:S(2)}) collective-permute-start(f32[2048]{0:T(1024)S(1)} %fusion.39), channel_id=1, source_target_pairs={{0,2},{2,0},{4,6},{6,4},{8,10},{10,8},{12,14},{14,12},{16,18},{18,... | collective-permute-start | bytes 24584 | tf_op jit(solution)/shard_map/ppermute | solution.py:26
  46.4 3.7 %collective-permute-start.10 = (f32[2048]{0:T(1024)S(1)}, f32[2048]{0:T(1024)S(1)}, u32[]{:S(2)}, u32[]{:S(2)}) collective-permute-start(f32[2048]{0:T(1024)S(1)} %add.151), channel_id=1, source_target_pairs={{0,4},{2,6},{4,0},{6,2},{8,12},{10,14},{12,8},{14,10},{16,20},{18,... | collective-permute-start | bytes 24584 | tf_op jit(solution)/shard_map/ppermute | solution.py:26
  50.0 3.7 %collective-permute-start.11 = (f32[2048]{0:T(1024)S(1)}, f32[2048]{0:T(1024)S(1)}, u32[]{:S(2)}, u32[]{:S(2)}) collective-permute-start(f32[2048]{0:T(1024)S(1)} %add.152), channel_id=1, source_target_pairs={{0,8},{2,10},{4,12},{6,14},{8,0},{10,2},{12,4},{14,6},{16,24},{18,... | collective-permute-start | bytes 24584 | tf_op jit(solution)/shard_map/ppermute | solution.py:26
  53.7 4.5 %collective-permute-start.12 = (f32[2048]{0:T(1024)S(1)}, f32[2048]{0:T(1024)S(1)}, u32[]{:S(2)}, u32[]{:S(2)}) collective-permute-start(f32[2048]{0:T(1024)S(1)} %add.153), channel_id=1, source_target_pairs={{0,16},{2,18},{4,20},{6,22},{8,24},{10,26},{12,28},{14,30},{16,0},... | collective-permute-start | bytes 24584 | tf_op jit(solution)/shard_map/ppermute | solution.py:26
  (1 other events, 0.7 us)

commit v2 on v1

--- a/solution.py
+++ b/solution.py
@@ -7,11 +7,12 @@
 CHUNK = 512
 
 
-def gather_doubling(x, axis):
+def gather_doubling(x, axis, first=1, last=None):
     n = lax.axis_size(axis)
+    last = n if last is None else last
     me = lax.axis_index(axis)
-    step = 1
-    while step < n:
+    step = first
+    while step < last:
         other = lax.ppermute(x, axis, [(i, i ^ step) for i in range(n)])
         low = (me // step) % 2 == 0
         x = jnp.where(low, jnp.concatenate([x, other], -1), jnp.concatenate([other, x], -1))
@@ -19,31 +20,33 @@
     return x
 
 
-def sum_butterfly(x, axis):
+def sum_butterfly(x, axis, last=None):
     n = lax.axis_size(axis)
+    last = n if last is None else last
     step = 1
-    while step < n:
+    while step < last:
         x = x + lax.ppermute(x, axis, [(i, i ^ step) for i in range(n)])
         step *= 2
     return x
 
 
-def potential_pass(qm_all, mm_pos, mm_charge):
-    mm_col = [mm_pos[c][:, None] for c in range(3)]
-    q_col = mm_charge[:, None]
-    chunks = qm_all.shape[1] // CHUNK
+def potential_pass(qm_some, mm_some):
+    chunks = mm_some.shape[1] // CHUNK
+    cols = [qm_some[c][None, :] for c in range(3)]
 
-    def body(block):
-        d = [block[c][None, :] - mm_col[c] for c in range(3)]
+    def body(running, block):
+        d = [cols[c] - block[:, c : c + 1] for c in range(3)]
         inverse = lax.rsqrt(d[0] * d[0] + d[1] * d[1] + d[2] * d[2] + SOFTEN)
-        weighted = inverse * q_col
+        weighted = inverse * block[:, 3:4]
         cubed = weighted * inverse * inverse
-        return jnp.stack(
+        part = jnp.stack(
             [jnp.sum(weighted, axis=0)] + [jnp.sum(d[c] * cubed, axis=0) for c in range(3)]
         )
+        return running + part, None
 
-    parts = lax.map(body, jnp.transpose(qm_all.reshape(3, chunks, CHUNK), (1, 0, 2)))
-    return jnp.transpose(parts, (1, 0, 2)).reshape(4, qm_all.shape[1])
+    stacked = jnp.transpose(mm_some.reshape(4, chunks, CHUNK), (1, 2, 0))
+    total, _ = lax.scan(body, jnp.zeros((4, qm_some.shape[1]), jnp.float32), stacked)
+    return total
 
 
 def force_pass(qm_all, effective, mm_pos):
@@ -82,6 +85,9 @@
     kinds = species_table.shape[0]
     coupling = float(mm_pos.shape[1] * blocks * lax.axis_size("rep")) ** (-0.5)
 
+    low_blocks = 1
+    while low_blocks * low_blocks < blocks:
+        low_blocks *= 2
     own = jnp.concatenate(
         [
             qm_pos,
@@ -90,16 +96,21 @@
         ],
         axis=0,
     )
-    known = gather_doubling(own, "blk")
-    qm_all = known[:3]
+    near = gather_doubling(own, "blk", 1, low_blocks)
+    mm_some = gather_doubling(
+        jnp.concatenate([mm_pos, mm_charge[None, :]], axis=0), "blk", low_blocks, blocks
+    )
+    partial = potential_pass(near[:3], mm_some)
+    total = sum_butterfly(sum_butterfly(partial, "rep"), "blk", low_blocks)
+    pull = lax.dynamic_slice_in_dim(total[1:4], (me % low_blocks) * rows, rows, axis=1)
+    known = gather_doubling(
+        jnp.concatenate([total[0:1] * coupling, near], axis=0), "blk", low_blocks, blocks
+    )
+    potential_all = known[0]
+    qm_all = known[1:4]
     atoms = qm_all.shape[1]
-    species_all = known[3].astype(jnp.int32)
-    live_all = ((jnp.arange(atoms) % rows).astype(jnp.float32) < known[4]).astype(jnp.float32)
-
-    partial = potential_pass(qm_all, mm_pos, mm_charge)
-    total = sum_butterfly(sum_butterfly(partial, "rep"), "blk")
-    potential_all = total[0] * coupling
-    pull = lax.dynamic_slice_in_dim(total[1:4], me * rows, rows, axis=1)
+    species_all = known[4].astype(jnp.int32)
+    live_all = ((jnp.arange(atoms) % rows).astype(jnp.float32) < known[5]).astype(jnp.float32)
 
     picks_all = (species_all[:, None] == jnp.arange(kinds)[None, :]).astype(jnp.bfloat16)
     base_all = jnp.dot(picks_all, species_table, preferred_element_type=jnp.float32)

time: 63.2 us -> 58.3 us (0.922)
  starting transfers between devices: 24.1 us -> 18 us
  waiting for transfers between devices: 21.6 us -> 24.3 us
  local copies, waits for them, and re-layouts: 2.91 us -> 1.27 us
    ppermute x9 -> x7, starting transfers between devices: 15.6 us -> 7.19 us  [sum_butterfly(): x = x + lax.ppermute(x, axis, [(i, i ^ step) for i in range(n)])]
    ppermute x4 -> x6, waiting for transfers between devices: 6 us -> 9.91 us  [gather_doubling(): other = lax.ppermute(x, axis, [(i, i ^ step) for i in range(n)])]
    ppermute x4 -> x6, starting transfers between devices: 8.55 us -> 10.8 us  [gather_doubling(): other = lax.ppermute(x, axis, [(i, i ^ step) for i in range(n)])]
    unnamed x24, local copies, waits for them, and re-layouts: 2.72 us -> 1.06 us
    ppermute x9 -> x7, waiting for transfers between devices: 15.5 us -> 14.4 us  [sum_butterfly(): x = x + lax.ppermute(x, axis, [(i, i ^ step) for i in range(n)])]
  transfers between devices with their start and end apart: 13 -> 13, of which waited for: 13 -> 11; matrix products, arithmetic and copies ran while one was open for 0% -> 0% of each run, Pallas kernels for 0% -> 0%
where the time goes in v2:
time: 58.3 us; the launch traced here: 58 us
  waiting for transfers between devices  24.3 us (42%)
  starting transfers between devices  18 us (31%)
  other arithmetic  9.19 us (16%)
  matrix products  3.3 us (6%)
  between operations  1.64 us (3%)
  local copies, waits for them, and re-layouts  1.27 us (2%)
    ppermute x7, waiting for transfers between devices, sum_butterfly(): x = x + lax.ppermute(x, axis, [(i, i ^ step) for i in range(n)])  14.4 us
    ppermute x6, starting transfers between devices, gather_doubling(): other = lax.ppermute(x, axis, [(i, i ^ step) for i in range(n)])  10.8 us
    ppermute x6, waiting for transfers between devices, gather_doubling(): other = lax.ppermute(x, axis, [(i, i ^ step) for i in range(n)])  9.91 us
    ppermute x7, starting transfers between devices, sum_butterfly(): x = x + lax.ppermute(x, axis, [(i, i ^ step) for i in range(n)])  7.19 us
    reduce_sum x4, other arithmetic, body(): jnp.sum(weighted, axis=0)  3.2 us
    reduce_sum x4, other arithmetic, body(): jnp.sum(d[c] * weight, axis=0)  3.04 us
    dot_general x1, matrix products, on_device(): jnp.dot(picks_all, species_table, preferred_element_type=jnp.float32)  1.8 us
  transfers between devices with their start and end apart: 13, of which 11 were waited for; matrix products, arithmetic and copies ran while one was open for 0% of the time, Pallas kernels for 0%

profile of v2, /device:TPU:0, one launch (start us, length us, event | category | flops | bytes accessed | tf_op | source)
XLA Modules:
  0.0 58.0 jit_solution(8392990306927721303)
XLA Ops:
  2.1 3.1 %collective-permute-start.2 = (f32[4,512]{1,0:T(4,128)S(1)}, f32[4,512]{1,0:T(4,128)S(1)}, u32[]{:S(2)}, u32[]{:S(2)}) collective-permute-start(f32[4,512]{1,0:T(4,128)S(1)} %pad_maximum_fusion.1), channel_id=1, source_target_pairs={{0,8},{2,10},{4,12},{6,14},{8,0},{10,2},{12,4},{14,6},{16,24},{18,... | collective-permute-start | bytes 24584 | tf_op jit(solution)/shard_map/ppermute | solution.py:16
  5.2 1.6 %collective-permute-start.1 = (f32[5,256]{1,0:T(8,128)S(1)}, f32[5,256]{1,0:T(8,128)S(1)}, u32[]{:S(2)}, u32[]{:S(2)}) collective-permute-start(f32[5,256]{1,0:T(8,128)S(1)} %maximum_select_fusion.6), channel_id=1, source_target_pairs={{0,4},{2,6},{4,0},{6,2},{8,12},{10,14},{12,8},{14,10},{16,20},{18,... | collective-permute-start | bytes 15368 | tf_op jit(solution)/shard_map/ppermute | solution.py:16
  6.8 2.1 %collective-permute-done.1 = f32[5,256]{1,0:T(8,128)S(1)} collective-permute-done((f32[5,256]{1,0:T(8,128)S(1)}, f32[5,256]{1,0:T(8,128)S(1)}, u32[]{:S(2)}, u32[]{:S(2)}) %collective-permute-start.1) | collective-permute-done | bytes 5152 | tf_op jit(solution)/shard_map/ppermute | solution.py:16
  9.0 2.7 %collective-permute-start.3 = (f32[4,1024]{1,0:T(4,128)S(1)}, f32[4,1024]{1,0:T(4,128)S(1)}, u32[]{:S(2)}, u32[]{:S(2)}) collective-permute-start(f32[4,1024]{1,0:T(4,128)S(1)} %maximum_select_fusion.5), channel_id=1, source_target_pairs={{0,16},{2,18},{4,20},{6,22},{8,24},{10,26},{12,28},{14,30},{16,0},... | collective-permute-start | bytes 49160 | tf_op jit(solution)/shard_map/ppermute | solution.py:16
  11.6 2.2 %collective-permute-done.3 = f32[4,1024]{1,0:T(4,128)S(1)} collective-permute-done((f32[4,1024]{1,0:T(4,128)S(1)}, f32[4,1024]{1,0:T(4,128)S(1)}, u32[]{:S(2)}, u32[]{:S(2)}) %collective-permute-start.3) | collective-permute-done | bytes 16416 | tf_op jit(solution)/shard_map/ppermute | solution.py:16
  13.8 3.5 %while.22 = (s32[]{:T(128)}, f32[4,512]{1,0:T(4,128)S(1)}, f32[1,512]{1,0:T(1,128)S(1)}, f32[4,512,4]{1,2,0:T(4,128)S(1)}, f32[1,512]{1,0:T(1,128)S(1)}, /*index=5*/f32[1,512]{1,0:T(1,128)S(1)}, s32[]{:T(128)}, s32[]{:T(128)}) while((s32[]{:T(128)}, f32[4,512]{1,0:T(4,128)S(1)}, f32[1,512]{1,0:T(1,128)S(1)}, ...), condition=%wide.region_5.6_spmd.clone, body=%wide.region_0.5_spmd.clone.sunk | while | flops 4988931 | bytes 79979 | solution.py:48
  13.8 0.8 %multiply_reduce_fusion.6 = (f32[512]{0:T(512)S(1)}, f32[512]{0:T(512)S(1)}, f32[512]{0:T(512)S(1)}, f32[512]{0:T(512)S(1)}) fusion(f32[512]{0:T(512)S(1)} %bitcast.127, f32[512]{0:T(512)S(1)} %bitcast.128, f32[512]{0:T(512)S(1)} %bitcast.139, f32[512]{0:T(512)S(1)} %bitcast.129, f32[512]{0:T(512)S(1)} %bitcast.140, f32[512]{0:T(512)S(1)} %bitcast.126, ...), kind=kLoop, calls=%fused_computation.1.clone.1 | loop fusion | flops 4978688 | bytes 22528 | tf_op jit(solution)/shard_map/while/body/eval_jaxpr/reduce_sum | solution.py:43
  17.3 1.6 %collective-permute-start.4 = (f32[4,512]{1,0:T(4,128)S(1)}, f32[4,512]{1,0:T(4,128)S(1)}, u32[]{:S(2)}, u32[]{:S(2)}) collective-permute-start(f32[4,512]{1,0:T(4,128)S(1)} %get-tuple-element.57), channel_id=1, source_target_pairs={{0,1},{1,0},{2,3},{3,2},{4,5},{5,4},{6,7},{7,6},{8,9},{9,8},{10,11... | collective-permute-start | bytes 24584 | tf_op jit(solution)/shard_map/ppermute | solution.py:28
  18.9 2.2 %collective-permute-done.4 = f32[4,512]{1,0:T(4,128)S(1)} collective-permute-done((f32[4,512]{1,0:T(4,128)S(1)}, f32[4,512]{1,0:T(4,128)S(1)}, u32[]{:S(2)}, u32[]{:S(2)}) %collective-permute-start.4) | collective-permute-done | bytes 8224 | tf_op jit(solution)/shard_map/ppermute | solution.py:28
  21.0 1.2 %collective-permute-done.5 = f32[4,512]{1,0:T(4,128)S(1)} collective-permute-done((f32[4,512]{1,0:T(4,128)S(1)}, f32[4,512]{1,0:T(4,128)S(1)}, u32[]{:S(2)}, u32[]{:S(2)}) %collective-permute-start.5) | collective-permute-done | bytes 8224 | tf_op jit(solution)/shard_map/ppermute | solution.py:28
  22.2 1.5 %collective-permute-start.6 = (f32[4,512]{1,0:T(4,128)S(1)}, f32[4,512]{1,0:T(4,128)S(1)}, u32[]{:S(2)}, u32[]{:S(2)}) collective-permute-start(f32[4,512]{1,0:T(4,128)S(1)} %add.138), channel_id=1, source_target_pairs={{0,4},{2,6},{4,0},{6,2},{8,12},{10,14},{12,8},{14,10},{16,20},{18,... | collective-permute-start | bytes 24584 | tf_op jit(solution)/shard_map/ppermute | solution.py:28
  23.7 2.1 %collective-permute-done.6 = f32[4,512]{1,0:T(4,128)S(1)} collective-permute-done((f32[4,512]{1,0:T(4,128)S(1)}, f32[4,512]{1,0:T(4,128)S(1)}, u32[]{:S(2)}, u32[]{:S(2)}) %collective-permute-start.6) | collective-permute-done | bytes 8224 | tf_op jit(solution)/shard_map/ppermute | solution.py:28
  26.6 3.1 %collective-permute-done.7 = f32[6,512]{1,0:T(8,128)S(1)} collective-permute-done((f32[6,512]{1,0:T(8,128)S(1)}, f32[6,512]{1,0:T(8,128)S(1)}, u32[]{:S(2)}, u32[]{:S(2)}) %collective-permute-start.7) | collective-permute-done | bytes 12320 | tf_op jit(solution)/shard_map/ppermute | solution.py:16
  29.7 2.5 %collective-permute-start.8 = (f32[6,1024]{1,0:T(8,128)S(1)}, f32[6,1024]{1,0:T(8,128)S(1)}, u32[]{:S(2)}, u32[]{:S(2)}) collective-permute-start(f32[6,1024]{1,0:T(8,128)S(1)} %maximum_select_fusion.2), channel_id=1, source_target_pairs={{0,16},{2,18},{4,20},{6,22},{8,24},{10,26},{12,28},{14,30},{16,0},... | collective-permute-start | bytes 73736 | tf_op jit(solution)/shard_map/ppermute | solution.py:16
  32.3 2.5 %collective-permute-done.8 = f32[6,1024]{1,0:T(8,128)S(1)} collective-permute-done((f32[6,1024]{1,0:T(8,128)S(1)}, f32[6,1024]{1,0:T(8,128)S(1)}, u32[]{:S(2)}, u32[]{:S(2)}) %collective-permute-start.8) | collective-permute-done | bytes 24608 | tf_op jit(solution)/shard_map/ppermute | solution.py:16
  35.5 1.8 %fusion.16 = bf16[2048,128]{1,0:T(8,128)(2,1)S(1)} fusion(bf16[8,128]{1,0:T(8,128)(2,1)S(1)} %copy-done.7, f32[128]{0:T(128)S(1)} %copy-done.11, f32[2048]{0:T(1024)S(1)} %bitcast.137, s32[2048]{0:T(1024)S(1)} %bitcast.138, f32[2048]{0:T(1024)S(1)} %get-tuple-element.127), kind=kOutput, calls=%fused_computation.36 | convolution fusion | flops 5259264 | bytes 551424 | tf_op jit(solution)/shard_map/dot_general | solution.py:116
  37.4 0.8 %fusion.17 = bf16[128,128]{1,0:T(8,128)(2,1)S(1)} fusion(bf16[128,128]{1,0:T(8,128)(2,1)S(1)} %copy-done.6, bf16[2048,128]{1,0:T(8,128)(2,1)S(1)} %fusion.16, s32[128]{0:T(128)S(1)} %get-tuple-element.147, s32[128]{0:T(128)S(1)} %get-tuple-element.148, s32[128]{0:T(128)S(1)} %get-tuple-element.149, s32[128]{0:T(128)S(1)} %get-tuple-element.146, ...), kind=kOutput, calls=%fused_computation.38 | convolution fusion | flops 75563008 | bytes 624644 | tf_op jit(solution)/shard_map/dot_general | solution.py:131
  40.3 1.2 %collective-permute-done.9 = f32[2048]{0:T(1024)S(1)} collective-permute-done((f32[2048]{0:T(1024)S(1)}, f32[2048]{0:T(1024)S(1)}, u32[]{:S(2)}, u32[]{:S(2)}) %collective-permute-start.9) | collective-permute-done | bytes 8224 | tf_op jit(solution)/shard_map/ppermute | solution.py:28
  41.5 1.5 %collective-permute-start.10 = (f32[2048]{0:T(1024)S(1)}, f32[2048]{0:T(1024)S(1)}, u32[]{:S(2)}, u32[]{:S(2)}) collective-permute-start(f32[2048]{0:T(1024)S(1)} %add.155), channel_id=1, source_target_pairs={{0,4},{2,6},{4,0},{6,2},{8,12},{10,14},{12,8},{14,10},{16,20},{18,... | collective-permute-start | bytes 24584 | tf_op jit(solution)/shard_map/ppermute | solution.py:28
  43.0 2.1 %collective-permute-done.10 = f32[2048]{0:T(1024)S(1)} collective-permute-done((f32[2048]{0:T(1024)S(1)}, f32[2048]{0:T(1024)S(1)}, u32[]{:S(2)}, u32[]{:S(2)}) %collective-permute-start.10) | collective-permute-done | bytes 8224 | tf_op jit(solution)/shard_map/ppermute | solution.py:28
  45.4 3.4 %collective-permute-done.11 = f32[2048]{0:T(1024)S(1)} collective-permute-done((f32[2048]{0:T(1024)S(1)}, f32[2048]{0:T(1024)S(1)}, u32[]{:S(2)}, u32[]{:S(2)}) %collective-permute-start.11) | collective-permute-done | bytes 8224 | tf_op jit(solution)/shard_map/ppermute | solution.py:28
  48.8 2.3 %collective-permute-start.12 = (f32[2048]{0:T(1024)S(1)}, f32[2048]{0:T(1024)S(1)}, u32[]{:S(2)}, u32[]{:S(2)}) collective-permute-start(f32[2048]{0:T(1024)S(1)} %add.157), channel_id=1, source_target_pairs={{0,16},{2,18},{4,20},{6,22},{8,24},{10,26},{12,28},{14,30},{16,0},... | collective-permute-start | bytes 24584 | tf_op jit(solution)/shard_map/ppermute | solution.py:28
  51.1 2.2 %collective-permute-done.12 = f32[2048]{0:T(1024)S(1)} collective-permute-done((f32[2048]{0:T(1024)S(1)}, f32[2048]{0:T(1024)S(1)}, u32[]{:S(2)}, u32[]{:S(2)}) %collective-permute-start.12) | collective-permute-done | bytes 8224 | tf_op jit(solution)/shard_map/ppermute | solution.py:28
  53.5 3.4 %while.23 = (s32[]{:T(128)}, f32[3,512]{1,0:T(4,128)S(1)}, f32[4,512,4]{1,2,0:T(4,128)S(1)}, f32[3,512]{1,0:T(4,128)S(1)}, s32[]{:T(128)}, /*index=5*/s32[]{:T(128)}) while((s32[]{:T(128)}, f32[3,512]{1,0:T(4,128)S(1)}, f32[4,512,4]{1,2,0:T(4,128)S(1)}, f32[3,512]{1,0:T(4,128)S(1)}, s32[]{:T(128)}, /*index=5*/s32[]{:T(128)}) %tuple.86), condition=%wide.region_15.16_spmd.clone, body=%wide.region_11.15_spmd.clone.sunk | while | flops 4723203 | bytes 84059 | solution.py:63
  (108 shorter events, 11.6 us)
Async XLA Ops:
  0.6 37.6 %copy-start = (bf16[128,256]{1,0:T(8,128)(2,1)S(1)}, bf16[128,256]{1,0:T(8,128)(2,1)}, u32[]{:S(2)}) copy-start(bf16[128,256]{1,0:T(8,128)(2,1)} %param.27) | copy-start | bytes 196612
  0.6 0.7 %copy-start.10 = (s32[128]{0:T(128)S(1)}, s32[128]{0:T(128)}, u32[]{:S(2)}) copy-start(s32[128]{0:T(128)} %param.18) | copy-start | bytes 1540
  0.7 0.7 %copy-start.3 = (f32[3,128]{1,0:T(4,128)S(1)}, f32[3,128]{1,0:T(4,128)}, u32[]{:S(2)}) copy-start(f32[3,128]{1,0:T(4,128)} %param.17) | copy-start | bytes 4612
  1.3 0.7 %copy-start.1 = (f32[3,512]{1,0:T(4,128)S(1)}, f32[3,512]{1,0:T(4,128)}, u32[]{:S(2)}) copy-start(f32[3,512]{1,0:T(4,128)} %param.22) | copy-start | bytes 18436
  1.4 0.7 %copy-start.2 = (f32[512]{0:T(512)S(1)}, f32[512]{0:T(512)}, u32[]{:S(2)}) copy-start(f32[512]{0:T(512)} %param.23) | copy-start | bytes 6148
  1.4 3.8 %collective-permute-start = (f32[5,128]{1,0:T(8,128)S(1)}, f32[5,128]{1,0:T(8,128)S(1)}, u32[]{:S(2)}, u32[]{:S(2)}) collective-permute-start(f32[5,128]{1,0:T(8,128)S(1)} %pad_maximum_fusion.2), channel_id=1, source_target_pairs={{0,2},{2,0},{4,6},{6,4},{8,10},{10,8},{12,14},{14,12},{16,18},{18,... | collective-permute-start | bytes 7688 | tf_op jit(solution)/shard_map/ppermute | solution.py:16
  2.1 6.8 %collective-permute-start.2 = (f32[4,512]{1,0:T(4,128)S(1)}, f32[4,512]{1,0:T(4,128)S(1)}, u32[]{:S(2)}, u32[]{:S(2)}) collective-permute-start(f32[4,512]{1,0:T(4,128)S(1)} %pad_maximum_fusion.1), channel_id=1, source_target_pairs={{0,8},{2,10},{4,12},{6,14},{8,0},{10,2},{12,4},{14,6},{16,24},{18,... | collective-permute-start | bytes 24584 | tf_op jit(solution)/shard_map/ppermute | solution.py:16
  5.2 3.7 %collective-permute-start.1 = (f32[5,256]{1,0:T(8,128)S(1)}, f32[5,256]{1,0:T(8,128)S(1)}, u32[]{:S(2)}, u32[]{:S(2)}) collective-permute-start(f32[5,256]{1,0:T(8,128)S(1)} %maximum_select_fusion.6), channel_id=1, source_target_pairs={{0,4},{2,6},{4,0},{6,2},{8,12},{10,14},{12,8},{14,10},{16,20},{18,... | collective-permute-start | bytes 15368 | tf_op jit(solution)/shard_map/ppermute | solution.py:16
  9.0 4.8 %collective-permute-start.3 = (f32[4,1024]{1,0:T(4,128)S(1)}, f32[4,1024]{1,0:T(4,128)S(1)}, u32[]{:S(2)}, u32[]{:S(2)}) collective-permute-start(f32[4,1024]{1,0:T(4,128)S(1)} %maximum_select_fusion.5), channel_id=1, source_target_pairs={{0,16},{2,18},{4,20},{6,22},{8,24},{10,26},{12,28},{14,30},{16,0},... | collective-permute-start | bytes 49160 | tf_op jit(solution)/shard_map/ppermute | solution.py:16
  17.3 3.7 %collective-permute-start.4 = (f32[4,512]{1,0:T(4,128)S(1)}, f32[4,512]{1,0:T(4,128)S(1)}, u32[]{:S(2)}, u32[]{:S(2)}) collective-permute-start(f32[4,512]{1,0:T(4,128)S(1)} %get-tuple-element.57), channel_id=1, source_target_pairs={{0,1},{1,0},{2,3},{3,2},{4,5},{5,4},{6,7},{7,6},{8,9},{9,8},{10,11... | collective-permute-start | bytes 24584 | tf_op jit(solution)/shard_map/ppermute | solution.py:28
  21.0 1.2 %collective-permute-start.5 = (f32[4,512]{1,0:T(4,128)S(1)}, f32[4,512]{1,0:T(4,128)S(1)}, u32[]{:S(2)}, u32[]{:S(2)}) collective-permute-start(f32[4,512]{1,0:T(4,128)S(1)} %add.137), channel_id=1, source_target_pairs={{0,2},{2,0},{4,6},{6,4},{8,10},{10,8},{12,14},{14,12},{16,18},{18,... | collective-permute-start | bytes 24584 | tf_op jit(solution)/shard_map/ppermute | solution.py:28
  22.2 3.7 %collective-permute-start.6 = (f32[4,512]{1,0:T(4,128)S(1)}, f32[4,512]{1,0:T(4,128)S(1)}, u32[]{:S(2)}, u32[]{:S(2)}) collective-permute-start(f32[4,512]{1,0:T(4,128)S(1)} %add.138), channel_id=1, source_target_pairs={{0,4},{2,6},{4,0},{6,2},{8,12},{10,14},{12,8},{14,10},{16,20},{18,... | collective-permute-start | bytes 24584 | tf_op jit(solution)/shard_map/ppermute | solution.py:28
  25.9 0.7 %copy-start.4 = (s32[128,4]{0,1:T(4,128)S(1)}, s32[128,4]{0,1:T(4,128)}, u32[]{:S(2)}) copy-start(s32[128,4]{0,1:T(4,128)} %param.21) | copy-start | bytes 6148
  25.9 0.7 %copy-start.5 = (s32[128,4]{0,1:T(4,128)S(1)}, s32[128,4]{0,1:T(4,128)}, u32[]{:S(2)}) copy-start(s32[128,4]{0,1:T(4,128)} %param.20) | copy-start | bytes 6148
  25.9 3.8 %collective-permute-start.7 = (f32[6,512]{1,0:T(8,128)S(1)}, f32[6,512]{1,0:T(8,128)S(1)}, u32[]{:S(2)}, u32[]{:S(2)}) collective-permute-start(f32[6,512]{1,0:T(8,128)S(1)} %pad_maximum_fusion), channel_id=1, source_target_pairs={{0,8},{2,10},{4,12},{6,14},{8,0},{10,2},{12,4},{14,6},{16,24},{18,... | collective-permute-start | bytes 36872 | tf_op jit(solution)/shard_map/ppermute | solution.py:16
  29.7 5.1 %collective-permute-start.8 = (f32[6,1024]{1,0:T(8,128)S(1)}, f32[6,1024]{1,0:T(8,128)S(1)}, u32[]{:S(2)}, u32[]{:S(2)}) collective-permute-start(f32[6,1024]{1,0:T(8,128)S(1)} %maximum_select_fusion.2), channel_id=1, source_target_pairs={{0,16},{2,18},{4,20},{6,22},{8,24},{10,26},{12,28},{14,30},{16,0},... | collective-permute-start | bytes 73736 | tf_op jit(solution)/shard_map/ppermute | solution.py:16
  34.8 0.7 %copy-start.7 = (bf16[8,128]{1,0:T(8,128)(2,1)S(1)}, bf16[8,128]{1,0:T(8,128)(2,1)}, u32[]{:S(2)}) copy-start(bf16[8,128]{1,0:T(8,128)(2,1)} %param.24) | copy-start | bytes 6148
  35.5 1.8 %copy-start.6 = (bf16[128,128]{1,0:T(8,128)(2,1)S(1)}, bf16[128,128]{1,0:T(8,128)(2,1)}, u32[]{:S(2)}) copy-start(bf16[128,128]{1,0:T(8,128)(2,1)} %param.26) | copy-start | bytes 98308
  37.3 0.8 %copy-start.8 = (f32[256]{0:T(256)S(1)}, f32[256]{0:T(256)}, u32[]{:S(2)}) copy-start(f32[256]{0:T(256)} %param.29) | copy-start | bytes 3076
  37.4 0.8 %copy-start.9 = (f32[256]{0:T(256)S(1)}, f32[256]{0:T(256)}, u32[]{:S(2)}) copy-start(f32[256]{0:T(256)} %param.28) | copy-start | bytes 3076
  40.2 1.2 %collective-permute-start.9 = (f32[2048]{0:T(1024)S(1)}, f32[2048]{0:T(1024)S(1)}, u32[]{:S(2)}, u32[]{:S(2)}) collective-permute-start(f32[2048]{0:T(1024)S(1)} %fusion.39), channel_id=1, source_target_pairs={{0,2},{2,0},{4,6},{6,4},{8,10},{10,8},{12,14},{14,12},{16,18},{18,... | collective-permute-start | bytes 24584 | tf_op jit(solution)/shard_map/ppermute | solution.py:28
  41.5 3.7 %collective-permute-start.10 = (f32[2048]{0:T(1024)S(1)}, f32[2048]{0:T(1024)S(1)}, u32[]{:S(2)}, u32[]{:S(2)}) collective-permute-start(f32[2048]{0:T(1024)S(1)} %add.155), channel_id=1, source_target_pairs={{0,4},{2,6},{4,0},{6,2},{8,12},{10,14},{12,8},{14,10},{16,20},{18,... | collective-permute-start | bytes 24584 | tf_op jit(solution)/shard_map/ppermute | solution.py:28
  45.1 3.7 %collective-permute-start.11 = (f32[2048]{0:T(1024)S(1)}, f32[2048]{0:T(1024)S(1)}, u32[]{:S(2)}, u32[]{:S(2)}) collective-permute-start(f32[2048]{0:T(1024)S(1)} %add.156), channel_id=1, source_target_pairs={{0,8},{2,10},{4,12},{6,14},{8,0},{10,2},{12,4},{14,6},{16,24},{18,... | collective-permute-start | bytes 24584 | tf_op jit(solution)/shard_map/ppermute | solution.py:28
  48.8 4.5 %collective-permute-start.12 = (f32[2048]{0:T(1024)S(1)}, f32[2048]{0:T(1024)S(1)}, u32[]{:S(2)}, u32[]{:S(2)}) collective-permute-start(f32[2048]{0:T(1024)S(1)} %add.157), channel_id=1, source_target_pairs={{0,16},{2,18},{4,20},{6,22},{8,24},{10,26},{12,28},{14,30},{16,0},... | collective-permute-start | bytes 24584 | tf_op jit(solution)/shard_map/ppermute | solution.py:28
  (1 other events, 0.7 us)

commit v3 on v2

--- a/solution.py
+++ b/solution.py
@@ -49,18 +49,30 @@
     return total
 
 
-def force_pass(qm_all, effective, mm_pos):
+def force_geometry(qm_all, mm_pos):
+    chunks = qm_all.shape[1] // CHUNK
+    stacked = jnp.transpose(qm_all.reshape(3, chunks, CHUNK), (1, 2, 0))
+
+    def body(block):
+        d = [block[:, c : c + 1] - mm_pos[c][None, :] for c in range(3)]
+        inverse = lax.rsqrt(d[0] * d[0] + d[1] * d[1] + d[2] * d[2] + SOFTEN)
+        return inverse * inverse * inverse
+
+    return lax.map(body, stacked)
+
+
+def force_pass(qm_all, effective, mm_pos, cubes):
     chunks = qm_all.shape[1] // CHUNK
     stacked = jnp.concatenate([qm_all, effective[None, :]], axis=0)
     stacked = jnp.transpose(stacked.reshape(4, chunks, CHUNK), (1, 2, 0))
 
-    def body(running, block):
+    def body(running, item):
+        block, cube = item
+        weight = cube * block[:, 3:4]
         d = [block[:, c : c + 1] - mm_pos[c][None, :] for c in range(3)]
-        inverse = lax.rsqrt(d[0] * d[0] + d[1] * d[1] + d[2] * d[2] + SOFTEN)
-        weight = inverse * inverse * inverse * block[:, 3:4]
         return running + jnp.stack([jnp.sum(d[c] * weight, axis=0) for c in range(3)]), None
 
-    total, _ = lax.scan(body, jnp.zeros((3, mm_pos.shape[1]), jnp.float32), stacked)
+    total, _ = lax.scan(body, jnp.zeros((3, mm_pos.shape[1]), jnp.float32), (stacked, cubes))
     return total
 
 
@@ -97,10 +109,14 @@
         axis=0,
     )
     near = gather_doubling(own, "blk", 1, low_blocks)
-    mm_some = gather_doubling(
-        jnp.concatenate([mm_pos, mm_charge[None, :]], axis=0), "blk", low_blocks, blocks
-    )
+    mm_some = jnp.concatenate([mm_pos, mm_charge[None, :]], axis=0)
     partial = potential_pass(near[:3], mm_some)
+    step = low_blocks
+    while step < blocks:
+        other = lax.ppermute(mm_some, "blk", [(i, i ^ step) for i in range(blocks)])
+        partial = partial + potential_pass(near[:3], other)
+        mm_some = jnp.concatenate([mm_some, other], -1)
+        step *= 2
     total = sum_butterfly(sum_butterfly(partial, "rep"), "blk", low_blocks)
     pull = lax.dynamic_slice_in_dim(total[1:4], (me % low_blocks) * rows, rows, axis=1)
     known = gather_doubling(
@@ -111,6 +127,7 @@
     atoms = qm_all.shape[1]
     species_all = known[4].astype(jnp.int32)
     live_all = ((jnp.arange(atoms) % rows).astype(jnp.float32) < known[5]).astype(jnp.float32)
+    cubes = force_geometry(qm_all, mm_pos)
 
     picks_all = (species_all[:, None] == jnp.arange(kinds)[None, :]).astype(jnp.bfloat16)
     base_all = jnp.dot(picks_all, species_table, preferred_element_type=jnp.float32)
@@ -155,7 +172,7 @@
     effective = lax.dynamic_slice_in_dim(effective_all, me * rows, rows)
 
     qm_force = pull * (effective * coupling)[None, :]
-    mm_force = force_pass(qm_all, effective_all, mm_pos) * (-coupling * mm_charge)[None, :]
+    mm_force = force_pass(qm_all, effective_all, mm_pos, cubes) * (-coupling * mm_charge)[None, :]
     return (atom_energy, qm_force, mm_force)
 
 

time: 58.3 us -> 67.2 us (1.15)
  other arithmetic: 9.19 us -> 23.1 us
  waiting for transfers between devices: 24.3 us -> 19.9 us
  local copies, waits for them, and re-layouts: 1.27 us -> 0.29 us
    dynamic_update_slice x0 -> x4, other arithmetic: none -> 5.95 us  [force_geometry(): return lax.map(body, stacked)]
    ppermute x6 -> x4, starting transfers between devices: 10.8 us -> 4.99 us  [gather_doubling(): other = lax.ppermute(x, axis, [(i, i ^ step) for i in range(n)])]
    ppermute x0 -> x2, starting transfers between devices: none -> 5.26 us  [on_device(): other = lax.ppermute(mm_some, 'blk', [(i, i ^ step) for i in range(blocks)])]
    reduce_sum x4, other arithmetic: 3.04 us -> 6.65 us  [body(): jnp.sum(d[c] * weight, axis=0)]
    ppermute x7, waiting for transfers between devices: 14.4 us -> 11.8 us  [sum_butterfly(): x = x + lax.ppermute(x, axis, [(i, i ^ step) for i in range(n)])]
    ppermute x6 -> x4, waiting for transfers between devices: 9.91 us -> 7.81 us  [gather_doubling(): other = lax.ppermute(x, axis, [(i, i ^ step) for i in range(n)])]
    concatenate x2, other arithmetic: 0.02 us -> 1.45 us  [the longest x1 0.72 us: on_device(): mm_some = jnp.concatenate([mm_some, other], -1)]
    unnamed x24 -> x20, local copies, waits for them, and re-layouts: 1.06 us -> 0.06 us
  transfers between devices with their start and end apart: 13 -> 13, of which waited for: 11 -> 10; matrix products, arithmetic and copies ran while one was open for 0% -> 15% of each run, Pallas kernels for 0% -> 0%
where the time goes in v3:
time: 67.2 us; the launch traced here: 66.7 us
  other arithmetic  23.1 us (34%)
  waiting for transfers between devices  19.9 us (30%)
  starting transfers between devices  18.1 us (27%)
  matrix products  3.33 us (5%)
  between operations  1.65 us (2%)
    ppermute x7, waiting for transfers between devices, sum_butterfly(): x = x + lax.ppermute(x, axis, [(i, i ^ step) for i in range(n)])  11.8 us
    ppermute x4, waiting for transfers between devices, gather_doubling(): other = lax.ppermute(x, axis, [(i, i ^ step) for i in range(n)])  7.81 us
    ppermute x7, starting transfers between devices, sum_butterfly(): x = x + lax.ppermute(x, axis, [(i, i ^ step) for i in range(n)])  7.81 us
    reduce_sum x4, other arithmetic, body(): jnp.sum(d[c] * weight, axis=0)  6.65 us
    dynamic_update_slice x4, other arithmetic, force_geometry(): return lax.map(body, stacked)  5.95 us
    ppermute x2, starting transfers between devices, on_device(): other = lax.ppermute(mm_some, 'blk', [(i, i ^ step) for i in range(blocks)])  5.26 us
    ppermute x4, starting transfers between devices, gather_doubling(): other = lax.ppermute(x, axis, [(i, i ^ step) for i in range(n)])  4.99 us
    reduce_sum x3, other arithmetic, body(): jnp.sum(weighted, axis=0)  3.36 us
  transfers between devices with their start and end apart: 13, of which 10 were waited for; matrix products, arithmetic and copies ran while one was open for 15% of the time, Pallas kernels for 0%

profile of v3, /device:TPU:0, one launch (start us, length us, event | category | flops | bytes accessed | tf_op | source)
XLA Modules:
  0.0 66.7 jit_solution(13932143718060383031)
XLA Ops:
  3.9 2.6 %collective-permute-start.2 = (f32[4,512]{1,0:T(4,128)S(1)}, f32[4,512]{1,0:T(4,128)S(1)}, u32[]{:S(2)}, u32[]{:S(2)}) collective-permute-start(f32[4,512]{1,0:T(4,128)S(1)} %pad_maximum_fusion.2), channel_id=1, source_target_pairs={{0,8},{2,10},{4,12},{6,14},{8,0},{10,2},{12,4},{14,6},{16,24},{18,... | collective-permute-start | bytes 24584 | tf_op jit(solution)/shard_map/ppermute | solution.py:116
  8.0 1.6 %collective-permute-start.1 = (f32[5,256]{1,0:T(8,128)S(1)}, f32[5,256]{1,0:T(8,128)S(1)}, u32[]{:S(2)}, u32[]{:S(2)}) collective-permute-start(f32[5,256]{1,0:T(8,128)S(1)} %maximum_select_fusion.3), channel_id=1, source_target_pairs={{0,4},{2,6},{4,0},{6,2},{8,12},{10,14},{12,8},{14,10},{16,20},{18,... | collective-permute-start | bytes 15368 | tf_op jit(solution)/shard_map/ppermute | solution.py:16
  9.6 2.1 %collective-permute-done.1 = f32[5,256]{1,0:T(8,128)S(1)} collective-permute-done((f32[5,256]{1,0:T(8,128)S(1)}, f32[5,256]{1,0:T(8,128)S(1)}, u32[]{:S(2)}, u32[]{:S(2)}) %collective-permute-start.1) | collective-permute-done | bytes 5152 | tf_op jit(solution)/shard_map/ppermute | solution.py:16
  12.5 2.6 %collective-permute-start.3 = (f32[4,1024]{1,0:T(4,128)S(1)}, f32[4,1024]{1,0:T(4,128)S(1)}, u32[]{:S(2)}, u32[]{:S(2)}) collective-permute-start(f32[4,1024]{1,0:T(4,128)S(1)} %pad_maximum_fusion), channel_id=1, source_target_pairs={{0,16},{2,18},{4,20},{6,22},{8,24},{10,26},{12,28},{14,30},{16,0},... | collective-permute-start | bytes 49160 | tf_op jit(solution)/shard_map/ppermute | solution.py:116
  15.2 1.8 %multiply_reduce_fusion.4 = (f32[512]{0:T(512)S(1)}, f32[512]{0:T(512)S(1)}, f32[512]{0:T(512)S(1)}, f32[512]{0:T(512)S(1)}, f32[512]{0:T(512)S(1)}, /*index=5*/f32[512]{0:T(512)S(1)}, f32[512]{0:T(512)S(1)}, f32[512]{0:T(512)S(1)}) fusion(f32[512]{0:T(512)S(1)} %bitcast.234, f32[512]{0:T(512)S(1)} %bitcast.235, f32[512]{0:T(512)S(1)} %bitcast.236, ...), kind=kLoop, calls=%fused_computation.31 | loop fusion | flops 9957376 | bytes 38912 | tf_op jit(solution)/shard_map/while/body/eval_jaxpr/reduce_sum | solution.py:43
  17.2 1.7 %while.41 = (s32[]{:T(128)}, f32[4,512]{1,0:T(4,128)S(1)}, f32[1,512]{1,0:T(1,128)S(1)}, f32[2,512,4]{1,2,0:T(4,128)S(1)}, f32[1,512]{1,0:T(1,128)S(1)}, /*index=5*/f32[1,512]{1,0:T(1,128)S(1)}, s32[]{:T(128)}, s32[]{:T(128)}) while((s32[]{:T(128)}, f32[4,512]{1,0:T(4,128)S(1)}, f32[1,512]{1,0:T(1,128)S(1)}, ...), condition=%wide.region_13.14_spmd.clone, body=%wide.region_8.13_spmd.clone.sunk | while | flops 4988931 | bytes 79979 | solution.py:48
  19.0 1.6 %collective-permute-start.4 = (f32[4,512]{1,0:T(4,128)S(1)}, f32[4,512]{1,0:T(4,128)S(1)}, u32[]{:S(2)}, u32[]{:S(2)}) collective-permute-start(f32[4,512]{1,0:T(4,128)S(1)} %fusion.45), channel_id=1, source_target_pairs={{0,1},{1,0},{2,3},{3,2},{4,5},{5,4},{6,7},{7,6},{8,9},{9,8},{10,11... | collective-permute-start | bytes 24584 | tf_op jit(solution)/shard_map/ppermute | solution.py:28
  20.6 2.1 %collective-permute-done.4 = f32[4,512]{1,0:T(4,128)S(1)} collective-permute-done((f32[4,512]{1,0:T(4,128)S(1)}, f32[4,512]{1,0:T(4,128)S(1)}, u32[]{:S(2)}, u32[]{:S(2)}) %collective-permute-start.4) | collective-permute-done | bytes 8224 | tf_op jit(solution)/shard_map/ppermute | solution.py:28
  23.9 1.6 %collective-permute-start.6 = (f32[4,512]{1,0:T(4,128)S(1)}, f32[4,512]{1,0:T(4,128)S(1)}, u32[]{:S(2)}, u32[]{:S(2)}) collective-permute-start(f32[4,512]{1,0:T(4,128)S(1)} %add.206), channel_id=1, source_target_pairs={{0,4},{2,6},{4,0},{6,2},{8,12},{10,14},{12,8},{14,10},{16,20},{18,... | collective-permute-start | bytes 24584 | tf_op jit(solution)/shard_map/ppermute | solution.py:28
  25.5 2.1 %collective-permute-done.6 = f32[4,512]{1,0:T(4,128)S(1)} collective-permute-done((f32[4,512]{1,0:T(4,128)S(1)}, f32[4,512]{1,0:T(4,128)S(1)}, u32[]{:S(2)}, u32[]{:S(2)}) %collective-permute-start.6) | collective-permute-done | bytes 8224 | tf_op jit(solution)/shard_map/ppermute | solution.py:28
  28.0 3.4 %collective-permute-done.7 = f32[6,512]{1,0:T(8,128)S(1)} collective-permute-done((f32[6,512]{1,0:T(8,128)S(1)}, f32[6,512]{1,0:T(8,128)S(1)}, u32[]{:S(2)}, u32[]{:S(2)}) %collective-permute-start.7) | collective-permute-done | bytes 12320 | tf_op jit(solution)/shard_map/ppermute | solution.py:16
  31.4 2.7 %collective-permute-start.8 = (f32[6,1024]{1,0:T(8,128)S(1)}, f32[6,1024]{1,0:T(8,128)S(1)}, u32[]{:S(2)}, u32[]{:S(2)}) collective-permute-start(f32[6,1024]{1,0:T(8,128)S(1)} %maximum_select_fusion.1), channel_id=1, source_target_pairs={{0,16},{2,18},{4,20},{6,22},{8,24},{10,26},{12,28},{14,30},{16,0},... | collective-permute-start | bytes 73736 | tf_op jit(solution)/shard_map/ppermute | solution.py:16
  34.1 2.3 %collective-permute-done.8 = f32[6,1024]{1,0:T(8,128)S(1)} collective-permute-done((f32[6,1024]{1,0:T(8,128)S(1)}, f32[6,1024]{1,0:T(8,128)S(1)}, u32[]{:S(2)}, u32[]{:S(2)}) %collective-permute-start.8) | collective-permute-done | bytes 24608 | tf_op jit(solution)/shard_map/ppermute | solution.py:16
  36.4 1.8 %fusion.9 = bf16[2048,128]{1,0:T(8,128)(2,1)S(1)} fusion(bf16[8,128]{1,0:T(8,128)(2,1)S(1)} %copy-done.6, f32[128]{0:T(128)S(1)} %copy-done.9, f32[2048]{0:T(1024)S(1)} %bitcast.205, s32[2048]{0:T(1024)S(1)} %bitcast.222, f32[2048]{0:T(1024)S(1)} %get-tuple-element.216), kind=kOutput, calls=%fused_computation.28 | convolution fusion | flops 5259264 | bytes 551424 | tf_op jit(solution)/shard_map/dot_general | solution.py:133
  42.4 1.7 %collective-permute-start.10 = (f32[2048]{0:T(1024)S(1)}, f32[2048]{0:T(1024)S(1)}, u32[]{:S(2)}, u32[]{:S(2)}) collective-permute-start(f32[2048]{0:T(1024)S(1)} %add.223), channel_id=1, source_target_pairs={{0,4},{2,6},{4,0},{6,2},{8,12},{10,14},{12,8},{14,10},{16,20},{18,... | collective-permute-start | bytes 24584 | tf_op jit(solution)/shard_map/ppermute | solution.py:28
  44.1 1.9 %collective-permute-done.10 = f32[2048]{0:T(1024)S(1)} collective-permute-done((f32[2048]{0:T(1024)S(1)}, f32[2048]{0:T(1024)S(1)}, u32[]{:S(2)}, u32[]{:S(2)}) %collective-permute-start.10) | collective-permute-done | bytes 8224 | tf_op jit(solution)/shard_map/ppermute | solution.py:28
  46.3 3.4 %collective-permute-done.11 = f32[2048]{0:T(1024)S(1)} collective-permute-done((f32[2048]{0:T(1024)S(1)}, f32[2048]{0:T(1024)S(1)}, u32[]{:S(2)}, u32[]{:S(2)}) %collective-permute-start.11) | collective-permute-done | bytes 8224 | tf_op jit(solution)/shard_map/ppermute | solution.py:28
  49.7 2.5 %collective-permute-start.12 = (f32[2048]{0:T(1024)S(1)}, f32[2048]{0:T(1024)S(1)}, u32[]{:S(2)}, u32[]{:S(2)}) collective-permute-start(f32[2048]{0:T(1024)S(1)} %add.225), channel_id=1, source_target_pairs={{0,16},{2,18},{4,20},{6,22},{8,24},{10,26},{12,28},{14,30},{16,0},... | collective-permute-start | bytes 24584 | tf_op jit(solution)/shard_map/ppermute | solution.py:28
  52.3 6.1 %while.40 = (s32[]{:T(128)}, f32[4,512,512]{2,1,0:T(8,128)}, f32[4,512,3]{1,2,0:T(4,128)S(1)}, f32[3,512]{1,0:T(4,128)S(1)}, s32[]{:T(128)}) while((s32[]{:T(128)}, f32[4,512,512]{2,1,0:T(8,128)}, f32[4,512,3]{1,2,0:T(4,128)S(1)}, f32[3,512]{1,0:T(4,128)S(1)}, s32[]{:T(128)}) %tuple.132), condition=%wide.region_20.21_spmd, body=%wide.region_19.20_spmd.sunk | while | flops 2883586 | bytes 1097805 | solution.py:61
  58.4 7.0 %while.42 = (s32[]{:T(128)}, f32[3,512]{1,0:T(4,128)S(1)}, f32[4,512,4]{1,2,0:T(4,128)S(1)}, f32[3,512]{1,0:T(4,128)S(1)}, f32[4,512,512]{2,1,0:T(8,128)}, /*index=5*/s32[]{:T(128)}, s32[]{:T(128)}) while((s32[]{:T(128)}, f32[3,512]{1,0:T(4,128)S(1)}, f32[4,512,4]{1,2,0:T(4,128)S(1)}, f32[3,512]{1,0:T(4,128)S(1)}, ...), condition=%wide.region_25.26_spmd.clone, body=%wide.region_21.25_spmd.clone.sunk | while | flops 2626051 | bytes 1132647 | solution.py:75
  58.5 1.7 %multiply_reduce_fusion.13 = (f32[512]{0:T(512)S(1)}, f32[512]{0:T(512)S(1)}, f32[512]{0:T(512)S(1)}) fusion(f32[4,512,512]{2,1,0:T(8,128)} %get-tuple-element.456, s32[]{:T(128)S(6)} %copy.31, f32[512]{0:T(512)S(1)} %bitcast.188, f32[512]{0:T(512)S(1)} %bitcast.182, f32[512]{0:T(512)S(1)} %bitcast.189, f32[512]{0:T(512)S(1)} %bitcast.181, ...), kind=kLoop, calls=%fused_computation.23.clone.1 | loop fusion | flops 2619904 | bytes 1069060 | tf_op jit(solution)/shard_map/while/body/eval_jaxpr/reduce_sum | solution.py:73
  60.3 1.7 %multiply_reduce_fusion.13 = (f32[512]{0:T(512)S(1)}, f32[512]{0:T(512)S(1)}, f32[512]{0:T(512)S(1)}) fusion(f32[4,512,512]{2,1,0:T(8,128)} %get-tuple-element.456, s32[]{:T(128)S(6)} %copy.31, f32[512]{0:T(512)S(1)} %bitcast.188, f32[512]{0:T(512)S(1)} %bitcast.182, f32[512]{0:T(512)S(1)} %bitcast.189, f32[512]{0:T(512)S(1)} %bitcast.181, ...), kind=kLoop, calls=%fused_computation.23.clone.1 | loop fusion | flops 2619904 | bytes 1069060 | tf_op jit(solution)/shard_map/while/body/eval_jaxpr/reduce_sum | solution.py:73
  62.0 1.7 %multiply_reduce_fusion.13 = (f32[512]{0:T(512)S(1)}, f32[512]{0:T(512)S(1)}, f32[512]{0:T(512)S(1)}) fusion(f32[4,512,512]{2,1,0:T(8,128)} %get-tuple-element.456, s32[]{:T(128)S(6)} %copy.31, f32[512]{0:T(512)S(1)} %bitcast.188, f32[512]{0:T(512)S(1)} %bitcast.182, f32[512]{0:T(512)S(1)} %bitcast.189, f32[512]{0:T(512)S(1)} %bitcast.181, ...), kind=kLoop, calls=%fused_computation.23.clone.1 | loop fusion | flops 2619904 | bytes 1069060 | tf_op jit(solution)/shard_map/while/body/eval_jaxpr/reduce_sum | solution.py:73
  63.8 1.7 %multiply_reduce_fusion.13 = (f32[512]{0:T(512)S(1)}, f32[512]{0:T(512)S(1)}, f32[512]{0:T(512)S(1)}) fusion(f32[4,512,512]{2,1,0:T(8,128)} %get-tuple-element.456, s32[]{:T(128)S(6)} %copy.31, f32[512]{0:T(512)S(1)} %bitcast.188, f32[512]{0:T(512)S(1)} %bitcast.182, f32[512]{0:T(512)S(1)} %bitcast.189, f32[512]{0:T(512)S(1)} %bitcast.181, ...), kind=kLoop, calls=%fused_computation.23.clone.1 | loop fusion | flops 2619904 | bytes 1069060 | tf_op jit(solution)/shard_map/while/body/eval_jaxpr/reduce_sum | solution.py:73
  (116 shorter events, 20.2 us)
Async XLA Ops:
  0.6 38.5 %copy-start = (bf16[128,256]{1,0:T(8,128)(2,1)S(1)}, bf16[128,256]{1,0:T(8,128)(2,1)}, u32[]{:S(2)}) copy-start(bf16[128,256]{1,0:T(8,128)(2,1)} %param.29) | copy-start | bytes 196612
  0.6 27.3 %copy-start.3 = (s32[128,4]{0,1:T(4,128)S(1)}, s32[128,4]{0,1:T(4,128)}, u32[]{:S(2)}) copy-start(s32[128,4]{0,1:T(4,128)} %param.23) | copy-start | bytes 6148
  0.7 27.3 %copy-start.4 = (s32[128,4]{0,1:T(4,128)S(1)}, s32[128,4]{0,1:T(4,128)}, u32[]{:S(2)}) copy-start(s32[128,4]{0,1:T(4,128)} %param.22) | copy-start | bytes 6148
  0.7 35.8 %copy-start.6 = (bf16[8,128]{1,0:T(8,128)(2,1)S(1)}, bf16[8,128]{1,0:T(8,128)(2,1)}, u32[]{:S(2)}) copy-start(bf16[8,128]{1,0:T(8,128)(2,1)} %param.26) | copy-start | bytes 6148
  0.7 35.8 %copy-start.9 = (f32[128]{0:T(128)S(1)}, f32[128]{0:T(128)}, u32[]{:S(2)}) copy-start(f32[128]{0:T(128)} %param.27) | copy-start | bytes 1540
  0.7 37.6 %copy-start.5 = (bf16[128,128]{1,0:T(8,128)(2,1)S(1)}, bf16[128,128]{1,0:T(8,128)(2,1)}, u32[]{:S(2)}) copy-start(bf16[128,128]{1,0:T(8,128)(2,1)} %param.28) | copy-start | bytes 98308
  2.8 4.5 %collective-permute-start = (f32[5,128]{1,0:T(8,128)S(1)}, f32[5,128]{1,0:T(8,128)S(1)}, u32[]{:S(2)}, u32[]{:S(2)}) collective-permute-start(f32[5,128]{1,0:T(8,128)S(1)} %pad_maximum_fusion.3), channel_id=1, source_target_pairs={{0,2},{2,0},{4,6},{6,4},{8,10},{10,8},{12,14},{14,12},{16,18},{18,... | collective-permute-start | bytes 7688 | tf_op jit(solution)/shard_map/ppermute | solution.py:16
  3.9 7.8 %collective-permute-start.2 = (f32[4,512]{1,0:T(4,128)S(1)}, f32[4,512]{1,0:T(4,128)S(1)}, u32[]{:S(2)}, u32[]{:S(2)}) collective-permute-start(f32[4,512]{1,0:T(4,128)S(1)} %pad_maximum_fusion.2), channel_id=1, source_target_pairs={{0,8},{2,10},{4,12},{6,14},{8,0},{10,2},{12,4},{14,6},{16,24},{18,... | collective-permute-start | bytes 24584 | tf_op jit(solution)/shard_map/ppermute | solution.py:116
  8.0 3.7 %collective-permute-start.1 = (f32[5,256]{1,0:T(8,128)S(1)}, f32[5,256]{1,0:T(8,128)S(1)}, u32[]{:S(2)}, u32[]{:S(2)}) collective-permute-start(f32[5,256]{1,0:T(8,128)S(1)} %maximum_select_fusion.3), channel_id=1, source_target_pairs={{0,4},{2,6},{4,0},{6,2},{8,12},{10,14},{12,8},{14,10},{16,20},{18,... | collective-permute-start | bytes 15368 | tf_op jit(solution)/shard_map/ppermute | solution.py:16
  12.5 4.7 %collective-permute-start.3 = (f32[4,1024]{1,0:T(4,128)S(1)}, f32[4,1024]{1,0:T(4,128)S(1)}, u32[]{:S(2)}, u32[]{:S(2)}) collective-permute-start(f32[4,1024]{1,0:T(4,128)S(1)} %pad_maximum_fusion), channel_id=1, source_target_pairs={{0,16},{2,18},{4,20},{6,22},{8,24},{10,26},{12,28},{14,30},{16,0},... | collective-permute-start | bytes 49160 | tf_op jit(solution)/shard_map/ppermute | solution.py:116
  15.1 24.0 %copy-start.7 = (f32[256]{0:T(256)S(1)}, f32[256]{0:T(256)}, u32[]{:S(2)}) copy-start(f32[256]{0:T(256)} %param.31) | copy-start | bytes 3076
  15.1 24.0 %copy-start.8 = (f32[256]{0:T(256)S(1)}, f32[256]{0:T(256)}, u32[]{:S(2)}) copy-start(f32[256]{0:T(256)} %param.30) | copy-start | bytes 3076
  17.2 29.1 %copy-start.2 = (f32[512]{0:T(512)S(1)}, f32[512]{0:T(512)}, u32[]{:S(2)}) copy-start(f32[512]{0:T(512)} %param.25) | copy-start | bytes 6148
  17.2 35.1 %copy-start.1 = (f32[3,512]{1,0:T(4,128)S(1)}, f32[3,512]{1,0:T(4,128)}, u32[]{:S(2)}) copy-start(f32[3,512]{1,0:T(4,128)} %param.24) | copy-start | bytes 18436
  19.0 3.7 %collective-permute-start.4 = (f32[4,512]{1,0:T(4,128)S(1)}, f32[4,512]{1,0:T(4,128)S(1)}, u32[]{:S(2)}, u32[]{:S(2)}) collective-permute-start(f32[4,512]{1,0:T(4,128)S(1)} %fusion.45), channel_id=1, source_target_pairs={{0,1},{1,0},{2,3},{3,2},{4,5},{5,4},{6,7},{7,6},{8,9},{9,8},{10,11... | collective-permute-start | bytes 24584 | tf_op jit(solution)/shard_map/ppermute | solution.py:28
  22.7 1.2 %collective-permute-start.5 = (f32[4,512]{1,0:T(4,128)S(1)}, f32[4,512]{1,0:T(4,128)S(1)}, u32[]{:S(2)}, u32[]{:S(2)}) collective-permute-start(f32[4,512]{1,0:T(4,128)S(1)} %fusion.73), channel_id=1, source_target_pairs={{0,2},{2,0},{4,6},{6,4},{8,10},{10,8},{12,14},{14,12},{16,18},{18,... | collective-permute-start | bytes 24584 | tf_op jit(solution)/shard_map/ppermute | solution.py:28
  23.9 3.7 %collective-permute-start.6 = (f32[4,512]{1,0:T(4,128)S(1)}, f32[4,512]{1,0:T(4,128)S(1)}, u32[]{:S(2)}, u32[]{:S(2)}) collective-permute-start(f32[4,512]{1,0:T(4,128)S(1)} %add.206), channel_id=1, source_target_pairs={{0,4},{2,6},{4,0},{6,2},{8,12},{10,14},{12,8},{14,10},{16,20},{18,... | collective-permute-start | bytes 24584 | tf_op jit(solution)/shard_map/ppermute | solution.py:28
  27.6 3.8 %collective-permute-start.7 = (f32[6,512]{1,0:T(8,128)S(1)}, f32[6,512]{1,0:T(8,128)S(1)}, u32[]{:S(2)}, u32[]{:S(2)}) collective-permute-start(f32[6,512]{1,0:T(8,128)S(1)} %pad_maximum_fusion.1), channel_id=1, source_target_pairs={{0,8},{2,10},{4,12},{6,14},{8,0},{10,2},{12,4},{14,6},{16,24},{18,... | collective-permute-start | bytes 36872 | tf_op jit(solution)/shard_map/ppermute | solution.py:16
  31.4 4.9 %collective-permute-start.8 = (f32[6,1024]{1,0:T(8,128)S(1)}, f32[6,1024]{1,0:T(8,128)S(1)}, u32[]{:S(2)}, u32[]{:S(2)}) collective-permute-start(f32[6,1024]{1,0:T(8,128)S(1)} %maximum_select_fusion.1), channel_id=1, source_target_pairs={{0,16},{2,18},{4,20},{6,22},{8,24},{10,26},{12,28},{14,30},{16,0},... | collective-permute-start | bytes 73736 | tf_op jit(solution)/shard_map/ppermute | solution.py:16
  41.2 1.2 %collective-permute-start.9 = (f32[2048]{0:T(1024)S(1)}, f32[2048]{0:T(1024)S(1)}, u32[]{:S(2)}, u32[]{:S(2)}) collective-permute-start(f32[2048]{0:T(1024)S(1)} %fusion.46), channel_id=1, source_target_pairs={{0,2},{2,0},{4,6},{6,4},{8,10},{10,8},{12,14},{14,12},{16,18},{18,... | collective-permute-start | bytes 24584 | tf_op jit(solution)/shard_map/ppermute | solution.py:28
  42.4 3.7 %collective-permute-start.10 = (f32[2048]{0:T(1024)S(1)}, f32[2048]{0:T(1024)S(1)}, u32[]{:S(2)}, u32[]{:S(2)}) collective-permute-start(f32[2048]{0:T(1024)S(1)} %add.223), channel_id=1, source_target_pairs={{0,4},{2,6},{4,0},{6,2},{8,12},{10,14},{12,8},{14,10},{16,20},{18,... | collective-permute-start | bytes 24584 | tf_op jit(solution)/shard_map/ppermute | solution.py:28
  46.1 3.7 %collective-permute-start.11 = (f32[2048]{0:T(1024)S(1)}, f32[2048]{0:T(1024)S(1)}, u32[]{:S(2)}, u32[]{:S(2)}) collective-permute-start(f32[2048]{0:T(1024)S(1)} %add.224), channel_id=1, source_target_pairs={{0,8},{2,10},{4,12},{6,14},{8,0},{10,2},{12,4},{14,6},{16,24},{18,... | collective-permute-start | bytes 24584 | tf_op jit(solution)/shard_map/ppermute | solution.py:28
  49.7 8.6 %collective-permute-start.12 = (f32[2048]{0:T(1024)S(1)}, f32[2048]{0:T(1024)S(1)}, u32[]{:S(2)}, u32[]{:S(2)}) collective-permute-start(f32[2048]{0:T(1024)S(1)} %add.225), channel_id=1, source_target_pairs={{0,16},{2,18},{4,20},{6,22},{8,24},{10,26},{12,28},{14,30},{16,0},... | collective-permute-start | bytes 24584 | tf_op jit(solution)/shard_map/ppermute | solution.py:28

commit v4 on v2

--- a/solution.py
+++ b/solution.py
@@ -49,7 +49,7 @@
     return total
 
 
-def force_pass(qm_all, effective, mm_pos):
+def force_pass(qm_all, effective, mm_pos, scale):
     chunks = qm_all.shape[1] // CHUNK
     stacked = jnp.concatenate([qm_all, effective[None, :]], axis=0)
     stacked = jnp.transpose(stacked.reshape(4, chunks, CHUNK), (1, 2, 0))
@@ -57,7 +57,7 @@
     def body(running, block):
         d = [block[:, c : c + 1] - mm_pos[c][None, :] for c in range(3)]
         inverse = lax.rsqrt(d[0] * d[0] + d[1] * d[1] + d[2] * d[2] + SOFTEN)
-        weight = inverse * inverse * inverse * block[:, 3:4]
+        weight = inverse * inverse * inverse * block[:, 3:4] * scale[None, :]
         return running + jnp.stack([jnp.sum(d[c] * weight, axis=0) for c in range(3)]), None
 
     total, _ = lax.scan(body, jnp.zeros((3, mm_pos.shape[1]), jnp.float32), stacked)
@@ -112,21 +112,26 @@
     species_all = known[4].astype(jnp.int32)
     live_all = ((jnp.arange(atoms) % rows).astype(jnp.float32) < known[5]).astype(jnp.float32)
 
-    picks_all = (species_all[:, None] == jnp.arange(kinds)[None, :]).astype(jnp.bfloat16)
-    base_all = jnp.dot(picks_all, species_table, preferred_element_type=jnp.float32)
-    start_all = (
-        live_all[:, None] * (base_all + potential_all[:, None] * potential_gain[None, :])
-    ).astype(jnp.bfloat16)
     live = lax.dynamic_slice_in_dim(live_all, me * rows, rows)
     potential = lax.dynamic_slice_in_dim(potential_all, me * rows, rows)
-    start = lax.dynamic_slice_in_dim(start_all, me * rows, rows, axis=0)
+    table_t = species_table.T
+    base_t = jnp.broadcast_to(table_t[:, 0:1], (table_t.shape[0], atoms))
+    for kind in range(1, kinds):
+        base_t = jnp.where(species_all[None, :] == kind, table_t[:, kind : kind + 1], base_t)
+    base_t = base_t.astype(jnp.float32)
+    start_t = (
+        live_all[None, :] * (base_t + potential_gain[:, None] * potential_all[None, :])
+    ).astype(jnp.bfloat16)
+    start = lax.dynamic_slice_in_dim(start_t, me * rows, rows, axis=1).T
 
     ghost = ghost_owner * rows + ghost_slot
     columns = jnp.arange(atoms)[None, :]
     links = jnp.zeros((rows, atoms), jnp.bfloat16)
     for k in range(ghost.shape[1]):
         links = links + (ghost[:, k : k + 1] == columns).astype(jnp.bfloat16)
-    neighbour = jnp.dot(links, start_all, preferred_element_type=jnp.float32).astype(jnp.bfloat16)
+    neighbour = lax.dot_general(
+        links, start_t, (((1,), (1,)), ((), ())), preferred_element_type=jnp.float32
+    ).astype(jnp.bfloat16)
 
     mixed = start.astype(jnp.float32) + jnp.dot(
         neighbour, message_weight, preferred_element_type=jnp.float32
@@ -155,7 +160,7 @@
     effective = lax.dynamic_slice_in_dim(effective_all, me * rows, rows)
 
     qm_force = pull * (effective * coupling)[None, :]
-    mm_force = force_pass(qm_all, effective_all, mm_pos) * (-coupling * mm_charge)[None, :]
+    mm_force = force_pass(qm_all, effective_all, mm_pos, -coupling * mm_charge)
     return (atom_energy, qm_force, mm_force)
 
 

time: 58.3 us -> 59.2 us (1.015)
  other arithmetic: 9.19 us -> 11.8 us
  matrix products: 3.3 us -> 1.5 us
    convert_element_type x1, other arithmetic: 0.01 us -> 2.9 us  [on_device(): start_t = (live_all[None, :] * (base_t + potential_gain[:, None] * potent...]
    dot_general x1 -> x0, matrix products: 1.8 us -> none  [on_device(): jnp.dot(picks_all, species_table, preferred_element_type=jnp.float32)]
    mul x2 -> x1, other arithmetic: 0.61 us -> 0.01 us  [on_device(): mm_force = force_pass(qm_all, effective_all, mm_pos, -coupling * mm_charge)]
where the time goes in v4:
time: 59.2 us; the launch traced here: 58.9 us
  waiting for transfers between devices  24.3 us (41%)
  starting transfers between devices  18 us (30%)
  other arithmetic  11.8 us (20%)
  between operations  1.64 us (3%)
  matrix products  1.5 us (3%)
  local copies, waits for them, and re-layouts  1.28 us (2%)
    ppermute x7, waiting for transfers between devices, sum_butterfly(): x = x + lax.ppermute(x, axis, [(i, i ^ step) for i in range(n)])  14.4 us
    ppermute x6, starting transfers between devices, gather_doubling(): other = lax.ppermute(x, axis, [(i, i ^ step) for i in range(n)])  10.8 us
    ppermute x6, waiting for transfers between devices, gather_doubling(): other = lax.ppermute(x, axis, [(i, i ^ step) for i in range(n)])  9.91 us
    ppermute x7, starting transfers between devices, sum_butterfly(): x = x + lax.ppermute(x, axis, [(i, i ^ step) for i in range(n)])  7.19 us
    reduce_sum x4, other arithmetic, body(): jnp.sum(weighted, axis=0)  3.21 us
    reduce_sum x4, other arithmetic, body(): jnp.sum(d[c] * weight, axis=0)  3.19 us
    convert_element_type x1, other arithmetic, on_device(): start_t = (live_all[None, :] * (base_t + potential_gain[:, None] * potent...  2.9 us
  transfers between devices with their start and end apart: 13, of which 11 were waited for; matrix products, arithmetic and copies ran while one was open for 0% of the time, Pallas kernels for 0%

profile of v4, /device:TPU:0, one launch (start us, length us, event | category | flops | bytes accessed | tf_op | source)
XLA Modules:
  0.0 58.9 jit_solution(14824795091474729244)
XLA Ops:
  2.1 3.1 %collective-permute-start.2 = (f32[4,512]{1,0:T(4,128)S(1)}, f32[4,512]{1,0:T(4,128)S(1)}, u32[]{:S(2)}, u32[]{:S(2)}) collective-permute-start(f32[4,512]{1,0:T(4,128)S(1)} %pad_maximum_fusion.1), channel_id=1, source_target_pairs={{0,8},{2,10},{4,12},{6,14},{8,0},{10,2},{12,4},{14,6},{16,24},{18,... | collective-permute-start | bytes 24584 | tf_op jit(solution)/shard_map/ppermute | solution.py:16
  5.2 1.6 %collective-permute-start.1 = (f32[5,256]{1,0:T(8,128)S(1)}, f32[5,256]{1,0:T(8,128)S(1)}, u32[]{:S(2)}, u32[]{:S(2)}) collective-permute-start(f32[5,256]{1,0:T(8,128)S(1)} %maximum_select_fusion.6), channel_id=1, source_target_pairs={{0,4},{2,6},{4,0},{6,2},{8,12},{10,14},{12,8},{14,10},{16,20},{18,... | collective-permute-start | bytes 15368 | tf_op jit(solution)/shard_map/ppermute | solution.py:16
  6.8 2.1 %collective-permute-done.1 = f32[5,256]{1,0:T(8,128)S(1)} collective-permute-done((f32[5,256]{1,0:T(8,128)S(1)}, f32[5,256]{1,0:T(8,128)S(1)}, u32[]{:S(2)}, u32[]{:S(2)}) %collective-permute-start.1) | collective-permute-done | bytes 5152 | tf_op jit(solution)/shard_map/ppermute | solution.py:16
  9.0 2.7 %collective-permute-start.3 = (f32[4,1024]{1,0:T(4,128)S(1)}, f32[4,1024]{1,0:T(4,128)S(1)}, u32[]{:S(2)}, u32[]{:S(2)}) collective-permute-start(f32[4,1024]{1,0:T(4,128)S(1)} %maximum_select_fusion.5), channel_id=1, source_target_pairs={{0,16},{2,18},{4,20},{6,22},{8,24},{10,26},{12,28},{14,30},{16,0},... | collective-permute-start | bytes 49160 | tf_op jit(solution)/shard_map/ppermute | solution.py:16
  11.6 2.2 %collective-permute-done.3 = f32[4,1024]{1,0:T(4,128)S(1)} collective-permute-done((f32[4,1024]{1,0:T(4,128)S(1)}, f32[4,1024]{1,0:T(4,128)S(1)}, u32[]{:S(2)}, u32[]{:S(2)}) %collective-permute-start.3) | collective-permute-done | bytes 16416 | tf_op jit(solution)/shard_map/ppermute | solution.py:16
  13.8 3.5 %while.22 = (s32[]{:T(128)}, f32[4,512]{1,0:T(4,128)S(1)}, f32[1,512]{1,0:T(1,128)S(1)}, f32[4,512,4]{1,2,0:T(4,128)S(1)}, f32[1,512]{1,0:T(1,128)S(1)}, /*index=5*/f32[1,512]{1,0:T(1,128)S(1)}, s32[]{:T(128)}, s32[]{:T(128)}) while((s32[]{:T(128)}, f32[4,512]{1,0:T(4,128)S(1)}, f32[1,512]{1,0:T(1,128)S(1)}, ...), condition=%wide.region_5.6_spmd.clone, body=%wide.region_0.5_spmd.clone.sunk | while | flops 4988931 | bytes 79979 | solution.py:48
  13.8 0.8 %multiply_reduce_fusion.6 = (f32[512]{0:T(512)S(1)}, f32[512]{0:T(512)S(1)}, f32[512]{0:T(512)S(1)}, f32[512]{0:T(512)S(1)}) fusion(f32[512]{0:T(512)S(1)} %bitcast.147, f32[512]{0:T(512)S(1)} %bitcast.148, f32[512]{0:T(512)S(1)} %bitcast.159, f32[512]{0:T(512)S(1)} %bitcast.149, f32[512]{0:T(512)S(1)} %bitcast.160, f32[512]{0:T(512)S(1)} %bitcast.146, ...), kind=kLoop, calls=%fused_computation.1.clone.1 | loop fusion | flops 4978688 | bytes 22528 | tf_op jit(solution)/shard_map/while/body/eval_jaxpr/reduce_sum | solution.py:43
  17.3 1.6 %collective-permute-start.4 = (f32[4,512]{1,0:T(4,128)S(1)}, f32[4,512]{1,0:T(4,128)S(1)}, u32[]{:S(2)}, u32[]{:S(2)}) collective-permute-start(f32[4,512]{1,0:T(4,128)S(1)} %get-tuple-element.62), channel_id=1, source_target_pairs={{0,1},{1,0},{2,3},{3,2},{4,5},{5,4},{6,7},{7,6},{8,9},{9,8},{10,11... | collective-permute-start | bytes 24584 | tf_op jit(solution)/shard_map/ppermute | solution.py:28
  18.9 2.2 %collective-permute-done.4 = f32[4,512]{1,0:T(4,128)S(1)} collective-permute-done((f32[4,512]{1,0:T(4,128)S(1)}, f32[4,512]{1,0:T(4,128)S(1)}, u32[]{:S(2)}, u32[]{:S(2)}) %collective-permute-start.4) | collective-permute-done | bytes 8224 | tf_op jit(solution)/shard_map/ppermute | solution.py:28
  21.0 1.2 %collective-permute-done.5 = f32[4,512]{1,0:T(4,128)S(1)} collective-permute-done((f32[4,512]{1,0:T(4,128)S(1)}, f32[4,512]{1,0:T(4,128)S(1)}, u32[]{:S(2)}, u32[]{:S(2)}) %collective-permute-start.5) | collective-permute-done | bytes 8224 | tf_op jit(solution)/shard_map/ppermute | solution.py:28
  22.2 1.5 %collective-permute-start.6 = (f32[4,512]{1,0:T(4,128)S(1)}, f32[4,512]{1,0:T(4,128)S(1)}, u32[]{:S(2)}, u32[]{:S(2)}) collective-permute-start(f32[4,512]{1,0:T(4,128)S(1)} %add.143), channel_id=1, source_target_pairs={{0,4},{2,6},{4,0},{6,2},{8,12},{10,14},{12,8},{14,10},{16,20},{18,... | collective-permute-start | bytes 24584 | tf_op jit(solution)/shard_map/ppermute | solution.py:28
  23.7 2.1 %collective-permute-done.6 = f32[4,512]{1,0:T(4,128)S(1)} collective-permute-done((f32[4,512]{1,0:T(4,128)S(1)}, f32[4,512]{1,0:T(4,128)S(1)}, u32[]{:S(2)}, u32[]{:S(2)}) %collective-permute-start.6) | collective-permute-done | bytes 8224 | tf_op jit(solution)/shard_map/ppermute | solution.py:28
  26.6 3.1 %collective-permute-done.7 = f32[6,512]{1,0:T(8,128)S(1)} collective-permute-done((f32[6,512]{1,0:T(8,128)S(1)}, f32[6,512]{1,0:T(8,128)S(1)}, u32[]{:S(2)}, u32[]{:S(2)}) %collective-permute-start.7) | collective-permute-done | bytes 12320 | tf_op jit(solution)/shard_map/ppermute | solution.py:16
  29.7 2.5 %collective-permute-start.8 = (f32[6,1024]{1,0:T(8,128)S(1)}, f32[6,1024]{1,0:T(8,128)S(1)}, u32[]{:S(2)}, u32[]{:S(2)}) collective-permute-start(f32[6,1024]{1,0:T(8,128)S(1)} %maximum_select_fusion.2), channel_id=1, source_target_pairs={{0,16},{2,18},{4,20},{6,22},{8,24},{10,26},{12,28},{14,30},{16,0},... | collective-permute-start | bytes 73736 | tf_op jit(solution)/shard_map/ppermute | solution.py:16
  32.3 2.5 %collective-permute-done.8 = f32[6,1024]{1,0:T(8,128)S(1)} collective-permute-done((f32[6,1024]{1,0:T(8,128)S(1)}, f32[6,1024]{1,0:T(8,128)S(1)}, u32[]{:S(2)}, u32[]{:S(2)}) %collective-permute-start.8) | collective-permute-done | bytes 24608 | tf_op jit(solution)/shard_map/ppermute | solution.py:16
  35.7 2.9 %multiply_convert_fusion = bf16[128,2048]{0,1:T(8,128)(2,1)S(1)} fusion(f32[2048]{0:T(1024)S(1)} %bitcast.150, f32[128]{0:T(128)S(1)} %copy-done.8, f32[2048]{0:T(1024)S(1)} %bitcast.151, pred[2048]{0:T(1024)(128)(4,1)S(1)} %get-tuple-element.118, pred[2048]{0:T(1024)(128)(4,1)S(1)} %get-tuple-element.117, pred[2048]{0:T(1024)(128)(4,1)S(1)} %get-tuple-element.116, ...), kind=kLoop, calls=%fused_computation.47 | loop fusion | flops 3145728 | bytes 557568 | tf_op jit(solution)/shard_map/convert_element_type | solution.py:124
  38.6 0.8 %fusion.16 = bf16[128,128]{1,0:T(8,128)(2,1)S(1)} fusion(bf16[128,128]{1,0:T(8,128)(2,1)S(1)} %copy-done.9, bf16[128,2048]{0,1:T(8,128)(2,1)S(1)} %multiply_convert_fusion, s32[128]{0:T(128)S(1)} %get-tuple-element.162, s32[128]{0:T(128)S(1)} %get-tuple-element.163, s32[128]{0:T(128)S(1)} %get-tuple-element.164, s32[128]{0:T(128)S(1)} %get-tuple-element.161, ...), kind=kOutput, calls=%fused_computation.36 | convolution fusion | flops 75563008 | bytes 624644 | tf_op jit(solution)/shard_map/dot_general | solution.py:136
  41.6 1.2 %collective-permute-done.9 = f32[2048]{0:T(1024)S(1)} collective-permute-done((f32[2048]{0:T(1024)S(1)}, f32[2048]{0:T(1024)S(1)}, u32[]{:S(2)}, u32[]{:S(2)}) %collective-permute-start.9) | collective-permute-done | bytes 8224 | tf_op jit(solution)/shard_map/ppermute | solution.py:28
  42.8 1.5 %collective-permute-start.10 = (f32[2048]{0:T(1024)S(1)}, f32[2048]{0:T(1024)S(1)}, u32[]{:S(2)}, u32[]{:S(2)}) collective-permute-start(f32[2048]{0:T(1024)S(1)} %add.161), channel_id=1, source_target_pairs={{0,4},{2,6},{4,0},{6,2},{8,12},{10,14},{12,8},{14,10},{16,20},{18,... | collective-permute-start | bytes 24584 | tf_op jit(solution)/shard_map/ppermute | solution.py:28
  44.3 2.1 %collective-permute-done.10 = f32[2048]{0:T(1024)S(1)} collective-permute-done((f32[2048]{0:T(1024)S(1)}, f32[2048]{0:T(1024)S(1)}, u32[]{:S(2)}, u32[]{:S(2)}) %collective-permute-start.10) | collective-permute-done | bytes 8224 | tf_op jit(solution)/shard_map/ppermute | solution.py:28
  46.6 3.4 %collective-permute-done.11 = f32[2048]{0:T(1024)S(1)} collective-permute-done((f32[2048]{0:T(1024)S(1)}, f32[2048]{0:T(1024)S(1)}, u32[]{:S(2)}, u32[]{:S(2)}) %collective-permute-start.11) | collective-permute-done | bytes 8224 | tf_op jit(solution)/shard_map/ppermute | solution.py:28
  50.1 2.3 %collective-permute-start.12 = (f32[2048]{0:T(1024)S(1)}, f32[2048]{0:T(1024)S(1)}, u32[]{:S(2)}, u32[]{:S(2)}) collective-permute-start(f32[2048]{0:T(1024)S(1)} %add.163), channel_id=1, source_target_pairs={{0,16},{2,18},{4,20},{6,22},{8,24},{10,26},{12,28},{14,30},{16,0},... | collective-permute-start | bytes 24584 | tf_op jit(solution)/shard_map/ppermute | solution.py:28
  52.4 2.2 %collective-permute-done.12 = f32[2048]{0:T(1024)S(1)} collective-permute-done((f32[2048]{0:T(1024)S(1)}, f32[2048]{0:T(1024)S(1)}, u32[]{:S(2)}, u32[]{:S(2)}) %collective-permute-start.12) | collective-permute-done | bytes 8224 | tf_op jit(solution)/shard_map/ppermute | solution.py:28
  54.7 3.6 %while.23 = (s32[]{:T(128)}, f32[3,512]{1,0:T(4,128)S(1)}, f32[4,512,4]{1,2,0:T(4,128)S(1)}, f32[3,512]{1,0:T(4,128)S(1)}, f32[512]{0:T(512)S(1)}, /*index=5*/s32[]{:T(128)}, s32[]{:T(128)}) while((s32[]{:T(128)}, f32[3,512]{1,0:T(4,128)S(1)}, f32[4,512,4]{1,2,0:T(4,128)S(1)}, f32[3,512]{1,0:T(4,128)S(1)}, f32[512]{0:T(512)S(1)}, ...), condition=%wide.region_15.16_spmd.clone, body=%wide.region_11.15_spmd.clone.sunk | while | flops 4985347 | bytes 86115 | solution.py:63
  (111 shorter events, 11.4 us)
Async XLA Ops:
  0.6 38.8 %copy-start = (bf16[128,256]{1,0:T(8,128)(2,1)S(1)}, bf16[128,256]{1,0:T(8,128)(2,1)}, u32[]{:S(2)}) copy-start(bf16[128,256]{1,0:T(8,128)(2,1)} %param.27) | copy-start | bytes 196612
  0.6 0.7 %copy-start.12 = (s32[128]{0:T(128)S(1)}, s32[128]{0:T(128)}, u32[]{:S(2)}) copy-start(s32[128]{0:T(128)} %param.18) | copy-start | bytes 1540
  0.7 0.7 %copy-start.5 = (f32[3,128]{1,0:T(4,128)S(1)}, f32[3,128]{1,0:T(4,128)}, u32[]{:S(2)}) copy-start(f32[3,128]{1,0:T(4,128)} %param.17) | copy-start | bytes 4612
  1.3 0.7 %copy-start.1 = (f32[3,512]{1,0:T(4,128)S(1)}, f32[3,512]{1,0:T(4,128)}, u32[]{:S(2)}) copy-start(f32[3,512]{1,0:T(4,128)} %param.22) | copy-start | bytes 18436
  1.4 0.7 %copy-start.3 = (f32[512]{0:T(512)S(1)}, f32[512]{0:T(512)}, u32[]{:S(2)}) copy-start(f32[512]{0:T(512)} %param.23) | copy-start | bytes 6148
  1.4 3.8 %collective-permute-start = (f32[5,128]{1,0:T(8,128)S(1)}, f32[5,128]{1,0:T(8,128)S(1)}, u32[]{:S(2)}, u32[]{:S(2)}) collective-permute-start(f32[5,128]{1,0:T(8,128)S(1)} %pad_maximum_fusion.2), channel_id=1, source_target_pairs={{0,2},{2,0},{4,6},{6,4},{8,10},{10,8},{12,14},{14,12},{16,18},{18,... | collective-permute-start | bytes 7688 | tf_op jit(solution)/shard_map/ppermute | solution.py:16
  2.1 6.8 %collective-permute-start.2 = (f32[4,512]{1,0:T(4,128)S(1)}, f32[4,512]{1,0:T(4,128)S(1)}, u32[]{:S(2)}, u32[]{:S(2)}) collective-permute-start(f32[4,512]{1,0:T(4,128)S(1)} %pad_maximum_fusion.1), channel_id=1, source_target_pairs={{0,8},{2,10},{4,12},{6,14},{8,0},{10,2},{12,4},{14,6},{16,24},{18,... | collective-permute-start | bytes 24584 | tf_op jit(solution)/shard_map/ppermute | solution.py:16
  5.2 3.7 %collective-permute-start.1 = (f32[5,256]{1,0:T(8,128)S(1)}, f32[5,256]{1,0:T(8,128)S(1)}, u32[]{:S(2)}, u32[]{:S(2)}) collective-permute-start(f32[5,256]{1,0:T(8,128)S(1)} %maximum_select_fusion.6), channel_id=1, source_target_pairs={{0,4},{2,6},{4,0},{6,2},{8,12},{10,14},{12,8},{14,10},{16,20},{18,... | collective-permute-start | bytes 15368 | tf_op jit(solution)/shard_map/ppermute | solution.py:16
  9.0 4.8 %collective-permute-start.3 = (f32[4,1024]{1,0:T(4,128)S(1)}, f32[4,1024]{1,0:T(4,128)S(1)}, u32[]{:S(2)}, u32[]{:S(2)}) collective-permute-start(f32[4,1024]{1,0:T(4,128)S(1)} %maximum_select_fusion.5), channel_id=1, source_target_pairs={{0,16},{2,18},{4,20},{6,22},{8,24},{10,26},{12,28},{14,30},{16,0},... | collective-permute-start | bytes 49160 | tf_op jit(solution)/shard_map/ppermute | solution.py:16
  17.3 3.7 %collective-permute-start.4 = (f32[4,512]{1,0:T(4,128)S(1)}, f32[4,512]{1,0:T(4,128)S(1)}, u32[]{:S(2)}, u32[]{:S(2)}) collective-permute-start(f32[4,512]{1,0:T(4,128)S(1)} %get-tuple-element.62), channel_id=1, source_target_pairs={{0,1},{1,0},{2,3},{3,2},{4,5},{5,4},{6,7},{7,6},{8,9},{9,8},{10,11... | collective-permute-start | bytes 24584 | tf_op jit(solution)/shard_map/ppermute | solution.py:28
  21.0 1.2 %collective-permute-start.5 = (f32[4,512]{1,0:T(4,128)S(1)}, f32[4,512]{1,0:T(4,128)S(1)}, u32[]{:S(2)}, u32[]{:S(2)}) collective-permute-start(f32[4,512]{1,0:T(4,128)S(1)} %add.142), channel_id=1, source_target_pairs={{0,2},{2,0},{4,6},{6,4},{8,10},{10,8},{12,14},{14,12},{16,18},{18,... | collective-permute-start | bytes 24584 | tf_op jit(solution)/shard_map/ppermute | solution.py:28
  22.2 1.5 %copy-start.4 = (bf16[8,128]{1,0:T(8,128)(2,1)S(1)}, bf16[8,128]{1,0:T(8,128)(2,1)}, u32[]{:S(2)}) copy-start(bf16[8,128]{1,0:T(8,128)(2,1)} %param.24) | copy-start | bytes 6148
  22.2 3.7 %collective-permute-start.6 = (f32[4,512]{1,0:T(4,128)S(1)}, f32[4,512]{1,0:T(4,128)S(1)}, u32[]{:S(2)}, u32[]{:S(2)}) collective-permute-start(f32[4,512]{1,0:T(4,128)S(1)} %add.143), channel_id=1, source_target_pairs={{0,4},{2,6},{4,0},{6,2},{8,12},{10,14},{12,8},{14,10},{16,20},{18,... | collective-permute-start | bytes 24584 | tf_op jit(solution)/shard_map/ppermute | solution.py:28
  25.9 0.7 %copy-start.6 = (s32[128,4]{0,1:T(4,128)S(1)}, s32[128,4]{0,1:T(4,128)}, u32[]{:S(2)}) copy-start(s32[128,4]{0,1:T(4,128)} %param.21) | copy-start | bytes 6148
  25.9 0.7 %copy-start.7 = (s32[128,4]{0,1:T(4,128)S(1)}, s32[128,4]{0,1:T(4,128)}, u32[]{:S(2)}) copy-start(s32[128,4]{0,1:T(4,128)} %param.20) | copy-start | bytes 6148
  25.9 3.8 %collective-permute-start.7 = (f32[6,512]{1,0:T(8,128)S(1)}, f32[6,512]{1,0:T(8,128)S(1)}, u32[]{:S(2)}, u32[]{:S(2)}) collective-permute-start(f32[6,512]{1,0:T(8,128)S(1)} %pad_maximum_fusion), channel_id=1, source_target_pairs={{0,8},{2,10},{4,12},{6,14},{8,0},{10,2},{12,4},{14,6},{16,24},{18,... | collective-permute-start | bytes 36872 | tf_op jit(solution)/shard_map/ppermute | solution.py:16
  29.7 5.1 %collective-permute-start.8 = (f32[6,1024]{1,0:T(8,128)S(1)}, f32[6,1024]{1,0:T(8,128)S(1)}, u32[]{:S(2)}, u32[]{:S(2)}) collective-permute-start(f32[6,1024]{1,0:T(8,128)S(1)} %maximum_select_fusion.2), channel_id=1, source_target_pairs={{0,16},{2,18},{4,20},{6,22},{8,24},{10,26},{12,28},{14,30},{16,0},... | collective-permute-start | bytes 73736 | tf_op jit(solution)/shard_map/ppermute | solution.py:16
  35.7 2.9 %copy-start.9 = (bf16[128,128]{1,0:T(8,128)(2,1)S(1)}, bf16[128,128]{1,0:T(8,128)(2,1)}, u32[]{:S(2)}) copy-start(bf16[128,128]{1,0:T(8,128)(2,1)} %param.26) | copy-start | bytes 98308
  38.6 0.8 %copy-start.10 = (f32[256]{0:T(256)S(1)}, f32[256]{0:T(256)}, u32[]{:S(2)}) copy-start(f32[256]{0:T(256)} %param.29) | copy-start | bytes 3076
  38.6 0.8 %copy-start.11 = (f32[256]{0:T(256)S(1)}, f32[256]{0:T(256)}, u32[]{:S(2)}) copy-start(f32[256]{0:T(256)} %param.28) | copy-start | bytes 3076
  41.5 1.2 %collective-permute-start.9 = (f32[2048]{0:T(1024)S(1)}, f32[2048]{0:T(1024)S(1)}, u32[]{:S(2)}, u32[]{:S(2)}) collective-permute-start(f32[2048]{0:T(1024)S(1)} %fusion.38), channel_id=1, source_target_pairs={{0,2},{2,0},{4,6},{6,4},{8,10},{10,8},{12,14},{14,12},{16,18},{18,... | collective-permute-start | bytes 24584 | tf_op jit(solution)/shard_map/ppermute | solution.py:28
  42.8 3.7 %collective-permute-start.10 = (f32[2048]{0:T(1024)S(1)}, f32[2048]{0:T(1024)S(1)}, u32[]{:S(2)}, u32[]{:S(2)}) collective-permute-start(f32[2048]{0:T(1024)S(1)} %add.161), channel_id=1, source_target_pairs={{0,4},{2,6},{4,0},{6,2},{8,12},{10,14},{12,8},{14,10},{16,20},{18,... | collective-permute-start | bytes 24584 | tf_op jit(solution)/shard_map/ppermute | solution.py:28
  46.4 3.7 %collective-permute-start.11 = (f32[2048]{0:T(1024)S(1)}, f32[2048]{0:T(1024)S(1)}, u32[]{:S(2)}, u32[]{:S(2)}) collective-permute-start(f32[2048]{0:T(1024)S(1)} %add.162), channel_id=1, source_target_pairs={{0,8},{2,10},{4,12},{6,14},{8,0},{10,2},{12,4},{14,6},{16,24},{18,... | collective-permute-start | bytes 24584 | tf_op jit(solution)/shard_map/ppermute | solution.py:28
  50.1 4.5 %collective-permute-start.12 = (f32[2048]{0:T(1024)S(1)}, f32[2048]{0:T(1024)S(1)}, u32[]{:S(2)}, u32[]{:S(2)}) collective-permute-start(f32[2048]{0:T(1024)S(1)} %add.163), channel_id=1, source_target_pairs={{0,16},{2,18},{4,20},{6,22},{8,24},{10,26},{12,28},{14,30},{16,0},... | collective-permute-start | bytes 24584 | tf_op jit(solution)/shard_map/ppermute | solution.py:28
  (2 other events, 1.3 us)

commit v5 on v4

--- a/solution.py
+++ b/solution.py
@@ -114,11 +114,8 @@
 
     live = lax.dynamic_slice_in_dim(live_all, me * rows, rows)
     potential = lax.dynamic_slice_in_dim(potential_all, me * rows, rows)
-    table_t = species_table.T
-    base_t = jnp.broadcast_to(table_t[:, 0:1], (table_t.shape[0], atoms))
-    for kind in range(1, kinds):
-        base_t = jnp.where(species_all[None, :] == kind, table_t[:, kind : kind + 1], base_t)
-    base_t = base_t.astype(jnp.float32)
+    picks_t = (jnp.arange(kinds)[:, None] == species_all[None, :]).astype(jnp.bfloat16)
+    base_t = jnp.dot(species_table.T, picks_t, preferred_element_type=jnp.float32)
     start_t = (
         live_all[None, :] * (base_t + potential_gain[:, None] * potential_all[None, :])
     ).astype(jnp.bfloat16)

time: 59.2 us -> 57 us (0.963)
  other arithmetic: 11.8 us -> 8.78 us
  matrix products: 1.5 us -> 2.39 us
    convert_element_type x1 -> x0, other arithmetic: 2.9 us -> none  [on_device(): start_t = (live_all[None, :] * (base_t + potential_gain[:, None] * potent...]
    dot_general x0 -> x1, matrix products: none -> 0.9 us  [on_device(): jnp.dot(species_table.T, picks_t, preferred_element_type=jnp.float32)]
where the time goes in v5:
time: 57 us; the launch traced here: 56.8 us
  waiting for transfers between devices  24.3 us (43%)
  starting transfers between devices  18 us (32%)
  other arithmetic  8.78 us (15%)
  matrix products  2.39 us (4%)
  between operations  1.65 us (3%)
  local copies, waits for them, and re-layouts  1.27 us (2%)
    ppermute x7, waiting for transfers between devices, sum_butterfly(): x = x + lax.ppermute(x, axis, [(i, i ^ step) for i in range(n)])  14.4 us
    ppermute x6, starting transfers between devices, gather_doubling(): other = lax.ppermute(x, axis, [(i, i ^ step) for i in range(n)])  10.8 us
    ppermute x6, waiting for transfers between devices, gather_doubling(): other = lax.ppermute(x, axis, [(i, i ^ step) for i in range(n)])  9.91 us
    ppermute x7, starting transfers between devices, sum_butterfly(): x = x + lax.ppermute(x, axis, [(i, i ^ step) for i in range(n)])  7.19 us
    reduce_sum x4, other arithmetic, body(): jnp.sum(weighted, axis=0)  3.2 us
    reduce_sum x4, other arithmetic, body(): jnp.sum(d[c] * weight, axis=0)  3.19 us
  transfers between devices with their start and end apart: 13, of which 11 were waited for; matrix products, arithmetic and copies ran while one was open for 0% of the time, Pallas kernels for 0%

profile of v5, /device:TPU:0, one launch (start us, length us, event | category | flops | bytes accessed | tf_op | source)
XLA Modules:
  0.0 56.8 jit_solution(14269885668651337261)
XLA Ops:
  2.1 3.1 %collective-permute-start.2 = (f32[4,512]{1,0:T(4,128)S(1)}, f32[4,512]{1,0:T(4,128)S(1)}, u32[]{:S(2)}, u32[]{:S(2)}) collective-permute-start(f32[4,512]{1,0:T(4,128)S(1)} %pad_maximum_fusion.1), channel_id=1, source_target_pairs={{0,8},{2,10},{4,12},{6,14},{8,0},{10,2},{12,4},{14,6},{16,24},{18,... | collective-permute-start | bytes 24584 | tf_op jit(solution)/shard_map/ppermute | solution.py:16
  5.2 1.6 %collective-permute-start.1 = (f32[5,256]{1,0:T(8,128)S(1)}, f32[5,256]{1,0:T(8,128)S(1)}, u32[]{:S(2)}, u32[]{:S(2)}) collective-permute-start(f32[5,256]{1,0:T(8,128)S(1)} %maximum_select_fusion.6), channel_id=1, source_target_pairs={{0,4},{2,6},{4,0},{6,2},{8,12},{10,14},{12,8},{14,10},{16,20},{18,... | collective-permute-start | bytes 15368 | tf_op jit(solution)/shard_map/ppermute | solution.py:16
  6.8 2.1 %collective-permute-done.1 = f32[5,256]{1,0:T(8,128)S(1)} collective-permute-done((f32[5,256]{1,0:T(8,128)S(1)}, f32[5,256]{1,0:T(8,128)S(1)}, u32[]{:S(2)}, u32[]{:S(2)}) %collective-permute-start.1) | collective-permute-done | bytes 5152 | tf_op jit(solution)/shard_map/ppermute | solution.py:16
  9.0 2.7 %collective-permute-start.3 = (f32[4,1024]{1,0:T(4,128)S(1)}, f32[4,1024]{1,0:T(4,128)S(1)}, u32[]{:S(2)}, u32[]{:S(2)}) collective-permute-start(f32[4,1024]{1,0:T(4,128)S(1)} %maximum_select_fusion.5), channel_id=1, source_target_pairs={{0,16},{2,18},{4,20},{6,22},{8,24},{10,26},{12,28},{14,30},{16,0},... | collective-permute-start | bytes 49160 | tf_op jit(solution)/shard_map/ppermute | solution.py:16
  11.6 2.2 %collective-permute-done.3 = f32[4,1024]{1,0:T(4,128)S(1)} collective-permute-done((f32[4,1024]{1,0:T(4,128)S(1)}, f32[4,1024]{1,0:T(4,128)S(1)}, u32[]{:S(2)}, u32[]{:S(2)}) %collective-permute-start.3) | collective-permute-done | bytes 16416 | tf_op jit(solution)/shard_map/ppermute | solution.py:16
  13.8 3.5 %while.22 = (s32[]{:T(128)}, f32[4,512]{1,0:T(4,128)S(1)}, f32[1,512]{1,0:T(1,128)S(1)}, f32[4,512,4]{1,2,0:T(4,128)S(1)}, f32[1,512]{1,0:T(1,128)S(1)}, /*index=5*/f32[1,512]{1,0:T(1,128)S(1)}, s32[]{:T(128)}, s32[]{:T(128)}) while((s32[]{:T(128)}, f32[4,512]{1,0:T(4,128)S(1)}, f32[1,512]{1,0:T(1,128)S(1)}, ...), condition=%wide.region_5.6_spmd.clone, body=%wide.region_0.5_spmd.clone.sunk | while | flops 4988931 | bytes 79979 | solution.py:48
  13.8 0.8 %multiply_reduce_fusion.6 = (f32[512]{0:T(512)S(1)}, f32[512]{0:T(512)S(1)}, f32[512]{0:T(512)S(1)}, f32[512]{0:T(512)S(1)}) fusion(f32[512]{0:T(512)S(1)} %bitcast.140, f32[512]{0:T(512)S(1)} %bitcast.141, f32[512]{0:T(512)S(1)} %bitcast.152, f32[512]{0:T(512)S(1)} %bitcast.142, f32[512]{0:T(512)S(1)} %bitcast.153, f32[512]{0:T(512)S(1)} %bitcast.139, ...), kind=kLoop, calls=%fused_computation.1.clone.1 | loop fusion | flops 4978688 | bytes 22528 | tf_op jit(solution)/shard_map/while/body/eval_jaxpr/reduce_sum | solution.py:43
  17.3 1.6 %collective-permute-start.4 = (f32[4,512]{1,0:T(4,128)S(1)}, f32[4,512]{1,0:T(4,128)S(1)}, u32[]{:S(2)}, u32[]{:S(2)}) collective-permute-start(f32[4,512]{1,0:T(4,128)S(1)} %get-tuple-element.62), channel_id=1, source_target_pairs={{0,1},{1,0},{2,3},{3,2},{4,5},{5,4},{6,7},{7,6},{8,9},{9,8},{10,11... | collective-permute-start | bytes 24584 | tf_op jit(solution)/shard_map/ppermute | solution.py:28
  18.9 2.2 %collective-permute-done.4 = f32[4,512]{1,0:T(4,128)S(1)} collective-permute-done((f32[4,512]{1,0:T(4,128)S(1)}, f32[4,512]{1,0:T(4,128)S(1)}, u32[]{:S(2)}, u32[]{:S(2)}) %collective-permute-start.4) | collective-permute-done | bytes 8224 | tf_op jit(solution)/shard_map/ppermute | solution.py:28
  21.0 1.2 %collective-permute-done.5 = f32[4,512]{1,0:T(4,128)S(1)} collective-permute-done((f32[4,512]{1,0:T(4,128)S(1)}, f32[4,512]{1,0:T(4,128)S(1)}, u32[]{:S(2)}, u32[]{:S(2)}) %collective-permute-start.5) | collective-permute-done | bytes 8224 | tf_op jit(solution)/shard_map/ppermute | solution.py:28
  22.2 1.5 %collective-permute-start.6 = (f32[4,512]{1,0:T(4,128)S(1)}, f32[4,512]{1,0:T(4,128)S(1)}, u32[]{:S(2)}, u32[]{:S(2)}) collective-permute-start(f32[4,512]{1,0:T(4,128)S(1)} %add.143), channel_id=1, source_target_pairs={{0,4},{2,6},{4,0},{6,2},{8,12},{10,14},{12,8},{14,10},{16,20},{18,... | collective-permute-start | bytes 24584 | tf_op jit(solution)/shard_map/ppermute | solution.py:28
  23.7 2.1 %collective-permute-done.6 = f32[4,512]{1,0:T(4,128)S(1)} collective-permute-done((f32[4,512]{1,0:T(4,128)S(1)}, f32[4,512]{1,0:T(4,128)S(1)}, u32[]{:S(2)}, u32[]{:S(2)}) %collective-permute-start.6) | collective-permute-done | bytes 8224 | tf_op jit(solution)/shard_map/ppermute | solution.py:28
  26.6 3.1 %collective-permute-done.7 = f32[6,512]{1,0:T(8,128)S(1)} collective-permute-done((f32[6,512]{1,0:T(8,128)S(1)}, f32[6,512]{1,0:T(8,128)S(1)}, u32[]{:S(2)}, u32[]{:S(2)}) %collective-permute-start.7) | collective-permute-done | bytes 12320 | tf_op jit(solution)/shard_map/ppermute | solution.py:16
  29.7 2.5 %collective-permute-start.8 = (f32[6,1024]{1,0:T(8,128)S(1)}, f32[6,1024]{1,0:T(8,128)S(1)}, u32[]{:S(2)}, u32[]{:S(2)}) collective-permute-start(f32[6,1024]{1,0:T(8,128)S(1)} %maximum_select_fusion.2), channel_id=1, source_target_pairs={{0,16},{2,18},{4,20},{6,22},{8,24},{10,26},{12,28},{14,30},{16,0},... | collective-permute-start | bytes 73736 | tf_op jit(solution)/shard_map/ppermute | solution.py:16
  32.3 2.5 %collective-permute-done.8 = f32[6,1024]{1,0:T(8,128)S(1)} collective-permute-done((f32[6,1024]{1,0:T(8,128)S(1)}, f32[6,1024]{1,0:T(8,128)S(1)}, u32[]{:S(2)}, u32[]{:S(2)}) %collective-permute-start.8) | collective-permute-done | bytes 24608 | tf_op jit(solution)/shard_map/ppermute | solution.py:16
  35.6 0.9 %fusion.18 = bf16[128,2048]{0,1:T(8,128)(2,1)S(1)} fusion(bf16[8,128]{1,0:T(8,128)(2,1)S(1)} %copy-done.8, f32[2048]{0:T(1024)S(1)} %bitcast.149, f32[128]{0:T(128)S(1)} %copy-done.12, f32[2048]{0:T(1024)S(1)} %bitcast.150, s32[2048]{0:T(1024)S(1)} %bitcast.151), kind=kOutput, calls=%fused_computation.38 | convolution fusion | flops 5259264 | bytes 551424 | tf_op jit(solution)/shard_map/dot_general | solution.py:118
  36.5 0.8 %fusion.19 = bf16[128,128]{1,0:T(8,128)(2,1)S(1)} fusion(bf16[128,128]{1,0:T(8,128)(2,1)S(1)} %copy-done.7, bf16[128,2048]{0,1:T(8,128)(2,1)S(1)} %fusion.18, s32[128]{0:T(128)S(1)} %get-tuple-element.155, s32[128]{0:T(128)S(1)} %get-tuple-element.156, s32[128]{0:T(128)S(1)} %get-tuple-element.157, s32[128]{0:T(128)S(1)} %get-tuple-element.154, ...), kind=kOutput, calls=%fused_computation.40 | convolution fusion | flops 75563008 | bytes 624644 | tf_op jit(solution)/shard_map/dot_general | solution.py:133
  39.4 1.2 %collective-permute-done.9 = f32[2048]{0:T(1024)S(1)} collective-permute-done((f32[2048]{0:T(1024)S(1)}, f32[2048]{0:T(1024)S(1)}, u32[]{:S(2)}, u32[]{:S(2)}) %collective-permute-start.9) | collective-permute-done | bytes 8224 | tf_op jit(solution)/shard_map/ppermute | solution.py:28
  40.6 1.5 %collective-permute-start.10 = (f32[2048]{0:T(1024)S(1)}, f32[2048]{0:T(1024)S(1)}, u32[]{:S(2)}, u32[]{:S(2)}) collective-permute-start(f32[2048]{0:T(1024)S(1)} %add.161), channel_id=1, source_target_pairs={{0,4},{2,6},{4,0},{6,2},{8,12},{10,14},{12,8},{14,10},{16,20},{18,... | collective-permute-start | bytes 24584 | tf_op jit(solution)/shard_map/ppermute | solution.py:28
  42.1 2.1 %collective-permute-done.10 = f32[2048]{0:T(1024)S(1)} collective-permute-done((f32[2048]{0:T(1024)S(1)}, f32[2048]{0:T(1024)S(1)}, u32[]{:S(2)}, u32[]{:S(2)}) %collective-permute-start.10) | collective-permute-done | bytes 8224 | tf_op jit(solution)/shard_map/ppermute | solution.py:28
  44.5 3.4 %collective-permute-done.11 = f32[2048]{0:T(1024)S(1)} collective-permute-done((f32[2048]{0:T(1024)S(1)}, f32[2048]{0:T(1024)S(1)}, u32[]{:S(2)}, u32[]{:S(2)}) %collective-permute-start.11) | collective-permute-done | bytes 8224 | tf_op jit(solution)/shard_map/ppermute | solution.py:28
  47.9 2.3 %collective-permute-start.12 = (f32[2048]{0:T(1024)S(1)}, f32[2048]{0:T(1024)S(1)}, u32[]{:S(2)}, u32[]{:S(2)}) collective-permute-start(f32[2048]{0:T(1024)S(1)} %add.163), channel_id=1, source_target_pairs={{0,16},{2,18},{4,20},{6,22},{8,24},{10,26},{12,28},{14,30},{16,0},... | collective-permute-start | bytes 24584 | tf_op jit(solution)/shard_map/ppermute | solution.py:28
  50.2 2.2 %collective-permute-done.12 = f32[2048]{0:T(1024)S(1)} collective-permute-done((f32[2048]{0:T(1024)S(1)}, f32[2048]{0:T(1024)S(1)}, u32[]{:S(2)}, u32[]{:S(2)}) %collective-permute-start.12) | collective-permute-done | bytes 8224 | tf_op jit(solution)/shard_map/ppermute | solution.py:28
  52.6 3.6 %while.23 = (s32[]{:T(128)}, f32[3,512]{1,0:T(4,128)S(1)}, f32[4,512,4]{1,2,0:T(4,128)S(1)}, f32[3,512]{1,0:T(4,128)S(1)}, f32[512]{0:T(512)S(1)}, /*index=5*/s32[]{:T(128)}, s32[]{:T(128)}) while((s32[]{:T(128)}, f32[3,512]{1,0:T(4,128)S(1)}, f32[4,512,4]{1,2,0:T(4,128)S(1)}, f32[3,512]{1,0:T(4,128)S(1)}, f32[512]{0:T(512)S(1)}, ...), condition=%wide.region_15.16_spmd.clone, body=%wide.region_11.15_spmd.clone.sunk | while | flops 4985347 | bytes 86115 | solution.py:63
  (110 shorter events, 11.2 us)
Async XLA Ops:
  0.6 36.7 %copy-start = (bf16[128,256]{1,0:T(8,128)(2,1)S(1)}, bf16[128,256]{1,0:T(8,128)(2,1)}, u32[]{:S(2)}) copy-start(bf16[128,256]{1,0:T(8,128)(2,1)} %param.27) | copy-start | bytes 196612
  0.6 0.7 %copy-start.11 = (s32[128]{0:T(128)S(1)}, s32[128]{0:T(128)}, u32[]{:S(2)}) copy-start(s32[128]{0:T(128)} %param.18) | copy-start | bytes 1540
  0.7 0.7 %copy-start.4 = (f32[3,128]{1,0:T(4,128)S(1)}, f32[3,128]{1,0:T(4,128)}, u32[]{:S(2)}) copy-start(f32[3,128]{1,0:T(4,128)} %param.17) | copy-start | bytes 4612
  1.3 0.7 %copy-start.1 = (f32[3,512]{1,0:T(4,128)S(1)}, f32[3,512]{1,0:T(4,128)}, u32[]{:S(2)}) copy-start(f32[3,512]{1,0:T(4,128)} %param.22) | copy-start | bytes 18436
  1.4 0.7 %copy-start.3 = (f32[512]{0:T(512)S(1)}, f32[512]{0:T(512)}, u32[]{:S(2)}) copy-start(f32[512]{0:T(512)} %param.23) | copy-start | bytes 6148
  1.4 3.8 %collective-permute-start = (f32[5,128]{1,0:T(8,128)S(1)}, f32[5,128]{1,0:T(8,128)S(1)}, u32[]{:S(2)}, u32[]{:S(2)}) collective-permute-start(f32[5,128]{1,0:T(8,128)S(1)} %pad_maximum_fusion.2), channel_id=1, source_target_pairs={{0,2},{2,0},{4,6},{6,4},{8,10},{10,8},{12,14},{14,12},{16,18},{18,... | collective-permute-start | bytes 7688 | tf_op jit(solution)/shard_map/ppermute | solution.py:16
  2.1 6.8 %collective-permute-start.2 = (f32[4,512]{1,0:T(4,128)S(1)}, f32[4,512]{1,0:T(4,128)S(1)}, u32[]{:S(2)}, u32[]{:S(2)}) collective-permute-start(f32[4,512]{1,0:T(4,128)S(1)} %pad_maximum_fusion.1), channel_id=1, source_target_pairs={{0,8},{2,10},{4,12},{6,14},{8,0},{10,2},{12,4},{14,6},{16,24},{18,... | collective-permute-start | bytes 24584 | tf_op jit(solution)/shard_map/ppermute | solution.py:16
  5.2 3.7 %collective-permute-start.1 = (f32[5,256]{1,0:T(8,128)S(1)}, f32[5,256]{1,0:T(8,128)S(1)}, u32[]{:S(2)}, u32[]{:S(2)}) collective-permute-start(f32[5,256]{1,0:T(8,128)S(1)} %maximum_select_fusion.6), channel_id=1, source_target_pairs={{0,4},{2,6},{4,0},{6,2},{8,12},{10,14},{12,8},{14,10},{16,20},{18,... | collective-permute-start | bytes 15368 | tf_op jit(solution)/shard_map/ppermute | solution.py:16
  9.0 4.8 %collective-permute-start.3 = (f32[4,1024]{1,0:T(4,128)S(1)}, f32[4,1024]{1,0:T(4,128)S(1)}, u32[]{:S(2)}, u32[]{:S(2)}) collective-permute-start(f32[4,1024]{1,0:T(4,128)S(1)} %maximum_select_fusion.5), channel_id=1, source_target_pairs={{0,16},{2,18},{4,20},{6,22},{8,24},{10,26},{12,28},{14,30},{16,0},... | collective-permute-start | bytes 49160 | tf_op jit(solution)/shard_map/ppermute | solution.py:16
  17.3 3.7 %collective-permute-start.4 = (f32[4,512]{1,0:T(4,128)S(1)}, f32[4,512]{1,0:T(4,128)S(1)}, u32[]{:S(2)}, u32[]{:S(2)}) collective-permute-start(f32[4,512]{1,0:T(4,128)S(1)} %get-tuple-element.62), channel_id=1, source_target_pairs={{0,1},{1,0},{2,3},{3,2},{4,5},{5,4},{6,7},{7,6},{8,9},{9,8},{10,11... | collective-permute-start | bytes 24584 | tf_op jit(solution)/shard_map/ppermute | solution.py:28
  21.0 1.2 %collective-permute-start.5 = (f32[4,512]{1,0:T(4,128)S(1)}, f32[4,512]{1,0:T(4,128)S(1)}, u32[]{:S(2)}, u32[]{:S(2)}) collective-permute-start(f32[4,512]{1,0:T(4,128)S(1)} %add.142), channel_id=1, source_target_pairs={{0,2},{2,0},{4,6},{6,4},{8,10},{10,8},{12,14},{14,12},{16,18},{18,... | collective-permute-start | bytes 24584 | tf_op jit(solution)/shard_map/ppermute | solution.py:28
  22.2 3.7 %collective-permute-start.6 = (f32[4,512]{1,0:T(4,128)S(1)}, f32[4,512]{1,0:T(4,128)S(1)}, u32[]{:S(2)}, u32[]{:S(2)}) collective-permute-start(f32[4,512]{1,0:T(4,128)S(1)} %add.143), channel_id=1, source_target_pairs={{0,4},{2,6},{4,0},{6,2},{8,12},{10,14},{12,8},{14,10},{16,20},{18,... | collective-permute-start | bytes 24584 | tf_op jit(solution)/shard_map/ppermute | solution.py:28
  25.9 0.7 %copy-start.5 = (s32[128,4]{0,1:T(4,128)S(1)}, s32[128,4]{0,1:T(4,128)}, u32[]{:S(2)}) copy-start(s32[128,4]{0,1:T(4,128)} %param.21) | copy-start | bytes 6148
  25.9 0.7 %copy-start.6 = (s32[128,4]{0,1:T(4,128)S(1)}, s32[128,4]{0,1:T(4,128)}, u32[]{:S(2)}) copy-start(s32[128,4]{0,1:T(4,128)} %param.20) | copy-start | bytes 6148
  25.9 3.8 %collective-permute-start.7 = (f32[6,512]{1,0:T(8,128)S(1)}, f32[6,512]{1,0:T(8,128)S(1)}, u32[]{:S(2)}, u32[]{:S(2)}) collective-permute-start(f32[6,512]{1,0:T(8,128)S(1)} %pad_maximum_fusion), channel_id=1, source_target_pairs={{0,8},{2,10},{4,12},{6,14},{8,0},{10,2},{12,4},{14,6},{16,24},{18,... | collective-permute-start | bytes 36872 | tf_op jit(solution)/shard_map/ppermute | solution.py:16
  29.7 5.1 %collective-permute-start.8 = (f32[6,1024]{1,0:T(8,128)S(1)}, f32[6,1024]{1,0:T(8,128)S(1)}, u32[]{:S(2)}, u32[]{:S(2)}) collective-permute-start(f32[6,1024]{1,0:T(8,128)S(1)} %maximum_select_fusion.2), channel_id=1, source_target_pairs={{0,16},{2,18},{4,20},{6,22},{8,24},{10,26},{12,28},{14,30},{16,0},... | collective-permute-start | bytes 73736 | tf_op jit(solution)/shard_map/ppermute | solution.py:16
  34.9 0.7 %copy-start.8 = (bf16[8,128]{1,0:T(8,128)(2,1)S(1)}, bf16[8,128]{1,0:T(8,128)(2,1)}, u32[]{:S(2)}) copy-start(bf16[8,128]{1,0:T(8,128)(2,1)} %param.24) | copy-start | bytes 6148
  35.6 0.9 %copy-start.7 = (bf16[128,128]{1,0:T(8,128)(2,1)S(1)}, bf16[128,128]{1,0:T(8,128)(2,1)}, u32[]{:S(2)}) copy-start(bf16[128,128]{1,0:T(8,128)(2,1)} %param.26) | copy-start | bytes 98308
  36.5 0.8 %copy-start.9 = (f32[256]{0:T(256)S(1)}, f32[256]{0:T(256)}, u32[]{:S(2)}) copy-start(f32[256]{0:T(256)} %param.29) | copy-start | bytes 3076
  36.5 0.8 %copy-start.10 = (f32[256]{0:T(256)S(1)}, f32[256]{0:T(256)}, u32[]{:S(2)}) copy-start(f32[256]{0:T(256)} %param.28) | copy-start | bytes 3076
  39.4 1.2 %collective-permute-start.9 = (f32[2048]{0:T(1024)S(1)}, f32[2048]{0:T(1024)S(1)}, u32[]{:S(2)}, u32[]{:S(2)}) collective-permute-start(f32[2048]{0:T(1024)S(1)} %fusion.42), channel_id=1, source_target_pairs={{0,2},{2,0},{4,6},{6,4},{8,10},{10,8},{12,14},{14,12},{16,18},{18,... | collective-permute-start | bytes 24584 | tf_op jit(solution)/shard_map/ppermute | solution.py:28
  40.6 3.7 %collective-permute-start.10 = (f32[2048]{0:T(1024)S(1)}, f32[2048]{0:T(1024)S(1)}, u32[]{:S(2)}, u32[]{:S(2)}) collective-permute-start(f32[2048]{0:T(1024)S(1)} %add.161), channel_id=1, source_target_pairs={{0,4},{2,6},{4,0},{6,2},{8,12},{10,14},{12,8},{14,10},{16,20},{18,... | collective-permute-start | bytes 24584 | tf_op jit(solution)/shard_map/ppermute | solution.py:28
  44.3 3.7 %collective-permute-start.11 = (f32[2048]{0:T(1024)S(1)}, f32[2048]{0:T(1024)S(1)}, u32[]{:S(2)}, u32[]{:S(2)}) collective-permute-start(f32[2048]{0:T(1024)S(1)} %add.162), channel_id=1, source_target_pairs={{0,8},{2,10},{4,12},{6,14},{8,0},{10,2},{12,4},{14,6},{16,24},{18,... | collective-permute-start | bytes 24584 | tf_op jit(solution)/shard_map/ppermute | solution.py:28
  47.9 4.5 %collective-permute-start.12 = (f32[2048]{0:T(1024)S(1)}, f32[2048]{0:T(1024)S(1)}, u32[]{:S(2)}, u32[]{:S(2)}) collective-permute-start(f32[2048]{0:T(1024)S(1)} %add.163), channel_id=1, source_target_pairs={{0,16},{2,18},{4,20},{6,22},{8,24},{10,26},{12,28},{14,30},{16,0},... | collective-permute-start | bytes 24584 | tf_op jit(solution)/shard_map/ppermute | solution.py:28
  (2 other events, 1.3 us)

commit v6 on v5

--- a/solution.py
+++ b/solution.py
@@ -97,6 +97,7 @@
         axis=0,
     )
     near = gather_doubling(own, "blk", 1, low_blocks)
+    near, table_t = lax.optimization_barrier((near, species_table.T))
     mm_some = gather_doubling(
         jnp.concatenate([mm_pos, mm_charge[None, :]], axis=0), "blk", low_blocks, blocks
     )
@@ -115,7 +116,7 @@
     live = lax.dynamic_slice_in_dim(live_all, me * rows, rows)
     potential = lax.dynamic_slice_in_dim(potential_all, me * rows, rows)
     picks_t = (jnp.arange(kinds)[:, None] == species_all[None, :]).astype(jnp.bfloat16)
-    base_t = jnp.dot(species_table.T, picks_t, preferred_element_type=jnp.float32)
+    base_t = jnp.dot(table_t, picks_t, preferred_element_type=jnp.float32)
     start_t = (
         live_all[None, :] * (base_t + potential_gain[:, None] * potential_all[None, :])
     ).astype(jnp.bfloat16)
@@ -153,9 +154,12 @@
     local = charge_part + live * jnp.sum(back_mixed * potential_gain[None, :], axis=1)
     placed = (jnp.arange(atoms) // rows == me).astype(jnp.float32)
     local_all = jnp.tile(local, atoms // rows) * placed
-    effective_all = sum_butterfly(spread + local_all, "blk")
-    effective = lax.dynamic_slice_in_dim(effective_all, me * rows, rows)
-
+    part = sum_butterfly(spread + local_all, "blk", blocks // 2)
+    other = lax.ppermute(part, "blk", [(i, i ^ (blocks // 2)) for i in range(blocks)])
+    effective_all = part + other
+    effective = lax.dynamic_slice_in_dim(part, me * rows, rows) + lax.dynamic_slice_in_dim(
+        other, me * rows, rows
+    )
     qm_force = pull * (effective * coupling)[None, :]
     mm_force = force_pass(qm_all, effective_all, mm_pos, -coupling * mm_charge)
     return (atom_energy, qm_force, mm_force)

time: 57 us -> 56.9 us (level)
    ppermute x0 -> x1, starting transfers between devices: none -> 2.29 us  [on_device(): lax.ppermute(part, 'blk', [(i, i ^ blocks // 2) for i in range(blocks)])]
    ppermute x7 -> x6, starting transfers between devices: 7.19 us -> 4.9 us  [sum_butterfly(): x = x + lax.ppermute(x, axis, [(i, i ^ step) for i in range(n)])]
    ppermute x7 -> x6, waiting for transfers between devices: 14.4 us -> 12.2 us  [sum_butterfly(): x = x + lax.ppermute(x, axis, [(i, i ^ step) for i in range(n)])]
    ppermute x0 -> x1, waiting for transfers between devices: none -> 2.23 us  [on_device(): lax.ppermute(part, 'blk', [(i, i ^ blocks // 2) for i in range(blocks)])]
where the time goes in v6:
time: 56.9 us; the launch traced here: 56.6 us
  waiting for transfers between devices  24.3 us (43%)
  starting transfers between devices  18 us (32%)
  other arithmetic  8.78 us (15%)
  matrix products  1.87 us (3%)
  local copies, waits for them, and re-layouts  1.66 us (3%)
  between operations  1.64 us (3%)
    ppermute x6, waiting for transfers between devices, sum_butterfly(): x = x + lax.ppermute(x, axis, [(i, i ^ step) for i in range(n)])  12.2 us
    ppermute x6, starting transfers between devices, gather_doubling(): other = lax.ppermute(x, axis, [(i, i ^ step) for i in range(n)])  10.8 us
    ppermute x6, waiting for transfers between devices, gather_doubling(): other = lax.ppermute(x, axis, [(i, i ^ step) for i in range(n)])  9.91 us
    ppermute x6, starting transfers between devices, sum_butterfly(): x = x + lax.ppermute(x, axis, [(i, i ^ step) for i in range(n)])  4.9 us
    reduce_sum x4, other arithmetic, body(): jnp.sum(weighted, axis=0)  3.2 us
    reduce_sum x4, other arithmetic, body(): jnp.sum(d[c] * weight, axis=0)  3.19 us
    ppermute x1, starting transfers between devices, on_device(): lax.ppermute(part, 'blk', [(i, i ^ blocks // 2) for i in range(blocks)])  2.29 us
    ppermute x1, waiting for transfers between devices, on_device(): lax.ppermute(part, 'blk', [(i, i ^ blocks // 2) for i in range(blocks)])  2.23 us
  transfers between devices with their start and end apart: 13, of which 11 were waited for; matrix products, arithmetic and copies ran while one was open for 0% of the time, Pallas kernels for 0%

profile of v6, /device:TPU:0, one launch (start us, length us, event | category | flops | bytes accessed | tf_op | source)
XLA Modules:
  0.0 56.6 jit_solution(1142540131121911395)
XLA Ops:
  2.1 3.1 %collective-permute-start.2 = (f32[4,512]{1,0:T(4,128)S(1)}, f32[4,512]{1,0:T(4,128)S(1)}, u32[]{:S(2)}, u32[]{:S(2)}) collective-permute-start(f32[4,512]{1,0:T(4,128)S(1)} %pad_maximum_fusion.1), channel_id=1, source_target_pairs={{0,8},{2,10},{4,12},{6,14},{8,0},{10,2},{12,4},{14,6},{16,24},{18,... | collective-permute-start | bytes 24584 | tf_op jit(solution)/shard_map/ppermute | solution.py:16
  5.2 1.6 %collective-permute-start.1 = (f32[5,256]{1,0:T(8,128)S(1)}, f32[5,256]{1,0:T(8,128)S(1)}, u32[]{:S(2)}, u32[]{:S(2)}) collective-permute-start(f32[5,256]{1,0:T(8,128)S(1)} %maximum_select_fusion.6), channel_id=1, source_target_pairs={{0,4},{2,6},{4,0},{6,2},{8,12},{10,14},{12,8},{14,10},{16,20},{18,... | collective-permute-start | bytes 15368 | tf_op jit(solution)/shard_map/ppermute | solution.py:16
  6.8 2.1 %collective-permute-done.1 = f32[5,256]{1,0:T(8,128)S(1)} collective-permute-done((f32[5,256]{1,0:T(8,128)S(1)}, f32[5,256]{1,0:T(8,128)S(1)}, u32[]{:S(2)}, u32[]{:S(2)}) %collective-permute-start.1) | collective-permute-done | bytes 5152 | tf_op jit(solution)/shard_map/ppermute | solution.py:16
  9.0 2.7 %collective-permute-start.3 = (f32[4,1024]{1,0:T(4,128)S(1)}, f32[4,1024]{1,0:T(4,128)S(1)}, u32[]{:S(2)}, u32[]{:S(2)}) collective-permute-start(f32[4,1024]{1,0:T(4,128)S(1)} %maximum_select_fusion.5), channel_id=1, source_target_pairs={{0,16},{2,18},{4,20},{6,22},{8,24},{10,26},{12,28},{14,30},{16,0},... | collective-permute-start | bytes 49160 | tf_op jit(solution)/shard_map/ppermute | solution.py:16
  11.6 2.2 %collective-permute-done.3 = f32[4,1024]{1,0:T(4,128)S(1)} collective-permute-done((f32[4,1024]{1,0:T(4,128)S(1)}, f32[4,1024]{1,0:T(4,128)S(1)}, u32[]{:S(2)}, u32[]{:S(2)}) %collective-permute-start.3) | collective-permute-done | bytes 16416 | tf_op jit(solution)/shard_map/ppermute | solution.py:16
  13.8 3.5 %while.22 = (s32[]{:T(128)}, f32[4,512]{1,0:T(4,128)S(1)}, f32[1,512]{1,0:T(1,128)S(1)}, f32[4,512,4]{1,2,0:T(4,128)S(1)}, f32[1,512]{1,0:T(1,128)S(1)}, /*index=5*/f32[1,512]{1,0:T(1,128)S(1)}, s32[]{:T(128)}, s32[]{:T(128)}) while((s32[]{:T(128)}, f32[4,512]{1,0:T(4,128)S(1)}, f32[1,512]{1,0:T(1,128)S(1)}, ...), condition=%wide.region_5.6_spmd.clone, body=%wide.region_0.5_spmd.clone.sunk | while | flops 4988931 | bytes 79979 | solution.py:48
  13.8 0.8 %multiply_reduce_fusion.6 = (f32[512]{0:T(512)S(1)}, f32[512]{0:T(512)S(1)}, f32[512]{0:T(512)S(1)}, f32[512]{0:T(512)S(1)}) fusion(f32[512]{0:T(512)S(1)} %bitcast.133, f32[512]{0:T(512)S(1)} %bitcast.134, f32[512]{0:T(512)S(1)} %bitcast.145, f32[512]{0:T(512)S(1)} %bitcast.135, f32[512]{0:T(512)S(1)} %bitcast.146, f32[512]{0:T(512)S(1)} %bitcast.132, ...), kind=kLoop, calls=%fused_computation.1.clone.1 | loop fusion | flops 4978688 | bytes 22528 | tf_op jit(solution)/shard_map/while/body/eval_jaxpr/reduce_sum | solution.py:43
  14.7 0.8 %multiply_reduce_fusion.6 = (f32[512]{0:T(512)S(1)}, f32[512]{0:T(512)S(1)}, f32[512]{0:T(512)S(1)}, f32[512]{0:T(512)S(1)}) fusion(f32[512]{0:T(512)S(1)} %bitcast.133, f32[512]{0:T(512)S(1)} %bitcast.134, f32[512]{0:T(512)S(1)} %bitcast.145, f32[512]{0:T(512)S(1)} %bitcast.135, f32[512]{0:T(512)S(1)} %bitcast.146, f32[512]{0:T(512)S(1)} %bitcast.132, ...), kind=kLoop, calls=%fused_computation.1.clone.1 | loop fusion | flops 4978688 | bytes 22528 | tf_op jit(solution)/shard_map/while/body/eval_jaxpr/reduce_sum | solution.py:43
  15.6 0.8 %multiply_reduce_fusion.6 = (f32[512]{0:T(512)S(1)}, f32[512]{0:T(512)S(1)}, f32[512]{0:T(512)S(1)}, f32[512]{0:T(512)S(1)}) fusion(f32[512]{0:T(512)S(1)} %bitcast.133, f32[512]{0:T(512)S(1)} %bitcast.134, f32[512]{0:T(512)S(1)} %bitcast.145, f32[512]{0:T(512)S(1)} %bitcast.135, f32[512]{0:T(512)S(1)} %bitcast.146, f32[512]{0:T(512)S(1)} %bitcast.132, ...), kind=kLoop, calls=%fused_computation.1.clone.1 | loop fusion | flops 4978688 | bytes 22528 | tf_op jit(solution)/shard_map/while/body/eval_jaxpr/reduce_sum | solution.py:43
  17.3 1.6 %collective-permute-start.4 = (f32[4,512]{1,0:T(4,128)S(1)}, f32[4,512]{1,0:T(4,128)S(1)}, u32[]{:S(2)}, u32[]{:S(2)}) collective-permute-start(f32[4,512]{1,0:T(4,128)S(1)} %get-tuple-element.65), channel_id=1, source_target_pairs={{0,1},{1,0},{2,3},{3,2},{4,5},{5,4},{6,7},{7,6},{8,9},{9,8},{10,11... | collective-permute-start | bytes 24584 | tf_op jit(solution)/shard_map/ppermute | solution.py:28
  18.9 2.2 %collective-permute-done.4 = f32[4,512]{1,0:T(4,128)S(1)} collective-permute-done((f32[4,512]{1,0:T(4,128)S(1)}, f32[4,512]{1,0:T(4,128)S(1)}, u32[]{:S(2)}, u32[]{:S(2)}) %collective-permute-start.4) | collective-permute-done | bytes 8224 | tf_op jit(solution)/shard_map/ppermute | solution.py:28
  21.0 1.2 %collective-permute-done.5 = f32[4,512]{1,0:T(4,128)S(1)} collective-permute-done((f32[4,512]{1,0:T(4,128)S(1)}, f32[4,512]{1,0:T(4,128)S(1)}, u32[]{:S(2)}, u32[]{:S(2)}) %collective-permute-start.5) | collective-permute-done | bytes 8224 | tf_op jit(solution)/shard_map/ppermute | solution.py:28
  22.2 1.5 %collective-permute-start.6 = (f32[4,512]{1,0:T(4,128)S(1)}, f32[4,512]{1,0:T(4,128)S(1)}, u32[]{:S(2)}, u32[]{:S(2)}) collective-permute-start(f32[4,512]{1,0:T(4,128)S(1)} %add.147), channel_id=1, source_target_pairs={{0,4},{2,6},{4,0},{6,2},{8,12},{10,14},{12,8},{14,10},{16,20},{18,... | collective-permute-start | bytes 24584 | tf_op jit(solution)/shard_map/ppermute | solution.py:28
  23.7 2.1 %collective-permute-done.6 = f32[4,512]{1,0:T(4,128)S(1)} collective-permute-done((f32[4,512]{1,0:T(4,128)S(1)}, f32[4,512]{1,0:T(4,128)S(1)}, u32[]{:S(2)}, u32[]{:S(2)}) %collective-permute-start.6) | collective-permute-done | bytes 8224 | tf_op jit(solution)/shard_map/ppermute | solution.py:28
  26.6 3.1 %collective-permute-done.7 = f32[6,512]{1,0:T(8,128)S(1)} collective-permute-done((f32[6,512]{1,0:T(8,128)S(1)}, f32[6,512]{1,0:T(8,128)S(1)}, u32[]{:S(2)}, u32[]{:S(2)}) %collective-permute-start.7) | collective-permute-done | bytes 12320 | tf_op jit(solution)/shard_map/ppermute | solution.py:16
  29.7 2.5 %collective-permute-start.8 = (f32[6,1024]{1,0:T(8,128)S(1)}, f32[6,1024]{1,0:T(8,128)S(1)}, u32[]{:S(2)}, u32[]{:S(2)}) collective-permute-start(f32[6,1024]{1,0:T(8,128)S(1)} %maximum_select_fusion.2), channel_id=1, source_target_pairs={{0,16},{2,18},{4,20},{6,22},{8,24},{10,26},{12,28},{14,30},{16,0},... | collective-permute-start | bytes 73736 | tf_op jit(solution)/shard_map/ppermute | solution.py:16
  32.3 2.5 %collective-permute-done.8 = f32[6,1024]{1,0:T(8,128)S(1)} collective-permute-done((f32[6,1024]{1,0:T(8,128)S(1)}, f32[6,1024]{1,0:T(8,128)S(1)}, u32[]{:S(2)}, u32[]{:S(2)}) %collective-permute-start.8) | collective-permute-done | bytes 24608 | tf_op jit(solution)/shard_map/ppermute | solution.py:16
  39.3 1.2 %collective-permute-done.9 = f32[2048]{0:T(1024)S(1)} collective-permute-done((f32[2048]{0:T(1024)S(1)}, f32[2048]{0:T(1024)S(1)}, u32[]{:S(2)}, u32[]{:S(2)}) %collective-permute-start.9) | collective-permute-done | bytes 8224 | tf_op jit(solution)/shard_map/ppermute | solution.py:28
  40.5 1.5 %collective-permute-start.10 = (f32[2048]{0:T(1024)S(1)}, f32[2048]{0:T(1024)S(1)}, u32[]{:S(2)}, u32[]{:S(2)}) collective-permute-start(f32[2048]{0:T(1024)S(1)} %add.165), channel_id=1, source_target_pairs={{0,4},{2,6},{4,0},{6,2},{8,12},{10,14},{12,8},{14,10},{16,20},{18,... | collective-permute-start | bytes 24584 | tf_op jit(solution)/shard_map/ppermute | solution.py:28
  42.0 2.1 %collective-permute-done.10 = f32[2048]{0:T(1024)S(1)} collective-permute-done((f32[2048]{0:T(1024)S(1)}, f32[2048]{0:T(1024)S(1)}, u32[]{:S(2)}, u32[]{:S(2)}) %collective-permute-start.10) | collective-permute-done | bytes 8224 | tf_op jit(solution)/shard_map/ppermute | solution.py:28
  44.4 3.4 %collective-permute-done.11 = f32[2048]{0:T(1024)S(1)} collective-permute-done((f32[2048]{0:T(1024)S(1)}, f32[2048]{0:T(1024)S(1)}, u32[]{:S(2)}, u32[]{:S(2)}) %collective-permute-start.11) | collective-permute-done | bytes 8224 | tf_op jit(solution)/shard_map/ppermute | solution.py:28
  47.8 2.3 %collective-permute-start.12 = (f32[2048]{0:T(1024)S(1)}, f32[2048]{0:T(1024)S(1)}, u32[]{:S(2)}, u32[]{:S(2)}) collective-permute-start(f32[2048]{0:T(1024)S(1)} %add.167), channel_id=1, source_target_pairs={{0,16},{2,18},{4,20},{6,22},{8,24},{10,26},{12,28},{14,30},{16,0},... | collective-permute-start | bytes 24584 | tf_op jit(solution)/shard_map/ppermute | solution.py:158
  50.1 2.2 %collective-permute-done.12 = f32[2048]{0:T(1024)S(1)} collective-permute-done((f32[2048]{0:T(1024)S(1)}, f32[2048]{0:T(1024)S(1)}, u32[]{:S(2)}, u32[]{:S(2)}) %collective-permute-start.12) | collective-permute-done | bytes 8224 | tf_op jit(solution)/shard_map/ppermute | solution.py:158
  52.4 3.6 %while.23 = (s32[]{:T(128)}, f32[3,512]{1,0:T(4,128)S(1)}, f32[4,512,4]{1,2,0:T(4,128)S(1)}, f32[3,512]{1,0:T(4,128)S(1)}, f32[512]{0:T(512)S(1)}, /*index=5*/s32[]{:T(128)}, s32[]{:T(128)}) while((s32[]{:T(128)}, f32[3,512]{1,0:T(4,128)S(1)}, f32[4,512,4]{1,2,0:T(4,128)S(1)}, f32[3,512]{1,0:T(4,128)S(1)}, f32[512]{0:T(512)S(1)}, ...), condition=%wide.region_15.16_spmd.clone, body=%wide.region_11.15_spmd.clone.sunk | while | flops 4985347 | bytes 86115 | solution.py:63
  (110 shorter events, 11.2 us)
Async XLA Ops:
  0.6 36.5 %copy-start = (bf16[128,256]{1,0:T(8,128)(2,1)S(1)}, bf16[128,256]{1,0:T(8,128)(2,1)}, u32[]{:S(2)}) copy-start(bf16[128,256]{1,0:T(8,128)(2,1)} %param.27) | copy-start | bytes 196612
  0.6 0.7 %copy-start.11 = (s32[128]{0:T(128)S(1)}, s32[128]{0:T(128)}, u32[]{:S(2)}) copy-start(s32[128]{0:T(128)} %param.18) | copy-start | bytes 1540
  0.7 0.7 %copy-start.4 = (f32[3,128]{1,0:T(4,128)S(1)}, f32[3,128]{1,0:T(4,128)}, u32[]{:S(2)}) copy-start(f32[3,128]{1,0:T(4,128)} %param.17) | copy-start | bytes 4612
  1.3 0.7 %copy-start.1 = (f32[3,512]{1,0:T(4,128)S(1)}, f32[3,512]{1,0:T(4,128)}, u32[]{:S(2)}) copy-start(f32[3,512]{1,0:T(4,128)} %param.22) | copy-start | bytes 18436
  1.4 0.7 %copy-start.3 = (f32[512]{0:T(512)S(1)}, f32[512]{0:T(512)}, u32[]{:S(2)}) copy-start(f32[512]{0:T(512)} %param.23) | copy-start | bytes 6148
  1.4 3.8 %collective-permute-start = (f32[5,128]{1,0:T(8,128)S(1)}, f32[5,128]{1,0:T(8,128)S(1)}, u32[]{:S(2)}, u32[]{:S(2)}) collective-permute-start(f32[5,128]{1,0:T(8,128)S(1)} %pad_maximum_fusion.2), channel_id=1, source_target_pairs={{0,2},{2,0},{4,6},{6,4},{8,10},{10,8},{12,14},{14,12},{16,18},{18,... | collective-permute-start | bytes 7688 | tf_op jit(solution)/shard_map/ppermute | solution.py:16
  2.1 6.8 %collective-permute-start.2 = (f32[4,512]{1,0:T(4,128)S(1)}, f32[4,512]{1,0:T(4,128)S(1)}, u32[]{:S(2)}, u32[]{:S(2)}) collective-permute-start(f32[4,512]{1,0:T(4,128)S(1)} %pad_maximum_fusion.1), channel_id=1, source_target_pairs={{0,8},{2,10},{4,12},{6,14},{8,0},{10,2},{12,4},{14,6},{16,24},{18,... | collective-permute-start | bytes 24584 | tf_op jit(solution)/shard_map/ppermute | solution.py:16
  5.2 3.7 %collective-permute-start.1 = (f32[5,256]{1,0:T(8,128)S(1)}, f32[5,256]{1,0:T(8,128)S(1)}, u32[]{:S(2)}, u32[]{:S(2)}) collective-permute-start(f32[5,256]{1,0:T(8,128)S(1)} %maximum_select_fusion.6), channel_id=1, source_target_pairs={{0,4},{2,6},{4,0},{6,2},{8,12},{10,14},{12,8},{14,10},{16,20},{18,... | collective-permute-start | bytes 15368 | tf_op jit(solution)/shard_map/ppermute | solution.py:16
  9.0 4.8 %collective-permute-start.3 = (f32[4,1024]{1,0:T(4,128)S(1)}, f32[4,1024]{1,0:T(4,128)S(1)}, u32[]{:S(2)}, u32[]{:S(2)}) collective-permute-start(f32[4,1024]{1,0:T(4,128)S(1)} %maximum_select_fusion.5), channel_id=1, source_target_pairs={{0,16},{2,18},{4,20},{6,22},{8,24},{10,26},{12,28},{14,30},{16,0},... | collective-permute-start | bytes 49160 | tf_op jit(solution)/shard_map/ppermute | solution.py:16
  17.3 3.7 %collective-permute-start.4 = (f32[4,512]{1,0:T(4,128)S(1)}, f32[4,512]{1,0:T(4,128)S(1)}, u32[]{:S(2)}, u32[]{:S(2)}) collective-permute-start(f32[4,512]{1,0:T(4,128)S(1)} %get-tuple-element.65), channel_id=1, source_target_pairs={{0,1},{1,0},{2,3},{3,2},{4,5},{5,4},{6,7},{7,6},{8,9},{9,8},{10,11... | collective-permute-start | bytes 24584 | tf_op jit(solution)/shard_map/ppermute | solution.py:28
  21.0 1.2 %collective-permute-start.5 = (f32[4,512]{1,0:T(4,128)S(1)}, f32[4,512]{1,0:T(4,128)S(1)}, u32[]{:S(2)}, u32[]{:S(2)}) collective-permute-start(f32[4,512]{1,0:T(4,128)S(1)} %add.146), channel_id=1, source_target_pairs={{0,2},{2,0},{4,6},{6,4},{8,10},{10,8},{12,14},{14,12},{16,18},{18,... | collective-permute-start | bytes 24584 | tf_op jit(solution)/shard_map/ppermute | solution.py:28
  22.2 3.7 %collective-permute-start.6 = (f32[4,512]{1,0:T(4,128)S(1)}, f32[4,512]{1,0:T(4,128)S(1)}, u32[]{:S(2)}, u32[]{:S(2)}) collective-permute-start(f32[4,512]{1,0:T(4,128)S(1)} %add.147), channel_id=1, source_target_pairs={{0,4},{2,6},{4,0},{6,2},{8,12},{10,14},{12,8},{14,10},{16,20},{18,... | collective-permute-start | bytes 24584 | tf_op jit(solution)/shard_map/ppermute | solution.py:28
  25.9 0.7 %copy-start.5 = (s32[128,4]{0,1:T(4,128)S(1)}, s32[128,4]{0,1:T(4,128)}, u32[]{:S(2)}) copy-start(s32[128,4]{0,1:T(4,128)} %param.21) | copy-start | bytes 6148
  25.9 0.7 %copy-start.6 = (s32[128,4]{0,1:T(4,128)S(1)}, s32[128,4]{0,1:T(4,128)}, u32[]{:S(2)}) copy-start(s32[128,4]{0,1:T(4,128)} %param.20) | copy-start | bytes 6148
  25.9 3.8 %collective-permute-start.7 = (f32[6,512]{1,0:T(8,128)S(1)}, f32[6,512]{1,0:T(8,128)S(1)}, u32[]{:S(2)}, u32[]{:S(2)}) collective-permute-start(f32[6,512]{1,0:T(8,128)S(1)} %pad_maximum_fusion), channel_id=1, source_target_pairs={{0,8},{2,10},{4,12},{6,14},{8,0},{10,2},{12,4},{14,6},{16,24},{18,... | collective-permute-start | bytes 36872 | tf_op jit(solution)/shard_map/ppermute | solution.py:16
  29.7 5.1 %collective-permute-start.8 = (f32[6,1024]{1,0:T(8,128)S(1)}, f32[6,1024]{1,0:T(8,128)S(1)}, u32[]{:S(2)}, u32[]{:S(2)}) collective-permute-start(f32[6,1024]{1,0:T(8,128)S(1)} %maximum_select_fusion.2), channel_id=1, source_target_pairs={{0,16},{2,18},{4,20},{6,22},{8,24},{10,26},{12,28},{14,30},{16,0},... | collective-permute-start | bytes 73736 | tf_op jit(solution)/shard_map/ppermute | solution.py:16
  34.9 0.7 %copy-start.8 = (bf16[8,128]{1,0:T(8,128)(2,1)S(1)}, bf16[8,128]{1,0:T(8,128)(2,1)}, u32[]{:S(2)}) copy-start(bf16[8,128]{1,0:T(8,128)(2,1)} %param.24) | copy-start | bytes 6148
  35.6 0.8 %copy-start.7 = (bf16[128,128]{1,0:T(8,128)(2,1)S(1)}, bf16[128,128]{1,0:T(8,128)(2,1)}, u32[]{:S(2)}) copy-start(bf16[128,128]{1,0:T(8,128)(2,1)} %param.26) | copy-start | bytes 98308
  36.3 0.8 %copy-start.9 = (f32[256]{0:T(256)S(1)}, f32[256]{0:T(256)}, u32[]{:S(2)}) copy-start(f32[256]{0:T(256)} %param.29) | copy-start | bytes 3076
  36.3 0.8 %copy-start.10 = (f32[256]{0:T(256)S(1)}, f32[256]{0:T(256)}, u32[]{:S(2)}) copy-start(f32[256]{0:T(256)} %param.28) | copy-start | bytes 3076
  39.2 1.2 %collective-permute-start.9 = (f32[2048]{0:T(1024)S(1)}, f32[2048]{0:T(1024)S(1)}, u32[]{:S(2)}, u32[]{:S(2)}) collective-permute-start(f32[2048]{0:T(1024)S(1)} %fusion.41), channel_id=1, source_target_pairs={{0,2},{2,0},{4,6},{6,4},{8,10},{10,8},{12,14},{14,12},{16,18},{18,... | collective-permute-start | bytes 24584 | tf_op jit(solution)/shard_map/ppermute | solution.py:28
  40.5 3.7 %collective-permute-start.10 = (f32[2048]{0:T(1024)S(1)}, f32[2048]{0:T(1024)S(1)}, u32[]{:S(2)}, u32[]{:S(2)}) collective-permute-start(f32[2048]{0:T(1024)S(1)} %add.165), channel_id=1, source_target_pairs={{0,4},{2,6},{4,0},{6,2},{8,12},{10,14},{12,8},{14,10},{16,20},{18,... | collective-permute-start | bytes 24584 | tf_op jit(solution)/shard_map/ppermute | solution.py:28
  44.1 3.7 %collective-permute-start.11 = (f32[2048]{0:T(1024)S(1)}, f32[2048]{0:T(1024)S(1)}, u32[]{:S(2)}, u32[]{:S(2)}) collective-permute-start(f32[2048]{0:T(1024)S(1)} %add.166), channel_id=1, source_target_pairs={{0,8},{2,10},{4,12},{6,14},{8,0},{10,2},{12,4},{14,6},{16,24},{18,... | collective-permute-start | bytes 24584 | tf_op jit(solution)/shard_map/ppermute | solution.py:28
  47.8 4.5 %collective-permute-start.12 = (f32[2048]{0:T(1024)S(1)}, f32[2048]{0:T(1024)S(1)}, u32[]{:S(2)}, u32[]{:S(2)}) collective-permute-start(f32[2048]{0:T(1024)S(1)} %add.167), channel_id=1, source_target_pairs={{0,16},{2,18},{4,20},{6,22},{8,24},{10,26},{12,28},{14,30},{16,0},... | collective-permute-start | bytes 24584 | tf_op jit(solution)/shard_map/ppermute | solution.py:158
  (2 other events, 1.4 us)

commit v7 on v6

--- a/solution.py
+++ b/solution.py
@@ -5,6 +5,7 @@
 
 SOFTEN = 0.25
 CHUNK = 512
+WHOLE = True
 
 
 def gather_doubling(x, axis, first=1, last=None):
@@ -31,7 +32,7 @@
 
 
 def potential_pass(qm_some, mm_some):
-    chunks = mm_some.shape[1] // CHUNK
+    chunks = 1 if WHOLE else mm_some.shape[1] // CHUNK
     cols = [qm_some[c][None, :] for c in range(3)]
 
     def body(running, block):
@@ -44,15 +45,15 @@
         )
         return running + part, None
 
-    stacked = jnp.transpose(mm_some.reshape(4, chunks, CHUNK), (1, 2, 0))
+    stacked = jnp.transpose(mm_some.reshape(4, chunks, -1), (1, 2, 0))
     total, _ = lax.scan(body, jnp.zeros((4, qm_some.shape[1]), jnp.float32), stacked)
     return total
 
 
 def force_pass(qm_all, effective, mm_pos, scale):
-    chunks = qm_all.shape[1] // CHUNK
+    chunks = 1 if WHOLE else qm_all.shape[1] // CHUNK
     stacked = jnp.concatenate([qm_all, effective[None, :]], axis=0)
-    stacked = jnp.transpose(stacked.reshape(4, chunks, CHUNK), (1, 2, 0))
+    stacked = jnp.transpose(stacked.reshape(4, chunks, -1), (1, 2, 0))
 
     def body(running, block):
         d = [block[:, c : c + 1] - mm_pos[c][None, :] for c in range(3)]

time: 56.9 us -> 60.2 us (1.058)
  other arithmetic: 8.78 us -> 12.9 us
  local copies, waits for them, and re-layouts: 1.66 us -> 0.5 us
    select_n x6 -> x5, other arithmetic: 0.05 us -> 1.58 us  [gather_doubling(): jnp.where(low, jnp.concatenate([x, other], -1), jnp.concatenate([other, x...]
    ppermute x6, waiting for transfers between devices: 12.2 us -> 13.5 us  [sum_butterfly(): x = x + lax.ppermute(x, axis, [(i, i ^ step) for i in range(n)])]
    ppermute x6, starting transfers between devices: 4.9 us -> 3.7 us  [sum_butterfly(): x = x + lax.ppermute(x, axis, [(i, i ^ step) for i in range(n)])]
    ppermute x6, starting transfers between devices: 10.8 us -> 11.9 us  [gather_doubling(): other = lax.ppermute(x, axis, [(i, i ^ step) for i in range(n)])]
    unnamed x26 -> x20, local copies, waits for them, and re-layouts: 1.46 us -> 0.42 us
    concatenate x1, other arithmetic: 0.01 us -> 0.72 us  [on_device(): jnp.concatenate([mm_pos, mm_charge[None, :]], axis=0)]
    concatenate x1, other arithmetic: 0.01 us -> 0.69 us  [on_device(): jnp.concatenate([qm_pos, species.astype(jnp.float32)[None, :], jnp.broadc...]
    broadcast_in_dim x1, other arithmetic: 0.01 us -> 0.66 us  [on_device(): species.astype(jnp.float32)[None, :]]
  transfers between devices with their start and end apart: 13 -> 13, of which waited for: 11 -> 12; matrix products, arithmetic and copies ran while one was open for 0% -> 1% of each run, Pallas kernels for 0% -> 0%
where the time goes in v7:
time: 60.2 us; the launch traced here: 59.8 us
  waiting for transfers between devices  24.7 us (41%)
  starting transfers between devices  18.2 us (30%)
  other arithmetic  12.9 us (21%)
  matrix products  1.87 us (3%)
  between operations  1.58 us (3%)
    ppermute x6, waiting for transfers between devices, sum_butterfly(): x = x + lax.ppermute(x, axis, [(i, i ^ step) for i in range(n)])  13.5 us
    ppermute x6, starting transfers between devices, gather_doubling(): other = lax.ppermute(x, axis, [(i, i ^ step) for i in range(n)])  11.9 us
    ppermute x6, waiting for transfers between devices, gather_doubling(): other = lax.ppermute(x, axis, [(i, i ^ step) for i in range(n)])  9.3 us
    ppermute x6, starting transfers between devices, sum_butterfly(): x = x + lax.ppermute(x, axis, [(i, i ^ step) for i in range(n)])  3.7 us
    reduce_sum x1, other arithmetic, body(): jnp.sum(weighted, axis=0)  3.27 us
    reduce_sum x1, other arithmetic, body(): jnp.sum(d[c] * weight, axis=0)  3.22 us
    ppermute x1, starting transfers between devices, on_device(): lax.ppermute(part, 'blk', [(i, i ^ blocks // 2) for i in range(blocks)])  2.61 us
    ppermute x1, waiting for transfers between devices, on_device(): lax.ppermute(part, 'blk', [(i, i ^ blocks // 2) for i in range(blocks)])  1.91 us
  transfers between devices with their start and end apart: 13, of which 12 were waited for; matrix products, arithmetic and copies ran while one was open for 1% of the time, Pallas kernels for 0%

profile of v7, /device:TPU:0, one launch (start us, length us, event | category | flops | bytes accessed | tf_op | source)
XLA Modules:
  0.0 59.8 jit_solution(1812618998513830509)
XLA Ops:
  3.1 0.8 %collective-permute-done = f32[5,128]{1,0:T(8,128)S(1)} collective-permute-done((f32[5,128]{1,0:T(8,128)S(1)}, f32[5,128]{1,0:T(8,128)S(1)}, u32[]{:S(2)}, u32[]{:S(2)}) %collective-permute-start) | collective-permute-done | bytes 2592 | tf_op jit(solution)/shard_map/ppermute | solution.py:17
  4.7 2.9 %collective-permute-start.1 = (f32[5,256]{1,0:T(8,128)S(1)}, f32[5,256]{1,0:T(8,128)S(1)}, u32[]{:S(2)}, u32[]{:S(2)}) collective-permute-start(f32[5,256]{1,0:T(8,128)S(1)} %maximum_select_fusion.5), channel_id=1, source_target_pairs={{0,4},{2,6},{4,0},{6,2},{8,12},{10,14},{12,8},{14,10},{16,20},{18,... | collective-permute-start | bytes 15368 | tf_op jit(solution)/shard_map/ppermute | solution.py:17
  8.3 1.6 %collective-permute-start.2 = (f32[4,512]{1,0:T(4,128)S(1)}, f32[4,512]{1,0:T(4,128)S(1)}, u32[]{:S(2)}, u32[]{:S(2)}) collective-permute-start(f32[4,512]{1,0:T(4,128)S(1)} %pad_maximum_fusion.1), channel_id=1, source_target_pairs={{0,8},{2,10},{4,12},{6,14},{8,0},{10,2},{12,4},{14,6},{16,24},{18,... | collective-permute-start | bytes 24584 | tf_op jit(solution)/shard_map/ppermute | solution.py:17
  10.0 2.1 %collective-permute-done.2 = f32[4,512]{1,0:T(4,128)S(1)} collective-permute-done((f32[4,512]{1,0:T(4,128)S(1)}, f32[4,512]{1,0:T(4,128)S(1)}, u32[]{:S(2)}, u32[]{:S(2)}) %collective-permute-start.2) | collective-permute-done | bytes 8224 | tf_op jit(solution)/shard_map/ppermute | solution.py:17
  12.0 0.8 %maximum_select_fusion.4 = f32[4,1024]{1,0:T(4,128)S(1)} fusion(f32[4,512]{1,0:T(4,128)S(1)} %collective-permute-done.2, f32[1,512]{1,0:T(1,128)} %bitcast.73, f32[3,512]{1,0:T(4,128)} %param.18, pred[]{:T(512)S(6)} %eq.106), kind=kLoop, calls=%fused_computation.71 | loop fusion | flops 20480 | bytes 32769 | tf_op jit(solution)/shard_map/jit(_where)/select_n | solution.py:19
  12.8 2.7 %collective-permute-start.3 = (f32[4,1024]{1,0:T(4,128)S(1)}, f32[4,1024]{1,0:T(4,128)S(1)}, u32[]{:S(2)}, u32[]{:S(2)}) collective-permute-start(f32[4,1024]{1,0:T(4,128)S(1)} %maximum_select_fusion.4), channel_id=1, source_target_pairs={{0,16},{2,18},{4,20},{6,22},{8,24},{10,26},{12,28},{14,30},{16,0},... | collective-permute-start | bytes 49160 | tf_op jit(solution)/shard_map/ppermute | solution.py:17
  15.5 2.0 %collective-permute-done.3 = f32[4,1024]{1,0:T(4,128)S(1)} collective-permute-done((f32[4,1024]{1,0:T(4,128)S(1)}, f32[4,1024]{1,0:T(4,128)S(1)}, u32[]{:S(2)}, u32[]{:S(2)}) %collective-permute-start.3) | collective-permute-done | bytes 16416 | tf_op jit(solution)/shard_map/ppermute | solution.py:17
  17.6 3.3 %multiply_reduce_fusion = (f32[512]{0:T(512)S(1)}, f32[512]{0:T(512)S(1)}, f32[512]{0:T(512)S(1)}, f32[512]{0:T(512)S(1)}) fusion(f32[2048]{0:T(1024)S(1)} %bitcast.95, f32[2048]{0:T(1024)S(1)} %bitcast.96, f32[512]{0:T(512)S(1)} %bitcast.105, f32[2048]{0:T(1024)S(1)} %bitcast.97, f32[512]{0:T(512)S(1)} %bitcast.106, f32[2048]{0:T(1024)S(1)} %bitcast.94, ...), kind=kLoop, calls=%fused_computation.8 | loop fusion | flops 19920896 | bytes 47104 | tf_op jit(solution)/shard_map/while/body/eval_jaxpr/reduce_sum | solution.py:44
  20.9 1.6 %collective-permute-start.4 = (f32[4,512]{1,0:T(4,128)S(1)}, f32[4,512]{1,0:T(4,128)S(1)}, u32[]{:S(2)}, u32[]{:S(2)}) collective-permute-start(f32[4,512]{1,0:T(4,128)S(1)} %pad_maximum_fusion.2), channel_id=1, source_target_pairs={{0,1},{1,0},{2,3},{3,2},{4,5},{5,4},{6,7},{7,6},{8,9},{9,8},{10,11... | collective-permute-start | bytes 24584 | tf_op jit(solution)/shard_map/ppermute | solution.py:29
  22.5 2.2 %collective-permute-done.4 = f32[4,512]{1,0:T(4,128)S(1)} collective-permute-done((f32[4,512]{1,0:T(4,128)S(1)}, f32[4,512]{1,0:T(4,128)S(1)}, u32[]{:S(2)}, u32[]{:S(2)}) %collective-permute-start.4) | collective-permute-done | bytes 8224 | tf_op jit(solution)/shard_map/ppermute | solution.py:29
  24.7 1.2 %collective-permute-done.5 = f32[4,512]{1,0:T(4,128)S(1)} collective-permute-done((f32[4,512]{1,0:T(4,128)S(1)}, f32[4,512]{1,0:T(4,128)S(1)}, u32[]{:S(2)}, u32[]{:S(2)}) %collective-permute-start.5) | collective-permute-done | bytes 8224 | tf_op jit(solution)/shard_map/ppermute | solution.py:29
  26.2 3.5 %collective-permute-done.6 = f32[4,512]{1,0:T(4,128)S(1)} collective-permute-done((f32[4,512]{1,0:T(4,128)S(1)}, f32[4,512]{1,0:T(4,128)S(1)}, u32[]{:S(2)}, u32[]{:S(2)}) %collective-permute-start.6) | collective-permute-done | bytes 8224 | tf_op jit(solution)/shard_map/ppermute | solution.py:29
  29.7 1.6 %collective-permute-start.7 = (f32[6,512]{1,0:T(8,128)S(1)}, f32[6,512]{1,0:T(8,128)S(1)}, u32[]{:S(2)}, u32[]{:S(2)}) collective-permute-start(f32[6,512]{1,0:T(8,128)S(1)} %pad_maximum_fusion), channel_id=1, source_target_pairs={{0,8},{2,10},{4,12},{6,14},{8,0},{10,2},{12,4},{14,6},{16,24},{18,... | collective-permute-start | bytes 36872 | tf_op jit(solution)/shard_map/ppermute | solution.py:17
  31.3 2.2 %collective-permute-done.7 = f32[6,512]{1,0:T(8,128)S(1)} collective-permute-done((f32[6,512]{1,0:T(8,128)S(1)}, f32[6,512]{1,0:T(8,128)S(1)}, u32[]{:S(2)}, u32[]{:S(2)}) %collective-permute-start.7) | collective-permute-done | bytes 12320 | tf_op jit(solution)/shard_map/ppermute | solution.py:17
  33.5 2.7 %collective-permute-start.8 = (f32[6,1024]{1,0:T(8,128)S(1)}, f32[6,1024]{1,0:T(8,128)S(1)}, u32[]{:S(2)}, u32[]{:S(2)}) collective-permute-start(f32[6,1024]{1,0:T(8,128)S(1)} %maximum_select_fusion.2), channel_id=1, source_target_pairs={{0,16},{2,18},{4,20},{6,22},{8,24},{10,26},{12,28},{14,30},{16,0},... | collective-permute-start | bytes 73736 | tf_op jit(solution)/shard_map/ppermute | solution.py:17
  36.1 2.2 %collective-permute-done.8 = f32[6,1024]{1,0:T(8,128)S(1)} collective-permute-done((f32[6,1024]{1,0:T(8,128)S(1)}, f32[6,1024]{1,0:T(8,128)S(1)}, u32[]{:S(2)}, u32[]{:S(2)}) %collective-permute-start.8) | collective-permute-done | bytes 24608 | tf_op jit(solution)/shard_map/ppermute | solution.py:17
  39.2 0.8 %fusion.18 = bf16[128,128]{0,1:T(8,128)(2,1)S(1)} fusion(bf16[128,128]{1,0:T(8,128)(2,1)S(1)} %copy-done.5, bf16[128,2048]{1,0:T(8,128)(2,1)S(1)} %fusion.17, s32[128]{0:T(128)S(1)} %get-tuple-element.70, s32[128]{0:T(128)S(1)} %get-tuple-element.71, s32[128]{0:T(128)S(1)} %get-tuple-element.72, s32[128]{0:T(128)S(1)} %get-tuple-element.69, s32[]{:T(128)S(6)} %select_n.154), kind=kOutput, calls=%fused_computation.35 | convolution fusion | flops 75563008 | bytes 624644 | tf_op jit(solution)/shard_map/dot_general | solution.py:135
  42.2 1.2 %collective-permute-done.9 = f32[2048]{0:T(1024)S(1)} collective-permute-done((f32[2048]{0:T(1024)S(1)}, f32[2048]{0:T(1024)S(1)}, u32[]{:S(2)}, u32[]{:S(2)}) %collective-permute-start.9) | collective-permute-done | bytes 8224 | tf_op jit(solution)/shard_map/ppermute | solution.py:29
  43.5 3.5 %collective-permute-done.10 = f32[2048]{0:T(1024)S(1)} collective-permute-done((f32[2048]{0:T(1024)S(1)}, f32[2048]{0:T(1024)S(1)}, u32[]{:S(2)}, u32[]{:S(2)}) %collective-permute-start.10) | collective-permute-done | bytes 8224 | tf_op jit(solution)/shard_map/ppermute | solution.py:29
  47.0 1.6 %collective-permute-start.11 = (f32[2048]{0:T(1024)S(1)}, f32[2048]{0:T(1024)S(1)}, u32[]{:S(2)}, u32[]{:S(2)}) collective-permute-start(f32[2048]{0:T(1024)S(1)} %add.171), channel_id=1, source_target_pairs={{0,8},{2,10},{4,12},{6,14},{8,0},{10,2},{12,4},{14,6},{16,24},{18,... | collective-permute-start | bytes 24584 | tf_op jit(solution)/shard_map/ppermute | solution.py:29
  48.6 2.1 %collective-permute-done.11 = f32[2048]{0:T(1024)S(1)} collective-permute-done((f32[2048]{0:T(1024)S(1)}, f32[2048]{0:T(1024)S(1)}, u32[]{:S(2)}, u32[]{:S(2)}) %collective-permute-start.11) | collective-permute-done | bytes 8224 | tf_op jit(solution)/shard_map/ppermute | solution.py:29
  50.7 2.6 %collective-permute-start.12 = (f32[2048]{0:T(1024)S(1)}, f32[2048]{0:T(1024)S(1)}, u32[]{:S(2)}, u32[]{:S(2)}) collective-permute-start(f32[2048]{0:T(1024)S(1)} %add.172), channel_id=1, source_target_pairs={{0,16},{2,18},{4,20},{6,22},{8,24},{10,26},{12,28},{14,30},{16,0},... | collective-permute-start | bytes 24584 | tf_op jit(solution)/shard_map/ppermute | solution.py:159
  53.3 1.9 %collective-permute-done.12 = f32[2048]{0:T(1024)S(1)} collective-permute-done((f32[2048]{0:T(1024)S(1)}, f32[2048]{0:T(1024)S(1)}, u32[]{:S(2)}, u32[]{:S(2)}) %collective-permute-start.12) | collective-permute-done | bytes 8224 | tf_op jit(solution)/shard_map/ppermute | solution.py:159
  55.9 3.2 %fusion.11 = (f32[512]{0:T(512)S(1)}, f32[512]{0:T(512)S(1)}, f32[512]{0:T(512)S(1)}) fusion(f32[512]{0:T(512)S(1)} %bitcast.102, f32[2048]{0:T(1024)S(1)} %bitcast.93, f32[512]{0:T(512)S(1)} %broadcast_multiply_fusion, f32[2048]{0:T(1024)S(1)} %bitcast.91, f32[512]{0:T(512)S(1)} %bitcast.103, f32[2048]{0:T(1024)S(1)} %bitcast.92, f32[512]{0:T(512)S(1)} %bitcast.101, ...), kind=kLoop, calls=%fused_computation.26 | loop fusion | flops 19921408 | bytes 47104 | tf_op jit(solution)/shard_map/while/body/eval_jaxpr/reduce_sum | solution.py:62
  (69 shorter events, 8.2 us)
Async XLA Ops:
  0.6 39.4 %copy-start = (bf16[128,256]{1,0:T(8,128)(2,1)S(1)}, bf16[128,256]{1,0:T(8,128)(2,1)}, u32[]{:S(2)}) copy-start(bf16[128,256]{1,0:T(8,128)(2,1)} %param.23) | copy-start | bytes 196612
  2.7 1.3 %collective-permute-start = (f32[5,128]{1,0:T(8,128)S(1)}, f32[5,128]{1,0:T(8,128)S(1)}, u32[]{:S(2)}, u32[]{:S(2)}) collective-permute-start(f32[5,128]{1,0:T(8,128)S(1)} %pad_maximum_fusion.4), channel_id=1, source_target_pairs={{0,2},{2,0},{4,6},{6,4},{8,10},{10,8},{12,14},{14,12},{16,18},{18,... | collective-permute-start | bytes 7688 | tf_op jit(solution)/shard_map/ppermute | solution.py:17
  4.7 5.2 %collective-permute-start.1 = (f32[5,256]{1,0:T(8,128)S(1)}, f32[5,256]{1,0:T(8,128)S(1)}, u32[]{:S(2)}, u32[]{:S(2)}) collective-permute-start(f32[5,256]{1,0:T(8,128)S(1)} %maximum_select_fusion.5), channel_id=1, source_target_pairs={{0,4},{2,6},{4,0},{6,2},{8,12},{10,14},{12,8},{14,10},{16,20},{18,... | collective-permute-start | bytes 15368 | tf_op jit(solution)/shard_map/ppermute | solution.py:17
  8.3 3.7 %collective-permute-start.2 = (f32[4,512]{1,0:T(4,128)S(1)}, f32[4,512]{1,0:T(4,128)S(1)}, u32[]{:S(2)}, u32[]{:S(2)}) collective-permute-start(f32[4,512]{1,0:T(4,128)S(1)} %pad_maximum_fusion.1), channel_id=1, source_target_pairs={{0,8},{2,10},{4,12},{6,14},{8,0},{10,2},{12,4},{14,6},{16,24},{18,... | collective-permute-start | bytes 24584 | tf_op jit(solution)/shard_map/ppermute | solution.py:17
  12.8 4.7 %collective-permute-start.3 = (f32[4,1024]{1,0:T(4,128)S(1)}, f32[4,1024]{1,0:T(4,128)S(1)}, u32[]{:S(2)}, u32[]{:S(2)}) collective-permute-start(f32[4,1024]{1,0:T(4,128)S(1)} %maximum_select_fusion.4), channel_id=1, source_target_pairs={{0,16},{2,18},{4,20},{6,22},{8,24},{10,26},{12,28},{14,30},{16,0},... | collective-permute-start | bytes 49160 | tf_op jit(solution)/shard_map/ppermute | solution.py:17
  17.6 13.7 %copy-start.3 = (s32[128,4]{0,1:T(4,128)S(1)}, s32[128,4]{0,1:T(4,128)}, u32[]{:S(2)}) copy-start(s32[128,4]{0,1:T(4,128)} %param.17) | copy-start | bytes 6148
  17.6 13.7 %copy-start.4 = (s32[128,4]{0,1:T(4,128)S(1)}, s32[128,4]{0,1:T(4,128)}, u32[]{:S(2)}) copy-start(s32[128,4]{0,1:T(4,128)} %param.16) | copy-start | bytes 6148
  17.6 20.9 %copy-start.6 = (bf16[8,128]{1,0:T(8,128)(2,1)S(1)}, bf16[8,128]{1,0:T(8,128)(2,1)}, u32[]{:S(2)}) copy-start(bf16[8,128]{1,0:T(8,128)(2,1)} %param.20) | copy-start | bytes 6148
  17.6 20.9 %copy-start.9 = (f32[128]{0:T(128)S(1)}, f32[128]{0:T(128)}, u32[]{:S(2)}) copy-start(f32[128]{0:T(128)} %param.21) | copy-start | bytes 1540
  20.9 3.7 %collective-permute-start.4 = (f32[4,512]{1,0:T(4,128)S(1)}, f32[4,512]{1,0:T(4,128)S(1)}, u32[]{:S(2)}, u32[]{:S(2)}) collective-permute-start(f32[4,512]{1,0:T(4,128)S(1)} %pad_maximum_fusion.2), channel_id=1, source_target_pairs={{0,1},{1,0},{2,3},{3,2},{4,5},{5,4},{6,7},{7,6},{8,9},{9,8},{10,11... | collective-permute-start | bytes 24584 | tf_op jit(solution)/shard_map/ppermute | solution.py:29
  24.7 1.2 %collective-permute-start.5 = (f32[4,512]{1,0:T(4,128)S(1)}, f32[4,512]{1,0:T(4,128)S(1)}, u32[]{:S(2)}, u32[]{:S(2)}) collective-permute-start(f32[4,512]{1,0:T(4,128)S(1)} %fusion.48), channel_id=1, source_target_pairs={{0,2},{2,0},{4,6},{6,4},{8,10},{10,8},{12,14},{14,12},{16,18},{18,... | collective-permute-start | bytes 24584 | tf_op jit(solution)/shard_map/ppermute | solution.py:29
  25.9 3.7 %collective-permute-start.6 = (f32[4,512]{1,0:T(4,128)S(1)}, f32[4,512]{1,0:T(4,128)S(1)}, u32[]{:S(2)}, u32[]{:S(2)}) collective-permute-start(f32[4,512]{1,0:T(4,128)S(1)} %fusion.63), channel_id=1, source_target_pairs={{0,4},{2,6},{4,0},{6,2},{8,12},{10,14},{12,8},{14,10},{16,20},{18,... | collective-permute-start | bytes 24584 | tf_op jit(solution)/shard_map/ppermute | solution.py:29
  29.7 3.8 %collective-permute-start.7 = (f32[6,512]{1,0:T(8,128)S(1)}, f32[6,512]{1,0:T(8,128)S(1)}, u32[]{:S(2)}, u32[]{:S(2)}) collective-permute-start(f32[6,512]{1,0:T(8,128)S(1)} %pad_maximum_fusion), channel_id=1, source_target_pairs={{0,8},{2,10},{4,12},{6,14},{8,0},{10,2},{12,4},{14,6},{16,24},{18,... | collective-permute-start | bytes 36872 | tf_op jit(solution)/shard_map/ppermute | solution.py:17
  33.5 4.9 %collective-permute-start.8 = (f32[6,1024]{1,0:T(8,128)S(1)}, f32[6,1024]{1,0:T(8,128)S(1)}, u32[]{:S(2)}, u32[]{:S(2)}) collective-permute-start(f32[6,1024]{1,0:T(8,128)S(1)} %maximum_select_fusion.2), channel_id=1, source_target_pairs={{0,16},{2,18},{4,20},{6,22},{8,24},{10,26},{12,28},{14,30},{16,0},... | collective-permute-start | bytes 73736 | tf_op jit(solution)/shard_map/ppermute | solution.py:17
  38.4 0.8 %copy-start.5 = (bf16[128,128]{1,0:T(8,128)(2,1)S(1)}, bf16[128,128]{1,0:T(8,128)(2,1)}, u32[]{:S(2)}) copy-start(bf16[128,128]{1,0:T(8,128)(2,1)} %param.22) | copy-start | bytes 98308
  39.2 0.8 %copy-start.7 = (f32[256]{0:T(256)S(1)}, f32[256]{0:T(256)}, u32[]{:S(2)}) copy-start(f32[256]{0:T(256)} %param.25) | copy-start | bytes 3076
  39.2 0.8 %copy-start.8 = (f32[256]{0:T(256)S(1)}, f32[256]{0:T(256)}, u32[]{:S(2)}) copy-start(f32[256]{0:T(256)} %param.24) | copy-start | bytes 3076
  40.9 7.6 %copy-start.1 = (f32[3,512]{1,0:T(4,128)S(1)}, f32[3,512]{1,0:T(4,128)}, u32[]{:S(2)}) copy-start(f32[3,512]{1,0:T(4,128)} %param.18) | copy-start | bytes 18436
  40.9 12.3 %copy-start.2 = (f32[512]{0:T(512)S(1)}, f32[512]{0:T(512)}, u32[]{:S(2)}) copy-start(f32[512]{0:T(512)} %param.19) | copy-start | bytes 6148
  42.1 1.2 %collective-permute-start.9 = (f32[2048]{0:T(1024)S(1)}, f32[2048]{0:T(1024)S(1)}, u32[]{:S(2)}, u32[]{:S(2)}) collective-permute-start(f32[2048]{0:T(1024)S(1)} %fusion.41), channel_id=1, source_target_pairs={{0,2},{2,0},{4,6},{6,4},{8,10},{10,8},{12,14},{14,12},{16,18},{18,... | collective-permute-start | bytes 24584 | tf_op jit(solution)/shard_map/ppermute | solution.py:29
  43.3 3.7 %collective-permute-start.10 = (f32[2048]{0:T(1024)S(1)}, f32[2048]{0:T(1024)S(1)}, u32[]{:S(2)}, u32[]{:S(2)}) collective-permute-start(f32[2048]{0:T(1024)S(1)} %add.170), channel_id=1, source_target_pairs={{0,4},{2,6},{4,0},{6,2},{8,12},{10,14},{12,8},{14,10},{16,20},{18,... | collective-permute-start | bytes 24584 | tf_op jit(solution)/shard_map/ppermute | solution.py:29
  47.0 3.7 %collective-permute-start.11 = (f32[2048]{0:T(1024)S(1)}, f32[2048]{0:T(1024)S(1)}, u32[]{:S(2)}, u32[]{:S(2)}) collective-permute-start(f32[2048]{0:T(1024)S(1)} %add.171), channel_id=1, source_target_pairs={{0,8},{2,10},{4,12},{6,14},{8,0},{10,2},{12,4},{14,6},{16,24},{18,... | collective-permute-start | bytes 24584 | tf_op jit(solution)/shard_map/ppermute | solution.py:29
  50.7 4.5 %collective-permute-start.12 = (f32[2048]{0:T(1024)S(1)}, f32[2048]{0:T(1024)S(1)}, u32[]{:S(2)}, u32[]{:S(2)}) collective-permute-start(f32[2048]{0:T(1024)S(1)} %add.172), channel_id=1, source_target_pairs={{0,16},{2,18},{4,20},{6,22},{8,24},{10,26},{12,28},{14,30},{16,0},... | collective-permute-start | bytes 24584 | tf_op jit(solution)/shard_map/ppermute | solution.py:159

commit v8 on v6

--- a/solution.py
+++ b/solution.py
@@ -1,6 +1,8 @@
 import jax
 import jax.numpy as jnp
 from jax import lax
+from jax.experimental import pallas as pl
+from jax.experimental.pallas import tpu as pltpu
 from jax.sharding import PartitionSpec as P
 
 SOFTEN = 0.25
@@ -62,6 +64,67 @@
 
     total, _ = lax.scan(body, jnp.zeros((3, mm_pos.shape[1]), jnp.float32), stacked)
     return total
+
+
+def network_kernel(
+    ghost_ref, start_t_ref, start_ref, live_ref, pot_ref, live_all_ref,
+    mw_ref, hw_ref, er_ref, cr_ref, pg_ref, energy_ref, spread_ref, local_ref,
+):
+    rows, atoms = ghost_ref.shape[0], start_t_ref.shape[1]
+    columns = lax.broadcasted_iota(jnp.int32, (rows, atoms), 1)
+    links = jnp.zeros((rows, atoms), jnp.float32)
+    for k in range(ghost_ref.shape[1]):
+        links = links + (ghost_ref[:, k : k + 1] == columns).astype(jnp.float32)
+    contract_last = (((1,), (1,)), ((), ()))
+    neighbour = lax.dot_general(
+        links.astype(jnp.bfloat16), start_t_ref[...], contract_last,
+        preferred_element_type=jnp.float32,
+    ).astype(jnp.bfloat16)
+    mw = mw_ref[...]
+    hw = hw_ref[...]
+    er = er_ref[...]
+    cr = cr_ref[...]
+    pg = pg_ref[...]
+    live = live_ref[...]
+    potential = pot_ref[...]
+    mixed = start_ref[...].astype(jnp.float32) + jnp.dot(
+        neighbour, mw, preferred_element_type=jnp.float32
+    )
+    before = jnp.dot(mixed.astype(jnp.bfloat16), hw, preferred_element_type=jnp.float32)
+    sigma = jax.nn.sigmoid(before)
+    active = before * sigma
+    energy_part = live * jnp.sum(active * er, axis=1, keepdims=True)
+    charge_part = live * jnp.sum(active * cr, axis=1, keepdims=True)
+    energy_ref[...] = energy_part + charge_part * potential
+    back_active = live * (er + potential * cr)
+    back_before = (back_active * sigma * (1.0 + before * (1.0 - sigma))).astype(jnp.bfloat16)
+    back_mixed = lax.dot_general(back_before, hw, contract_last, preferred_element_type=jnp.float32)
+    back_sum = lax.dot_general(
+        back_mixed.astype(jnp.bfloat16), mw, contract_last, preferred_element_type=jnp.float32
+    ).astype(jnp.bfloat16)
+    sent = jnp.sum(back_sum.astype(jnp.float32) * pg, axis=1, keepdims=True)
+    spread_ref[...] = jnp.sum(links * sent, axis=0, keepdims=True) * live_all_ref[...]
+    local_ref[...] = charge_part + live * jnp.sum(back_mixed * pg, axis=1, keepdims=True)
+
+
+def network(ghost, start_t, start, live, potential, live_all, mw, hw, er, cr, pg):
+    rows, atoms = ghost.shape[0], start_t.shape[1]
+    vmem = pl.BlockSpec(memory_space=pltpu.VMEM)
+    return pl.pallas_call(
+        network_kernel,
+        out_shape=(
+            jax.ShapeDtypeStruct((rows, 1), jnp.float32),
+            jax.ShapeDtypeStruct((1, atoms), jnp.float32),
+            jax.ShapeDtypeStruct((rows, 1), jnp.float32),
+        ),
+        in_specs=[vmem] * 11,
+        out_specs=(vmem, vmem, vmem),
+        cost_estimate=pl.CostEstimate(
+            flops=2 * rows * (atoms * 128 + 4 * 128 * 256), transcendentals=rows * 256,
+            bytes_accessed=atoms * 128 * 2 + 4 * 128 * 256,
+        ),
+    )(ghost, start_t, start, live[:, None], potential[:, None], live_all[None, :],
+      mw, hw, er[None, :], cr[None, :], pg[None, :])
 
 
 def on_device(
@@ -123,35 +186,13 @@
     start = lax.dynamic_slice_in_dim(start_t, me * rows, rows, axis=1).T
 
     ghost = ghost_owner * rows + ghost_slot
-    columns = jnp.arange(atoms)[None, :]
-    links = jnp.zeros((rows, atoms), jnp.bfloat16)
-    for k in range(ghost.shape[1]):
-        links = links + (ghost[:, k : k + 1] == columns).astype(jnp.bfloat16)
-    neighbour = lax.dot_general(
-        links, start_t, (((1,), (1,)), ((), ())), preferred_element_type=jnp.float32
-    ).astype(jnp.bfloat16)
-
-    mixed = start.astype(jnp.float32) + jnp.dot(
-        neighbour, message_weight, preferred_element_type=jnp.float32
-    )
-    before = jnp.dot(mixed.astype(jnp.bfloat16), hidden_weight, preferred_element_type=jnp.float32)
-    sigma = jax.nn.sigmoid(before)
-    active = before * sigma
-    energy_part = live * jnp.sum(active * energy_readout[None, :], axis=1)
-    charge_part = live * jnp.sum(active * charge_readout[None, :], axis=1)
-    atom_energy = energy_part + charge_part * potential
-    back_active = live[:, None] * (
-        energy_readout[None, :] + potential[:, None] * charge_readout[None, :]
-    )
-    back_before = (back_active * sigma * (1.0 + before * (1.0 - sigma))).astype(jnp.bfloat16)
-    back_mixed = jnp.dot(back_before, hidden_weight.T, preferred_element_type=jnp.float32)
-    back_sum = jnp.dot(
-        back_mixed.astype(jnp.bfloat16), message_weight.T, preferred_element_type=jnp.float32
-    ).astype(jnp.bfloat16)
-
-    sent = jnp.sum(back_sum.astype(jnp.float32) * potential_gain[None, :], axis=1)
-    spread = jnp.sum(links.astype(jnp.float32) * sent[:, None], axis=0) * live_all
-    local = charge_part + live * jnp.sum(back_mixed * potential_gain[None, :], axis=1)
+    energy_col, spread_row, local_col = network(
+        ghost, start_t, start, live, potential, live_all, message_weight, hidden_weight,
+        energy_readout, charge_readout, potential_gain,
+    )
+    atom_energy = energy_col[:, 0]
+    spread = spread_row[0]
+    local = local_col[:, 0]
     placed = (jnp.arange(atoms) // rows == me).astype(jnp.float32)
     local_all = jnp.tile(local, atoms // rows) * placed
     part = sum_butterfly(spread + local_all, "blk", blocks // 2)

time: 56.9 us -> 61.5 us (1.081)
  local copies, waits for them, and re-layouts: 1.66 us -> 4.88 us
  Pallas kernels: 0 us -> 3.16 us
  waiting for transfers between devices: 24.3 us -> 23.1 us
  matrix products: 1.87 us -> 0.89 us
    pallas_call x0 -> x1, Pallas kernels: none -> 3.16 us  [network(): pl.pallas_call(network_kernel, out_shape=(jax.ShapeDtypeStruct((rows, 1),...]
    pallas_call x0 -> x2, other arithmetic: none -> 1.58 us  [network(): pl.pallas_call(network_kernel, out_shape=(jax.ShapeDtypeStruct((rows, 1),...]
    dot_general x4 -> x0, matrix products: 1.52 us -> none  [the longest x1 0.79 us: on_device(): jnp.dot(neighbour, message_weight, preferred_element_type=jnp.float32)]
    broadcast_in_dim x0 -> x3, local copies, waits for them, and re-layouts: none -> 1.48 us  [the longest x2 0.74 us: network(): potential[:, None]]
    convert_element_type x0 -> x1, local copies, waits for them, and re-layouts: none -> 1.03 us  [on_device(): start_t = (live_all[None, :] * (base_t + potential_gain[:, None] * potent...]
    add x0 -> x1, local copies, waits for them, and re-layouts: none -> 0.73 us  [on_device(): ghost = ghost_owner * rows + ghost_slot]
    reduce_sum x1 -> x0, other arithmetic: 0.7 us -> none  [on_device(): jnp.sum(links.astype(jnp.float32) * sent[:, None], axis=0) * live_all]
    ppermute x1, waiting for transfers between devices: 2.23 us -> 1.59 us  [on_device(): lax.ppermute(part, 'blk', [(i, i ^ blocks // 2) for i in range(blocks)])]
  transfers between devices with their start and end apart: 13 -> 13, of which waited for: 11 -> 11; matrix products, arithmetic and copies ran while one was open for 0% -> 2% of each run, Pallas kernels for 0% -> 0%
where the time goes in v8:
time: 61.5 us; the launch traced here: 61.2 us
  waiting for transfers between devices  23.1 us (38%)
  starting transfers between devices  18.1 us (29%)
  other arithmetic  9.13 us (15%)
  local copies, waits for them, and re-layouts  4.88 us (8%)
  Pallas kernels  3.16 us (5%)
  between operations  1.62 us (3%)
  matrix products  0.89 us (1%)
    ppermute x6, waiting for transfers between devices, sum_butterfly(): x = x + lax.ppermute(x, axis, [(i, i ^ step) for i in range(n)])  12.2 us
    ppermute x6, starting transfers between devices, gather_doubling(): other = lax.ppermute(x, axis, [(i, i ^ step) for i in range(n)])  10.8 us
    ppermute x6, waiting for transfers between devices, gather_doubling(): other = lax.ppermute(x, axis, [(i, i ^ step) for i in range(n)])  9.37 us
    ppermute x6, starting transfers between devices, sum_butterfly(): x = x + lax.ppermute(x, axis, [(i, i ^ step) for i in range(n)])  4.97 us
    reduce_sum x4, other arithmetic, body(): jnp.sum(weighted, axis=0)  3.2 us
    reduce_sum x4, other arithmetic, body(): jnp.sum(d[c] * weight, axis=0)  3.19 us
    pallas_call x1, Pallas kernels, network(): pl.pallas_call(network_kernel, out_shape=(jax.ShapeDtypeStruct((rows, 1),...  3.16 us
    ppermute x1, starting transfers between devices, on_device(): lax.ppermute(part, 'blk', [(i, i ^ blocks // 2) for i in range(blocks)])  2.29 us
  transfers between devices with their start and end apart: 13, of which 11 were waited for; matrix products, arithmetic and copies ran while one was open for 2% of the time, Pallas kernels for 0%

profile of v8, /device:TPU:0, one launch (start us, length us, event | category | flops | bytes accessed | tf_op | source)
XLA Modules:
  0.0 61.2 jit_solution(6014034519642748381)
XLA Ops:
  2.1 3.1 %collective-permute-start.2 = (f32[4,512]{1,0:T(4,128)S(1)}, f32[4,512]{1,0:T(4,128)S(1)}, u32[]{:S(2)}, u32[]{:S(2)}) collective-permute-start(f32[4,512]{1,0:T(4,128)S(1)} %pad_maximum_fusion.1), channel_id=1, source_target_pairs={{0,8},{2,10},{4,12},{6,14},{8,0},{10,2},{12,4},{14,6},{16,24},{18,... | collective-permute-start | bytes 24584 | tf_op jit(solution)/shard_map/ppermute | solution.py:18
  5.2 1.6 %collective-permute-start.1 = (f32[5,256]{1,0:T(8,128)S(1)}, f32[5,256]{1,0:T(8,128)S(1)}, u32[]{:S(2)}, u32[]{:S(2)}) collective-permute-start(f32[5,256]{1,0:T(8,128)S(1)} %maximum_select_fusion.6), channel_id=1, source_target_pairs={{0,4},{2,6},{4,0},{6,2},{8,12},{10,14},{12,8},{14,10},{16,20},{18,... | collective-permute-start | bytes 15368 | tf_op jit(solution)/shard_map/ppermute | solution.py:18
  6.8 2.1 %collective-permute-done.1 = f32[5,256]{1,0:T(8,128)S(1)} collective-permute-done((f32[5,256]{1,0:T(8,128)S(1)}, f32[5,256]{1,0:T(8,128)S(1)}, u32[]{:S(2)}, u32[]{:S(2)}) %collective-permute-start.1) | collective-permute-done | bytes 5152 | tf_op jit(solution)/shard_map/ppermute | solution.py:18
  9.0 2.7 %collective-permute-start.3 = (f32[4,1024]{1,0:T(4,128)S(1)}, f32[4,1024]{1,0:T(4,128)S(1)}, u32[]{:S(2)}, u32[]{:S(2)}) collective-permute-start(f32[4,1024]{1,0:T(4,128)S(1)} %maximum_select_fusion.5), channel_id=1, source_target_pairs={{0,16},{2,18},{4,20},{6,22},{8,24},{10,26},{12,28},{14,30},{16,0},... | collective-permute-start | bytes 49160 | tf_op jit(solution)/shard_map/ppermute | solution.py:18
  11.6 2.2 %collective-permute-done.3 = f32[4,1024]{1,0:T(4,128)S(1)} collective-permute-done((f32[4,1024]{1,0:T(4,128)S(1)}, f32[4,1024]{1,0:T(4,128)S(1)}, u32[]{:S(2)}, u32[]{:S(2)}) %collective-permute-start.3) | collective-permute-done | bytes 16416 | tf_op jit(solution)/shard_map/ppermute | solution.py:18
  13.8 3.5 %while.22 = (s32[]{:T(128)}, f32[4,512]{1,0:T(4,128)S(1)}, f32[1,512]{1,0:T(1,128)S(1)}, f32[4,512,4]{1,2,0:T(4,128)S(1)}, f32[1,512]{1,0:T(1,128)S(1)}, /*index=5*/f32[1,512]{1,0:T(1,128)S(1)}, s32[]{:T(128)}, s32[]{:T(128)}) while((s32[]{:T(128)}, f32[4,512]{1,0:T(4,128)S(1)}, f32[1,512]{1,0:T(1,128)S(1)}, ...), condition=%wide.region_5.6_spmd.clone, body=%wide.region_0.5_spmd.clone.sunk | while | flops 4988931 | bytes 79971 | solution.py:50
  17.3 1.6 %collective-permute-start.4 = (f32[4,512]{1,0:T(4,128)S(1)}, f32[4,512]{1,0:T(4,128)S(1)}, u32[]{:S(2)}, u32[]{:S(2)}) collective-permute-start(f32[4,512]{1,0:T(4,128)S(1)} %get-tuple-element.68), channel_id=1, source_target_pairs={{0,1},{1,0},{2,3},{3,2},{4,5},{5,4},{6,7},{7,6},{8,9},{9,8},{10,11... | collective-permute-start | bytes 24584 | tf_op jit(solution)/shard_map/ppermute | solution.py:30
  18.9 2.2 %collective-permute-done.4 = f32[4,512]{1,0:T(4,128)S(1)} collective-permute-done((f32[4,512]{1,0:T(4,128)S(1)}, f32[4,512]{1,0:T(4,128)S(1)}, u32[]{:S(2)}, u32[]{:S(2)}) %collective-permute-start.4) | collective-permute-done | bytes 8224 | tf_op jit(solution)/shard_map/ppermute | solution.py:30
  21.1 1.2 %collective-permute-done.5 = f32[4,512]{1,0:T(4,128)S(1)} collective-permute-done((f32[4,512]{1,0:T(4,128)S(1)}, f32[4,512]{1,0:T(4,128)S(1)}, u32[]{:S(2)}, u32[]{:S(2)}) %collective-permute-start.5) | collective-permute-done | bytes 8224 | tf_op jit(solution)/shard_map/ppermute | solution.py:30
  22.3 1.5 %collective-permute-start.6 = (f32[4,512]{1,0:T(4,128)S(1)}, f32[4,512]{1,0:T(4,128)S(1)}, u32[]{:S(2)}, u32[]{:S(2)}) collective-permute-start(f32[4,512]{1,0:T(4,128)S(1)} %add.118), channel_id=1, source_target_pairs={{0,4},{2,6},{4,0},{6,2},{8,12},{10,14},{12,8},{14,10},{16,20},{18,... | collective-permute-start | bytes 24584 | tf_op jit(solution)/shard_map/ppermute | solution.py:30
  23.8 2.1 %collective-permute-done.6 = f32[4,512]{1,0:T(4,128)S(1)} collective-permute-done((f32[4,512]{1,0:T(4,128)S(1)}, f32[4,512]{1,0:T(4,128)S(1)}, u32[]{:S(2)}, u32[]{:S(2)}) %collective-permute-start.6) | collective-permute-done | bytes 8224 | tf_op jit(solution)/shard_map/ppermute | solution.py:30
  26.4 3.3 %collective-permute-done.7 = f32[6,512]{1,0:T(8,128)S(1)} collective-permute-done((f32[6,512]{1,0:T(8,128)S(1)}, f32[6,512]{1,0:T(8,128)S(1)}, u32[]{:S(2)}, u32[]{:S(2)}) %collective-permute-start.7) | collective-permute-done | bytes 12320 | tf_op jit(solution)/shard_map/ppermute | solution.py:18
  29.8 2.5 %collective-permute-start.8 = (f32[6,1024]{1,0:T(8,128)S(1)}, f32[6,1024]{1,0:T(8,128)S(1)}, u32[]{:S(2)}, u32[]{:S(2)}) collective-permute-start(f32[6,1024]{1,0:T(8,128)S(1)} %maximum_select_fusion.2), channel_id=1, source_target_pairs={{0,16},{2,18},{4,20},{6,22},{8,24},{10,26},{12,28},{14,30},{16,0},... | collective-permute-start | bytes 73736 | tf_op jit(solution)/shard_map/ppermute | solution.py:18
  33.1 1.8 %collective-permute-done.8 = f32[6,1024]{1,0:T(8,128)S(1)} collective-permute-done((f32[6,1024]{1,0:T(8,128)S(1)}, f32[6,1024]{1,0:T(8,128)S(1)}, u32[]{:S(2)}, u32[]{:S(2)}) %collective-permute-start.8) | collective-permute-done | bytes 24608 | tf_op jit(solution)/shard_map/ppermute | solution.py:18
  36.5 1.0 %copy.41.start_t_ref = bf16[128,2048]{1,0:T(8,128)(2,1)} copy(bf16[128,2048]{0,1:T(8,128)(2,1)S(1)} %fusion.17) | data formatting | bytes 1048576 | tf_op jit(solution)/shard_map/convert_element_type | solution.py:185
  39.7 3.2 %shard_map.148 = (f32[128,1]{1,0:T(8,128)}, f32[1,2048]{1,0:T(1,128)}, f32[128,1]{1,0:T(8,128)}) custom-call(s32[128,4]{1,0:T(8,128)} %copy.40.ghost_ref, bf16[128,2048]{1,0:T(8,128)(2,1)} %copy.41.start_t_ref, bf16[128,128]{1,0:T(8,128)(2,1)} %dynamic-slice_bitcast_fusion.2.start_ref, f32[128,1]{1,0:T(8,128)} %copy.42.live_ref, f32[128,1]{1,0:T(8,128)} %copy.43.pot_ref, ...), custom_call_target="tpu_custom_call" | custom-call | flops 100663296 | bytes 655360 | tf_op jit(solution)/shard_map/pallas_call | solution.py:113
  42.9 1.0 %reduce.1 = f32[128]{0:T(128)S(1)} reduce(f32[128,1]{1,0:T(8,128)} %get-tuple-element.72, f32[]{:T(128)} %constant.155), dimensions={1}, to_apply=%get-tuple-element.72.reduce_sub_computation | reduce | bytes 1028 | tf_op jit(solution)/shard_map/pallas_call | solution.py:113
  43.9 1.2 %collective-permute-done.9 = f32[2048]{0:T(1024)S(1)} collective-permute-done((f32[2048]{0:T(1024)S(1)}, f32[2048]{0:T(1024)S(1)}, u32[]{:S(2)}, u32[]{:S(2)}) %collective-permute-start.9) | collective-permute-done | bytes 8224 | tf_op jit(solution)/shard_map/ppermute | solution.py:30
  45.1 1.5 %collective-permute-start.10 = (f32[2048]{0:T(1024)S(1)}, f32[2048]{0:T(1024)S(1)}, u32[]{:S(2)}, u32[]{:S(2)}) collective-permute-start(f32[2048]{0:T(1024)S(1)} %add.126), channel_id=1, source_target_pairs={{0,4},{2,6},{4,0},{6,2},{8,12},{10,14},{12,8},{14,10},{16,20},{18,... | collective-permute-start | bytes 24584 | tf_op jit(solution)/shard_map/ppermute | solution.py:30
  46.6 2.1 %collective-permute-done.10 = f32[2048]{0:T(1024)S(1)} collective-permute-done((f32[2048]{0:T(1024)S(1)}, f32[2048]{0:T(1024)S(1)}, u32[]{:S(2)}, u32[]{:S(2)}) %collective-permute-start.10) | collective-permute-done | bytes 8224 | tf_op jit(solution)/shard_map/ppermute | solution.py:30
  49.0 3.4 %collective-permute-done.11 = f32[2048]{0:T(1024)S(1)} collective-permute-done((f32[2048]{0:T(1024)S(1)}, f32[2048]{0:T(1024)S(1)}, u32[]{:S(2)}, u32[]{:S(2)}) %collective-permute-start.11) | collective-permute-done | bytes 8224 | tf_op jit(solution)/shard_map/ppermute | solution.py:30
  52.4 2.3 %collective-permute-start.12 = (f32[2048]{0:T(1024)S(1)}, f32[2048]{0:T(1024)S(1)}, u32[]{:S(2)}, u32[]{:S(2)}) collective-permute-start(f32[2048]{0:T(1024)S(1)} %add.128), channel_id=1, source_target_pairs={{0,16},{2,18},{4,20},{6,22},{8,24},{10,26},{12,28},{14,30},{16,0},... | collective-permute-start | bytes 24584 | tf_op jit(solution)/shard_map/ppermute | solution.py:199
  55.4 1.6 %collective-permute-done.12 = f32[2048]{0:T(1024)S(1)} collective-permute-done((f32[2048]{0:T(1024)S(1)}, f32[2048]{0:T(1024)S(1)}, u32[]{:S(2)}, u32[]{:S(2)}) %collective-permute-start.12) | collective-permute-done | bytes 8224 | tf_op jit(solution)/shard_map/ppermute | solution.py:199
  57.0 3.6 %while.23 = (s32[]{:T(128)}, f32[3,512]{1,0:T(4,128)S(1)}, f32[4,512,4]{1,2,0:T(4,128)S(1)}, f32[3,512]{1,0:T(4,128)S(1)}, f32[512]{0:T(512)S(1)}, /*index=5*/s32[]{:T(128)}, s32[]{:T(128)}) while((s32[]{:T(128)}, f32[3,512]{1,0:T(4,128)S(1)}, f32[4,512,4]{1,2,0:T(4,128)S(1)}, f32[3,512]{1,0:T(4,128)S(1)}, f32[512]{0:T(512)S(1)}, ...), condition=%wide.region_10.11_spmd.clone, body=%wide.region_6.10_spmd.clone.sunk | while | flops 4985347 | bytes 86107 | solution.py:65
  (111 shorter events, 14.3 us)
Async XLA Ops:
  0.6 8.3 %copy-start = (bf16[8,128]{1,0:T(8,128)(2,1)S(1)}, bf16[8,128]{1,0:T(8,128)(2,1)}, u32[]{:S(2)}) copy-start(bf16[8,128]{1,0:T(8,128)(2,1)} %param.24) | copy-start | bytes 6148
  0.6 0.7 %copy-start.11 = (s32[128]{0:T(128)S(1)}, s32[128]{0:T(128)}, u32[]{:S(2)}) copy-start(s32[128]{0:T(128)} %param.18) | copy-start | bytes 1540
  0.7 0.7 %copy-start.7 = (f32[3,128]{1,0:T(4,128)S(1)}, f32[3,128]{1,0:T(4,128)}, u32[]{:S(2)}) copy-start(f32[3,128]{1,0:T(4,128)} %param.17) | copy-start | bytes 4612
  1.3 0.7 %copy-start.1 = (f32[3,512]{1,0:T(4,128)S(1)}, f32[3,512]{1,0:T(4,128)}, u32[]{:S(2)}) copy-start(f32[3,512]{1,0:T(4,128)} %param.22) | copy-start | bytes 18436
  1.4 0.7 %copy-start.5 = (f32[512]{0:T(512)S(1)}, f32[512]{0:T(512)}, u32[]{:S(2)}) copy-start(f32[512]{0:T(512)} %param.23) | copy-start | bytes 6148
  1.4 3.8 %collective-permute-start = (f32[5,128]{1,0:T(8,128)S(1)}, f32[5,128]{1,0:T(8,128)S(1)}, u32[]{:S(2)}, u32[]{:S(2)}) collective-permute-start(f32[5,128]{1,0:T(8,128)S(1)} %pad_maximum_fusion.2), channel_id=1, source_target_pairs={{0,2},{2,0},{4,6},{6,4},{8,10},{10,8},{12,14},{14,12},{16,18},{18,... | collective-permute-start | bytes 7688 | tf_op jit(solution)/shard_map/ppermute | solution.py:18
  2.1 6.8 %collective-permute-start.2 = (f32[4,512]{1,0:T(4,128)S(1)}, f32[4,512]{1,0:T(4,128)S(1)}, u32[]{:S(2)}, u32[]{:S(2)}) collective-permute-start(f32[4,512]{1,0:T(4,128)S(1)} %pad_maximum_fusion.1), channel_id=1, source_target_pairs={{0,8},{2,10},{4,12},{6,14},{8,0},{10,2},{12,4},{14,6},{16,24},{18,... | collective-permute-start | bytes 24584 | tf_op jit(solution)/shard_map/ppermute | solution.py:18
  5.2 3.7 %collective-permute-start.1 = (f32[5,256]{1,0:T(8,128)S(1)}, f32[5,256]{1,0:T(8,128)S(1)}, u32[]{:S(2)}, u32[]{:S(2)}) collective-permute-start(f32[5,256]{1,0:T(8,128)S(1)} %maximum_select_fusion.6), channel_id=1, source_target_pairs={{0,4},{2,6},{4,0},{6,2},{8,12},{10,14},{12,8},{14,10},{16,20},{18,... | collective-permute-start | bytes 15368 | tf_op jit(solution)/shard_map/ppermute | solution.py:18
  9.0 4.8 %collective-permute-start.3 = (f32[4,1024]{1,0:T(4,128)S(1)}, f32[4,1024]{1,0:T(4,128)S(1)}, u32[]{:S(2)}, u32[]{:S(2)}) collective-permute-start(f32[4,1024]{1,0:T(4,128)S(1)} %maximum_select_fusion.5), channel_id=1, source_target_pairs={{0,16},{2,18},{4,20},{6,22},{8,24},{10,26},{12,28},{14,30},{16,0},... | collective-permute-start | bytes 49160 | tf_op jit(solution)/shard_map/ppermute | solution.py:18
  17.3 3.7 %collective-permute-start.4 = (f32[4,512]{1,0:T(4,128)S(1)}, f32[4,512]{1,0:T(4,128)S(1)}, u32[]{:S(2)}, u32[]{:S(2)}) collective-permute-start(f32[4,512]{1,0:T(4,128)S(1)} %get-tuple-element.68), channel_id=1, source_target_pairs={{0,1},{1,0},{2,3},{3,2},{4,5},{5,4},{6,7},{7,6},{8,9},{9,8},{10,11... | collective-permute-start | bytes 24584 | tf_op jit(solution)/shard_map/ppermute | solution.py:30
  21.0 2.8 %copy-start.8 = (s32[128,4]{0,1:T(4,128)S(1)}, s32[128,4]{0,1:T(4,128)}, u32[]{:S(2)}) copy-start(s32[128,4]{0,1:T(4,128)} %param.21) | copy-start | bytes 6148
  21.0 2.8 %copy-start.9 = (s32[128,4]{0,1:T(4,128)S(1)}, s32[128,4]{0,1:T(4,128)}, u32[]{:S(2)}) copy-start(s32[128,4]{0,1:T(4,128)} %param.20) | copy-start | bytes 6148
  21.0 1.2 %collective-permute-start.5 = (f32[4,512]{1,0:T(4,128)S(1)}, f32[4,512]{1,0:T(4,128)S(1)}, u32[]{:S(2)}, u32[]{:S(2)}) collective-permute-start(f32[4,512]{1,0:T(4,128)S(1)} %add.117), channel_id=1, source_target_pairs={{0,2},{2,0},{4,6},{6,4},{8,10},{10,8},{12,14},{14,12},{16,18},{18,... | collective-permute-start | bytes 24584 | tf_op jit(solution)/shard_map/ppermute | solution.py:30
  22.3 3.7 %collective-permute-start.6 = (f32[4,512]{1,0:T(4,128)S(1)}, f32[4,512]{1,0:T(4,128)S(1)}, u32[]{:S(2)}, u32[]{:S(2)}) collective-permute-start(f32[4,512]{1,0:T(4,128)S(1)} %add.118), channel_id=1, source_target_pairs={{0,4},{2,6},{4,0},{6,2},{8,12},{10,14},{12,8},{14,10},{16,20},{18,... | collective-permute-start | bytes 24584 | tf_op jit(solution)/shard_map/ppermute | solution.py:30
  26.0 3.8 %collective-permute-start.7 = (f32[6,512]{1,0:T(8,128)S(1)}, f32[6,512]{1,0:T(8,128)S(1)}, u32[]{:S(2)}, u32[]{:S(2)}) collective-permute-start(f32[6,512]{1,0:T(8,128)S(1)} %pad_maximum_fusion), channel_id=1, source_target_pairs={{0,8},{2,10},{4,12},{6,14},{8,0},{10,2},{12,4},{14,6},{16,24},{18,... | collective-permute-start | bytes 36872 | tf_op jit(solution)/shard_map/ppermute | solution.py:18
  29.8 5.1 %collective-permute-start.8 = (f32[6,1024]{1,0:T(8,128)S(1)}, f32[6,1024]{1,0:T(8,128)S(1)}, u32[]{:S(2)}, u32[]{:S(2)}) collective-permute-start(f32[6,1024]{1,0:T(8,128)S(1)} %maximum_select_fusion.2), channel_id=1, source_target_pairs={{0,16},{2,18},{4,20},{6,22},{8,24},{10,26},{12,28},{14,30},{16,0},... | collective-permute-start | bytes 73736 | tf_op jit(solution)/shard_map/ppermute | solution.py:18
  34.9 1.6 %copy-start.4 = (f32[1,2048]{1,0:T(1,128)}, f32[1,2048]{1,0:T(1,128)S(1)}, u32[]{:S(2)}) copy-start(f32[1,2048]{1,0:T(1,128)S(1)} %compare_convert_fusion.live_all_ref) | copy-start | bytes 24580
  42.9 1.0 %copy-start.6 = (f32[1,2048]{1,0:T(1,128)S(1)}, f32[1,2048]{1,0:T(1,128)}, u32[]{:S(2)}) copy-start(f32[1,2048]{1,0:T(1,128)} %get-tuple-element.71) | copy-start | bytes 24580
  43.9 1.2 %collective-permute-start.9 = (f32[2048]{0:T(1024)S(1)}, f32[2048]{0:T(1024)S(1)}, u32[]{:S(2)}, u32[]{:S(2)}) collective-permute-start(f32[2048]{0:T(1024)S(1)} %fusion.23), channel_id=1, source_target_pairs={{0,2},{2,0},{4,6},{6,4},{8,10},{10,8},{12,14},{14,12},{16,18},{18,... | collective-permute-start | bytes 24584 | tf_op jit(solution)/shard_map/ppermute | solution.py:30
  45.1 3.7 %collective-permute-start.10 = (f32[2048]{0:T(1024)S(1)}, f32[2048]{0:T(1024)S(1)}, u32[]{:S(2)}, u32[]{:S(2)}) collective-permute-start(f32[2048]{0:T(1024)S(1)} %add.126), channel_id=1, source_target_pairs={{0,4},{2,6},{4,0},{6,2},{8,12},{10,14},{12,8},{14,10},{16,20},{18,... | collective-permute-start | bytes 24584 | tf_op jit(solution)/shard_map/ppermute | solution.py:30
  48.8 6.0 %copy-start.3 = (f32[128,1]{1,0:T(8,128)S(1)}, f32[128,1]{1,0:T(8,128)}, u32[]{:S(2)}) copy-start(f32[128,1]{1,0:T(8,128)} %get-tuple-element.70) | copy-start | bytes 1540
  48.8 3.7 %collective-permute-start.11 = (f32[2048]{0:T(1024)S(1)}, f32[2048]{0:T(1024)S(1)}, u32[]{:S(2)}, u32[]{:S(2)}) collective-permute-start(f32[2048]{0:T(1024)S(1)} %add.127), channel_id=1, source_target_pairs={{0,8},{2,10},{4,12},{6,14},{8,0},{10,2},{12,4},{14,6},{16,24},{18,... | collective-permute-start | bytes 24584 | tf_op jit(solution)/shard_map/ppermute | solution.py:30
  52.4 4.5 %collective-permute-start.12 = (f32[2048]{0:T(1024)S(1)}, f32[2048]{0:T(1024)S(1)}, u32[]{:S(2)}, u32[]{:S(2)}) collective-permute-start(f32[2048]{0:T(1024)S(1)} %add.128), channel_id=1, source_target_pairs={{0,16},{2,18},{4,20},{6,22},{8,24},{10,26},{12,28},{14,30},{16,0},... | collective-permute-start | bytes 24584 | tf_op jit(solution)/shard_map/ppermute | solution.py:199
  60.6 0.7 %copy-start.2 = (f32[3,512]{1,0:T(4,128)}, f32[3,512]{1,0:T(4,128)S(1)}, u32[]{:S(2)}) copy-start(f32[3,512]{1,0:T(4,128)S(1)} %get-tuple-element.66) | copy-start | bytes 18436
  (1 other events, 0.7 us)

commit v9 on v7

--- a/solution.py
+++ b/solution.py
@@ -4,8 +4,7 @@
 from jax.sharding import PartitionSpec as P
 
 SOFTEN = 0.25
-CHUNK = 512
-WHOLE = True
+CHUNK = 1024
 
 
 def gather_doubling(x, axis, first=1, last=None):
@@ -32,7 +31,7 @@
 
 
 def potential_pass(qm_some, mm_some):
-    chunks = 1 if WHOLE else mm_some.shape[1] // CHUNK
+    chunks = max(1, mm_some.shape[1] // CHUNK)
     cols = [qm_some[c][None, :] for c in range(3)]
 
     def body(running, block):
@@ -51,7 +50,7 @@
 
 
 def force_pass(qm_all, effective, mm_pos, scale):
-    chunks = 1 if WHOLE else qm_all.shape[1] // CHUNK
+    chunks = max(1, qm_all.shape[1] // CHUNK)
     stacked = jnp.concatenate([qm_all, effective[None, :]], axis=0)
     stacked = jnp.transpose(stacked.reshape(4, chunks, -1), (1, 2, 0))
 
@@ -98,7 +97,9 @@
         axis=0,
     )
     near = gather_doubling(own, "blk", 1, low_blocks)
-    near, table_t = lax.optimization_barrier((near, species_table.T))
+    near, table_t, mixing = lax.optimization_barrier(
+        (near, species_table.T.astype(jnp.float32), message_weight.astype(jnp.float32))
+    )
     mm_some = gather_doubling(
         jnp.concatenate([mm_pos, mm_charge[None, :]], axis=0), "blk", low_blocks, blocks
     )
@@ -117,7 +118,7 @@
     live = lax.dynamic_slice_in_dim(live_all, me * rows, rows)
     potential = lax.dynamic_slice_in_dim(potential_all, me * rows, rows)
     picks_t = (jnp.arange(kinds)[:, None] == species_all[None, :]).astype(jnp.bfloat16)
-    base_t = jnp.dot(table_t, picks_t, preferred_element_type=jnp.float32)
+    base_t = jnp.dot(table_t, picks_t.astype(jnp.float32), preferred_element_type=jnp.float32)
     start_t = (
         live_all[None, :] * (base_t + potential_gain[:, None] * potential_all[None, :])
     ).astype(jnp.bfloat16)
@@ -133,7 +134,7 @@
     ).astype(jnp.bfloat16)
 
     mixed = start.astype(jnp.float32) + jnp.dot(
-        neighbour, message_weight, preferred_element_type=jnp.float32
+        neighbour.astype(jnp.float32), mixing, preferred_element_type=jnp.float32
     )
     before = jnp.dot(mixed.astype(jnp.bfloat16), hidden_weight, preferred_element_type=jnp.float32)
     sigma = jax.nn.sigmoid(before)
@@ -147,7 +148,8 @@
     back_before = (back_active * sigma * (1.0 + before * (1.0 - sigma))).astype(jnp.bfloat16)
     back_mixed = jnp.dot(back_before, hidden_weight.T, preferred_element_type=jnp.float32)
     back_sum = jnp.dot(
-        back_mixed.astype(jnp.bfloat16), message_weight.T, preferred_element_type=jnp.float32
+        back_mixed.astype(jnp.bfloat16).astype(jnp.float32), mixing.T,
+        preferred_element_type=jnp.float32,
     ).astype(jnp.bfloat16)
 
     sent = jnp.sum(back_sum.astype(jnp.float32) * potential_gain[None, :], axis=1)

time: 60.2 us -> 59.1 us (0.982)
  waiting for transfers between devices: 24.7 us -> 23.3 us
    ppermute x6, starting transfers between devices: 11.9 us -> 10.4 us  [gather_doubling(): other = lax.ppermute(x, axis, [(i, i ^ step) for i in range(n)])]
    ppermute x6, waiting for transfers between devices: 13.5 us -> 12 us  [sum_butterfly(): x = x + lax.ppermute(x, axis, [(i, i ^ step) for i in range(n)])]
    ppermute x6, starting transfers between devices: 3.7 us -> 5.07 us  [sum_butterfly(): x = x + lax.ppermute(x, axis, [(i, i ^ step) for i in range(n)])]
    concatenate x0 -> x1, other arithmetic: none -> 0.72 us  [gather_doubling(): jnp.concatenate([x, other], -1)]
    another operation x2 -> x0, other arithmetic: 0.62 us -> none  [the longest x1 0.61 us: body(): jnp.stack([jnp.sum(d[c] * weight, axis=0) for c in range(3)])]
    reduce_sum x1 -> x2, other arithmetic: 3.22 us -> 3.27 us  [body(): jnp.sum(d[c] * weight, axis=0)]
    reduce_sum x1 -> x2, other arithmetic: 3.27 us -> 3.3 us  [body(): jnp.sum(weighted, axis=0)]
    select_n x5 -> x6, other arithmetic: 1.58 us -> 1.59 us  [gather_doubling(): jnp.where(low, jnp.concatenate([x, other], -1), jnp.concatenate([other, x...]
  transfers between devices with their start and end apart: 13 -> 13, of which waited for: 12 -> 11; matrix products, arithmetic and copies ran while one was open for 1% -> 4% of each run, Pallas kernels for 0% -> 0%
where the time goes in v9:
time: 59.1 us; the launch traced here: 58.5 us
  waiting for transfers between devices  23.3 us (39%)
  starting transfers between devices  17.9 us (30%)
  other arithmetic  13.2 us (22%)
  matrix products  1.86 us (3%)
  between operations  1.59 us (3%)
    ppermute x6, waiting for transfers between devices, sum_butterfly(): x = x + lax.ppermute(x, axis, [(i, i ^ step) for i in range(n)])  12 us
    ppermute x6, starting transfers between devices, gather_doubling(): other = lax.ppermute(x, axis, [(i, i ^ step) for i in range(n)])  10.4 us
    ppermute x6, waiting for transfers between devices, gather_doubling(): other = lax.ppermute(x, axis, [(i, i ^ step) for i in range(n)])  9.18 us
    ppermute x6, starting transfers between devices, sum_butterfly(): x = x + lax.ppermute(x, axis, [(i, i ^ step) for i in range(n)])  5.07 us
    reduce_sum x2, other arithmetic, body(): jnp.sum(weighted, axis=0)  3.3 us
    reduce_sum x2, other arithmetic, body(): jnp.sum(d[c] * weight, axis=0)  3.27 us
    ppermute x1, starting transfers between devices, on_device(): lax.ppermute(part, 'blk', [(i, i ^ blocks // 2) for i in range(blocks)])  2.41 us
    ppermute x1, waiting for transfers between devices, on_device(): lax.ppermute(part, 'blk', [(i, i ^ blocks // 2) for i in range(blocks)])  2.11 us
  transfers between devices with their start and end apart: 13, of which 11 were waited for; matrix products, arithmetic and copies ran while one was open for 4% of the time, Pallas kernels for 0%

profile of v9, /device:TPU:0, one launch (start us, length us, event | category | flops | bytes accessed | tf_op | source)
XLA Modules:
  0.0 58.5 jit_solution(12604166348926531332)
XLA Ops:
  3.8 2.6 %collective-permute-start.2 = (f32[4,512]{1,0:T(4,128)S(1)}, f32[4,512]{1,0:T(4,128)S(1)}, u32[]{:S(2)}, u32[]{:S(2)}) collective-permute-start(f32[4,512]{1,0:T(4,128)S(1)} %pad_maximum_fusion.1), channel_id=1, source_target_pairs={{0,8},{2,10},{4,12},{6,14},{8,0},{10,2},{12,4},{14,6},{16,24},{18,... | collective-permute-start | bytes 24584 | tf_op jit(solution)/shard_map/ppermute | solution.py:16
  7.2 1.6 %collective-permute-start.1 = (f32[5,256]{1,0:T(8,128)S(1)}, f32[5,256]{1,0:T(8,128)S(1)}, u32[]{:S(2)}, u32[]{:S(2)}) collective-permute-start(f32[5,256]{1,0:T(8,128)S(1)} %maximum_select_fusion.6), channel_id=1, source_target_pairs={{0,4},{2,6},{4,0},{6,2},{8,12},{10,14},{12,8},{14,10},{16,20},{18,... | collective-permute-start | bytes 15368 | tf_op jit(solution)/shard_map/ppermute | solution.py:16
  9.5 1.4 %collective-permute-done.1 = f32[5,256]{1,0:T(8,128)S(1)} collective-permute-done((f32[5,256]{1,0:T(8,128)S(1)}, f32[5,256]{1,0:T(8,128)S(1)}, u32[]{:S(2)}, u32[]{:S(2)}) %collective-permute-start.1) | collective-permute-done | bytes 5152 | tf_op jit(solution)/shard_map/ppermute | solution.py:16
  11.8 2.7 %collective-permute-start.3 = (f32[4,1024]{1,0:T(4,128)S(1)}, f32[4,1024]{1,0:T(4,128)S(1)}, u32[]{:S(2)}, u32[]{:S(2)}) collective-permute-start(f32[4,1024]{1,0:T(4,128)S(1)} %maximum_select_fusion.5), channel_id=1, source_target_pairs={{0,16},{2,18},{4,20},{6,22},{8,24},{10,26},{12,28},{14,30},{16,0},... | collective-permute-start | bytes 49160 | tf_op jit(solution)/shard_map/ppermute | solution.py:16
  14.4 2.0 %collective-permute-done.3 = f32[4,1024]{1,0:T(4,128)S(1)} collective-permute-done((f32[4,1024]{1,0:T(4,128)S(1)}, f32[4,1024]{1,0:T(4,128)S(1)}, u32[]{:S(2)}, u32[]{:S(2)}) %collective-permute-start.3) | collective-permute-done | bytes 16416 | tf_op jit(solution)/shard_map/ppermute | solution.py:16
  16.5 3.5 %while.22 = (s32[]{:T(128)}, f32[4,512]{1,0:T(4,128)S(1)}, f32[1,512]{1,0:T(1,128)S(1)}, f32[2,1024,4]{1,2,0:T(4,128)S(1)}, f32[1,512]{1,0:T(1,128)S(1)}, /*index=5*/f32[1,512]{1,0:T(1,128)S(1)}, s32[]{:T(128)}, s32[]{:T(128)}) while((s32[]{:T(128)}, f32[4,512]{1,0:T(4,128)S(1)}, f32[1,512]{1,0:T(1,128)S(1)}, ...), condition=%wide.region_5.6_spmd.clone, body=%wide.region_0.5_spmd.clone.sunk | while | flops 9969667 | bytes 120939 | solution.py:48
  16.6 1.7 %multiply_reduce_fusion.6 = (f32[512]{0:T(512)S(1)}, f32[512]{0:T(512)S(1)}, f32[512]{0:T(512)S(1)}, f32[512]{0:T(512)S(1)}) fusion(f32[1024]{0:T(1024)S(1)} %bitcast.123, f32[1024]{0:T(1024)S(1)} %bitcast.124, f32[512]{0:T(512)S(1)} %bitcast.147, f32[1024]{0:T(1024)S(1)} %bitcast.125, f32[512]{0:T(512)S(1)} %bitcast.148, f32[1024]{0:T(1024)S(1)} %bitcast.122, ...), kind=kLoop, calls=%fused_computation.1.clone.1 | loop fusion | flops 9959424 | bytes 30720 | tf_op jit(solution)/shard_map/while/body/eval_jaxpr/reduce_sum | solution.py:43
  18.3 1.7 %multiply_reduce_fusion.6 = (f32[512]{0:T(512)S(1)}, f32[512]{0:T(512)S(1)}, f32[512]{0:T(512)S(1)}, f32[512]{0:T(512)S(1)}) fusion(f32[1024]{0:T(1024)S(1)} %bitcast.123, f32[1024]{0:T(1024)S(1)} %bitcast.124, f32[512]{0:T(512)S(1)} %bitcast.147, f32[1024]{0:T(1024)S(1)} %bitcast.125, f32[512]{0:T(512)S(1)} %bitcast.148, f32[1024]{0:T(1024)S(1)} %bitcast.122, ...), kind=kLoop, calls=%fused_computation.1.clone.1 | loop fusion | flops 9959424 | bytes 30720 | tf_op jit(solution)/shard_map/while/body/eval_jaxpr/reduce_sum | solution.py:43
  20.0 1.6 %collective-permute-start.4 = (f32[4,512]{1,0:T(4,128)S(1)}, f32[4,512]{1,0:T(4,128)S(1)}, u32[]{:S(2)}, u32[]{:S(2)}) collective-permute-start(f32[4,512]{1,0:T(4,128)S(1)} %get-tuple-element.66), channel_id=1, source_target_pairs={{0,1},{1,0},{2,3},{3,2},{4,5},{5,4},{6,7},{7,6},{8,9},{9,8},{10,11... | collective-permute-start | bytes 24584 | tf_op jit(solution)/shard_map/ppermute | solution.py:28
  21.6 2.1 %collective-permute-done.4 = f32[4,512]{1,0:T(4,128)S(1)} collective-permute-done((f32[4,512]{1,0:T(4,128)S(1)}, f32[4,512]{1,0:T(4,128)S(1)}, u32[]{:S(2)}, u32[]{:S(2)}) %collective-permute-start.4) | collective-permute-done | bytes 8224 | tf_op jit(solution)/shard_map/ppermute | solution.py:28
  23.7 1.2 %collective-permute-done.5 = f32[4,512]{1,0:T(4,128)S(1)} collective-permute-done((f32[4,512]{1,0:T(4,128)S(1)}, f32[4,512]{1,0:T(4,128)S(1)}, u32[]{:S(2)}, u32[]{:S(2)}) %collective-permute-start.5) | collective-permute-done | bytes 8224 | tf_op jit(solution)/shard_map/ppermute | solution.py:28
  24.9 1.6 %collective-permute-start.6 = (f32[4,512]{1,0:T(4,128)S(1)}, f32[4,512]{1,0:T(4,128)S(1)}, u32[]{:S(2)}, u32[]{:S(2)}) collective-permute-start(f32[4,512]{1,0:T(4,128)S(1)} %add.147), channel_id=1, source_target_pairs={{0,4},{2,6},{4,0},{6,2},{8,12},{10,14},{12,8},{14,10},{16,20},{18,... | collective-permute-start | bytes 24584 | tf_op jit(solution)/shard_map/ppermute | solution.py:28
  26.5 2.1 %collective-permute-done.6 = f32[4,512]{1,0:T(4,128)S(1)} collective-permute-done((f32[4,512]{1,0:T(4,128)S(1)}, f32[4,512]{1,0:T(4,128)S(1)}, u32[]{:S(2)}, u32[]{:S(2)}) %collective-permute-start.6) | collective-permute-done | bytes 8224 | tf_op jit(solution)/shard_map/ppermute | solution.py:28
  29.0 3.3 %collective-permute-done.7 = f32[6,512]{1,0:T(8,128)S(1)} collective-permute-done((f32[6,512]{1,0:T(8,128)S(1)}, f32[6,512]{1,0:T(8,128)S(1)}, u32[]{:S(2)}, u32[]{:S(2)}) %collective-permute-start.7) | collective-permute-done | bytes 12320 | tf_op jit(solution)/shard_map/ppermute | solution.py:16
  32.4 2.7 %collective-permute-start.8 = (f32[6,1024]{1,0:T(8,128)S(1)}, f32[6,1024]{1,0:T(8,128)S(1)}, u32[]{:S(2)}, u32[]{:S(2)}) collective-permute-start(f32[6,1024]{1,0:T(8,128)S(1)} %maximum_select_fusion.2), channel_id=1, source_target_pairs={{0,16},{2,18},{4,20},{6,22},{8,24},{10,26},{12,28},{14,30},{16,0},... | collective-permute-start | bytes 73736 | tf_op jit(solution)/shard_map/ppermute | solution.py:16
  35.1 2.4 %collective-permute-done.8 = f32[6,1024]{1,0:T(8,128)S(1)} collective-permute-done((f32[6,1024]{1,0:T(8,128)S(1)}, f32[6,1024]{1,0:T(8,128)S(1)}, u32[]{:S(2)}, u32[]{:S(2)}) %collective-permute-start.8) | collective-permute-done | bytes 24608 | tf_op jit(solution)/shard_map/ppermute | solution.py:16
  42.4 1.6 %collective-permute-start.10 = (f32[2048]{0:T(1024)S(1)}, f32[2048]{0:T(1024)S(1)}, u32[]{:S(2)}, u32[]{:S(2)}) collective-permute-start(f32[2048]{0:T(1024)S(1)} %add.165), channel_id=1, source_target_pairs={{0,4},{2,6},{4,0},{6,2},{8,12},{10,14},{12,8},{14,10},{16,20},{18,... | collective-permute-start | bytes 24584 | tf_op jit(solution)/shard_map/ppermute | solution.py:28
  44.0 2.1 %collective-permute-done.10 = f32[2048]{0:T(1024)S(1)} collective-permute-done((f32[2048]{0:T(1024)S(1)}, f32[2048]{0:T(1024)S(1)}, u32[]{:S(2)}, u32[]{:S(2)}) %collective-permute-start.10) | collective-permute-done | bytes 8224 | tf_op jit(solution)/shard_map/ppermute | solution.py:28
  46.3 3.4 %collective-permute-done.11 = f32[2048]{0:T(1024)S(1)} collective-permute-done((f32[2048]{0:T(1024)S(1)}, f32[2048]{0:T(1024)S(1)}, u32[]{:S(2)}, u32[]{:S(2)}) %collective-permute-start.11) | collective-permute-done | bytes 8224 | tf_op jit(solution)/shard_map/ppermute | solution.py:28
  49.8 2.4 %collective-permute-start.12 = (f32[2048]{0:T(1024)S(1)}, f32[2048]{0:T(1024)S(1)}, u32[]{:S(2)}, u32[]{:S(2)}) collective-permute-start(f32[2048]{0:T(1024)S(1)} %add.167), channel_id=1, source_target_pairs={{0,16},{2,18},{4,20},{6,22},{8,24},{10,26},{12,28},{14,30},{16,0},... | collective-permute-start | bytes 24584 | tf_op jit(solution)/shard_map/ppermute | solution.py:161
  52.2 2.1 %collective-permute-done.12 = f32[2048]{0:T(1024)S(1)} collective-permute-done((f32[2048]{0:T(1024)S(1)}, f32[2048]{0:T(1024)S(1)}, u32[]{:S(2)}, u32[]{:S(2)}) %collective-permute-start.12) | collective-permute-done | bytes 8224 | tf_op jit(solution)/shard_map/ppermute | solution.py:161
  54.3 3.5 %while.23 = (s32[]{:T(128)}, f32[3,512]{1,0:T(4,128)S(1)}, f32[2,1024,4]{1,2,0:T(4,128)S(1)}, f32[3,512]{1,0:T(4,128)S(1)}, f32[512]{0:T(512)S(1)}, /*index=5*/s32[]{:T(128)}, s32[]{:T(128)}) while((s32[]{:T(128)}, f32[3,512]{1,0:T(4,128)S(1)}, f32[2,1024,4]{1,2,0:T(4,128)S(1)}, f32[3,512]{1,0:T(4,128)S(1)}, f32[512]{0:T(512)S(1)}, ...), condition=%wide.region_15.16_spmd.clone, body=%wide.region_11.15_spmd.clone.sunk | while | flops 9966083 | bytes 127075 | solution.py:63
  54.4 1.6 %fusion.70 = (f32[512]{0:T(512)S(1)}, f32[512]{0:T(512)S(1)}, f32[512]{0:T(512)S(1)}) fusion(f32[512]{0:T(512)S(1)} %bitcast.137, f32[1024]{0:T(1024)S(1)} %bitcast.121, f32[512]{0:T(512)S(1)} %get-tuple-element.315, f32[1024]{0:T(1024)S(1)} %bitcast.119, f32[512]{0:T(512)S(1)} %bitcast.136, f32[1024]{0:T(1024)S(1)} %bitcast.120, ...), kind=kLoop, calls=%fused_computation.28.clone.1 | loop fusion | flops 9959936 | bytes 30720 | tf_op jit(solution)/shard_map/while/body/eval_jaxpr/reduce_sum | solution.py:61
  56.2 1.6 %fusion.70 = (f32[512]{0:T(512)S(1)}, f32[512]{0:T(512)S(1)}, f32[512]{0:T(512)S(1)}) fusion(f32[512]{0:T(512)S(1)} %bitcast.137, f32[1024]{0:T(1024)S(1)} %bitcast.121, f32[512]{0:T(512)S(1)} %get-tuple-element.315, f32[1024]{0:T(1024)S(1)} %bitcast.119, f32[512]{0:T(512)S(1)} %bitcast.136, f32[1024]{0:T(1024)S(1)} %bitcast.120, ...), kind=kLoop, calls=%fused_computation.28.clone.1 | loop fusion | flops 9959936 | bytes 30720 | tf_op jit(solution)/shard_map/while/body/eval_jaxpr/reduce_sum | solution.py:61
  (88 shorter events, 11.4 us)
Async XLA Ops:
  0.6 38.5 %copy-start = (bf16[128,256]{1,0:T(8,128)(2,1)S(1)}, bf16[128,256]{1,0:T(8,128)(2,1)}, u32[]{:S(2)}) copy-start(bf16[128,256]{1,0:T(8,128)(2,1)} %param.27) | copy-start | bytes 196612
  2.7 3.8 %collective-permute-start = (f32[5,128]{1,0:T(8,128)S(1)}, f32[5,128]{1,0:T(8,128)S(1)}, u32[]{:S(2)}, u32[]{:S(2)}) collective-permute-start(f32[5,128]{1,0:T(8,128)S(1)} %pad_maximum_fusion.2), channel_id=1, source_target_pairs={{0,2},{2,0},{4,6},{6,4},{8,10},{10,8},{12,14},{14,12},{16,18},{18,... | collective-permute-start | bytes 7688 | tf_op jit(solution)/shard_map/ppermute | solution.py:16
  3.8 7.1 %collective-permute-start.2 = (f32[4,512]{1,0:T(4,128)S(1)}, f32[4,512]{1,0:T(4,128)S(1)}, u32[]{:S(2)}, u32[]{:S(2)}) collective-permute-start(f32[4,512]{1,0:T(4,128)S(1)} %pad_maximum_fusion.1), channel_id=1, source_target_pairs={{0,8},{2,10},{4,12},{6,14},{8,0},{10,2},{12,4},{14,6},{16,24},{18,... | collective-permute-start | bytes 24584 | tf_op jit(solution)/shard_map/ppermute | solution.py:16
  7.2 3.7 %collective-permute-start.1 = (f32[5,256]{1,0:T(8,128)S(1)}, f32[5,256]{1,0:T(8,128)S(1)}, u32[]{:S(2)}, u32[]{:S(2)}) collective-permute-start(f32[5,256]{1,0:T(8,128)S(1)} %maximum_select_fusion.6), channel_id=1, source_target_pairs={{0,4},{2,6},{4,0},{6,2},{8,12},{10,14},{12,8},{14,10},{16,20},{18,... | collective-permute-start | bytes 15368 | tf_op jit(solution)/shard_map/ppermute | solution.py:16
  11.8 4.7 %collective-permute-start.3 = (f32[4,1024]{1,0:T(4,128)S(1)}, f32[4,1024]{1,0:T(4,128)S(1)}, u32[]{:S(2)}, u32[]{:S(2)}) collective-permute-start(f32[4,1024]{1,0:T(4,128)S(1)} %maximum_select_fusion.5), channel_id=1, source_target_pairs={{0,16},{2,18},{4,20},{6,22},{8,24},{10,26},{12,28},{14,30},{16,0},... | collective-permute-start | bytes 49160 | tf_op jit(solution)/shard_map/ppermute | solution.py:16
  16.5 12.6 %copy-start.4 = (s32[128,4]{0,1:T(4,128)S(1)}, s32[128,4]{0,1:T(4,128)}, u32[]{:S(2)}) copy-start(s32[128,4]{0,1:T(4,128)} %param.21) | copy-start | bytes 6148
  16.5 12.6 %copy-start.5 = (s32[128,4]{0,1:T(4,128)S(1)}, s32[128,4]{0,1:T(4,128)}, u32[]{:S(2)}) copy-start(s32[128,4]{0,1:T(4,128)} %param.20) | copy-start | bytes 6148
  16.5 21.1 %copy-start.7 = (bf16[8,128]{1,0:T(8,128)(2,1)S(1)}, bf16[8,128]{1,0:T(8,128)(2,1)}, u32[]{:S(2)}) copy-start(bf16[8,128]{1,0:T(8,128)(2,1)} %param.24) | copy-start | bytes 6148
  16.5 21.1 %copy-start.10 = (f32[128]{0:T(128)S(1)}, f32[128]{0:T(128)}, u32[]{:S(2)}) copy-start(f32[128]{0:T(128)} %param.25) | copy-start | bytes 1540
  20.0 3.7 %collective-permute-start.4 = (f32[4,512]{1,0:T(4,128)S(1)}, f32[4,512]{1,0:T(4,128)S(1)}, u32[]{:S(2)}, u32[]{:S(2)}) collective-permute-start(f32[4,512]{1,0:T(4,128)S(1)} %get-tuple-element.66), channel_id=1, source_target_pairs={{0,1},{1,0},{2,3},{3,2},{4,5},{5,4},{6,7},{7,6},{8,9},{9,8},{10,11... | collective-permute-start | bytes 24584 | tf_op jit(solution)/shard_map/ppermute | solution.py:28
  23.7 1.2 %collective-permute-start.5 = (f32[4,512]{1,0:T(4,128)S(1)}, f32[4,512]{1,0:T(4,128)S(1)}, u32[]{:S(2)}, u32[]{:S(2)}) collective-permute-start(f32[4,512]{1,0:T(4,128)S(1)} %add.146), channel_id=1, source_target_pairs={{0,2},{2,0},{4,6},{6,4},{8,10},{10,8},{12,14},{14,12},{16,18},{18,... | collective-permute-start | bytes 24584 | tf_op jit(solution)/shard_map/ppermute | solution.py:28
  24.9 3.7 %collective-permute-start.6 = (f32[4,512]{1,0:T(4,128)S(1)}, f32[4,512]{1,0:T(4,128)S(1)}, u32[]{:S(2)}, u32[]{:S(2)}) collective-permute-start(f32[4,512]{1,0:T(4,128)S(1)} %add.147), channel_id=1, source_target_pairs={{0,4},{2,6},{4,0},{6,2},{8,12},{10,14},{12,8},{14,10},{16,20},{18,... | collective-permute-start | bytes 24584 | tf_op jit(solution)/shard_map/ppermute | solution.py:28
  28.6 3.8 %collective-permute-start.7 = (f32[6,512]{1,0:T(8,128)S(1)}, f32[6,512]{1,0:T(8,128)S(1)}, u32[]{:S(2)}, u32[]{:S(2)}) collective-permute-start(f32[6,512]{1,0:T(8,128)S(1)} %pad_maximum_fusion), channel_id=1, source_target_pairs={{0,8},{2,10},{4,12},{6,14},{8,0},{10,2},{12,4},{14,6},{16,24},{18,... | collective-permute-start | bytes 36872 | tf_op jit(solution)/shard_map/ppermute | solution.py:16
  32.4 5.1 %collective-permute-start.8 = (f32[6,1024]{1,0:T(8,128)S(1)}, f32[6,1024]{1,0:T(8,128)S(1)}, u32[]{:S(2)}, u32[]{:S(2)}) collective-permute-start(f32[6,1024]{1,0:T(8,128)S(1)} %maximum_select_fusion.2), channel_id=1, source_target_pairs={{0,16},{2,18},{4,20},{6,22},{8,24},{10,26},{12,28},{14,30},{16,0},... | collective-permute-start | bytes 73736 | tf_op jit(solution)/shard_map/ppermute | solution.py:16
  37.5 0.8 %copy-start.6 = (bf16[128,128]{1,0:T(8,128)(2,1)S(1)}, bf16[128,128]{1,0:T(8,128)(2,1)}, u32[]{:S(2)}) copy-start(bf16[128,128]{1,0:T(8,128)(2,1)} %param.26) | copy-start | bytes 98308
  38.3 0.8 %copy-start.8 = (f32[256]{0:T(256)S(1)}, f32[256]{0:T(256)}, u32[]{:S(2)}) copy-start(f32[256]{0:T(256)} %param.29) | copy-start | bytes 3076
  38.3 0.8 %copy-start.9 = (f32[256]{0:T(256)S(1)}, f32[256]{0:T(256)}, u32[]{:S(2)}) copy-start(f32[256]{0:T(256)} %param.28) | copy-start | bytes 3076
  40.0 12.1 %copy-start.3 = (f32[512]{0:T(512)S(1)}, f32[512]{0:T(512)}, u32[]{:S(2)}) copy-start(f32[512]{0:T(512)} %param.23) | copy-start | bytes 6148
  40.0 14.3 %copy-start.1 = (f32[3,512]{1,0:T(4,128)S(1)}, f32[3,512]{1,0:T(4,128)}, u32[]{:S(2)}) copy-start(f32[3,512]{1,0:T(4,128)} %param.22) | copy-start | bytes 18436
  41.2 1.2 %collective-permute-start.9 = (f32[2048]{0:T(1024)S(1)}, f32[2048]{0:T(1024)S(1)}, u32[]{:S(2)}, u32[]{:S(2)}) collective-permute-start(f32[2048]{0:T(1024)S(1)} %fusion.41), channel_id=1, source_target_pairs={{0,2},{2,0},{4,6},{6,4},{8,10},{10,8},{12,14},{14,12},{16,18},{18,... | collective-permute-start | bytes 24584 | tf_op jit(solution)/shard_map/ppermute | solution.py:28
  42.4 3.7 %collective-permute-start.10 = (f32[2048]{0:T(1024)S(1)}, f32[2048]{0:T(1024)S(1)}, u32[]{:S(2)}, u32[]{:S(2)}) collective-permute-start(f32[2048]{0:T(1024)S(1)} %add.165), channel_id=1, source_target_pairs={{0,4},{2,6},{4,0},{6,2},{8,12},{10,14},{12,8},{14,10},{16,20},{18,... | collective-permute-start | bytes 24584 | tf_op jit(solution)/shard_map/ppermute | solution.py:28
  46.1 3.7 %collective-permute-start.11 = (f32[2048]{0:T(1024)S(1)}, f32[2048]{0:T(1024)S(1)}, u32[]{:S(2)}, u32[]{:S(2)}) collective-permute-start(f32[2048]{0:T(1024)S(1)} %add.166), channel_id=1, source_target_pairs={{0,8},{2,10},{4,12},{6,14},{8,0},{10,2},{12,4},{14,6},{16,24},{18,... | collective-permute-start | bytes 24584 | tf_op jit(solution)/shard_map/ppermute | solution.py:28
  49.8 4.5 %collective-permute-start.12 = (f32[2048]{0:T(1024)S(1)}, f32[2048]{0:T(1024)S(1)}, u32[]{:S(2)}, u32[]{:S(2)}) collective-permute-start(f32[2048]{0:T(1024)S(1)} %add.167), channel_id=1, source_target_pairs={{0,16},{2,18},{4,20},{6,22},{8,24},{10,26},{12,28},{14,30},{16,0},... | collective-permute-start | bytes 24584 | tf_op jit(solution)/shard_map/ppermute | solution.py:161
  57.8 0.7 %copy-start.2 = (f32[3,512]{1,0:T(4,128)}, f32[3,512]{1,0:T(4,128)S(1)}, u32[]{:S(2)}) copy-start(f32[3,512]{1,0:T(4,128)S(1)} %get-tuple-element.64) | copy-start | bytes 18436

commit v10 on v9

--- a/solution.py
+++ b/solution.py
@@ -4,7 +4,7 @@
 from jax.sharding import PartitionSpec as P
 
 SOFTEN = 0.25
-CHUNK = 1024
+CHUNK = 512
 
 
 def gather_doubling(x, axis, first=1, last=None):
@@ -31,7 +31,7 @@
 
 
 def potential_pass(qm_some, mm_some):
-    chunks = max(1, mm_some.shape[1] // CHUNK)
+    chunks = mm_some.shape[1] // CHUNK
     cols = [qm_some[c][None, :] for c in range(3)]
 
     def body(running, block):
@@ -44,15 +44,15 @@
         )
         return running + part, None
 
-    stacked = jnp.transpose(mm_some.reshape(4, chunks, -1), (1, 2, 0))
+    stacked = jnp.transpose(mm_some.reshape(4, chunks, CHUNK), (1, 2, 0))
     total, _ = lax.scan(body, jnp.zeros((4, qm_some.shape[1]), jnp.float32), stacked)
     return total
 
 
 def force_pass(qm_all, effective, mm_pos, scale):
-    chunks = max(1, qm_all.shape[1] // CHUNK)
+    chunks = qm_all.shape[1] // CHUNK
     stacked = jnp.concatenate([qm_all, effective[None, :]], axis=0)
-    stacked = jnp.transpose(stacked.reshape(4, chunks, -1), (1, 2, 0))
+    stacked = jnp.transpose(stacked.reshape(4, chunks, CHUNK), (1, 2, 0))
 
     def body(running, block):
         d = [block[:, c : c + 1] - mm_pos[c][None, :] for c in range(3)]

time: 59.1 us -> 56.9 us (0.963)
  other arithmetic: 13.2 us -> 8.78 us
  local copies, waits for them, and re-layouts: 0.57 us -> 1.66 us
  waiting for transfers between devices: 23.3 us -> 24.3 us
    select_n x6, other arithmetic: 1.59 us -> 0.05 us  [gather_doubling(): jnp.where(low, jnp.concatenate([x, other], -1), jnp.concatenate([other, x...]
    unnamed x22 -> x26, local copies, waits for them, and re-layouts: 0.43 us -> 1.46 us
    ppermute x6, waiting for transfers between devices: 9.18 us -> 9.91 us  [gather_doubling(): other = lax.ppermute(x, axis, [(i, i ^ step) for i in range(n)])]
    concatenate x1, other arithmetic: 0.72 us -> 0.01 us  [on_device(): jnp.concatenate([mm_pos, mm_charge[None, :]], axis=0)]
    concatenate x1, other arithmetic: 0.72 us -> 0.01 us  [gather_doubling(): jnp.concatenate([x, other], -1)]
    concatenate x1, other arithmetic: 0.69 us -> 0.01 us  [on_device(): jnp.concatenate([qm_pos, species.astype(jnp.float32)[None, :], jnp.broadc...]
    broadcast_in_dim x1, other arithmetic: 0.66 us -> 0.01 us  [on_device(): species.astype(jnp.float32)[None, :]]
    reduce_sum x2 -> x4, other arithmetic: 3.3 us -> 3.2 us  [body(): jnp.sum(weighted, axis=0)]
  transfers between devices with their start and end apart: 13 -> 13, of which waited for: 11 -> 11; matrix products, arithmetic and copies ran while one was open for 4% -> 0% of each run, Pallas kernels for 0% -> 0%
where the time goes in v10:
time: 56.9 us; the launch traced here: 56.6 us
  waiting for transfers between devices  24.3 us (43%)
  starting transfers between devices  18 us (32%)
  other arithmetic  8.78 us (15%)
  matrix products  1.87 us (3%)
  local copies, waits for them, and re-layouts  1.66 us (3%)
  between operations  1.64 us (3%)
    ppermute x6, waiting for transfers between devices, sum_butterfly(): x = x + lax.ppermute(x, axis, [(i, i ^ step) for i in range(n)])  12.2 us
    ppermute x6, starting transfers between devices, gather_doubling(): other = lax.ppermute(x, axis, [(i, i ^ step) for i in range(n)])  10.8 us
    ppermute x6, waiting for transfers between devices, gather_doubling(): other = lax.ppermute(x, axis, [(i, i ^ step) for i in range(n)])  9.91 us
    ppermute x6, starting transfers between devices, sum_butterfly(): x = x + lax.ppermute(x, axis, [(i, i ^ step) for i in range(n)])  4.9 us
    reduce_sum x4, other arithmetic, body(): jnp.sum(weighted, axis=0)  3.2 us
    reduce_sum x4, other arithmetic, body(): jnp.sum(d[c] * weight, axis=0)  3.19 us
    ppermute x1, starting transfers between devices, on_device(): lax.ppermute(part, 'blk', [(i, i ^ blocks // 2) for i in range(blocks)])  2.29 us
    ppermute x1, waiting for transfers between devices, on_device(): lax.ppermute(part, 'blk', [(i, i ^ blocks // 2) for i in range(blocks)])  2.23 us
  transfers between devices with their start and end apart: 13, of which 11 were waited for; matrix products, arithmetic and copies ran while one was open for 0% of the time, Pallas kernels for 0%

profile of v10, /device:TPU:0, one launch (start us, length us, event | category | flops | bytes accessed | tf_op | source)
XLA Modules:
  0.0 56.6 jit_solution(14145297085119366925)
XLA Ops:
  2.1 3.1 %collective-permute-start.2 = (f32[4,512]{1,0:T(4,128)S(1)}, f32[4,512]{1,0:T(4,128)S(1)}, u32[]{:S(2)}, u32[]{:S(2)}) collective-permute-start(f32[4,512]{1,0:T(4,128)S(1)} %pad_maximum_fusion.1), channel_id=1, source_target_pairs={{0,8},{2,10},{4,12},{6,14},{8,0},{10,2},{12,4},{14,6},{16,24},{18,... | collective-permute-start | bytes 24584 | tf_op jit(solution)/shard_map/ppermute | solution.py:16
  5.2 1.6 %collective-permute-start.1 = (f32[5,256]{1,0:T(8,128)S(1)}, f32[5,256]{1,0:T(8,128)S(1)}, u32[]{:S(2)}, u32[]{:S(2)}) collective-permute-start(f32[5,256]{1,0:T(8,128)S(1)} %maximum_select_fusion.6), channel_id=1, source_target_pairs={{0,4},{2,6},{4,0},{6,2},{8,12},{10,14},{12,8},{14,10},{16,20},{18,... | collective-permute-start | bytes 15368 | tf_op jit(solution)/shard_map/ppermute | solution.py:16
  6.8 2.1 %collective-permute-done.1 = f32[5,256]{1,0:T(8,128)S(1)} collective-permute-done((f32[5,256]{1,0:T(8,128)S(1)}, f32[5,256]{1,0:T(8,128)S(1)}, u32[]{:S(2)}, u32[]{:S(2)}) %collective-permute-start.1) | collective-permute-done | bytes 5152 | tf_op jit(solution)/shard_map/ppermute | solution.py:16
  9.0 2.7 %collective-permute-start.3 = (f32[4,1024]{1,0:T(4,128)S(1)}, f32[4,1024]{1,0:T(4,128)S(1)}, u32[]{:S(2)}, u32[]{:S(2)}) collective-permute-start(f32[4,1024]{1,0:T(4,128)S(1)} %maximum_select_fusion.5), channel_id=1, source_target_pairs={{0,16},{2,18},{4,20},{6,22},{8,24},{10,26},{12,28},{14,30},{16,0},... | collective-permute-start | bytes 49160 | tf_op jit(solution)/shard_map/ppermute | solution.py:16
  11.6 2.2 %collective-permute-done.3 = f32[4,1024]{1,0:T(4,128)S(1)} collective-permute-done((f32[4,1024]{1,0:T(4,128)S(1)}, f32[4,1024]{1,0:T(4,128)S(1)}, u32[]{:S(2)}, u32[]{:S(2)}) %collective-permute-start.3) | collective-permute-done | bytes 16416 | tf_op jit(solution)/shard_map/ppermute | solution.py:16
  13.8 3.5 %while.22 = (s32[]{:T(128)}, f32[4,512]{1,0:T(4,128)S(1)}, f32[1,512]{1,0:T(1,128)S(1)}, f32[4,512,4]{1,2,0:T(4,128)S(1)}, f32[1,512]{1,0:T(1,128)S(1)}, /*index=5*/f32[1,512]{1,0:T(1,128)S(1)}, s32[]{:T(128)}, s32[]{:T(128)}) while((s32[]{:T(128)}, f32[4,512]{1,0:T(4,128)S(1)}, f32[1,512]{1,0:T(1,128)S(1)}, ...), condition=%wide.region_5.6_spmd.clone, body=%wide.region_0.5_spmd.clone.sunk | while | flops 4988931 | bytes 79979 | solution.py:48
  13.8 0.8 %multiply_reduce_fusion.6 = (f32[512]{0:T(512)S(1)}, f32[512]{0:T(512)S(1)}, f32[512]{0:T(512)S(1)}, f32[512]{0:T(512)S(1)}) fusion(f32[512]{0:T(512)S(1)} %bitcast.135, f32[512]{0:T(512)S(1)} %bitcast.136, f32[512]{0:T(512)S(1)} %bitcast.147, f32[512]{0:T(512)S(1)} %bitcast.137, f32[512]{0:T(512)S(1)} %bitcast.148, f32[512]{0:T(512)S(1)} %bitcast.134, ...), kind=kLoop, calls=%fused_computation.1.clone.1 | loop fusion | flops 4978688 | bytes 22528 | tf_op jit(solution)/shard_map/while/body/eval_jaxpr/reduce_sum | solution.py:43
  14.7 0.8 %multiply_reduce_fusion.6 = (f32[512]{0:T(512)S(1)}, f32[512]{0:T(512)S(1)}, f32[512]{0:T(512)S(1)}, f32[512]{0:T(512)S(1)}) fusion(f32[512]{0:T(512)S(1)} %bitcast.135, f32[512]{0:T(512)S(1)} %bitcast.136, f32[512]{0:T(512)S(1)} %bitcast.147, f32[512]{0:T(512)S(1)} %bitcast.137, f32[512]{0:T(512)S(1)} %bitcast.148, f32[512]{0:T(512)S(1)} %bitcast.134, ...), kind=kLoop, calls=%fused_computation.1.clone.1 | loop fusion | flops 4978688 | bytes 22528 | tf_op jit(solution)/shard_map/while/body/eval_jaxpr/reduce_sum | solution.py:43
  15.6 0.8 %multiply_reduce_fusion.6 = (f32[512]{0:T(512)S(1)}, f32[512]{0:T(512)S(1)}, f32[512]{0:T(512)S(1)}, f32[512]{0:T(512)S(1)}) fusion(f32[512]{0:T(512)S(1)} %bitcast.135, f32[512]{0:T(512)S(1)} %bitcast.136, f32[512]{0:T(512)S(1)} %bitcast.147, f32[512]{0:T(512)S(1)} %bitcast.137, f32[512]{0:T(512)S(1)} %bitcast.148, f32[512]{0:T(512)S(1)} %bitcast.134, ...), kind=kLoop, calls=%fused_computation.1.clone.1 | loop fusion | flops 4978688 | bytes 22528 | tf_op jit(solution)/shard_map/while/body/eval_jaxpr/reduce_sum | solution.py:43
  17.3 1.6 %collective-permute-start.4 = (f32[4,512]{1,0:T(4,128)S(1)}, f32[4,512]{1,0:T(4,128)S(1)}, u32[]{:S(2)}, u32[]{:S(2)}) collective-permute-start(f32[4,512]{1,0:T(4,128)S(1)} %get-tuple-element.66), channel_id=1, source_target_pairs={{0,1},{1,0},{2,3},{3,2},{4,5},{5,4},{6,7},{7,6},{8,9},{9,8},{10,11... | collective-permute-start | bytes 24584 | tf_op jit(solution)/shard_map/ppermute | solution.py:28
  18.9 2.2 %collective-permute-done.4 = f32[4,512]{1,0:T(4,128)S(1)} collective-permute-done((f32[4,512]{1,0:T(4,128)S(1)}, f32[4,512]{1,0:T(4,128)S(1)}, u32[]{:S(2)}, u32[]{:S(2)}) %collective-permute-start.4) | collective-permute-done | bytes 8224 | tf_op jit(solution)/shard_map/ppermute | solution.py:28
  21.0 1.2 %collective-permute-done.5 = f32[4,512]{1,0:T(4,128)S(1)} collective-permute-done((f32[4,512]{1,0:T(4,128)S(1)}, f32[4,512]{1,0:T(4,128)S(1)}, u32[]{:S(2)}, u32[]{:S(2)}) %collective-permute-start.5) | collective-permute-done | bytes 8224 | tf_op jit(solution)/shard_map/ppermute | solution.py:28
  22.2 1.5 %collective-permute-start.6 = (f32[4,512]{1,0:T(4,128)S(1)}, f32[4,512]{1,0:T(4,128)S(1)}, u32[]{:S(2)}, u32[]{:S(2)}) collective-permute-start(f32[4,512]{1,0:T(4,128)S(1)} %add.147), channel_id=1, source_target_pairs={{0,4},{2,6},{4,0},{6,2},{8,12},{10,14},{12,8},{14,10},{16,20},{18,... | collective-permute-start | bytes 24584 | tf_op jit(solution)/shard_map/ppermute | solution.py:28
  23.7 2.1 %collective-permute-done.6 = f32[4,512]{1,0:T(4,128)S(1)} collective-permute-done((f32[4,512]{1,0:T(4,128)S(1)}, f32[4,512]{1,0:T(4,128)S(1)}, u32[]{:S(2)}, u32[]{:S(2)}) %collective-permute-start.6) | collective-permute-done | bytes 8224 | tf_op jit(solution)/shard_map/ppermute | solution.py:28
  26.6 3.1 %collective-permute-done.7 = f32[6,512]{1,0:T(8,128)S(1)} collective-permute-done((f32[6,512]{1,0:T(8,128)S(1)}, f32[6,512]{1,0:T(8,128)S(1)}, u32[]{:S(2)}, u32[]{:S(2)}) %collective-permute-start.7) | collective-permute-done | bytes 12320 | tf_op jit(solution)/shard_map/ppermute | solution.py:16
  29.7 2.5 %collective-permute-start.8 = (f32[6,1024]{1,0:T(8,128)S(1)}, f32[6,1024]{1,0:T(8,128)S(1)}, u32[]{:S(2)}, u32[]{:S(2)}) collective-permute-start(f32[6,1024]{1,0:T(8,128)S(1)} %maximum_select_fusion.2), channel_id=1, source_target_pairs={{0,16},{2,18},{4,20},{6,22},{8,24},{10,26},{12,28},{14,30},{16,0},... | collective-permute-start | bytes 73736 | tf_op jit(solution)/shard_map/ppermute | solution.py:16
  32.3 2.5 %collective-permute-done.8 = f32[6,1024]{1,0:T(8,128)S(1)} collective-permute-done((f32[6,1024]{1,0:T(8,128)S(1)}, f32[6,1024]{1,0:T(8,128)S(1)}, u32[]{:S(2)}, u32[]{:S(2)}) %collective-permute-start.8) | collective-permute-done | bytes 24608 | tf_op jit(solution)/shard_map/ppermute | solution.py:16
  39.3 1.2 %collective-permute-done.9 = f32[2048]{0:T(1024)S(1)} collective-permute-done((f32[2048]{0:T(1024)S(1)}, f32[2048]{0:T(1024)S(1)}, u32[]{:S(2)}, u32[]{:S(2)}) %collective-permute-start.9) | collective-permute-done | bytes 8224 | tf_op jit(solution)/shard_map/ppermute | solution.py:28
  40.5 1.5 %collective-permute-start.10 = (f32[2048]{0:T(1024)S(1)}, f32[2048]{0:T(1024)S(1)}, u32[]{:S(2)}, u32[]{:S(2)}) collective-permute-start(f32[2048]{0:T(1024)S(1)} %add.165), channel_id=1, source_target_pairs={{0,4},{2,6},{4,0},{6,2},{8,12},{10,14},{12,8},{14,10},{16,20},{18,... | collective-permute-start | bytes 24584 | tf_op jit(solution)/shard_map/ppermute | solution.py:28
  42.0 2.1 %collective-permute-done.10 = f32[2048]{0:T(1024)S(1)} collective-permute-done((f32[2048]{0:T(1024)S(1)}, f32[2048]{0:T(1024)S(1)}, u32[]{:S(2)}, u32[]{:S(2)}) %collective-permute-start.10) | collective-permute-done | bytes 8224 | tf_op jit(solution)/shard_map/ppermute | solution.py:28
  44.4 3.4 %collective-permute-done.11 = f32[2048]{0:T(1024)S(1)} collective-permute-done((f32[2048]{0:T(1024)S(1)}, f32[2048]{0:T(1024)S(1)}, u32[]{:S(2)}, u32[]{:S(2)}) %collective-permute-start.11) | collective-permute-done | bytes 8224 | tf_op jit(solution)/shard_map/ppermute | solution.py:28
  47.8 2.3 %collective-permute-start.12 = (f32[2048]{0:T(1024)S(1)}, f32[2048]{0:T(1024)S(1)}, u32[]{:S(2)}, u32[]{:S(2)}) collective-permute-start(f32[2048]{0:T(1024)S(1)} %add.167), channel_id=1, source_target_pairs={{0,16},{2,18},{4,20},{6,22},{8,24},{10,26},{12,28},{14,30},{16,0},... | collective-permute-start | bytes 24584 | tf_op jit(solution)/shard_map/ppermute | solution.py:161
  50.1 2.2 %collective-permute-done.12 = f32[2048]{0:T(1024)S(1)} collective-permute-done((f32[2048]{0:T(1024)S(1)}, f32[2048]{0:T(1024)S(1)}, u32[]{:S(2)}, u32[]{:S(2)}) %collective-permute-start.12) | collective-permute-done | bytes 8224 | tf_op jit(solution)/shard_map/ppermute | solution.py:161
  52.4 3.6 %while.23 = (s32[]{:T(128)}, f32[3,512]{1,0:T(4,128)S(1)}, f32[4,512,4]{1,2,0:T(4,128)S(1)}, f32[3,512]{1,0:T(4,128)S(1)}, f32[512]{0:T(512)S(1)}, /*index=5*/s32[]{:T(128)}, s32[]{:T(128)}) while((s32[]{:T(128)}, f32[3,512]{1,0:T(4,128)S(1)}, f32[4,512,4]{1,2,0:T(4,128)S(1)}, f32[3,512]{1,0:T(4,128)S(1)}, f32[512]{0:T(512)S(1)}, ...), condition=%wide.region_15.16_spmd.clone, body=%wide.region_11.15_spmd.clone.sunk | while | flops 4985347 | bytes 86115 | solution.py:63
  (110 shorter events, 11.2 us)
Async XLA Ops:
  0.6 36.5 %copy-start = (bf16[128,256]{1,0:T(8,128)(2,1)S(1)}, bf16[128,256]{1,0:T(8,128)(2,1)}, u32[]{:S(2)}) copy-start(bf16[128,256]{1,0:T(8,128)(2,1)} %param.27) | copy-start | bytes 196612
  0.6 0.7 %copy-start.11 = (s32[128]{0:T(128)S(1)}, s32[128]{0:T(128)}, u32[]{:S(2)}) copy-start(s32[128]{0:T(128)} %param.18) | copy-start | bytes 1540
  0.7 0.7 %copy-start.4 = (f32[3,128]{1,0:T(4,128)S(1)}, f32[3,128]{1,0:T(4,128)}, u32[]{:S(2)}) copy-start(f32[3,128]{1,0:T(4,128)} %param.17) | copy-start | bytes 4612
  1.3 0.7 %copy-start.1 = (f32[3,512]{1,0:T(4,128)S(1)}, f32[3,512]{1,0:T(4,128)}, u32[]{:S(2)}) copy-start(f32[3,512]{1,0:T(4,128)} %param.22) | copy-start | bytes 18436
  1.4 0.7 %copy-start.3 = (f32[512]{0:T(512)S(1)}, f32[512]{0:T(512)}, u32[]{:S(2)}) copy-start(f32[512]{0:T(512)} %param.23) | copy-start | bytes 6148
  1.4 3.8 %collective-permute-start = (f32[5,128]{1,0:T(8,128)S(1)}, f32[5,128]{1,0:T(8,128)S(1)}, u32[]{:S(2)}, u32[]{:S(2)}) collective-permute-start(f32[5,128]{1,0:T(8,128)S(1)} %pad_maximum_fusion.2), channel_id=1, source_target_pairs={{0,2},{2,0},{4,6},{6,4},{8,10},{10,8},{12,14},{14,12},{16,18},{18,... | collective-permute-start | bytes 7688 | tf_op jit(solution)/shard_map/ppermute | solution.py:16
  2.1 6.8 %collective-permute-start.2 = (f32[4,512]{1,0:T(4,128)S(1)}, f32[4,512]{1,0:T(4,128)S(1)}, u32[]{:S(2)}, u32[]{:S(2)}) collective-permute-start(f32[4,512]{1,0:T(4,128)S(1)} %pad_maximum_fusion.1), channel_id=1, source_target_pairs={{0,8},{2,10},{4,12},{6,14},{8,0},{10,2},{12,4},{14,6},{16,24},{18,... | collective-permute-start | bytes 24584 | tf_op jit(solution)/shard_map/ppermute | solution.py:16
  5.2 3.7 %collective-permute-start.1 = (f32[5,256]{1,0:T(8,128)S(1)}, f32[5,256]{1,0:T(8,128)S(1)}, u32[]{:S(2)}, u32[]{:S(2)}) collective-permute-start(f32[5,256]{1,0:T(8,128)S(1)} %maximum_select_fusion.6), channel_id=1, source_target_pairs={{0,4},{2,6},{4,0},{6,2},{8,12},{10,14},{12,8},{14,10},{16,20},{18,... | collective-permute-start | bytes 15368 | tf_op jit(solution)/shard_map/ppermute | solution.py:16
  9.0 4.8 %collective-permute-start.3 = (f32[4,1024]{1,0:T(4,128)S(1)}, f32[4,1024]{1,0:T(4,128)S(1)}, u32[]{:S(2)}, u32[]{:S(2)}) collective-permute-start(f32[4,1024]{1,0:T(4,128)S(1)} %maximum_select_fusion.5), channel_id=1, source_target_pairs={{0,16},{2,18},{4,20},{6,22},{8,24},{10,26},{12,28},{14,30},{16,0},... | collective-permute-start | bytes 49160 | tf_op jit(solution)/shard_map/ppermute | solution.py:16
  17.3 3.7 %collective-permute-start.4 = (f32[4,512]{1,0:T(4,128)S(1)}, f32[4,512]{1,0:T(4,128)S(1)}, u32[]{:S(2)}, u32[]{:S(2)}) collective-permute-start(f32[4,512]{1,0:T(4,128)S(1)} %get-tuple-element.66), channel_id=1, source_target_pairs={{0,1},{1,0},{2,3},{3,2},{4,5},{5,4},{6,7},{7,6},{8,9},{9,8},{10,11... | collective-permute-start | bytes 24584 | tf_op jit(solution)/shard_map/ppermute | solution.py:28
  21.0 1.2 %collective-permute-start.5 = (f32[4,512]{1,0:T(4,128)S(1)}, f32[4,512]{1,0:T(4,128)S(1)}, u32[]{:S(2)}, u32[]{:S(2)}) collective-permute-start(f32[4,512]{1,0:T(4,128)S(1)} %add.146), channel_id=1, source_target_pairs={{0,2},{2,0},{4,6},{6,4},{8,10},{10,8},{12,14},{14,12},{16,18},{18,... | collective-permute-start | bytes 24584 | tf_op jit(solution)/shard_map/ppermute | solution.py:28
  22.2 3.7 %collective-permute-start.6 = (f32[4,512]{1,0:T(4,128)S(1)}, f32[4,512]{1,0:T(4,128)S(1)}, u32[]{:S(2)}, u32[]{:S(2)}) collective-permute-start(f32[4,512]{1,0:T(4,128)S(1)} %add.147), channel_id=1, source_target_pairs={{0,4},{2,6},{4,0},{6,2},{8,12},{10,14},{12,8},{14,10},{16,20},{18,... | collective-permute-start | bytes 24584 | tf_op jit(solution)/shard_map/ppermute | solution.py:28
  25.9 0.7 %copy-start.5 = (s32[128,4]{0,1:T(4,128)S(1)}, s32[128,4]{0,1:T(4,128)}, u32[]{:S(2)}) copy-start(s32[128,4]{0,1:T(4,128)} %param.21) | copy-start | bytes 6148
  25.9 0.7 %copy-start.6 = (s32[128,4]{0,1:T(4,128)S(1)}, s32[128,4]{0,1:T(4,128)}, u32[]{:S(2)}) copy-start(s32[128,4]{0,1:T(4,128)} %param.20) | copy-start | bytes 6148
  25.9 3.8 %collective-permute-start.7 = (f32[6,512]{1,0:T(8,128)S(1)}, f32[6,512]{1,0:T(8,128)S(1)}, u32[]{:S(2)}, u32[]{:S(2)}) collective-permute-start(f32[6,512]{1,0:T(8,128)S(1)} %pad_maximum_fusion), channel_id=1, source_target_pairs={{0,8},{2,10},{4,12},{6,14},{8,0},{10,2},{12,4},{14,6},{16,24},{18,... | collective-permute-start | bytes 36872 | tf_op jit(solution)/shard_map/ppermute | solution.py:16
  29.7 5.1 %collective-permute-start.8 = (f32[6,1024]{1,0:T(8,128)S(1)}, f32[6,1024]{1,0:T(8,128)S(1)}, u32[]{:S(2)}, u32[]{:S(2)}) collective-permute-start(f32[6,1024]{1,0:T(8,128)S(1)} %maximum_select_fusion.2), channel_id=1, source_target_pairs={{0,16},{2,18},{4,20},{6,22},{8,24},{10,26},{12,28},{14,30},{16,0},... | collective-permute-start | bytes 73736 | tf_op jit(solution)/shard_map/ppermute | solution.py:16
  34.9 0.7 %copy-start.8 = (bf16[8,128]{1,0:T(8,128)(2,1)S(1)}, bf16[8,128]{1,0:T(8,128)(2,1)}, u32[]{:S(2)}) copy-start(bf16[8,128]{1,0:T(8,128)(2,1)} %param.24) | copy-start | bytes 6148
  35.6 0.8 %copy-start.7 = (bf16[128,128]{1,0:T(8,128)(2,1)S(1)}, bf16[128,128]{1,0:T(8,128)(2,1)}, u32[]{:S(2)}) copy-start(bf16[128,128]{1,0:T(8,128)(2,1)} %param.26) | copy-start | bytes 98308
  36.3 0.8 %copy-start.9 = (f32[256]{0:T(256)S(1)}, f32[256]{0:T(256)}, u32[]{:S(2)}) copy-start(f32[256]{0:T(256)} %param.29) | copy-start | bytes 3076
  36.3 0.8 %copy-start.10 = (f32[256]{0:T(256)S(1)}, f32[256]{0:T(256)}, u32[]{:S(2)}) copy-start(f32[256]{0:T(256)} %param.28) | copy-start | bytes 3076
  39.2 1.2 %collective-permute-start.9 = (f32[2048]{0:T(1024)S(1)}, f32[2048]{0:T(1024)S(1)}, u32[]{:S(2)}, u32[]{:S(2)}) collective-permute-start(f32[2048]{0:T(1024)S(1)} %fusion.41), channel_id=1, source_target_pairs={{0,2},{2,0},{4,6},{6,4},{8,10},{10,8},{12,14},{14,12},{16,18},{18,... | collective-permute-start | bytes 24584 | tf_op jit(solution)/shard_map/ppermute | solution.py:28
  40.5 3.7 %collective-permute-start.10 = (f32[2048]{0:T(1024)S(1)}, f32[2048]{0:T(1024)S(1)}, u32[]{:S(2)}, u32[]{:S(2)}) collective-permute-start(f32[2048]{0:T(1024)S(1)} %add.165), channel_id=1, source_target_pairs={{0,4},{2,6},{4,0},{6,2},{8,12},{10,14},{12,8},{14,10},{16,20},{18,... | collective-permute-start | bytes 24584 | tf_op jit(solution)/shard_map/ppermute | solution.py:28
  44.1 3.7 %collective-permute-start.11 = (f32[2048]{0:T(1024)S(1)}, f32[2048]{0:T(1024)S(1)}, u32[]{:S(2)}, u32[]{:S(2)}) collective-permute-start(f32[2048]{0:T(1024)S(1)} %add.166), channel_id=1, source_target_pairs={{0,8},{2,10},{4,12},{6,14},{8,0},{10,2},{12,4},{14,6},{16,24},{18,... | collective-permute-start | bytes 24584 | tf_op jit(solution)/shard_map/ppermute | solution.py:28
  47.8 4.5 %collective-permute-start.12 = (f32[2048]{0:T(1024)S(1)}, f32[2048]{0:T(1024)S(1)}, u32[]{:S(2)}, u32[]{:S(2)}) collective-permute-start(f32[2048]{0:T(1024)S(1)} %add.167), channel_id=1, source_target_pairs={{0,16},{2,18},{4,20},{6,22},{8,24},{10,26},{12,28},{14,30},{16,0},... | collective-permute-start | bytes 24584 | tf_op jit(solution)/shard_map/ppermute | solution.py:161
  (2 other events, 1.4 us)

commit v11 on v6

--- a/solution.py
+++ b/solution.py
@@ -97,7 +97,11 @@
         axis=0,
     )
     near = gather_doubling(own, "blk", 1, low_blocks)
-    near, table_t = lax.optimization_barrier((near, species_table.T))
+    finite = near[0:1, 0:1] == near[0:1, 0:1]
+    table_t = jnp.where(finite, species_table.T, jnp.zeros_like(species_table.T))
+    mixing = jnp.where(finite, message_weight, jnp.zeros_like(message_weight))
+    gain = jnp.where(finite[0], potential_gain, jnp.zeros_like(potential_gain))
+    near, table_t, mixing, gain = lax.optimization_barrier((near, table_t, mixing, gain))
     mm_some = gather_doubling(
         jnp.concatenate([mm_pos, mm_charge[None, :]], axis=0), "blk", low_blocks, blocks
     )
@@ -118,7 +122,7 @@
     picks_t = (jnp.arange(kinds)[:, None] == species_all[None, :]).astype(jnp.bfloat16)
     base_t = jnp.dot(table_t, picks_t, preferred_element_type=jnp.float32)
     start_t = (
-        live_all[None, :] * (base_t + potential_gain[:, None] * potential_all[None, :])
+        live_all[None, :] * (base_t + gain[:, None] * potential_all[None, :])
     ).astype(jnp.bfloat16)
     start = lax.dynamic_slice_in_dim(start_t, me * rows, rows, axis=1).T
 
@@ -132,7 +136,7 @@
     ).astype(jnp.bfloat16)
 
     mixed = start.astype(jnp.float32) + jnp.dot(
-        neighbour, message_weight, preferred_element_type=jnp.float32
+        neighbour, mixing, preferred_element_type=jnp.float32
     )
     before = jnp.dot(mixed.astype(jnp.bfloat16), hidden_weight, preferred_element_type=jnp.float32)
     sigma = jax.nn.sigmoid(before)
@@ -146,12 +150,12 @@
     back_before = (back_active * sigma * (1.0 + before * (1.0 - sigma))).astype(jnp.bfloat16)
     back_mixed = jnp.dot(back_before, hidden_weight.T, preferred_element_type=jnp.float32)
     back_sum = jnp.dot(
-        back_mixed.astype(jnp.bfloat16), message_weight.T, preferred_element_type=jnp.float32
+        back_mixed.astype(jnp.bfloat16), mixing.T, preferred_element_type=jnp.float32
     ).astype(jnp.bfloat16)
 
-    sent = jnp.sum(back_sum.astype(jnp.float32) * potential_gain[None, :], axis=1)
+    sent = jnp.sum(back_sum.astype(jnp.float32) * gain[None, :], axis=1)
     spread = jnp.sum(links.astype(jnp.float32) * sent[:, None], axis=0) * live_all
-    local = charge_part + live * jnp.sum(back_mixed * potential_gain[None, :], axis=1)
+    local = charge_part + live * jnp.sum(back_mixed * gain[None, :], axis=1)
     placed = (jnp.arange(atoms) // rows == me).astype(jnp.float32)
     local_all = jnp.tile(local, atoms // rows) * placed
     part = sum_butterfly(spread + local_all, "blk", blocks // 2)

time: 56.9 us -> 58.4 us (1.026)
  between operations: 1.64 us -> 2.99 us
  transfers between devices with their start and end apart: 13 -> 13, of which waited for: 11 -> 11; matrix products, arithmetic and copies ran while one was open for 0% -> 1% of each run, Pallas kernels for 0% -> 0%
where the time goes in v11:
time: 58.4 us; the launch traced here: 58.1 us
  waiting for transfers between devices  24.3 us (42%)
  starting transfers between devices  18 us (31%)
  other arithmetic  8.79 us (15%)
  between operations  2.99 us (5%)
  matrix products  1.88 us (3%)
  local copies, waits for them, and re-layouts  1.77 us (3%)
    ppermute x6, waiting for transfers between devices, sum_butterfly(): x = x + lax.ppermute(x, axis, [(i, i ^ step) for i in range(n)])  12.2 us
    ppermute x6, starting transfers between devices, gather_doubling(): other = lax.ppermute(x, axis, [(i, i ^ step) for i in range(n)])  10.8 us
    ppermute x6, waiting for transfers between devices, gather_doubling(): other = lax.ppermute(x, axis, [(i, i ^ step) for i in range(n)])  9.89 us
    ppermute x6, starting transfers between devices, sum_butterfly(): x = x + lax.ppermute(x, axis, [(i, i ^ step) for i in range(n)])  4.9 us
    reduce_sum x4, other arithmetic, body(): jnp.sum(weighted, axis=0)  3.2 us
    reduce_sum x4, other arithmetic, body(): jnp.sum(d[c] * weight, axis=0)  3.19 us
    ppermute x1, starting transfers between devices, on_device(): lax.ppermute(part, 'blk', [(i, i ^ blocks // 2) for i in range(blocks)])  2.29 us
    ppermute x1, waiting for transfers between devices, on_device(): lax.ppermute(part, 'blk', [(i, i ^ blocks // 2) for i in range(blocks)])  2.23 us
  transfers between devices with their start and end apart: 13, of which 11 were waited for; matrix products, arithmetic and copies ran while one was open for 1% of the time, Pallas kernels for 0%

profile of v11, /device:TPU:0, one launch (start us, length us, event | category | flops | bytes accessed | tf_op | source)
XLA Modules:
  0.0 58.1 jit_solution(4150041580231223841)
XLA Ops:
  2.1 3.1 %collective-permute-start.2 = (f32[4,512]{1,0:T(4,128)S(1)}, f32[4,512]{1,0:T(4,128)S(1)}, u32[]{:S(2)}, u32[]{:S(2)}) collective-permute-start(f32[4,512]{1,0:T(4,128)S(1)} %pad_maximum_fusion.1), channel_id=1, source_target_pairs={{0,8},{2,10},{4,12},{6,14},{8,0},{10,2},{12,4},{14,6},{16,24},{18,... | collective-permute-start | bytes 24584 | tf_op jit(solution)/shard_map/ppermute | solution.py:16
  5.2 1.6 %collective-permute-start.1 = (f32[5,256]{1,0:T(8,128)S(1)}, f32[5,256]{1,0:T(8,128)S(1)}, u32[]{:S(2)}, u32[]{:S(2)}) collective-permute-start(f32[5,256]{1,0:T(8,128)S(1)} %maximum_select_fusion.6), channel_id=1, source_target_pairs={{0,4},{2,6},{4,0},{6,2},{8,12},{10,14},{12,8},{14,10},{16,20},{18,... | collective-permute-start | bytes 15368 | tf_op jit(solution)/shard_map/ppermute | solution.py:16
  6.8 2.1 %collective-permute-done.1 = f32[5,256]{1,0:T(8,128)S(1)} collective-permute-done((f32[5,256]{1,0:T(8,128)S(1)}, f32[5,256]{1,0:T(8,128)S(1)}, u32[]{:S(2)}, u32[]{:S(2)}) %collective-permute-start.1) | collective-permute-done | bytes 5152 | tf_op jit(solution)/shard_map/ppermute | solution.py:16
  11.5 2.7 %collective-permute-start.3 = (f32[4,1024]{1,0:T(4,128)S(1)}, f32[4,1024]{1,0:T(4,128)S(1)}, u32[]{:S(2)}, u32[]{:S(2)}) collective-permute-start(f32[4,1024]{1,0:T(4,128)S(1)} %maximum_select_fusion.5), channel_id=1, source_target_pairs={{0,16},{2,18},{4,20},{6,22},{8,24},{10,26},{12,28},{14,30},{16,0},... | collective-permute-start | bytes 49160 | tf_op jit(solution)/shard_map/ppermute | solution.py:16
  14.1 2.2 %collective-permute-done.3 = f32[4,1024]{1,0:T(4,128)S(1)} collective-permute-done((f32[4,1024]{1,0:T(4,128)S(1)}, f32[4,1024]{1,0:T(4,128)S(1)}, u32[]{:S(2)}, u32[]{:S(2)}) %collective-permute-start.3) | collective-permute-done | bytes 16416 | tf_op jit(solution)/shard_map/ppermute | solution.py:16
  16.3 3.5 %while.22 = (s32[]{:T(128)}, f32[4,512]{1,0:T(4,128)S(1)}, f32[1,512]{1,0:T(1,128)S(1)}, f32[4,512,4]{1,2,0:T(4,128)S(1)}, f32[1,512]{1,0:T(1,128)S(1)}, /*index=5*/f32[1,512]{1,0:T(1,128)S(1)}, s32[]{:T(128)}, s32[]{:T(128)}) while((s32[]{:T(128)}, f32[4,512]{1,0:T(4,128)S(1)}, f32[1,512]{1,0:T(1,128)S(1)}, ...), condition=%wide.region_5.6_spmd.clone, body=%wide.region_0.5_spmd.clone.sunk | while | flops 4988931 | bytes 79979 | solution.py:48
  16.4 0.8 %multiply_reduce_fusion.6 = (f32[512]{0:T(512)S(1)}, f32[512]{0:T(512)S(1)}, f32[512]{0:T(512)S(1)}, f32[512]{0:T(512)S(1)}) fusion(f32[512]{0:T(512)S(1)} %bitcast.135, f32[512]{0:T(512)S(1)} %bitcast.136, f32[512]{0:T(512)S(1)} %bitcast.147, f32[512]{0:T(512)S(1)} %bitcast.137, f32[512]{0:T(512)S(1)} %bitcast.148, f32[512]{0:T(512)S(1)} %bitcast.134, ...), kind=kLoop, calls=%fused_computation.1.clone.1 | loop fusion | flops 4978688 | bytes 22528 | tf_op jit(solution)/shard_map/while/body/eval_jaxpr/reduce_sum | solution.py:43
  17.2 0.8 %multiply_reduce_fusion.6 = (f32[512]{0:T(512)S(1)}, f32[512]{0:T(512)S(1)}, f32[512]{0:T(512)S(1)}, f32[512]{0:T(512)S(1)}) fusion(f32[512]{0:T(512)S(1)} %bitcast.135, f32[512]{0:T(512)S(1)} %bitcast.136, f32[512]{0:T(512)S(1)} %bitcast.147, f32[512]{0:T(512)S(1)} %bitcast.137, f32[512]{0:T(512)S(1)} %bitcast.148, f32[512]{0:T(512)S(1)} %bitcast.134, ...), kind=kLoop, calls=%fused_computation.1.clone.1 | loop fusion | flops 4978688 | bytes 22528 | tf_op jit(solution)/shard_map/while/body/eval_jaxpr/reduce_sum | solution.py:43
  18.1 0.8 %multiply_reduce_fusion.6 = (f32[512]{0:T(512)S(1)}, f32[512]{0:T(512)S(1)}, f32[512]{0:T(512)S(1)}, f32[512]{0:T(512)S(1)}) fusion(f32[512]{0:T(512)S(1)} %bitcast.135, f32[512]{0:T(512)S(1)} %bitcast.136, f32[512]{0:T(512)S(1)} %bitcast.147, f32[512]{0:T(512)S(1)} %bitcast.137, f32[512]{0:T(512)S(1)} %bitcast.148, f32[512]{0:T(512)S(1)} %bitcast.134, ...), kind=kLoop, calls=%fused_computation.1.clone.1 | loop fusion | flops 4978688 | bytes 22528 | tf_op jit(solution)/shard_map/while/body/eval_jaxpr/reduce_sum | solution.py:43
  19.8 1.6 %collective-permute-start.4 = (f32[4,512]{1,0:T(4,128)S(1)}, f32[4,512]{1,0:T(4,128)S(1)}, u32[]{:S(2)}, u32[]{:S(2)}) collective-permute-start(f32[4,512]{1,0:T(4,128)S(1)} %get-tuple-element.67), channel_id=1, source_target_pairs={{0,1},{1,0},{2,3},{3,2},{4,5},{5,4},{6,7},{7,6},{8,9},{9,8},{10,11... | collective-permute-start | bytes 24584 | tf_op jit(solution)/shard_map/ppermute | solution.py:28
  21.4 2.2 %collective-permute-done.4 = f32[4,512]{1,0:T(4,128)S(1)} collective-permute-done((f32[4,512]{1,0:T(4,128)S(1)}, f32[4,512]{1,0:T(4,128)S(1)}, u32[]{:S(2)}, u32[]{:S(2)}) %collective-permute-start.4) | collective-permute-done | bytes 8224 | tf_op jit(solution)/shard_map/ppermute | solution.py:28
  23.6 1.2 %collective-permute-done.5 = f32[4,512]{1,0:T(4,128)S(1)} collective-permute-done((f32[4,512]{1,0:T(4,128)S(1)}, f32[4,512]{1,0:T(4,128)S(1)}, u32[]{:S(2)}, u32[]{:S(2)}) %collective-permute-start.5) | collective-permute-done | bytes 8224 | tf_op jit(solution)/shard_map/ppermute | solution.py:28
  24.7 1.5 %collective-permute-start.6 = (f32[4,512]{1,0:T(4,128)S(1)}, f32[4,512]{1,0:T(4,128)S(1)}, u32[]{:S(2)}, u32[]{:S(2)}) collective-permute-start(f32[4,512]{1,0:T(4,128)S(1)} %add.147), channel_id=1, source_target_pairs={{0,4},{2,6},{4,0},{6,2},{8,12},{10,14},{12,8},{14,10},{16,20},{18,... | collective-permute-start | bytes 24584 | tf_op jit(solution)/shard_map/ppermute | solution.py:28
  26.2 2.1 %collective-permute-done.6 = f32[4,512]{1,0:T(4,128)S(1)} collective-permute-done((f32[4,512]{1,0:T(4,128)S(1)}, f32[4,512]{1,0:T(4,128)S(1)}, u32[]{:S(2)}, u32[]{:S(2)}) %collective-permute-start.6) | collective-permute-done | bytes 8224 | tf_op jit(solution)/shard_map/ppermute | solution.py:28
  29.1 3.1 %collective-permute-done.7 = f32[6,512]{1,0:T(8,128)S(1)} collective-permute-done((f32[6,512]{1,0:T(8,128)S(1)}, f32[6,512]{1,0:T(8,128)S(1)}, u32[]{:S(2)}, u32[]{:S(2)}) %collective-permute-start.7) | collective-permute-done | bytes 12320 | tf_op jit(solution)/shard_map/ppermute | solution.py:16
  32.2 2.5 %collective-permute-start.8 = (f32[6,1024]{1,0:T(8,128)S(1)}, f32[6,1024]{1,0:T(8,128)S(1)}, u32[]{:S(2)}, u32[]{:S(2)}) collective-permute-start(f32[6,1024]{1,0:T(8,128)S(1)} %maximum_select_fusion.2), channel_id=1, source_target_pairs={{0,16},{2,18},{4,20},{6,22},{8,24},{10,26},{12,28},{14,30},{16,0},... | collective-permute-start | bytes 73736 | tf_op jit(solution)/shard_map/ppermute | solution.py:16
  34.8 2.5 %collective-permute-done.8 = f32[6,1024]{1,0:T(8,128)S(1)} collective-permute-done((f32[6,1024]{1,0:T(8,128)S(1)}, f32[6,1024]{1,0:T(8,128)S(1)}, u32[]{:S(2)}, u32[]{:S(2)}) %collective-permute-start.8) | collective-permute-done | bytes 24608 | tf_op jit(solution)/shard_map/ppermute | solution.py:16
  40.8 1.2 %collective-permute-done.9 = f32[2048]{0:T(1024)S(1)} collective-permute-done((f32[2048]{0:T(1024)S(1)}, f32[2048]{0:T(1024)S(1)}, u32[]{:S(2)}, u32[]{:S(2)}) %collective-permute-start.9) | collective-permute-done | bytes 8224 | tf_op jit(solution)/shard_map/ppermute | solution.py:28
  41.9 1.5 %collective-permute-start.10 = (f32[2048]{0:T(1024)S(1)}, f32[2048]{0:T(1024)S(1)}, u32[]{:S(2)}, u32[]{:S(2)}) collective-permute-start(f32[2048]{0:T(1024)S(1)} %add.165), channel_id=1, source_target_pairs={{0,4},{2,6},{4,0},{6,2},{8,12},{10,14},{12,8},{14,10},{16,20},{18,... | collective-permute-start | bytes 24584 | tf_op jit(solution)/shard_map/ppermute | solution.py:28
  43.4 2.1 %collective-permute-done.10 = f32[2048]{0:T(1024)S(1)} collective-permute-done((f32[2048]{0:T(1024)S(1)}, f32[2048]{0:T(1024)S(1)}, u32[]{:S(2)}, u32[]{:S(2)}) %collective-permute-start.10) | collective-permute-done | bytes 8224 | tf_op jit(solution)/shard_map/ppermute | solution.py:28
  45.8 3.4 %collective-permute-done.11 = f32[2048]{0:T(1024)S(1)} collective-permute-done((f32[2048]{0:T(1024)S(1)}, f32[2048]{0:T(1024)S(1)}, u32[]{:S(2)}, u32[]{:S(2)}) %collective-permute-start.11) | collective-permute-done | bytes 8224 | tf_op jit(solution)/shard_map/ppermute | solution.py:28
  49.2 2.3 %collective-permute-start.12 = (f32[2048]{0:T(1024)S(1)}, f32[2048]{0:T(1024)S(1)}, u32[]{:S(2)}, u32[]{:S(2)}) collective-permute-start(f32[2048]{0:T(1024)S(1)} %add.167), channel_id=1, source_target_pairs={{0,16},{2,18},{4,20},{6,22},{8,24},{10,26},{12,28},{14,30},{16,0},... | collective-permute-start | bytes 24584 | tf_op jit(solution)/shard_map/ppermute | solution.py:162
  51.6 2.2 %collective-permute-done.12 = f32[2048]{0:T(1024)S(1)} collective-permute-done((f32[2048]{0:T(1024)S(1)}, f32[2048]{0:T(1024)S(1)}, u32[]{:S(2)}, u32[]{:S(2)}) %collective-permute-start.12) | collective-permute-done | bytes 8224 | tf_op jit(solution)/shard_map/ppermute | solution.py:162
  53.8 3.6 %while.23 = (s32[]{:T(128)}, f32[3,512]{1,0:T(4,128)S(1)}, f32[4,512,4]{1,2,0:T(4,128)S(1)}, f32[3,512]{1,0:T(4,128)S(1)}, f32[512]{0:T(512)S(1)}, /*index=5*/s32[]{:T(128)}, s32[]{:T(128)}) while((s32[]{:T(128)}, f32[3,512]{1,0:T(4,128)S(1)}, f32[4,512,4]{1,2,0:T(4,128)S(1)}, f32[3,512]{1,0:T(4,128)S(1)}, f32[512]{0:T(512)S(1)}, ...), condition=%wide.region_15.16_spmd.clone, body=%wide.region_11.15_spmd.clone.sunk | while | flops 4985347 | bytes 86115 | solution.py:63
  (114 shorter events, 11.3 us)
Async XLA Ops:
  0.6 38.0 %copy-start = (bf16[128,256]{1,0:T(8,128)(2,1)S(1)}, bf16[128,256]{1,0:T(8,128)(2,1)}, u32[]{:S(2)}) copy-start(bf16[128,256]{1,0:T(8,128)(2,1)} %param.27) | copy-start | bytes 196612
  0.6 0.7 %copy-start.11 = (s32[128]{0:T(128)S(1)}, s32[128]{0:T(128)}, u32[]{:S(2)}) copy-start(s32[128]{0:T(128)} %param.18) | copy-start | bytes 1540
  0.7 0.7 %copy-start.5 = (f32[3,128]{1,0:T(4,128)S(1)}, f32[3,128]{1,0:T(4,128)}, u32[]{:S(2)}) copy-start(f32[3,128]{1,0:T(4,128)} %param.17) | copy-start | bytes 4612
  1.3 0.7 %copy-start.1 = (f32[3,512]{1,0:T(4,128)S(1)}, f32[3,512]{1,0:T(4,128)}, u32[]{:S(2)}) copy-start(f32[3,512]{1,0:T(4,128)} %param.22) | copy-start | bytes 18436
  1.4 0.7 %copy-start.3 = (f32[512]{0:T(512)S(1)}, f32[512]{0:T(512)}, u32[]{:S(2)}) copy-start(f32[512]{0:T(512)} %param.23) | copy-start | bytes 6148
  1.4 3.8 %collective-permute-start = (f32[5,128]{1,0:T(8,128)S(1)}, f32[5,128]{1,0:T(8,128)S(1)}, u32[]{:S(2)}, u32[]{:S(2)}) collective-permute-start(f32[5,128]{1,0:T(8,128)S(1)} %pad_maximum_fusion.2), channel_id=1, source_target_pairs={{0,2},{2,0},{4,6},{6,4},{8,10},{10,8},{12,14},{14,12},{16,18},{18,... | collective-permute-start | bytes 7688 | tf_op jit(solution)/shard_map/ppermute | solution.py:16
  2.1 9.4 %collective-permute-start.2 = (f32[4,512]{1,0:T(4,128)S(1)}, f32[4,512]{1,0:T(4,128)S(1)}, u32[]{:S(2)}, u32[]{:S(2)}) collective-permute-start(f32[4,512]{1,0:T(4,128)S(1)} %pad_maximum_fusion.1), channel_id=1, source_target_pairs={{0,8},{2,10},{4,12},{6,14},{8,0},{10,2},{12,4},{14,6},{16,24},{18,... | collective-permute-start | bytes 24584 | tf_op jit(solution)/shard_map/ppermute | solution.py:16
  5.2 3.7 %collective-permute-start.1 = (f32[5,256]{1,0:T(8,128)S(1)}, f32[5,256]{1,0:T(8,128)S(1)}, u32[]{:S(2)}, u32[]{:S(2)}) collective-permute-start(f32[5,256]{1,0:T(8,128)S(1)} %maximum_select_fusion.6), channel_id=1, source_target_pairs={{0,4},{2,6},{4,0},{6,2},{8,12},{10,14},{12,8},{14,10},{16,20},{18,... | collective-permute-start | bytes 15368 | tf_op jit(solution)/shard_map/ppermute | solution.py:16
  6.8 4.6 %copy-start.4 = (bf16[128,128]{1,0:T(8,128)(2,1)S(1)}, bf16[128,128]{1,0:T(8,128)(2,1)}, u32[]{:S(2)}) copy-start(bf16[128,128]{1,0:T(8,128)(2,1)} %param.26) | copy-start | bytes 98308
  8.9 1.8 %copy-start.12 = (f32[128]{0:T(128)S(1)}, f32[128]{0:T(128)}, u32[]{:S(2)}) copy-start(f32[128]{0:T(128)} %param.25) | copy-start | bytes 1540
  10.7 0.7 %copy-start.8 = (bf16[8,128]{1,0:T(8,128)(2,1)S(1)}, bf16[8,128]{1,0:T(8,128)(2,1)}, u32[]{:S(2)}) copy-start(bf16[8,128]{1,0:T(8,128)(2,1)} %param.24) | copy-start | bytes 6148
  11.5 4.8 %collective-permute-start.3 = (f32[4,1024]{1,0:T(4,128)S(1)}, f32[4,1024]{1,0:T(4,128)S(1)}, u32[]{:S(2)}, u32[]{:S(2)}) collective-permute-start(f32[4,1024]{1,0:T(4,128)S(1)} %maximum_select_fusion.5), channel_id=1, source_target_pairs={{0,16},{2,18},{4,20},{6,22},{8,24},{10,26},{12,28},{14,30},{16,0},... | collective-permute-start | bytes 49160 | tf_op jit(solution)/shard_map/ppermute | solution.py:16
  19.8 3.7 %collective-permute-start.4 = (f32[4,512]{1,0:T(4,128)S(1)}, f32[4,512]{1,0:T(4,128)S(1)}, u32[]{:S(2)}, u32[]{:S(2)}) collective-permute-start(f32[4,512]{1,0:T(4,128)S(1)} %get-tuple-element.67), channel_id=1, source_target_pairs={{0,1},{1,0},{2,3},{3,2},{4,5},{5,4},{6,7},{7,6},{8,9},{9,8},{10,11... | collective-permute-start | bytes 24584 | tf_op jit(solution)/shard_map/ppermute | solution.py:28
  23.6 1.2 %collective-permute-start.5 = (f32[4,512]{1,0:T(4,128)S(1)}, f32[4,512]{1,0:T(4,128)S(1)}, u32[]{:S(2)}, u32[]{:S(2)}) collective-permute-start(f32[4,512]{1,0:T(4,128)S(1)} %add.146), channel_id=1, source_target_pairs={{0,2},{2,0},{4,6},{6,4},{8,10},{10,8},{12,14},{14,12},{16,18},{18,... | collective-permute-start | bytes 24584 | tf_op jit(solution)/shard_map/ppermute | solution.py:28
  24.7 3.7 %collective-permute-start.6 = (f32[4,512]{1,0:T(4,128)S(1)}, f32[4,512]{1,0:T(4,128)S(1)}, u32[]{:S(2)}, u32[]{:S(2)}) collective-permute-start(f32[4,512]{1,0:T(4,128)S(1)} %add.147), channel_id=1, source_target_pairs={{0,4},{2,6},{4,0},{6,2},{8,12},{10,14},{12,8},{14,10},{16,20},{18,... | collective-permute-start | bytes 24584 | tf_op jit(solution)/shard_map/ppermute | solution.py:28
  28.4 0.7 %copy-start.7 = (s32[128,4]{0,1:T(4,128)S(1)}, s32[128,4]{0,1:T(4,128)}, u32[]{:S(2)}) copy-start(s32[128,4]{0,1:T(4,128)} %param.20) | copy-start | bytes 6148
  28.4 3.8 %collective-permute-start.7 = (f32[6,512]{1,0:T(8,128)S(1)}, f32[6,512]{1,0:T(8,128)S(1)}, u32[]{:S(2)}, u32[]{:S(2)}) collective-permute-start(f32[6,512]{1,0:T(8,128)S(1)} %pad_maximum_fusion), channel_id=1, source_target_pairs={{0,8},{2,10},{4,12},{6,14},{8,0},{10,2},{12,4},{14,6},{16,24},{18,... | collective-permute-start | bytes 36872 | tf_op jit(solution)/shard_map/ppermute | solution.py:16
  32.2 5.1 %collective-permute-start.8 = (f32[6,1024]{1,0:T(8,128)S(1)}, f32[6,1024]{1,0:T(8,128)S(1)}, u32[]{:S(2)}, u32[]{:S(2)}) collective-permute-start(f32[6,1024]{1,0:T(8,128)S(1)} %maximum_select_fusion.2), channel_id=1, source_target_pairs={{0,16},{2,18},{4,20},{6,22},{8,24},{10,26},{12,28},{14,30},{16,0},... | collective-permute-start | bytes 73736 | tf_op jit(solution)/shard_map/ppermute | solution.py:16
  37.8 0.8 %copy-start.9 = (f32[256]{0:T(256)S(1)}, f32[256]{0:T(256)}, u32[]{:S(2)}) copy-start(f32[256]{0:T(256)} %param.29) | copy-start | bytes 3076
  37.8 0.8 %copy-start.10 = (f32[256]{0:T(256)S(1)}, f32[256]{0:T(256)}, u32[]{:S(2)}) copy-start(f32[256]{0:T(256)} %param.28) | copy-start | bytes 3076
  40.7 1.2 %collective-permute-start.9 = (f32[2048]{0:T(1024)S(1)}, f32[2048]{0:T(1024)S(1)}, u32[]{:S(2)}, u32[]{:S(2)}) collective-permute-start(f32[2048]{0:T(1024)S(1)} %fusion.41), channel_id=1, source_target_pairs={{0,2},{2,0},{4,6},{6,4},{8,10},{10,8},{12,14},{14,12},{16,18},{18,... | collective-permute-start | bytes 24584 | tf_op jit(solution)/shard_map/ppermute | solution.py:28
  41.9 3.7 %collective-permute-start.10 = (f32[2048]{0:T(1024)S(1)}, f32[2048]{0:T(1024)S(1)}, u32[]{:S(2)}, u32[]{:S(2)}) collective-permute-start(f32[2048]{0:T(1024)S(1)} %add.165), channel_id=1, source_target_pairs={{0,4},{2,6},{4,0},{6,2},{8,12},{10,14},{12,8},{14,10},{16,20},{18,... | collective-permute-start | bytes 24584 | tf_op jit(solution)/shard_map/ppermute | solution.py:28
  45.6 3.7 %collective-permute-start.11 = (f32[2048]{0:T(1024)S(1)}, f32[2048]{0:T(1024)S(1)}, u32[]{:S(2)}, u32[]{:S(2)}) collective-permute-start(f32[2048]{0:T(1024)S(1)} %add.166), channel_id=1, source_target_pairs={{0,8},{2,10},{4,12},{6,14},{8,0},{10,2},{12,4},{14,6},{16,24},{18,... | collective-permute-start | bytes 24584 | tf_op jit(solution)/shard_map/ppermute | solution.py:28
  49.2 4.5 %collective-permute-start.12 = (f32[2048]{0:T(1024)S(1)}, f32[2048]{0:T(1024)S(1)}, u32[]{:S(2)}, u32[]{:S(2)}) collective-permute-start(f32[2048]{0:T(1024)S(1)} %add.167), channel_id=1, source_target_pairs={{0,16},{2,18},{4,20},{6,22},{8,24},{10,26},{12,28},{14,30},{16,0},... | collective-permute-start | bytes 24584 | tf_op jit(solution)/shard_map/ppermute | solution.py:162
  (2 other events, 1.4 us)

commit v12 on v6

--- a/solution.py
+++ b/solution.py
@@ -20,13 +20,16 @@
     return x
 
 
-def sum_butterfly(x, axis, last=None):
+def sum_butterfly(x, axis, last=None, first=1, downward=False):
     n = lax.axis_size(axis)
     last = n if last is None else last
-    step = 1
+    steps = []
+    step = first
     while step < last:
+        steps.append(step)
+        step *= 2
+    for step in reversed(steps) if downward else steps:
         x = x + lax.ppermute(x, axis, [(i, i ^ step) for i in range(n)])
-        step *= 2
     return x
 
 
@@ -102,7 +105,7 @@
         jnp.concatenate([mm_pos, mm_charge[None, :]], axis=0), "blk", low_blocks, blocks
     )
     partial = potential_pass(near[:3], mm_some)
-    total = sum_butterfly(sum_butterfly(partial, "rep"), "blk", low_blocks)
+    total = sum_butterfly(sum_butterfly(partial, "blk", low_blocks), "rep")
     pull = lax.dynamic_slice_in_dim(total[1:4], (me % low_blocks) * rows, rows, axis=1)
     known = gather_doubling(
         jnp.concatenate([total[0:1] * coupling, near], axis=0), "blk", low_blocks, blocks
@@ -154,8 +157,8 @@
     local = charge_part + live * jnp.sum(back_mixed * potential_gain[None, :], axis=1)
     placed = (jnp.arange(atoms) // rows == me).astype(jnp.float32)
     local_all = jnp.tile(local, atoms // rows) * placed
-    part = sum_butterfly(spread + local_all, "blk", blocks // 2)
-    other = lax.ppermute(part, "blk", [(i, i ^ (blocks // 2)) for i in range(blocks)])
+    part = sum_butterfly(spread + local_all, "blk", blocks, 2, downward=True)
+    other = lax.ppermute(part, "blk", [(i, i ^ 1) for i in range(blocks)])
     effective_all = part + other
     effective = lax.dynamic_slice_in_dim(part, me * rows, rows) + lax.dynamic_slice_in_dim(
         other, me * rows, rows

time: 56.9 us -> 56.9 us (level)
    ppermute x6, starting transfers between devices: 4.9 us -> 7.18 us  [sum_butterfly(): x = x + lax.ppermute(x, axis, [(i, i ^ step) for i in range(n)])]
    ppermute x1, starting transfers between devices: 2.29 us -> 0.01 us  [on_device(): other = lax.ppermute(part, 'blk', [(i, i ^ 1) for i in range(blocks)])]
    ppermute x1, waiting for transfers between devices: 2.23 us -> 1.1 us  [on_device(): other = lax.ppermute(part, 'blk', [(i, i ^ 1) for i in range(blocks)])]
    ppermute x6, waiting for transfers between devices: 12.2 us -> 13.3 us  [sum_butterfly(): x = x + lax.ppermute(x, axis, [(i, i ^ step) for i in range(n)])]
where the time goes in v12:
time: 56.9 us; the launch traced here: 56.6 us
  waiting for transfers between devices  24.3 us (43%)
  starting transfers between devices  18 us (32%)
  other arithmetic  8.78 us (15%)
  matrix products  1.87 us (3%)
  between operations  1.68 us (3%)
  local copies, waits for them, and re-layouts  1.66 us (3%)
    ppermute x6, waiting for transfers between devices, sum_butterfly(): x = x + lax.ppermute(x, axis, [(i, i ^ step) for i in range(n)])  13.3 us
    ppermute x6, starting transfers between devices, gather_doubling(): other = lax.ppermute(x, axis, [(i, i ^ step) for i in range(n)])  10.8 us
    ppermute x6, waiting for transfers between devices, gather_doubling(): other = lax.ppermute(x, axis, [(i, i ^ step) for i in range(n)])  9.91 us
    ppermute x6, starting transfers between devices, sum_butterfly(): x = x + lax.ppermute(x, axis, [(i, i ^ step) for i in range(n)])  7.18 us
    reduce_sum x4, other arithmetic, body(): jnp.sum(weighted, axis=0)  3.2 us
    reduce_sum x4, other arithmetic, body(): jnp.sum(d[c] * weight, axis=0)  3.19 us
    unnamed x26, local copies, waits for them, and re-layouts  1.46 us
  transfers between devices with their start and end apart: 13, of which 11 were waited for; matrix products, arithmetic and copies ran while one was open for 0% of the time, Pallas kernels for 0%

profile of v12, /device:TPU:0, one launch (start us, length us, event | category | flops | bytes accessed | tf_op | source)
XLA Modules:
  0.0 56.6 jit_solution(1587135729846970673)
XLA Ops:
  2.1 3.1 %collective-permute-start.2 = (f32[4,512]{1,0:T(4,128)S(1)}, f32[4,512]{1,0:T(4,128)S(1)}, u32[]{:S(2)}, u32[]{:S(2)}) collective-permute-start(f32[4,512]{1,0:T(4,128)S(1)} %pad_maximum_fusion.1), channel_id=1, source_target_pairs={{0,8},{2,10},{4,12},{6,14},{8,0},{10,2},{12,4},{14,6},{16,24},{18,... | collective-permute-start | bytes 24584 | tf_op jit(solution)/shard_map/ppermute | solution.py:16
  5.2 1.6 %collective-permute-start.1 = (f32[5,256]{1,0:T(8,128)S(1)}, f32[5,256]{1,0:T(8,128)S(1)}, u32[]{:S(2)}, u32[]{:S(2)}) collective-permute-start(f32[5,256]{1,0:T(8,128)S(1)} %maximum_select_fusion.6), channel_id=1, source_target_pairs={{0,4},{2,6},{4,0},{6,2},{8,12},{10,14},{12,8},{14,10},{16,20},{18,... | collective-permute-start | bytes 15368 | tf_op jit(solution)/shard_map/ppermute | solution.py:16
  6.8 2.1 %collective-permute-done.1 = f32[5,256]{1,0:T(8,128)S(1)} collective-permute-done((f32[5,256]{1,0:T(8,128)S(1)}, f32[5,256]{1,0:T(8,128)S(1)}, u32[]{:S(2)}, u32[]{:S(2)}) %collective-permute-start.1) | collective-permute-done | bytes 5152 | tf_op jit(solution)/shard_map/ppermute | solution.py:16
  9.0 2.7 %collective-permute-start.3 = (f32[4,1024]{1,0:T(4,128)S(1)}, f32[4,1024]{1,0:T(4,128)S(1)}, u32[]{:S(2)}, u32[]{:S(2)}) collective-permute-start(f32[4,1024]{1,0:T(4,128)S(1)} %maximum_select_fusion.5), channel_id=1, source_target_pairs={{0,16},{2,18},{4,20},{6,22},{8,24},{10,26},{12,28},{14,30},{16,0},... | collective-permute-start | bytes 49160 | tf_op jit(solution)/shard_map/ppermute | solution.py:16
  11.6 2.2 %collective-permute-done.3 = f32[4,1024]{1,0:T(4,128)S(1)} collective-permute-done((f32[4,1024]{1,0:T(4,128)S(1)}, f32[4,1024]{1,0:T(4,128)S(1)}, u32[]{:S(2)}, u32[]{:S(2)}) %collective-permute-start.3) | collective-permute-done | bytes 16416 | tf_op jit(solution)/shard_map/ppermute | solution.py:16
  13.8 3.5 %while.22 = (s32[]{:T(128)}, f32[4,512]{1,0:T(4,128)S(1)}, f32[1,512]{1,0:T(1,128)S(1)}, f32[4,512,4]{1,2,0:T(4,128)S(1)}, f32[1,512]{1,0:T(1,128)S(1)}, /*index=5*/f32[1,512]{1,0:T(1,128)S(1)}, s32[]{:T(128)}, s32[]{:T(128)}) while((s32[]{:T(128)}, f32[4,512]{1,0:T(4,128)S(1)}, f32[1,512]{1,0:T(1,128)S(1)}, ...), condition=%wide.region_5.6_spmd.clone, body=%wide.region_0.5_spmd.clone.sunk | while | flops 4988931 | bytes 79979 | solution.py:51
  13.8 0.8 %multiply_reduce_fusion.6 = (f32[512]{0:T(512)S(1)}, f32[512]{0:T(512)S(1)}, f32[512]{0:T(512)S(1)}, f32[512]{0:T(512)S(1)}) fusion(f32[512]{0:T(512)S(1)} %bitcast.133, f32[512]{0:T(512)S(1)} %bitcast.134, f32[512]{0:T(512)S(1)} %bitcast.145, f32[512]{0:T(512)S(1)} %bitcast.135, f32[512]{0:T(512)S(1)} %bitcast.146, f32[512]{0:T(512)S(1)} %bitcast.132, ...), kind=kLoop, calls=%fused_computation.1.clone.1 | loop fusion | flops 4978688 | bytes 22528 | tf_op jit(solution)/shard_map/while/body/eval_jaxpr/reduce_sum | solution.py:46
  14.7 0.8 %multiply_reduce_fusion.6 = (f32[512]{0:T(512)S(1)}, f32[512]{0:T(512)S(1)}, f32[512]{0:T(512)S(1)}, f32[512]{0:T(512)S(1)}) fusion(f32[512]{0:T(512)S(1)} %bitcast.133, f32[512]{0:T(512)S(1)} %bitcast.134, f32[512]{0:T(512)S(1)} %bitcast.145, f32[512]{0:T(512)S(1)} %bitcast.135, f32[512]{0:T(512)S(1)} %bitcast.146, f32[512]{0:T(512)S(1)} %bitcast.132, ...), kind=kLoop, calls=%fused_computation.1.clone.1 | loop fusion | flops 4978688 | bytes 22528 | tf_op jit(solution)/shard_map/while/body/eval_jaxpr/reduce_sum | solution.py:46
  15.6 0.8 %multiply_reduce_fusion.6 = (f32[512]{0:T(512)S(1)}, f32[512]{0:T(512)S(1)}, f32[512]{0:T(512)S(1)}, f32[512]{0:T(512)S(1)}) fusion(f32[512]{0:T(512)S(1)} %bitcast.133, f32[512]{0:T(512)S(1)} %bitcast.134, f32[512]{0:T(512)S(1)} %bitcast.145, f32[512]{0:T(512)S(1)} %bitcast.135, f32[512]{0:T(512)S(1)} %bitcast.146, f32[512]{0:T(512)S(1)} %bitcast.132, ...), kind=kLoop, calls=%fused_computation.1.clone.1 | loop fusion | flops 4978688 | bytes 22528 | tf_op jit(solution)/shard_map/while/body/eval_jaxpr/reduce_sum | solution.py:46
  17.4 1.2 %collective-permute-done.4 = f32[4,512]{1,0:T(4,128)S(1)} collective-permute-done((f32[4,512]{1,0:T(4,128)S(1)}, f32[4,512]{1,0:T(4,128)S(1)}, u32[]{:S(2)}, u32[]{:S(2)}) %collective-permute-start.4) | collective-permute-done | bytes 8224 | tf_op jit(solution)/shard_map/ppermute | solution.py:32
  18.5 1.5 %collective-permute-start.5 = (f32[4,512]{1,0:T(4,128)S(1)}, f32[4,512]{1,0:T(4,128)S(1)}, u32[]{:S(2)}, u32[]{:S(2)}) collective-permute-start(f32[4,512]{1,0:T(4,128)S(1)} %add.146), channel_id=1, source_target_pairs={{0,4},{2,6},{4,0},{6,2},{8,12},{10,14},{12,8},{14,10},{16,20},{18,... | collective-permute-start | bytes 24584 | tf_op jit(solution)/shard_map/ppermute | solution.py:32
  20.1 2.1 %collective-permute-done.5 = f32[4,512]{1,0:T(4,128)S(1)} collective-permute-done((f32[4,512]{1,0:T(4,128)S(1)}, f32[4,512]{1,0:T(4,128)S(1)}, u32[]{:S(2)}, u32[]{:S(2)}) %collective-permute-start.5) | collective-permute-done | bytes 8224 | tf_op jit(solution)/shard_map/ppermute | solution.py:32
  22.2 1.5 %collective-permute-start.6 = (f32[4,512]{1,0:T(4,128)S(1)}, f32[4,512]{1,0:T(4,128)S(1)}, u32[]{:S(2)}, u32[]{:S(2)}) collective-permute-start(f32[4,512]{1,0:T(4,128)S(1)} %add.147), channel_id=1, source_target_pairs={{0,1},{1,0},{2,3},{3,2},{4,5},{5,4},{6,7},{7,6},{8,9},{9,8},{10,11... | collective-permute-start | bytes 24584 | tf_op jit(solution)/shard_map/ppermute | solution.py:32
  23.7 2.2 %collective-permute-done.6 = f32[4,512]{1,0:T(4,128)S(1)} collective-permute-done((f32[4,512]{1,0:T(4,128)S(1)}, f32[4,512]{1,0:T(4,128)S(1)}, u32[]{:S(2)}, u32[]{:S(2)}) %collective-permute-start.6) | collective-permute-done | bytes 8224 | tf_op jit(solution)/shard_map/ppermute | solution.py:32
  26.6 3.1 %collective-permute-done.7 = f32[6,512]{1,0:T(8,128)S(1)} collective-permute-done((f32[6,512]{1,0:T(8,128)S(1)}, f32[6,512]{1,0:T(8,128)S(1)}, u32[]{:S(2)}, u32[]{:S(2)}) %collective-permute-start.7) | collective-permute-done | bytes 12320 | tf_op jit(solution)/shard_map/ppermute | solution.py:16
  29.7 2.5 %collective-permute-start.8 = (f32[6,1024]{1,0:T(8,128)S(1)}, f32[6,1024]{1,0:T(8,128)S(1)}, u32[]{:S(2)}, u32[]{:S(2)}) collective-permute-start(f32[6,1024]{1,0:T(8,128)S(1)} %maximum_select_fusion.2), channel_id=1, source_target_pairs={{0,16},{2,18},{4,20},{6,22},{8,24},{10,26},{12,28},{14,30},{16,0},... | collective-permute-start | bytes 73736 | tf_op jit(solution)/shard_map/ppermute | solution.py:16
  32.3 2.5 %collective-permute-done.8 = f32[6,1024]{1,0:T(8,128)S(1)} collective-permute-done((f32[6,1024]{1,0:T(8,128)S(1)}, f32[6,1024]{1,0:T(8,128)S(1)}, u32[]{:S(2)}, u32[]{:S(2)}) %collective-permute-start.8) | collective-permute-done | bytes 24608 | tf_op jit(solution)/shard_map/ppermute | solution.py:16
  39.2 2.4 %collective-permute-start.9 = (f32[2048]{0:T(1024)S(1)}, f32[2048]{0:T(1024)S(1)}, u32[]{:S(2)}, u32[]{:S(2)}) collective-permute-start(f32[2048]{0:T(1024)S(1)} %fusion.41), channel_id=1, source_target_pairs={{0,16},{2,18},{4,20},{6,22},{8,24},{10,26},{12,28},{14,30},{16,0},... | collective-permute-start | bytes 24584 | tf_op jit(solution)/shard_map/ppermute | solution.py:32
  41.6 2.3 %collective-permute-done.9 = f32[2048]{0:T(1024)S(1)} collective-permute-done((f32[2048]{0:T(1024)S(1)}, f32[2048]{0:T(1024)S(1)}, u32[]{:S(2)}, u32[]{:S(2)}) %collective-permute-start.9) | collective-permute-done | bytes 8224 | tf_op jit(solution)/shard_map/ppermute | solution.py:32
  44.1 3.4 %collective-permute-done.10 = f32[2048]{0:T(1024)S(1)} collective-permute-done((f32[2048]{0:T(1024)S(1)}, f32[2048]{0:T(1024)S(1)}, u32[]{:S(2)}, u32[]{:S(2)}) %collective-permute-start.10) | collective-permute-done | bytes 8224 | tf_op jit(solution)/shard_map/ppermute | solution.py:32
  47.5 1.5 %collective-permute-start.11 = (f32[2048]{0:T(1024)S(1)}, f32[2048]{0:T(1024)S(1)}, u32[]{:S(2)}, u32[]{:S(2)}) collective-permute-start(f32[2048]{0:T(1024)S(1)} %add.166), channel_id=1, source_target_pairs={{0,4},{2,6},{4,0},{6,2},{8,12},{10,14},{12,8},{14,10},{16,20},{18,... | collective-permute-start | bytes 24584 | tf_op jit(solution)/shard_map/ppermute | solution.py:32
  49.0 2.1 %collective-permute-done.11 = f32[2048]{0:T(1024)S(1)} collective-permute-done((f32[2048]{0:T(1024)S(1)}, f32[2048]{0:T(1024)S(1)}, u32[]{:S(2)}, u32[]{:S(2)}) %collective-permute-start.11) | collective-permute-done | bytes 8224 | tf_op jit(solution)/shard_map/ppermute | solution.py:32
  51.2 1.1 %collective-permute-done.12 = f32[2048]{0:T(1024)S(1)} collective-permute-done((f32[2048]{0:T(1024)S(1)}, f32[2048]{0:T(1024)S(1)}, u32[]{:S(2)}, u32[]{:S(2)}) %collective-permute-start.12) | collective-permute-done | bytes 8224 | tf_op jit(solution)/shard_map/ppermute | solution.py:161
  52.4 3.6 %while.23 = (s32[]{:T(128)}, f32[3,512]{1,0:T(4,128)S(1)}, f32[4,512,4]{1,2,0:T(4,128)S(1)}, f32[3,512]{1,0:T(4,128)S(1)}, f32[512]{0:T(512)S(1)}, /*index=5*/s32[]{:T(128)}, s32[]{:T(128)}) while((s32[]{:T(128)}, f32[3,512]{1,0:T(4,128)S(1)}, f32[4,512,4]{1,2,0:T(4,128)S(1)}, f32[3,512]{1,0:T(4,128)S(1)}, f32[512]{0:T(512)S(1)}, ...), condition=%wide.region_15.16_spmd.clone, body=%wide.region_11.15_spmd.clone.sunk | while | flops 4985347 | bytes 86115 | solution.py:66
  (110 shorter events, 11.2 us)
Async XLA Ops:
  0.6 36.5 %copy-start = (bf16[128,256]{1,0:T(8,128)(2,1)S(1)}, bf16[128,256]{1,0:T(8,128)(2,1)}, u32[]{:S(2)}) copy-start(bf16[128,256]{1,0:T(8,128)(2,1)} %param.27) | copy-start | bytes 196612
  0.6 0.7 %copy-start.11 = (s32[128]{0:T(128)S(1)}, s32[128]{0:T(128)}, u32[]{:S(2)}) copy-start(s32[128]{0:T(128)} %param.18) | copy-start | bytes 1540
  0.7 0.7 %copy-start.4 = (f32[3,128]{1,0:T(4,128)S(1)}, f32[3,128]{1,0:T(4,128)}, u32[]{:S(2)}) copy-start(f32[3,128]{1,0:T(4,128)} %param.17) | copy-start | bytes 4612
  1.3 0.7 %copy-start.1 = (f32[3,512]{1,0:T(4,128)S(1)}, f32[3,512]{1,0:T(4,128)}, u32[]{:S(2)}) copy-start(f32[3,512]{1,0:T(4,128)} %param.22) | copy-start | bytes 18436
  1.4 0.7 %copy-start.3 = (f32[512]{0:T(512)S(1)}, f32[512]{0:T(512)}, u32[]{:S(2)}) copy-start(f32[512]{0:T(512)} %param.23) | copy-start | bytes 6148
  1.4 3.8 %collective-permute-start = (f32[5,128]{1,0:T(8,128)S(1)}, f32[5,128]{1,0:T(8,128)S(1)}, u32[]{:S(2)}, u32[]{:S(2)}) collective-permute-start(f32[5,128]{1,0:T(8,128)S(1)} %pad_maximum_fusion.2), channel_id=1, source_target_pairs={{0,2},{2,0},{4,6},{6,4},{8,10},{10,8},{12,14},{14,12},{16,18},{18,... | collective-permute-start | bytes 7688 | tf_op jit(solution)/shard_map/ppermute | solution.py:16
  2.1 6.8 %collective-permute-start.2 = (f32[4,512]{1,0:T(4,128)S(1)}, f32[4,512]{1,0:T(4,128)S(1)}, u32[]{:S(2)}, u32[]{:S(2)}) collective-permute-start(f32[4,512]{1,0:T(4,128)S(1)} %pad_maximum_fusion.1), channel_id=1, source_target_pairs={{0,8},{2,10},{4,12},{6,14},{8,0},{10,2},{12,4},{14,6},{16,24},{18,... | collective-permute-start | bytes 24584 | tf_op jit(solution)/shard_map/ppermute | solution.py:16
  5.2 3.7 %collective-permute-start.1 = (f32[5,256]{1,0:T(8,128)S(1)}, f32[5,256]{1,0:T(8,128)S(1)}, u32[]{:S(2)}, u32[]{:S(2)}) collective-permute-start(f32[5,256]{1,0:T(8,128)S(1)} %maximum_select_fusion.6), channel_id=1, source_target_pairs={{0,4},{2,6},{4,0},{6,2},{8,12},{10,14},{12,8},{14,10},{16,20},{18,... | collective-permute-start | bytes 15368 | tf_op jit(solution)/shard_map/ppermute | solution.py:16
  9.0 4.8 %collective-permute-start.3 = (f32[4,1024]{1,0:T(4,128)S(1)}, f32[4,1024]{1,0:T(4,128)S(1)}, u32[]{:S(2)}, u32[]{:S(2)}) collective-permute-start(f32[4,1024]{1,0:T(4,128)S(1)} %maximum_select_fusion.5), channel_id=1, source_target_pairs={{0,16},{2,18},{4,20},{6,22},{8,24},{10,26},{12,28},{14,30},{16,0},... | collective-permute-start | bytes 49160 | tf_op jit(solution)/shard_map/ppermute | solution.py:16
  17.3 1.2 %collective-permute-start.4 = (f32[4,512]{1,0:T(4,128)S(1)}, f32[4,512]{1,0:T(4,128)S(1)}, u32[]{:S(2)}, u32[]{:S(2)}) collective-permute-start(f32[4,512]{1,0:T(4,128)S(1)} %get-tuple-element.65), channel_id=1, source_target_pairs={{0,2},{2,0},{4,6},{6,4},{8,10},{10,8},{12,14},{14,12},{16,18},{18,... | collective-permute-start | bytes 24584 | tf_op jit(solution)/shard_map/ppermute | solution.py:32
  18.5 3.7 %collective-permute-start.5 = (f32[4,512]{1,0:T(4,128)S(1)}, f32[4,512]{1,0:T(4,128)S(1)}, u32[]{:S(2)}, u32[]{:S(2)}) collective-permute-start(f32[4,512]{1,0:T(4,128)S(1)} %add.146), channel_id=1, source_target_pairs={{0,4},{2,6},{4,0},{6,2},{8,12},{10,14},{12,8},{14,10},{16,20},{18,... | collective-permute-start | bytes 24584 | tf_op jit(solution)/shard_map/ppermute | solution.py:32
  22.2 3.7 %collective-permute-start.6 = (f32[4,512]{1,0:T(4,128)S(1)}, f32[4,512]{1,0:T(4,128)S(1)}, u32[]{:S(2)}, u32[]{:S(2)}) collective-permute-start(f32[4,512]{1,0:T(4,128)S(1)} %add.147), channel_id=1, source_target_pairs={{0,1},{1,0},{2,3},{3,2},{4,5},{5,4},{6,7},{7,6},{8,9},{9,8},{10,11... | collective-permute-start | bytes 24584 | tf_op jit(solution)/shard_map/ppermute | solution.py:32
  25.9 0.7 %copy-start.5 = (s32[128,4]{0,1:T(4,128)S(1)}, s32[128,4]{0,1:T(4,128)}, u32[]{:S(2)}) copy-start(s32[128,4]{0,1:T(4,128)} %param.21) | copy-start | bytes 6148
  25.9 0.7 %copy-start.6 = (s32[128,4]{0,1:T(4,128)S(1)}, s32[128,4]{0,1:T(4,128)}, u32[]{:S(2)}) copy-start(s32[128,4]{0,1:T(4,128)} %param.20) | copy-start | bytes 6148
  25.9 3.8 %collective-permute-start.7 = (f32[6,512]{1,0:T(8,128)S(1)}, f32[6,512]{1,0:T(8,128)S(1)}, u32[]{:S(2)}, u32[]{:S(2)}) collective-permute-start(f32[6,512]{1,0:T(8,128)S(1)} %pad_maximum_fusion), channel_id=1, source_target_pairs={{0,8},{2,10},{4,12},{6,14},{8,0},{10,2},{12,4},{14,6},{16,24},{18,... | collective-permute-start | bytes 36872 | tf_op jit(solution)/shard_map/ppermute | solution.py:16
  29.7 5.1 %collective-permute-start.8 = (f32[6,1024]{1,0:T(8,128)S(1)}, f32[6,1024]{1,0:T(8,128)S(1)}, u32[]{:S(2)}, u32[]{:S(2)}) collective-permute-start(f32[6,1024]{1,0:T(8,128)S(1)} %maximum_select_fusion.2), channel_id=1, source_target_pairs={{0,16},{2,18},{4,20},{6,22},{8,24},{10,26},{12,28},{14,30},{16,0},... | collective-permute-start | bytes 73736 | tf_op jit(solution)/shard_map/ppermute | solution.py:16
  34.9 0.7 %copy-start.8 = (bf16[8,128]{1,0:T(8,128)(2,1)S(1)}, bf16[8,128]{1,0:T(8,128)(2,1)}, u32[]{:S(2)}) copy-start(bf16[8,128]{1,0:T(8,128)(2,1)} %param.24) | copy-start | bytes 6148
  35.6 0.8 %copy-start.7 = (bf16[128,128]{1,0:T(8,128)(2,1)S(1)}, bf16[128,128]{1,0:T(8,128)(2,1)}, u32[]{:S(2)}) copy-start(bf16[128,128]{1,0:T(8,128)(2,1)} %param.26) | copy-start | bytes 98308
  36.3 0.8 %copy-start.9 = (f32[256]{0:T(256)S(1)}, f32[256]{0:T(256)}, u32[]{:S(2)}) copy-start(f32[256]{0:T(256)} %param.29) | copy-start | bytes 3076
  36.3 0.8 %copy-start.10 = (f32[256]{0:T(256)S(1)}, f32[256]{0:T(256)}, u32[]{:S(2)}) copy-start(f32[256]{0:T(256)} %param.28) | copy-start | bytes 3076
  39.2 4.6 %collective-permute-start.9 = (f32[2048]{0:T(1024)S(1)}, f32[2048]{0:T(1024)S(1)}, u32[]{:S(2)}, u32[]{:S(2)}) collective-permute-start(f32[2048]{0:T(1024)S(1)} %fusion.41), channel_id=1, source_target_pairs={{0,16},{2,18},{4,20},{6,22},{8,24},{10,26},{12,28},{14,30},{16,0},... | collective-permute-start | bytes 24584 | tf_op jit(solution)/shard_map/ppermute | solution.py:32
  43.8 3.7 %collective-permute-start.10 = (f32[2048]{0:T(1024)S(1)}, f32[2048]{0:T(1024)S(1)}, u32[]{:S(2)}, u32[]{:S(2)}) collective-permute-start(f32[2048]{0:T(1024)S(1)} %add.165), channel_id=1, source_target_pairs={{0,8},{2,10},{4,12},{6,14},{8,0},{10,2},{12,4},{14,6},{16,24},{18,... | collective-permute-start | bytes 24584 | tf_op jit(solution)/shard_map/ppermute | solution.py:32
  47.5 3.7 %collective-permute-start.11 = (f32[2048]{0:T(1024)S(1)}, f32[2048]{0:T(1024)S(1)}, u32[]{:S(2)}, u32[]{:S(2)}) collective-permute-start(f32[2048]{0:T(1024)S(1)} %add.166), channel_id=1, source_target_pairs={{0,4},{2,6},{4,0},{6,2},{8,12},{10,14},{12,8},{14,10},{16,20},{18,... | collective-permute-start | bytes 24584 | tf_op jit(solution)/shard_map/ppermute | solution.py:32
  51.2 1.2 %collective-permute-start.12 = (f32[2048]{0:T(1024)S(1)}, f32[2048]{0:T(1024)S(1)}, u32[]{:S(2)}, u32[]{:S(2)}) collective-permute-start(f32[2048]{0:T(1024)S(1)} %add.167), channel_id=1, source_target_pairs={{0,2},{2,0},{4,6},{6,4},{8,10},{10,8},{12,14},{14,12},{16,18},{18,... | collective-permute-start | bytes 24584 | tf_op jit(solution)/shard_map/ppermute | solution.py:161
  (2 other events, 1.4 us)

commit v13 on v6

--- a/solution.py
+++ b/solution.py
@@ -107,6 +107,12 @@
     known = gather_doubling(
         jnp.concatenate([total[0:1] * coupling, near], axis=0), "blk", low_blocks, blocks
     )
+    ghost = ghost_owner * rows + ghost_slot
+    columns = jnp.arange(blocks * rows)[None, :]
+    links = jnp.zeros((rows, blocks * rows), jnp.bfloat16)
+    for k in range(ghost.shape[1]):
+        links = links + (ghost[:, k : k + 1] == columns).astype(jnp.bfloat16)
+    known, links = lax.optimization_barrier((known, links))
     potential_all = known[0]
     qm_all = known[1:4]
     atoms = qm_all.shape[1]
@@ -122,11 +128,6 @@
     ).astype(jnp.bfloat16)
     start = lax.dynamic_slice_in_dim(start_t, me * rows, rows, axis=1).T
 
-    ghost = ghost_owner * rows + ghost_slot
-    columns = jnp.arange(atoms)[None, :]
-    links = jnp.zeros((rows, atoms), jnp.bfloat16)
-    for k in range(ghost.shape[1]):
-        links = links + (ghost[:, k : k + 1] == columns).astype(jnp.bfloat16)
     neighbour = lax.dot_general(
         links, start_t, (((1,), (1,)), ((), ())), preferred_element_type=jnp.float32
     ).astype(jnp.bfloat16)

time: 56.9 us -> 56.3 us (0.989)
    add x0 -> x1, other arithmetic: none -> 0.63 us  [on_device(): links = links + (ghost[:, k:k + 1] == columns).astype(jnp.bfloat16)]
  transfers between devices with their start and end apart: 13 -> 13, of which waited for: 11 -> 11; matrix products, arithmetic and copies ran while one was open for 0% -> 1% of each run, Pallas kernels for 0% -> 0%
where the time goes in v13:
time: 56.3 us; the launch traced here: 56 us
  waiting for transfers between devices  23.8 us (42%)
  starting transfers between devices  18.1 us (32%)
  other arithmetic  8.91 us (16%)
  local copies, waits for them, and re-layouts  1.72 us (3%)
  between operations  1.63 us (3%)
  matrix products  1.49 us (3%)
    ppermute x6, waiting for transfers between devices, sum_butterfly(): x = x + lax.ppermute(x, axis, [(i, i ^ step) for i in range(n)])  12.1 us
    ppermute x6, starting transfers between devices, gather_doubling(): other = lax.ppermute(x, axis, [(i, i ^ step) for i in range(n)])  10.8 us
    ppermute x6, waiting for transfers between devices, gather_doubling(): other = lax.ppermute(x, axis, [(i, i ^ step) for i in range(n)])  9.46 us
    ppermute x6, starting transfers between devices, sum_butterfly(): x = x + lax.ppermute(x, axis, [(i, i ^ step) for i in range(n)])  4.97 us
    reduce_sum x4, other arithmetic, body(): jnp.sum(weighted, axis=0)  3.21 us
    reduce_sum x4, other arithmetic, body(): jnp.sum(d[c] * weight, axis=0)  3.19 us
    ppermute x1, starting transfers between devices, on_device(): lax.ppermute(part, 'blk', [(i, i ^ blocks // 2) for i in range(blocks)])  2.29 us
    ppermute x1, waiting for transfers between devices, on_device(): lax.ppermute(part, 'blk', [(i, i ^ blocks // 2) for i in range(blocks)])  2.23 us
  transfers between devices with their start and end apart: 13, of which 11 were waited for; matrix products, arithmetic and copies ran while one was open for 1% of the time, Pallas kernels for 0%

profile of v13, /device:TPU:0, one launch (start us, length us, event | category | flops | bytes accessed | tf_op | source)
XLA Modules:
  0.0 56.0 jit_solution(6829752886749147689)
XLA Ops:
  2.1 3.1 %collective-permute-start.2 = (f32[4,512]{1,0:T(4,128)S(1)}, f32[4,512]{1,0:T(4,128)S(1)}, u32[]{:S(2)}, u32[]{:S(2)}) collective-permute-start(f32[4,512]{1,0:T(4,128)S(1)} %pad_maximum_fusion.1), channel_id=1, source_target_pairs={{0,8},{2,10},{4,12},{6,14},{8,0},{10,2},{12,4},{14,6},{16,24},{18,... | collective-permute-start | bytes 24584 | tf_op jit(solution)/shard_map/ppermute | solution.py:16
  5.2 1.6 %collective-permute-start.1 = (f32[5,256]{1,0:T(8,128)S(1)}, f32[5,256]{1,0:T(8,128)S(1)}, u32[]{:S(2)}, u32[]{:S(2)}) collective-permute-start(f32[5,256]{1,0:T(8,128)S(1)} %maximum_select_fusion.6), channel_id=1, source_target_pairs={{0,4},{2,6},{4,0},{6,2},{8,12},{10,14},{12,8},{14,10},{16,20},{18,... | collective-permute-start | bytes 15368 | tf_op jit(solution)/shard_map/ppermute | solution.py:16
  6.8 2.1 %collective-permute-done.1 = f32[5,256]{1,0:T(8,128)S(1)} collective-permute-done((f32[5,256]{1,0:T(8,128)S(1)}, f32[5,256]{1,0:T(8,128)S(1)}, u32[]{:S(2)}, u32[]{:S(2)}) %collective-permute-start.1) | collective-permute-done | bytes 5152 | tf_op jit(solution)/shard_map/ppermute | solution.py:16
  9.0 2.7 %collective-permute-start.3 = (f32[4,1024]{1,0:T(4,128)S(1)}, f32[4,1024]{1,0:T(4,128)S(1)}, u32[]{:S(2)}, u32[]{:S(2)}) collective-permute-start(f32[4,1024]{1,0:T(4,128)S(1)} %maximum_select_fusion.5), channel_id=1, source_target_pairs={{0,16},{2,18},{4,20},{6,22},{8,24},{10,26},{12,28},{14,30},{16,0},... | collective-permute-start | bytes 49160 | tf_op jit(solution)/shard_map/ppermute | solution.py:16
  11.6 2.2 %collective-permute-done.3 = f32[4,1024]{1,0:T(4,128)S(1)} collective-permute-done((f32[4,1024]{1,0:T(4,128)S(1)}, f32[4,1024]{1,0:T(4,128)S(1)}, u32[]{:S(2)}, u32[]{:S(2)}) %collective-permute-start.3) | collective-permute-done | bytes 16416 | tf_op jit(solution)/shard_map/ppermute | solution.py:16
  13.8 3.5 %while.22 = (s32[]{:T(128)}, f32[4,512]{1,0:T(4,128)S(1)}, f32[1,512]{1,0:T(1,128)S(1)}, f32[4,512,4]{1,2,0:T(4,128)S(1)}, f32[1,512]{1,0:T(1,128)S(1)}, /*index=5*/f32[1,512]{1,0:T(1,128)S(1)}, s32[]{:T(128)}, s32[]{:T(128)}) while((s32[]{:T(128)}, f32[4,512]{1,0:T(4,128)S(1)}, f32[1,512]{1,0:T(1,128)S(1)}, ...), condition=%wide.region_5.6_spmd.clone, body=%wide.region_0.5_spmd.clone.sunk | while | flops 4988931 | bytes 79979 | solution.py:48
  13.8 0.8 %multiply_reduce_fusion.6 = (f32[512]{0:T(512)S(1)}, f32[512]{0:T(512)S(1)}, f32[512]{0:T(512)S(1)}, f32[512]{0:T(512)S(1)}) fusion(f32[512]{0:T(512)S(1)} %bitcast.134, f32[512]{0:T(512)S(1)} %bitcast.135, f32[512]{0:T(512)S(1)} %bitcast.146, f32[512]{0:T(512)S(1)} %bitcast.136, f32[512]{0:T(512)S(1)} %bitcast.147, f32[512]{0:T(512)S(1)} %bitcast.133, ...), kind=kLoop, calls=%fused_computation.1.clone.1 | loop fusion | flops 4978688 | bytes 22528 | tf_op jit(solution)/shard_map/while/body/eval_jaxpr/reduce_sum | solution.py:43
  14.7 0.8 %multiply_reduce_fusion.6 = (f32[512]{0:T(512)S(1)}, f32[512]{0:T(512)S(1)}, f32[512]{0:T(512)S(1)}, f32[512]{0:T(512)S(1)}) fusion(f32[512]{0:T(512)S(1)} %bitcast.134, f32[512]{0:T(512)S(1)} %bitcast.135, f32[512]{0:T(512)S(1)} %bitcast.146, f32[512]{0:T(512)S(1)} %bitcast.136, f32[512]{0:T(512)S(1)} %bitcast.147, f32[512]{0:T(512)S(1)} %bitcast.133, ...), kind=kLoop, calls=%fused_computation.1.clone.1 | loop fusion | flops 4978688 | bytes 22528 | tf_op jit(solution)/shard_map/while/body/eval_jaxpr/reduce_sum | solution.py:43
  15.6 0.8 %multiply_reduce_fusion.6 = (f32[512]{0:T(512)S(1)}, f32[512]{0:T(512)S(1)}, f32[512]{0:T(512)S(1)}, f32[512]{0:T(512)S(1)}) fusion(f32[512]{0:T(512)S(1)} %bitcast.134, f32[512]{0:T(512)S(1)} %bitcast.135, f32[512]{0:T(512)S(1)} %bitcast.146, f32[512]{0:T(512)S(1)} %bitcast.136, f32[512]{0:T(512)S(1)} %bitcast.147, f32[512]{0:T(512)S(1)} %bitcast.133, ...), kind=kLoop, calls=%fused_computation.1.clone.1 | loop fusion | flops 4978688 | bytes 22528 | tf_op jit(solution)/shard_map/while/body/eval_jaxpr/reduce_sum | solution.py:43
  17.3 1.6 %collective-permute-start.4 = (f32[4,512]{1,0:T(4,128)S(1)}, f32[4,512]{1,0:T(4,128)S(1)}, u32[]{:S(2)}, u32[]{:S(2)}) collective-permute-start(f32[4,512]{1,0:T(4,128)S(1)} %get-tuple-element.67), channel_id=1, source_target_pairs={{0,1},{1,0},{2,3},{3,2},{4,5},{5,4},{6,7},{7,6},{8,9},{9,8},{10,11... | collective-permute-start | bytes 24584 | tf_op jit(solution)/shard_map/ppermute | solution.py:28
  18.9 2.2 %collective-permute-done.4 = f32[4,512]{1,0:T(4,128)S(1)} collective-permute-done((f32[4,512]{1,0:T(4,128)S(1)}, f32[4,512]{1,0:T(4,128)S(1)}, u32[]{:S(2)}, u32[]{:S(2)}) %collective-permute-start.4) | collective-permute-done | bytes 8224 | tf_op jit(solution)/shard_map/ppermute | solution.py:28
  21.1 1.2 %collective-permute-done.5 = f32[4,512]{1,0:T(4,128)S(1)} collective-permute-done((f32[4,512]{1,0:T(4,128)S(1)}, f32[4,512]{1,0:T(4,128)S(1)}, u32[]{:S(2)}, u32[]{:S(2)}) %collective-permute-start.5) | collective-permute-done | bytes 8224 | tf_op jit(solution)/shard_map/ppermute | solution.py:28
  22.3 1.5 %collective-permute-start.6 = (f32[4,512]{1,0:T(4,128)S(1)}, f32[4,512]{1,0:T(4,128)S(1)}, u32[]{:S(2)}, u32[]{:S(2)}) collective-permute-start(f32[4,512]{1,0:T(4,128)S(1)} %add.147), channel_id=1, source_target_pairs={{0,4},{2,6},{4,0},{6,2},{8,12},{10,14},{12,8},{14,10},{16,20},{18,... | collective-permute-start | bytes 24584 | tf_op jit(solution)/shard_map/ppermute | solution.py:28
  23.8 2.1 %collective-permute-done.6 = f32[4,512]{1,0:T(4,128)S(1)} collective-permute-done((f32[4,512]{1,0:T(4,128)S(1)}, f32[4,512]{1,0:T(4,128)S(1)}, u32[]{:S(2)}, u32[]{:S(2)}) %collective-permute-start.6) | collective-permute-done | bytes 8224 | tf_op jit(solution)/shard_map/ppermute | solution.py:28
  26.4 3.3 %collective-permute-done.7 = f32[6,512]{1,0:T(8,128)S(1)} collective-permute-done((f32[6,512]{1,0:T(8,128)S(1)}, f32[6,512]{1,0:T(8,128)S(1)}, u32[]{:S(2)}, u32[]{:S(2)}) %collective-permute-start.7) | collective-permute-done | bytes 12320 | tf_op jit(solution)/shard_map/ppermute | solution.py:16
  29.8 2.5 %collective-permute-start.8 = (f32[6,1024]{1,0:T(8,128)S(1)}, f32[6,1024]{1,0:T(8,128)S(1)}, u32[]{:S(2)}, u32[]{:S(2)}) collective-permute-start(f32[6,1024]{1,0:T(8,128)S(1)} %maximum_select_fusion.2), channel_id=1, source_target_pairs={{0,16},{2,18},{4,20},{6,22},{8,24},{10,26},{12,28},{14,30},{16,0},... | collective-permute-start | bytes 73736 | tf_op jit(solution)/shard_map/ppermute | solution.py:16
  33.0 1.9 %collective-permute-done.8 = f32[6,1024]{1,0:T(8,128)S(1)} collective-permute-done((f32[6,1024]{1,0:T(8,128)S(1)}, f32[6,1024]{1,0:T(8,128)S(1)}, u32[]{:S(2)}, u32[]{:S(2)}) %collective-permute-start.8) | collective-permute-done | bytes 24608 | tf_op jit(solution)/shard_map/ppermute | solution.py:16
  38.7 1.2 %collective-permute-done.9 = f32[2048]{0:T(1024)S(1)} collective-permute-done((f32[2048]{0:T(1024)S(1)}, f32[2048]{0:T(1024)S(1)}, u32[]{:S(2)}, u32[]{:S(2)}) %collective-permute-start.9) | collective-permute-done | bytes 8224 | tf_op jit(solution)/shard_map/ppermute | solution.py:28
  39.9 1.5 %collective-permute-start.10 = (f32[2048]{0:T(1024)S(1)}, f32[2048]{0:T(1024)S(1)}, u32[]{:S(2)}, u32[]{:S(2)}) collective-permute-start(f32[2048]{0:T(1024)S(1)} %add.165), channel_id=1, source_target_pairs={{0,4},{2,6},{4,0},{6,2},{8,12},{10,14},{12,8},{14,10},{16,20},{18,... | collective-permute-start | bytes 24584 | tf_op jit(solution)/shard_map/ppermute | solution.py:28
  41.4 2.1 %collective-permute-done.10 = f32[2048]{0:T(1024)S(1)} collective-permute-done((f32[2048]{0:T(1024)S(1)}, f32[2048]{0:T(1024)S(1)}, u32[]{:S(2)}, u32[]{:S(2)}) %collective-permute-start.10) | collective-permute-done | bytes 8224 | tf_op jit(solution)/shard_map/ppermute | solution.py:28
  43.8 3.4 %collective-permute-done.11 = f32[2048]{0:T(1024)S(1)} collective-permute-done((f32[2048]{0:T(1024)S(1)}, f32[2048]{0:T(1024)S(1)}, u32[]{:S(2)}, u32[]{:S(2)}) %collective-permute-start.11) | collective-permute-done | bytes 8224 | tf_op jit(solution)/shard_map/ppermute | solution.py:28
  47.2 2.3 %collective-permute-start.12 = (f32[2048]{0:T(1024)S(1)}, f32[2048]{0:T(1024)S(1)}, u32[]{:S(2)}, u32[]{:S(2)}) collective-permute-start(f32[2048]{0:T(1024)S(1)} %add.167), channel_id=1, source_target_pairs={{0,16},{2,18},{4,20},{6,22},{8,24},{10,26},{12,28},{14,30},{16,0},... | collective-permute-start | bytes 24584 | tf_op jit(solution)/shard_map/ppermute | solution.py:159
  49.5 2.2 %collective-permute-done.12 = f32[2048]{0:T(1024)S(1)} collective-permute-done((f32[2048]{0:T(1024)S(1)}, f32[2048]{0:T(1024)S(1)}, u32[]{:S(2)}, u32[]{:S(2)}) %collective-permute-start.12) | collective-permute-done | bytes 8224 | tf_op jit(solution)/shard_map/ppermute | solution.py:159
  51.8 3.6 %while.23 = (s32[]{:T(128)}, f32[3,512]{1,0:T(4,128)S(1)}, f32[4,512,4]{1,2,0:T(4,128)S(1)}, f32[3,512]{1,0:T(4,128)S(1)}, f32[512]{0:T(512)S(1)}, /*index=5*/s32[]{:T(128)}, s32[]{:T(128)}) while((s32[]{:T(128)}, f32[3,512]{1,0:T(4,128)S(1)}, f32[4,512,4]{1,2,0:T(4,128)S(1)}, f32[3,512]{1,0:T(4,128)S(1)}, f32[512]{0:T(512)S(1)}, ...), condition=%wide.region_15.16_spmd.clone, body=%wide.region_11.15_spmd.clone.sunk | while | flops 4985347 | bytes 86115 | solution.py:63
  (111 shorter events, 11.1 us)
Async XLA Ops:
  0.6 36.2 %copy-start = (bf16[128,256]{1,0:T(8,128)(2,1)S(1)}, bf16[128,256]{1,0:T(8,128)(2,1)}, u32[]{:S(2)}) copy-start(bf16[128,256]{1,0:T(8,128)(2,1)} %param.27) | copy-start | bytes 196612
  0.6 0.7 %copy-start.11 = (s32[128]{0:T(128)S(1)}, s32[128]{0:T(128)}, u32[]{:S(2)}) copy-start(s32[128]{0:T(128)} %param.18) | copy-start | bytes 1540
  0.7 0.7 %copy-start.5 = (f32[3,128]{1,0:T(4,128)S(1)}, f32[3,128]{1,0:T(4,128)}, u32[]{:S(2)}) copy-start(f32[3,128]{1,0:T(4,128)} %param.17) | copy-start | bytes 4612
  1.3 0.7 %copy-start.1 = (f32[3,512]{1,0:T(4,128)S(1)}, f32[3,512]{1,0:T(4,128)}, u32[]{:S(2)}) copy-start(f32[3,512]{1,0:T(4,128)} %param.22) | copy-start | bytes 18436
  1.4 0.7 %copy-start.4 = (f32[512]{0:T(512)S(1)}, f32[512]{0:T(512)}, u32[]{:S(2)}) copy-start(f32[512]{0:T(512)} %param.23) | copy-start | bytes 6148
  1.4 3.8 %collective-permute-start = (f32[5,128]{1,0:T(8,128)S(1)}, f32[5,128]{1,0:T(8,128)S(1)}, u32[]{:S(2)}, u32[]{:S(2)}) collective-permute-start(f32[5,128]{1,0:T(8,128)S(1)} %pad_maximum_fusion.2), channel_id=1, source_target_pairs={{0,2},{2,0},{4,6},{6,4},{8,10},{10,8},{12,14},{14,12},{16,18},{18,... | collective-permute-start | bytes 7688 | tf_op jit(solution)/shard_map/ppermute | solution.py:16
  2.1 6.8 %collective-permute-start.2 = (f32[4,512]{1,0:T(4,128)S(1)}, f32[4,512]{1,0:T(4,128)S(1)}, u32[]{:S(2)}, u32[]{:S(2)}) collective-permute-start(f32[4,512]{1,0:T(4,128)S(1)} %pad_maximum_fusion.1), channel_id=1, source_target_pairs={{0,8},{2,10},{4,12},{6,14},{8,0},{10,2},{12,4},{14,6},{16,24},{18,... | collective-permute-start | bytes 24584 | tf_op jit(solution)/shard_map/ppermute | solution.py:16
  5.2 3.7 %collective-permute-start.1 = (f32[5,256]{1,0:T(8,128)S(1)}, f32[5,256]{1,0:T(8,128)S(1)}, u32[]{:S(2)}, u32[]{:S(2)}) collective-permute-start(f32[5,256]{1,0:T(8,128)S(1)} %maximum_select_fusion.6), channel_id=1, source_target_pairs={{0,4},{2,6},{4,0},{6,2},{8,12},{10,14},{12,8},{14,10},{16,20},{18,... | collective-permute-start | bytes 15368 | tf_op jit(solution)/shard_map/ppermute | solution.py:16
  9.0 4.8 %collective-permute-start.3 = (f32[4,1024]{1,0:T(4,128)S(1)}, f32[4,1024]{1,0:T(4,128)S(1)}, u32[]{:S(2)}, u32[]{:S(2)}) collective-permute-start(f32[4,1024]{1,0:T(4,128)S(1)} %maximum_select_fusion.5), channel_id=1, source_target_pairs={{0,16},{2,18},{4,20},{6,22},{8,24},{10,26},{12,28},{14,30},{16,0},... | collective-permute-start | bytes 49160 | tf_op jit(solution)/shard_map/ppermute | solution.py:16
  17.3 3.7 %collective-permute-start.4 = (f32[4,512]{1,0:T(4,128)S(1)}, f32[4,512]{1,0:T(4,128)S(1)}, u32[]{:S(2)}, u32[]{:S(2)}) collective-permute-start(f32[4,512]{1,0:T(4,128)S(1)} %get-tuple-element.67), channel_id=1, source_target_pairs={{0,1},{1,0},{2,3},{3,2},{4,5},{5,4},{6,7},{7,6},{8,9},{9,8},{10,11... | collective-permute-start | bytes 24584 | tf_op jit(solution)/shard_map/ppermute | solution.py:28
  21.0 2.8 %copy-start.6 = (s32[128,4]{0,1:T(4,128)S(1)}, s32[128,4]{0,1:T(4,128)}, u32[]{:S(2)}) copy-start(s32[128,4]{0,1:T(4,128)} %param.21) | copy-start | bytes 6148
  21.0 2.8 %copy-start.7 = (s32[128,4]{0,1:T(4,128)S(1)}, s32[128,4]{0,1:T(4,128)}, u32[]{:S(2)}) copy-start(s32[128,4]{0,1:T(4,128)} %param.20) | copy-start | bytes 6148
  21.0 1.2 %collective-permute-start.5 = (f32[4,512]{1,0:T(4,128)S(1)}, f32[4,512]{1,0:T(4,128)S(1)}, u32[]{:S(2)}, u32[]{:S(2)}) collective-permute-start(f32[4,512]{1,0:T(4,128)S(1)} %add.146), channel_id=1, source_target_pairs={{0,2},{2,0},{4,6},{6,4},{8,10},{10,8},{12,14},{14,12},{16,18},{18,... | collective-permute-start | bytes 24584 | tf_op jit(solution)/shard_map/ppermute | solution.py:28
  22.3 3.7 %collective-permute-start.6 = (f32[4,512]{1,0:T(4,128)S(1)}, f32[4,512]{1,0:T(4,128)S(1)}, u32[]{:S(2)}, u32[]{:S(2)}) collective-permute-start(f32[4,512]{1,0:T(4,128)S(1)} %add.147), channel_id=1, source_target_pairs={{0,4},{2,6},{4,0},{6,2},{8,12},{10,14},{12,8},{14,10},{16,20},{18,... | collective-permute-start | bytes 24584 | tf_op jit(solution)/shard_map/ppermute | solution.py:28
  26.0 3.8 %collective-permute-start.7 = (f32[6,512]{1,0:T(8,128)S(1)}, f32[6,512]{1,0:T(8,128)S(1)}, u32[]{:S(2)}, u32[]{:S(2)}) collective-permute-start(f32[6,512]{1,0:T(8,128)S(1)} %pad_maximum_fusion), channel_id=1, source_target_pairs={{0,8},{2,10},{4,12},{6,14},{8,0},{10,2},{12,4},{14,6},{16,24},{18,... | collective-permute-start | bytes 36872 | tf_op jit(solution)/shard_map/ppermute | solution.py:16
  29.8 5.1 %collective-permute-start.8 = (f32[6,1024]{1,0:T(8,128)S(1)}, f32[6,1024]{1,0:T(8,128)S(1)}, u32[]{:S(2)}, u32[]{:S(2)}) collective-permute-start(f32[6,1024]{1,0:T(8,128)S(1)} %maximum_select_fusion.2), channel_id=1, source_target_pairs={{0,16},{2,18},{4,20},{6,22},{8,24},{10,26},{12,28},{14,30},{16,0},... | collective-permute-start | bytes 73736 | tf_op jit(solution)/shard_map/ppermute | solution.py:16
  34.9 0.7 %copy-start.8 = (bf16[8,128]{1,0:T(8,128)(2,1)S(1)}, bf16[8,128]{1,0:T(8,128)(2,1)}, u32[]{:S(2)}) copy-start(bf16[8,128]{1,0:T(8,128)(2,1)} %param.24) | copy-start | bytes 6148
  35.6 0.8 %copy-start.3 = (bf16[128,128]{1,0:T(8,128)(2,1)S(1)}, bf16[128,128]{1,0:T(8,128)(2,1)}, u32[]{:S(2)}) copy-start(bf16[128,128]{1,0:T(8,128)(2,1)} %param.26) | copy-start | bytes 98308
  36.4 0.7 %copy-start.10 = (f32[256]{0:T(256)S(1)}, f32[256]{0:T(256)}, u32[]{:S(2)}) copy-start(f32[256]{0:T(256)} %param.28) | copy-start | bytes 3076
  38.6 1.2 %collective-permute-start.9 = (f32[2048]{0:T(1024)S(1)}, f32[2048]{0:T(1024)S(1)}, u32[]{:S(2)}, u32[]{:S(2)}) collective-permute-start(f32[2048]{0:T(1024)S(1)} %fusion.39), channel_id=1, source_target_pairs={{0,2},{2,0},{4,6},{6,4},{8,10},{10,8},{12,14},{14,12},{16,18},{18,... | collective-permute-start | bytes 24584 | tf_op jit(solution)/shard_map/ppermute | solution.py:28
  39.9 3.7 %collective-permute-start.10 = (f32[2048]{0:T(1024)S(1)}, f32[2048]{0:T(1024)S(1)}, u32[]{:S(2)}, u32[]{:S(2)}) collective-permute-start(f32[2048]{0:T(1024)S(1)} %add.165), channel_id=1, source_target_pairs={{0,4},{2,6},{4,0},{6,2},{8,12},{10,14},{12,8},{14,10},{16,20},{18,... | collective-permute-start | bytes 24584 | tf_op jit(solution)/shard_map/ppermute | solution.py:28
  43.5 3.7 %collective-permute-start.11 = (f32[2048]{0:T(1024)S(1)}, f32[2048]{0:T(1024)S(1)}, u32[]{:S(2)}, u32[]{:S(2)}) collective-permute-start(f32[2048]{0:T(1024)S(1)} %add.166), channel_id=1, source_target_pairs={{0,8},{2,10},{4,12},{6,14},{8,0},{10,2},{12,4},{14,6},{16,24},{18,... | collective-permute-start | bytes 24584 | tf_op jit(solution)/shard_map/ppermute | solution.py:28
  47.2 4.5 %collective-permute-start.12 = (f32[2048]{0:T(1024)S(1)}, f32[2048]{0:T(1024)S(1)}, u32[]{:S(2)}, u32[]{:S(2)}) collective-permute-start(f32[2048]{0:T(1024)S(1)} %add.167), channel_id=1, source_target_pairs={{0,16},{2,18},{4,20},{6,22},{8,24},{10,26},{12,28},{14,30},{16,0},... | collective-permute-start | bytes 24584 | tf_op jit(solution)/shard_map/ppermute | solution.py:159
  55.3 0.7 %copy-start.2 = (f32[3,512]{1,0:T(4,128)}, f32[3,512]{1,0:T(4,128)S(1)}, u32[]{:S(2)}) copy-start(f32[3,512]{1,0:T(4,128)S(1)} %get-tuple-element.65) | copy-start | bytes 18436
  (2 other events, 1.4 us)

commit v14 on v13

--- a/solution.py
+++ b/solution.py
@@ -97,7 +97,6 @@
         axis=0,
     )
     near = gather_doubling(own, "blk", 1, low_blocks)
-    near, table_t = lax.optimization_barrier((near, species_table.T))
     mm_some = gather_doubling(
         jnp.concatenate([mm_pos, mm_charge[None, :]], axis=0), "blk", low_blocks, blocks
     )
@@ -112,7 +111,11 @@
     links = jnp.zeros((rows, blocks * rows), jnp.bfloat16)
     for k in range(ghost.shape[1]):
         links = links + (ghost[:, k : k + 1] == columns).astype(jnp.bfloat16)
-    known, links = lax.optimization_barrier((known, links))
+    finite = near[0:1, 0:1] == near[0:1, 0:1]
+    weights = [species_table.T, message_weight, potential_gain, energy_readout, charge_readout]
+    weights = [jnp.where(finite.reshape((1,) * w.ndim), w, jnp.zeros_like(w)) for w in weights]
+    known, links, weights = lax.optimization_barrier((known, links, weights))
+    table_t, message_weight, potential_gain, energy_readout, charge_readout = weights
     potential_all = known[0]
     qm_all = known[1:4]
     atoms = qm_all.shape[1]

time: 56.3 us -> 55.5 us (0.986)
  waiting for transfers between devices: 23.8 us -> 22.4 us
  between operations: 1.63 us -> 3.01 us
  local copies, waits for them, and re-layouts: 1.72 us -> 0.99 us
    ppermute x6, waiting for transfers between devices: 12.1 us -> 9.95 us  [sum_butterfly(): x = x + lax.ppermute(x, axis, [(i, i ^ step) for i in range(n)])]
    unnamed x26, local copies, waits for them, and re-layouts: 1.52 us -> 0.28 us
    ppermute x6, waiting for transfers between devices: 9.46 us -> 10.1 us  [gather_doubling(): other = lax.ppermute(x, axis, [(i, i ^ step) for i in range(n)])]
  transfers between devices with their start and end apart: 13 -> 13, of which waited for: 11 -> 10; matrix products, arithmetic and copies ran while one was open for 1% -> 2% of each run, Pallas kernels for 0% -> 0%
where the time goes in v14:
time: 55.5 us; the launch traced here: 55.3 us
  waiting for transfers between devices  22.4 us (40%)
  starting transfers between devices  18.1 us (33%)
  other arithmetic  8.93 us (16%)
  between operations  3.01 us (5%)
  matrix products  1.5 us (3%)
  local copies, waits for them, and re-layouts  0.99 us (2%)
    ppermute x6, starting transfers between devices, gather_doubling(): other = lax.ppermute(x, axis, [(i, i ^ step) for i in range(n)])  11 us
    ppermute x6, waiting for transfers between devices, gather_doubling(): other = lax.ppermute(x, axis, [(i, i ^ step) for i in range(n)])  10.1 us
    ppermute x6, waiting for transfers between devices, sum_butterfly(): x = x + lax.ppermute(x, axis, [(i, i ^ step) for i in range(n)])  9.95 us
    ppermute x6, starting transfers between devices, sum_butterfly(): x = x + lax.ppermute(x, axis, [(i, i ^ step) for i in range(n)])  4.98 us
    reduce_sum x4, other arithmetic, body(): jnp.sum(weighted, axis=0)  3.21 us
    reduce_sum x4, other arithmetic, body(): jnp.sum(d[c] * weight, axis=0)  3.19 us
    ppermute x1, waiting for transfers between devices, on_device(): lax.ppermute(part, 'blk', [(i, i ^ blocks // 2) for i in range(blocks)])  2.34 us
    ppermute x1, starting transfers between devices, on_device(): lax.ppermute(part, 'blk', [(i, i ^ blocks // 2) for i in range(blocks)])  2.18 us
  transfers between devices with their start and end apart: 13, of which 10 were waited for; matrix products, arithmetic and copies ran while one was open for 2% of the time, Pallas kernels for 0%

profile of v14, /device:TPU:0, one launch (start us, length us, event | category | flops | bytes accessed | tf_op | source)
XLA Modules:
  0.0 55.3 jit_solution(5637931793225296486)
XLA Ops:
  2.1 3.1 %collective-permute-start.2 = (f32[4,512]{1,0:T(4,128)S(1)}, f32[4,512]{1,0:T(4,128)S(1)}, u32[]{:S(2)}, u32[]{:S(2)}) collective-permute-start(f32[4,512]{1,0:T(4,128)S(1)} %pad_maximum_fusion.1), channel_id=1, source_target_pairs={{0,8},{2,10},{4,12},{6,14},{8,0},{10,2},{12,4},{14,6},{16,24},{18,... | collective-permute-start | bytes 24584 | tf_op jit(solution)/shard_map/ppermute | solution.py:16
  5.3 1.6 %collective-permute-start.1 = (f32[5,256]{1,0:T(8,128)S(1)}, f32[5,256]{1,0:T(8,128)S(1)}, u32[]{:S(2)}, u32[]{:S(2)}) collective-permute-start(f32[5,256]{1,0:T(8,128)S(1)} %maximum_select_fusion.6), channel_id=1, source_target_pairs={{0,4},{2,6},{4,0},{6,2},{8,12},{10,14},{12,8},{14,10},{16,20},{18,... | collective-permute-start | bytes 15368 | tf_op jit(solution)/shard_map/ppermute | solution.py:16
  6.9 2.1 %collective-permute-done.1 = f32[5,256]{1,0:T(8,128)S(1)} collective-permute-done((f32[5,256]{1,0:T(8,128)S(1)}, f32[5,256]{1,0:T(8,128)S(1)}, u32[]{:S(2)}, u32[]{:S(2)}) %collective-permute-start.1) | collective-permute-done | bytes 5152 | tf_op jit(solution)/shard_map/ppermute | solution.py:16
  9.0 2.7 %collective-permute-start.3 = (f32[4,1024]{1,0:T(4,128)S(1)}, f32[4,1024]{1,0:T(4,128)S(1)}, u32[]{:S(2)}, u32[]{:S(2)}) collective-permute-start(f32[4,1024]{1,0:T(4,128)S(1)} %maximum_select_fusion.5), channel_id=1, source_target_pairs={{0,16},{2,18},{4,20},{6,22},{8,24},{10,26},{12,28},{14,30},{16,0},... | collective-permute-start | bytes 49160 | tf_op jit(solution)/shard_map/ppermute | solution.py:16
  11.7 2.2 %collective-permute-done.3 = f32[4,1024]{1,0:T(4,128)S(1)} collective-permute-done((f32[4,1024]{1,0:T(4,128)S(1)}, f32[4,1024]{1,0:T(4,128)S(1)}, u32[]{:S(2)}, u32[]{:S(2)}) %collective-permute-start.3) | collective-permute-done | bytes 16416 | tf_op jit(solution)/shard_map/ppermute | solution.py:16
  13.9 3.5 %while.22 = (s32[]{:T(128)}, f32[4,512]{1,0:T(4,128)S(1)}, f32[1,512]{1,0:T(1,128)S(1)}, f32[4,512,4]{1,2,0:T(4,128)S(1)}, f32[1,512]{1,0:T(1,128)S(1)}, /*index=5*/f32[1,512]{1,0:T(1,128)S(1)}, s32[]{:T(128)}, s32[]{:T(128)}) while((s32[]{:T(128)}, f32[4,512]{1,0:T(4,128)S(1)}, f32[1,512]{1,0:T(1,128)S(1)}, ...), condition=%wide.region_5.6_spmd.clone, body=%wide.region_0.5_spmd.clone.sunk | while | flops 4988931 | bytes 79979 | solution.py:48
  14.0 0.8 %multiply_reduce_fusion.6 = (f32[512]{0:T(512)S(1)}, f32[512]{0:T(512)S(1)}, f32[512]{0:T(512)S(1)}, f32[512]{0:T(512)S(1)}) fusion(f32[512]{0:T(512)S(1)} %bitcast.136, f32[512]{0:T(512)S(1)} %bitcast.137, f32[512]{0:T(512)S(1)} %bitcast.148, f32[512]{0:T(512)S(1)} %bitcast.138, f32[512]{0:T(512)S(1)} %bitcast.149, f32[512]{0:T(512)S(1)} %bitcast.135, ...), kind=kLoop, calls=%fused_computation.1.clone.1 | loop fusion | flops 4978688 | bytes 22528 | tf_op jit(solution)/shard_map/while/body/eval_jaxpr/reduce_sum | solution.py:43
  14.8 0.8 %multiply_reduce_fusion.6 = (f32[512]{0:T(512)S(1)}, f32[512]{0:T(512)S(1)}, f32[512]{0:T(512)S(1)}, f32[512]{0:T(512)S(1)}) fusion(f32[512]{0:T(512)S(1)} %bitcast.136, f32[512]{0:T(512)S(1)} %bitcast.137, f32[512]{0:T(512)S(1)} %bitcast.148, f32[512]{0:T(512)S(1)} %bitcast.138, f32[512]{0:T(512)S(1)} %bitcast.149, f32[512]{0:T(512)S(1)} %bitcast.135, ...), kind=kLoop, calls=%fused_computation.1.clone.1 | loop fusion | flops 4978688 | bytes 22528 | tf_op jit(solution)/shard_map/while/body/eval_jaxpr/reduce_sum | solution.py:43
  15.7 0.8 %multiply_reduce_fusion.6 = (f32[512]{0:T(512)S(1)}, f32[512]{0:T(512)S(1)}, f32[512]{0:T(512)S(1)}, f32[512]{0:T(512)S(1)}) fusion(f32[512]{0:T(512)S(1)} %bitcast.136, f32[512]{0:T(512)S(1)} %bitcast.137, f32[512]{0:T(512)S(1)} %bitcast.148, f32[512]{0:T(512)S(1)} %bitcast.138, f32[512]{0:T(512)S(1)} %bitcast.149, f32[512]{0:T(512)S(1)} %bitcast.135, ...), kind=kLoop, calls=%fused_computation.1.clone.1 | loop fusion | flops 4978688 | bytes 22528 | tf_op jit(solution)/shard_map/while/body/eval_jaxpr/reduce_sum | solution.py:43
  16.6 0.8 %multiply_reduce_fusion.6 = (f32[512]{0:T(512)S(1)}, f32[512]{0:T(512)S(1)}, f32[512]{0:T(512)S(1)}, f32[512]{0:T(512)S(1)}) fusion(f32[512]{0:T(512)S(1)} %bitcast.136, f32[512]{0:T(512)S(1)} %bitcast.137, f32[512]{0:T(512)S(1)} %bitcast.148, f32[512]{0:T(512)S(1)} %bitcast.138, f32[512]{0:T(512)S(1)} %bitcast.149, f32[512]{0:T(512)S(1)} %bitcast.135, ...), kind=kLoop, calls=%fused_computation.1.clone.1 | loop fusion | flops 4978688 | bytes 22528 | tf_op jit(solution)/shard_map/while/body/eval_jaxpr/reduce_sum | solution.py:43
  17.4 1.6 %collective-permute-start.4 = (f32[4,512]{1,0:T(4,128)S(1)}, f32[4,512]{1,0:T(4,128)S(1)}, u32[]{:S(2)}, u32[]{:S(2)}) collective-permute-start(f32[4,512]{1,0:T(4,128)S(1)} %get-tuple-element.69), channel_id=1, source_target_pairs={{0,1},{1,0},{2,3},{3,2},{4,5},{5,4},{6,7},{7,6},{8,9},{9,8},{10,11... | collective-permute-start | bytes 24584 | tf_op jit(solution)/shard_map/ppermute | solution.py:28
  21.6 1.1 %collective-permute-done.5 = f32[4,512]{1,0:T(4,128)S(1)} collective-permute-done((f32[4,512]{1,0:T(4,128)S(1)}, f32[4,512]{1,0:T(4,128)S(1)}, u32[]{:S(2)}, u32[]{:S(2)}) %collective-permute-start.5) | collective-permute-done | bytes 8224 | tf_op jit(solution)/shard_map/ppermute | solution.py:28
  22.7 1.5 %collective-permute-start.6 = (f32[4,512]{1,0:T(4,128)S(1)}, f32[4,512]{1,0:T(4,128)S(1)}, u32[]{:S(2)}, u32[]{:S(2)}) collective-permute-start(f32[4,512]{1,0:T(4,128)S(1)} %add.147), channel_id=1, source_target_pairs={{0,4},{2,6},{4,0},{6,2},{8,12},{10,14},{12,8},{14,10},{16,20},{18,... | collective-permute-start | bytes 24584 | tf_op jit(solution)/shard_map/ppermute | solution.py:28
  24.3 2.1 %collective-permute-done.6 = f32[4,512]{1,0:T(4,128)S(1)} collective-permute-done((f32[4,512]{1,0:T(4,128)S(1)}, f32[4,512]{1,0:T(4,128)S(1)}, u32[]{:S(2)}, u32[]{:S(2)}) %collective-permute-start.6) | collective-permute-done | bytes 8224 | tf_op jit(solution)/shard_map/ppermute | solution.py:28
  27.1 3.1 %collective-permute-done.7 = f32[6,512]{1,0:T(8,128)S(1)} collective-permute-done((f32[6,512]{1,0:T(8,128)S(1)}, f32[6,512]{1,0:T(8,128)S(1)}, u32[]{:S(2)}, u32[]{:S(2)}) %collective-permute-start.7) | collective-permute-done | bytes 12320 | tf_op jit(solution)/shard_map/ppermute | solution.py:16
  30.2 2.5 %collective-permute-start.8 = (f32[6,1024]{1,0:T(8,128)S(1)}, f32[6,1024]{1,0:T(8,128)S(1)}, u32[]{:S(2)}, u32[]{:S(2)}) collective-permute-start(f32[6,1024]{1,0:T(8,128)S(1)} %maximum_select_fusion.2), channel_id=1, source_target_pairs={{0,16},{2,18},{4,20},{6,22},{8,24},{10,26},{12,28},{14,30},{16,0},... | collective-permute-start | bytes 73736 | tf_op jit(solution)/shard_map/ppermute | solution.py:16
  32.8 2.6 %collective-permute-done.8 = f32[6,1024]{1,0:T(8,128)S(1)} collective-permute-done((f32[6,1024]{1,0:T(8,128)S(1)}, f32[6,1024]{1,0:T(8,128)S(1)}, u32[]{:S(2)}, u32[]{:S(2)}) %collective-permute-start.8) | collective-permute-done | bytes 24608 | tf_op jit(solution)/shard_map/ppermute | solution.py:16
  38.0 1.2 %collective-permute-done.9 = f32[2048]{0:T(1024)S(1)} collective-permute-done((f32[2048]{0:T(1024)S(1)}, f32[2048]{0:T(1024)S(1)}, u32[]{:S(2)}, u32[]{:S(2)}) %collective-permute-start.9) | collective-permute-done | bytes 8224 | tf_op jit(solution)/shard_map/ppermute | solution.py:28
  39.1 1.5 %collective-permute-start.10 = (f32[2048]{0:T(1024)S(1)}, f32[2048]{0:T(1024)S(1)}, u32[]{:S(2)}, u32[]{:S(2)}) collective-permute-start(f32[2048]{0:T(1024)S(1)} %add.165), channel_id=1, source_target_pairs={{0,4},{2,6},{4,0},{6,2},{8,12},{10,14},{12,8},{14,10},{16,20},{18,... | collective-permute-start | bytes 24584 | tf_op jit(solution)/shard_map/ppermute | solution.py:28
  40.6 2.1 %collective-permute-done.10 = f32[2048]{0:T(1024)S(1)} collective-permute-done((f32[2048]{0:T(1024)S(1)}, f32[2048]{0:T(1024)S(1)}, u32[]{:S(2)}, u32[]{:S(2)}) %collective-permute-start.10) | collective-permute-done | bytes 8224 | tf_op jit(solution)/shard_map/ppermute | solution.py:28
  43.0 3.4 %collective-permute-done.11 = f32[2048]{0:T(1024)S(1)} collective-permute-done((f32[2048]{0:T(1024)S(1)}, f32[2048]{0:T(1024)S(1)}, u32[]{:S(2)}, u32[]{:S(2)}) %collective-permute-start.11) | collective-permute-done | bytes 8224 | tf_op jit(solution)/shard_map/ppermute | solution.py:28
  46.4 2.2 %collective-permute-start.12 = (f32[2048]{0:T(1024)S(1)}, f32[2048]{0:T(1024)S(1)}, u32[]{:S(2)}, u32[]{:S(2)}) collective-permute-start(f32[2048]{0:T(1024)S(1)} %add.167), channel_id=1, source_target_pairs={{0,16},{2,18},{4,20},{6,22},{8,24},{10,26},{12,28},{14,30},{16,0},... | collective-permute-start | bytes 24584 | tf_op jit(solution)/shard_map/ppermute | solution.py:162
  48.6 2.3 %collective-permute-done.12 = f32[2048]{0:T(1024)S(1)} collective-permute-done((f32[2048]{0:T(1024)S(1)}, f32[2048]{0:T(1024)S(1)}, u32[]{:S(2)}, u32[]{:S(2)}) %collective-permute-start.12) | collective-permute-done | bytes 8224 | tf_op jit(solution)/shard_map/ppermute | solution.py:162
  51.0 3.6 %while.23 = (s32[]{:T(128)}, f32[3,512]{1,0:T(4,128)S(1)}, f32[4,512,4]{1,2,0:T(4,128)S(1)}, f32[3,512]{1,0:T(4,128)S(1)}, f32[512]{0:T(512)S(1)}, /*index=5*/s32[]{:T(128)}, s32[]{:T(128)}) while((s32[]{:T(128)}, f32[3,512]{1,0:T(4,128)S(1)}, f32[4,512,4]{1,2,0:T(4,128)S(1)}, f32[3,512]{1,0:T(4,128)S(1)}, f32[512]{0:T(512)S(1)}, ...), condition=%wide.region_15.16_spmd.clone, body=%wide.region_11.15_spmd.clone.sunk | while | flops 4985347 | bytes 86115 | solution.py:63
  (116 shorter events, 9.7 us)
Async XLA Ops:
  0.6 35.7 %copy-start = (bf16[128,256]{1,0:T(8,128)(2,1)S(1)}, bf16[128,256]{1,0:T(8,128)(2,1)}, u32[]{:S(2)}) copy-start(bf16[128,256]{1,0:T(8,128)(2,1)} %param.27) | copy-start | bytes 196612
  0.6 0.7 %copy-start.11 = (s32[128]{0:T(128)S(1)}, s32[128]{0:T(128)}, u32[]{:S(2)}) copy-start(s32[128]{0:T(128)} %param.18) | copy-start | bytes 1540
  0.7 0.7 %copy-start.5 = (f32[3,128]{1,0:T(4,128)S(1)}, f32[3,128]{1,0:T(4,128)}, u32[]{:S(2)}) copy-start(f32[3,128]{1,0:T(4,128)} %param.17) | copy-start | bytes 4612
  1.3 0.7 %copy-start.1 = (f32[3,512]{1,0:T(4,128)S(1)}, f32[3,512]{1,0:T(4,128)}, u32[]{:S(2)}) copy-start(f32[3,512]{1,0:T(4,128)} %param.22) | copy-start | bytes 18436
  1.4 0.7 %copy-start.3 = (f32[512]{0:T(512)S(1)}, f32[512]{0:T(512)}, u32[]{:S(2)}) copy-start(f32[512]{0:T(512)} %param.23) | copy-start | bytes 6148
  1.4 3.8 %collective-permute-start = (f32[5,128]{1,0:T(8,128)S(1)}, f32[5,128]{1,0:T(8,128)S(1)}, u32[]{:S(2)}, u32[]{:S(2)}) collective-permute-start(f32[5,128]{1,0:T(8,128)S(1)} %pad_maximum_fusion.2), channel_id=1, source_target_pairs={{0,2},{2,0},{4,6},{6,4},{8,10},{10,8},{12,14},{14,12},{16,18},{18,... | collective-permute-start | bytes 7688 | tf_op jit(solution)/shard_map/ppermute | solution.py:16
  2.1 3.1 %copy-start.6 = (s32[128,4]{0,1:T(4,128)S(1)}, s32[128,4]{0,1:T(4,128)}, u32[]{:S(2)}) copy-start(s32[128,4]{0,1:T(4,128)} %param.21) | copy-start | bytes 6148
  2.1 3.1 %copy-start.7 = (s32[128,4]{0,1:T(4,128)S(1)}, s32[128,4]{0,1:T(4,128)}, u32[]{:S(2)}) copy-start(s32[128,4]{0,1:T(4,128)} %param.20) | copy-start | bytes 6148
  2.1 6.9 %collective-permute-start.2 = (f32[4,512]{1,0:T(4,128)S(1)}, f32[4,512]{1,0:T(4,128)S(1)}, u32[]{:S(2)}, u32[]{:S(2)}) collective-permute-start(f32[4,512]{1,0:T(4,128)S(1)} %pad_maximum_fusion.1), channel_id=1, source_target_pairs={{0,8},{2,10},{4,12},{6,14},{8,0},{10,2},{12,4},{14,6},{16,24},{18,... | collective-permute-start | bytes 24584 | tf_op jit(solution)/shard_map/ppermute | solution.py:16
  5.3 3.7 %collective-permute-start.1 = (f32[5,256]{1,0:T(8,128)S(1)}, f32[5,256]{1,0:T(8,128)S(1)}, u32[]{:S(2)}, u32[]{:S(2)}) collective-permute-start(f32[5,256]{1,0:T(8,128)S(1)} %maximum_select_fusion.6), channel_id=1, source_target_pairs={{0,4},{2,6},{4,0},{6,2},{8,12},{10,14},{12,8},{14,10},{16,20},{18,... | collective-permute-start | bytes 15368 | tf_op jit(solution)/shard_map/ppermute | solution.py:16
  9.0 4.9 %collective-permute-start.3 = (f32[4,1024]{1,0:T(4,128)S(1)}, f32[4,1024]{1,0:T(4,128)S(1)}, u32[]{:S(2)}, u32[]{:S(2)}) collective-permute-start(f32[4,1024]{1,0:T(4,128)S(1)} %maximum_select_fusion.5), channel_id=1, source_target_pairs={{0,16},{2,18},{4,20},{6,22},{8,24},{10,26},{12,28},{14,30},{16,0},... | collective-permute-start | bytes 49160 | tf_op jit(solution)/shard_map/ppermute | solution.py:16
  17.4 4.0 %collective-permute-start.4 = (f32[4,512]{1,0:T(4,128)S(1)}, f32[4,512]{1,0:T(4,128)S(1)}, u32[]{:S(2)}, u32[]{:S(2)}) collective-permute-start(f32[4,512]{1,0:T(4,128)S(1)} %get-tuple-element.69), channel_id=1, source_target_pairs={{0,1},{1,0},{2,3},{3,2},{4,5},{5,4},{6,7},{7,6},{8,9},{9,8},{10,11... | collective-permute-start | bytes 24584 | tf_op jit(solution)/shard_map/ppermute | solution.py:28
  19.6 1.9 %copy-start.4 = (bf16[128,128]{1,0:T(8,128)(2,1)S(1)}, bf16[128,128]{1,0:T(8,128)(2,1)}, u32[]{:S(2)}) copy-start(bf16[128,128]{1,0:T(8,128)(2,1)} %param.26) | copy-start | bytes 98308
  21.5 1.2 %collective-permute-start.5 = (f32[4,512]{1,0:T(4,128)S(1)}, f32[4,512]{1,0:T(4,128)S(1)}, u32[]{:S(2)}, u32[]{:S(2)}) collective-permute-start(f32[4,512]{1,0:T(4,128)S(1)} %add.146), channel_id=1, source_target_pairs={{0,2},{2,0},{4,6},{6,4},{8,10},{10,8},{12,14},{14,12},{16,18},{18,... | collective-permute-start | bytes 24584 | tf_op jit(solution)/shard_map/ppermute | solution.py:28
  21.6 2.7 %copy-start.8 = (bf16[8,128]{1,0:T(8,128)(2,1)S(1)}, bf16[8,128]{1,0:T(8,128)(2,1)}, u32[]{:S(2)}) copy-start(bf16[8,128]{1,0:T(8,128)(2,1)} %param.24) | copy-start | bytes 6148
  22.7 3.7 %collective-permute-start.6 = (f32[4,512]{1,0:T(4,128)S(1)}, f32[4,512]{1,0:T(4,128)S(1)}, u32[]{:S(2)}, u32[]{:S(2)}) collective-permute-start(f32[4,512]{1,0:T(4,128)S(1)} %add.147), channel_id=1, source_target_pairs={{0,4},{2,6},{4,0},{6,2},{8,12},{10,14},{12,8},{14,10},{16,20},{18,... | collective-permute-start | bytes 24584 | tf_op jit(solution)/shard_map/ppermute | solution.py:28
  26.4 0.7 %copy-start.10 = (f32[256]{0:T(256)S(1)}, f32[256]{0:T(256)}, u32[]{:S(2)}) copy-start(f32[256]{0:T(256)} %param.28) | copy-start | bytes 3076
  26.4 3.8 %collective-permute-start.7 = (f32[6,512]{1,0:T(8,128)S(1)}, f32[6,512]{1,0:T(8,128)S(1)}, u32[]{:S(2)}, u32[]{:S(2)}) collective-permute-start(f32[6,512]{1,0:T(8,128)S(1)} %pad_maximum_fusion), channel_id=1, source_target_pairs={{0,8},{2,10},{4,12},{6,14},{8,0},{10,2},{12,4},{14,6},{16,24},{18,... | collective-permute-start | bytes 36872 | tf_op jit(solution)/shard_map/ppermute | solution.py:16
  27.1 5.7 %copy-start.12 = (f32[128]{0:T(128)S(1)}, f32[128]{0:T(128)}, u32[]{:S(2)}) copy-start(f32[128]{0:T(128)} %param.25) | copy-start | bytes 1540
  30.2 5.2 %collective-permute-start.8 = (f32[6,1024]{1,0:T(8,128)S(1)}, f32[6,1024]{1,0:T(8,128)S(1)}, u32[]{:S(2)}, u32[]{:S(2)}) collective-permute-start(f32[6,1024]{1,0:T(8,128)S(1)} %maximum_select_fusion.2), channel_id=1, source_target_pairs={{0,16},{2,18},{4,20},{6,22},{8,24},{10,26},{12,28},{14,30},{16,0},... | collective-permute-start | bytes 73736 | tf_op jit(solution)/shard_map/ppermute | solution.py:16
  37.9 1.2 %collective-permute-start.9 = (f32[2048]{0:T(1024)S(1)}, f32[2048]{0:T(1024)S(1)}, u32[]{:S(2)}, u32[]{:S(2)}) collective-permute-start(f32[2048]{0:T(1024)S(1)} %fusion.39), channel_id=1, source_target_pairs={{0,2},{2,0},{4,6},{6,4},{8,10},{10,8},{12,14},{14,12},{16,18},{18,... | collective-permute-start | bytes 24584 | tf_op jit(solution)/shard_map/ppermute | solution.py:28
  39.1 3.7 %collective-permute-start.10 = (f32[2048]{0:T(1024)S(1)}, f32[2048]{0:T(1024)S(1)}, u32[]{:S(2)}, u32[]{:S(2)}) collective-permute-start(f32[2048]{0:T(1024)S(1)} %add.165), channel_id=1, source_target_pairs={{0,4},{2,6},{4,0},{6,2},{8,12},{10,14},{12,8},{14,10},{16,20},{18,... | collective-permute-start | bytes 24584 | tf_op jit(solution)/shard_map/ppermute | solution.py:28
  42.8 3.7 %collective-permute-start.11 = (f32[2048]{0:T(1024)S(1)}, f32[2048]{0:T(1024)S(1)}, u32[]{:S(2)}, u32[]{:S(2)}) collective-permute-start(f32[2048]{0:T(1024)S(1)} %add.166), channel_id=1, source_target_pairs={{0,8},{2,10},{4,12},{6,14},{8,0},{10,2},{12,4},{14,6},{16,24},{18,... | collective-permute-start | bytes 24584 | tf_op jit(solution)/shard_map/ppermute | solution.py:28
  46.4 4.5 %collective-permute-start.12 = (f32[2048]{0:T(1024)S(1)}, f32[2048]{0:T(1024)S(1)}, u32[]{:S(2)}, u32[]{:S(2)}) collective-permute-start(f32[2048]{0:T(1024)S(1)} %add.167), channel_id=1, source_target_pairs={{0,16},{2,18},{4,20},{6,22},{8,24},{10,26},{12,28},{14,30},{16,0},... | collective-permute-start | bytes 24584 | tf_op jit(solution)/shard_map/ppermute | solution.py:162
  (2 other events, 1.4 us)

commit v15 on v14

--- a/solution.py
+++ b/solution.py
@@ -45,7 +45,7 @@
         return running + part, None
 
     stacked = jnp.transpose(mm_some.reshape(4, chunks, CHUNK), (1, 2, 0))
-    total, _ = lax.scan(body, jnp.zeros((4, qm_some.shape[1]), jnp.float32), stacked)
+    total, _ = lax.scan(body, jnp.zeros((4, qm_some.shape[1]), jnp.float32), stacked, unroll=True)
     return total
 
 
@@ -60,7 +60,7 @@
         weight = inverse * inverse * inverse * block[:, 3:4] * scale[None, :]
         return running + jnp.stack([jnp.sum(d[c] * weight, axis=0) for c in range(3)]), None
 
-    total, _ = lax.scan(body, jnp.zeros((3, mm_pos.shape[1]), jnp.float32), stacked)
+    total, _ = lax.scan(body, jnp.zeros((3, mm_pos.shape[1]), jnp.float32), stacked, unroll=True)
     return total
 
 

time: 55.5 us -> 56.9 us (1.025)
  other arithmetic: 8.93 us -> 10.5 us
    reduce_sum x4 -> x1, other arithmetic: 3.21 us -> 3.82 us  [body(): jnp.sum(weighted, axis=0)]
    reduce_sum x4 -> x2, other arithmetic: 3.19 us -> 3.61 us  [body(): jnp.sum(d[c] * weight, axis=0)]
where the time goes in v15:
time: 56.9 us; the launch traced here: 56.6 us
  waiting for transfers between devices  22.4 us (39%)
  starting transfers between devices  18.2 us (32%)
  other arithmetic  10.5 us (18%)
  between operations  3.07 us (5%)
  matrix products  1.5 us (3%)
  local copies, waits for them, and re-layouts  0.98 us (2%)
    ppermute x6, starting transfers between devices, gather_doubling(): other = lax.ppermute(x, axis, [(i, i ^ step) for i in range(n)])  11 us
    ppermute x6, waiting for transfers between devices, gather_doubling(): other = lax.ppermute(x, axis, [(i, i ^ step) for i in range(n)])  10.1 us
    ppermute x6, waiting for transfers between devices, sum_butterfly(): x = x + lax.ppermute(x, axis, [(i, i ^ step) for i in range(n)])  9.95 us
    ppermute x6, starting transfers between devices, sum_butterfly(): x = x + lax.ppermute(x, axis, [(i, i ^ step) for i in range(n)])  5.04 us
    reduce_sum x1, other arithmetic, body(): jnp.sum(weighted, axis=0)  3.82 us
    reduce_sum x2, other arithmetic, body(): jnp.sum(d[c] * weight, axis=0)  3.61 us
    ppermute x1, waiting for transfers between devices, on_device(): lax.ppermute(part, 'blk', [(i, i ^ blocks // 2) for i in range(blocks)])  2.32 us
    ppermute x1, starting transfers between devices, on_device(): lax.ppermute(part, 'blk', [(i, i ^ blocks // 2) for i in range(blocks)])  2.18 us
  transfers between devices with their start and end apart: 13, of which 10 were waited for; matrix products, arithmetic and copies ran while one was open for 2% of the time, Pallas kernels for 0%

profile of v15, /device:TPU:0, one launch (start us, length us, event | category | flops | bytes accessed | tf_op | source)
XLA Modules:
  0.0 56.6 jit_solution(3600790665320454511)
XLA Ops:
  2.1 3.1 %collective-permute-start.2 = (f32[4,512]{1,0:T(4,128)S(1)}, f32[4,512]{1,0:T(4,128)S(1)}, u32[]{:S(2)}, u32[]{:S(2)}) collective-permute-start(f32[4,512]{1,0:T(4,128)S(1)} %pad_maximum_fusion.1), channel_id=1, source_target_pairs={{0,8},{2,10},{4,12},{6,14},{8,0},{10,2},{12,4},{14,6},{16,24},{18,... | collective-permute-start | bytes 24584 | tf_op jit(solution)/shard_map/ppermute | solution.py:16
  5.3 1.6 %collective-permute-start.1 = (f32[5,256]{1,0:T(8,128)S(1)}, f32[5,256]{1,0:T(8,128)S(1)}, u32[]{:S(2)}, u32[]{:S(2)}) collective-permute-start(f32[5,256]{1,0:T(8,128)S(1)} %maximum_select_fusion.6), channel_id=1, source_target_pairs={{0,4},{2,6},{4,0},{6,2},{8,12},{10,14},{12,8},{14,10},{16,20},{18,... | collective-permute-start | bytes 15368 | tf_op jit(solution)/shard_map/ppermute | solution.py:16
  6.8 2.1 %collective-permute-done.1 = f32[5,256]{1,0:T(8,128)S(1)} collective-permute-done((f32[5,256]{1,0:T(8,128)S(1)}, f32[5,256]{1,0:T(8,128)S(1)}, u32[]{:S(2)}, u32[]{:S(2)}) %collective-permute-start.1) | collective-permute-done | bytes 5152 | tf_op jit(solution)/shard_map/ppermute | solution.py:16
  9.0 2.7 %collective-permute-start.3 = (f32[4,1024]{1,0:T(4,128)S(1)}, f32[4,1024]{1,0:T(4,128)S(1)}, u32[]{:S(2)}, u32[]{:S(2)}) collective-permute-start(f32[4,1024]{1,0:T(4,128)S(1)} %maximum_select_fusion.5), channel_id=1, source_target_pairs={{0,16},{2,18},{4,20},{6,22},{8,24},{10,26},{12,28},{14,30},{16,0},... | collective-permute-start | bytes 49160 | tf_op jit(solution)/shard_map/ppermute | solution.py:16
  11.7 2.2 %collective-permute-done.3 = f32[4,1024]{1,0:T(4,128)S(1)} collective-permute-done((f32[4,1024]{1,0:T(4,128)S(1)}, f32[4,1024]{1,0:T(4,128)S(1)}, u32[]{:S(2)}, u32[]{:S(2)}) %collective-permute-start.3) | collective-permute-done | bytes 16416 | tf_op jit(solution)/shard_map/ppermute | solution.py:16
  14.0 3.8 %multiply_reduce_fusion = (f32[512]{0:T(512)S(1)}, f32[512]{0:T(512)S(1)}, f32[512]{0:T(512)S(1)}, f32[512]{0:T(512)S(1)}, f32[512]{0:T(512)S(1)}, /*index=5*/f3...) fusion(f32[512]{0:T(512)S(1)} %bitcast.208, ...), kind=kLoop, calls=%fused_computation.35 | loop fusion | flops 19914752 | bytes 71680 | tf_op jit(solution)/shard_map/eval_jaxpr/reduce_sum | solution.py:43
  17.8 1.6 %collective-permute-start.4 = (f32[4,512]{1,0:T(4,128)S(1)}, f32[4,512]{1,0:T(4,128)S(1)}, u32[]{:S(2)}, u32[]{:S(2)}) collective-permute-start(f32[4,512]{1,0:T(4,128)S(1)} %fusion.88), channel_id=1, source_target_pairs={{0,1},{1,0},{2,3},{3,2},{4,5},{5,4},{6,7},{7,6},{8,9},{9,8},{10,11... | collective-permute-start | bytes 24584 | tf_op jit(solution)/shard_map/ppermute | solution.py:28
  19.4 0.6 %fusion.74 = bf16[128,2048]{1,0:T(8,128)(2,1)S(1)} fusion(s32[128]{0:T(128)S(1)} %get-tuple-element.118, s32[128]{0:T(128)S(1)} %get-tuple-element.119, s32[128]{0:T(128)S(1)} %get-tuple-element.120, s32[128]{0:T(128)S(1)} %get-tuple-element.117), kind=kLoop, calls=%fused_computation.143 | loop fusion | flops 4194304 | bytes 526336 | tf_op jit(solution)/shard_map/add | solution.py:113
  22.0 1.1 %collective-permute-done.5 = f32[4,512]{1,0:T(4,128)S(1)} collective-permute-done((f32[4,512]{1,0:T(4,128)S(1)}, f32[4,512]{1,0:T(4,128)S(1)}, u32[]{:S(2)}, u32[]{:S(2)}) %collective-permute-start.5) | collective-permute-done | bytes 8224 | tf_op jit(solution)/shard_map/ppermute | solution.py:28
  23.2 1.6 %collective-permute-start.6 = (f32[4,512]{1,0:T(4,128)S(1)}, f32[4,512]{1,0:T(4,128)S(1)}, u32[]{:S(2)}, u32[]{:S(2)}) collective-permute-start(f32[4,512]{1,0:T(4,128)S(1)} %fusion.122), channel_id=1, source_target_pairs={{0,4},{2,6},{4,0},{6,2},{8,12},{10,14},{12,8},{14,10},{16,20},{18,... | collective-permute-start | bytes 24584 | tf_op jit(solution)/shard_map/ppermute | solution.py:28
  24.8 2.1 %collective-permute-done.6 = f32[4,512]{1,0:T(4,128)S(1)} collective-permute-done((f32[4,512]{1,0:T(4,128)S(1)}, f32[4,512]{1,0:T(4,128)S(1)}, u32[]{:S(2)}, u32[]{:S(2)}) %collective-permute-start.6) | collective-permute-done | bytes 8224 | tf_op jit(solution)/shard_map/ppermute | solution.py:28
  27.6 3.1 %collective-permute-done.7 = f32[6,512]{1,0:T(8,128)S(1)} collective-permute-done((f32[6,512]{1,0:T(8,128)S(1)}, f32[6,512]{1,0:T(8,128)S(1)}, u32[]{:S(2)}, u32[]{:S(2)}) %collective-permute-start.7) | collective-permute-done | bytes 12320 | tf_op jit(solution)/shard_map/ppermute | solution.py:16
  30.8 2.5 %collective-permute-start.8 = (f32[6,1024]{1,0:T(8,128)S(1)}, f32[6,1024]{1,0:T(8,128)S(1)}, u32[]{:S(2)}, u32[]{:S(2)}) collective-permute-start(f32[6,1024]{1,0:T(8,128)S(1)} %maximum_select_fusion.2), channel_id=1, source_target_pairs={{0,16},{2,18},{4,20},{6,22},{8,24},{10,26},{12,28},{14,30},{16,0},... | collective-permute-start | bytes 73736 | tf_op jit(solution)/shard_map/ppermute | solution.py:16
  33.3 2.6 %collective-permute-done.8 = f32[6,1024]{1,0:T(8,128)S(1)} collective-permute-done((f32[6,1024]{1,0:T(8,128)S(1)}, f32[6,1024]{1,0:T(8,128)S(1)}, u32[]{:S(2)}, u32[]{:S(2)}) %collective-permute-start.8) | collective-permute-done | bytes 24608 | tf_op jit(solution)/shard_map/ppermute | solution.py:16
  37.2 0.6 %multiply_add_fusion.2 = (f32[128]{0:T(128)}, f32[128]{0:T(128)S(1)}, f32[128]{0:T(128)S(1)}) fusion(f32[128]{0:T(128)S(1)} %get-tuple-element.18, f32[128]{0:T(128)S(1)} %get-tuple-element.17, pred[2048]{0:T(1024)(128)(4,1)S(1)} %fusion.83, s32[]{:T(128)S(6)} %select_n.174, f32[1,2048]{1,0:T(1,128)S(1)} %get-tuple-element.69), kind=kLoop, calls=%fused_computation.215 | loop fusion | flops 640 | bytes 3204 | tf_op jit(solution)/shard_map/add | solution.py:146
  38.5 1.2 %collective-permute-done.9 = f32[2048]{0:T(1024)S(1)} collective-permute-done((f32[2048]{0:T(1024)S(1)}, f32[2048]{0:T(1024)S(1)}, u32[]{:S(2)}, u32[]{:S(2)}) %collective-permute-start.9) | collective-permute-done | bytes 8224 | tf_op jit(solution)/shard_map/ppermute | solution.py:28
  39.7 1.5 %collective-permute-start.10 = (f32[2048]{0:T(1024)S(1)}, f32[2048]{0:T(1024)S(1)}, u32[]{:S(2)}, u32[]{:S(2)}) collective-permute-start(f32[2048]{0:T(1024)S(1)} %add.240), channel_id=1, source_target_pairs={{0,4},{2,6},{4,0},{6,2},{8,12},{10,14},{12,8},{14,10},{16,20},{18,... | collective-permute-start | bytes 24584 | tf_op jit(solution)/shard_map/ppermute | solution.py:28
  41.2 2.1 %collective-permute-done.10 = f32[2048]{0:T(1024)S(1)} collective-permute-done((f32[2048]{0:T(1024)S(1)}, f32[2048]{0:T(1024)S(1)}, u32[]{:S(2)}, u32[]{:S(2)}) %collective-permute-start.10) | collective-permute-done | bytes 8224 | tf_op jit(solution)/shard_map/ppermute | solution.py:28
  43.6 3.4 %collective-permute-done.11 = f32[2048]{0:T(1024)S(1)} collective-permute-done((f32[2048]{0:T(1024)S(1)}, f32[2048]{0:T(1024)S(1)}, u32[]{:S(2)}, u32[]{:S(2)}) %collective-permute-start.11) | collective-permute-done | bytes 8224 | tf_op jit(solution)/shard_map/ppermute | solution.py:28
  47.0 2.2 %collective-permute-start.12 = (f32[2048]{0:T(1024)S(1)}, f32[2048]{0:T(1024)S(1)}, u32[]{:S(2)}, u32[]{:S(2)}) collective-permute-start(f32[2048]{0:T(1024)S(1)} %add.242), channel_id=1, source_target_pairs={{0,16},{2,18},{4,20},{6,22},{8,24},{10,26},{12,28},{14,30},{16,0},... | collective-permute-start | bytes 24584 | tf_op jit(solution)/shard_map/ppermute | solution.py:162
  49.2 2.3 %collective-permute-done.12 = f32[2048]{0:T(1024)S(1)} collective-permute-done((f32[2048]{0:T(1024)S(1)}, f32[2048]{0:T(1024)S(1)}, u32[]{:S(2)}, u32[]{:S(2)}) %collective-permute-start.12) | collective-permute-done | bytes 8224 | tf_op jit(solution)/shard_map/ppermute | solution.py:162
  52.4 0.8 %fusion.38 = (f32[512]{0:T(512)S(1)}, f32[512]{0:T(512)S(1)}, f32[512]{0:T(512)S(1)}) fusion(f32[512]{0:T(512)S(1)} %bitcast.224, f32[512]{0:T(512)S(1)} %bitcast.246, f32[512]{0:T(512)S(1)} %broadcast_multiply_fusion, f32[512]{0:T(512)S(1)} %bitcast.244, f32[512]{0:T(512)S(1)} %bitcast.226, f32[512]{0:T(512)S(1)} %bitcast.245, f32[512]{0:T(512)S(1)} %bitcast.222, ...), kind=kLoop, calls=%fused_computation.102 | loop fusion | flops 4979200 | bytes 22528 | tf_op jit(solution)/shard_map/eval_jaxpr/reduce_sum | solution.py:61
  53.2 2.8 %fusion.65 = (f32[512]{0:T(512)S(1)}, f32[512]{0:T(512)S(1)}, f32[512]{0:T(512)S(1)}, f32[512]{0:T(512)S(1)}, f32[512]{0:T(512)S(1)}, /*index=5*/f32[512]{0:T(51...) fusion(f32[512]{0:T(512)S(1)} %bitcast.238, f32[512]{0:T(512)S(1)} %bitcast.225, f32[512]{0:T(512)S(1)} %broadcast_multiply_fusion, ...), kind=kLoop, calls=%fused_computation.129 | loop fusion | flops 14937600 | bytes 51200 | tf_op jit(solution)/shard_map/eval_jaxpr/reduce_sum | solution.py:61
  56.0 0.6 %fusion.90 = f32[3,512]{1,0:T(4,128)} fusion(f32[1,512]{1,0:T(1,128)S(1)} %bitcast.211, f32[1,512]{1,0:T(1,128)S(1)} %bitcast.212, f32[1,512]{1,0:T(1,128)S(1)} %bitcast.210, f32[1,512]{1,0:T(1,128)S(1)} %bitcast.220, f32[1,512]{1,0:T(1,128)S(1)} %bitcast.219, f32[1,512]{1,0:T(1,128)S(1)} %bitcast.221, f32[1,512]{1,0:T(1,128)S(1)} %bitcast.217, ...), kind=kLoop, calls=%fused_computation.188 | loop fusion | flops 16896 | bytes 30720 | tf_op jit(solution)/shard_map/eval_jaxpr/add | solution.py:61
  (94 shorter events, 5.2 us)
Async XLA Ops:
  0.6 36.2 %copy-start = (bf16[128,256]{1,0:T(8,128)(2,1)S(1)}, bf16[128,256]{1,0:T(8,128)(2,1)}, u32[]{:S(2)}) copy-start(bf16[128,256]{1,0:T(8,128)(2,1)} %param.23) | copy-start | bytes 196612
  0.6 0.7 %copy-start.10 = (s32[128]{0:T(128)S(1)}, s32[128]{0:T(128)}, u32[]{:S(2)}) copy-start(s32[128]{0:T(128)} %param.14) | copy-start | bytes 1540
  0.7 0.7 %copy-start.4 = (f32[3,128]{1,0:T(4,128)S(1)}, f32[3,128]{1,0:T(4,128)}, u32[]{:S(2)}) copy-start(f32[3,128]{1,0:T(4,128)} %param.13) | copy-start | bytes 4612
  1.3 0.7 %copy-start.1 = (f32[3,512]{1,0:T(4,128)S(1)}, f32[3,512]{1,0:T(4,128)}, u32[]{:S(2)}) copy-start(f32[3,512]{1,0:T(4,128)} %param.18) | copy-start | bytes 18436
  1.4 0.7 %copy-start.2 = (f32[512]{0:T(512)S(1)}, f32[512]{0:T(512)}, u32[]{:S(2)}) copy-start(f32[512]{0:T(512)} %param.19) | copy-start | bytes 6148
  1.4 3.8 %collective-permute-start = (f32[5,128]{1,0:T(8,128)S(1)}, f32[5,128]{1,0:T(8,128)S(1)}, u32[]{:S(2)}, u32[]{:S(2)}) collective-permute-start(f32[5,128]{1,0:T(8,128)S(1)} %pad_maximum_fusion.2), channel_id=1, source_target_pairs={{0,2},{2,0},{4,6},{6,4},{8,10},{10,8},{12,14},{14,12},{16,18},{18,... | collective-permute-start | bytes 7688 | tf_op jit(solution)/shard_map/ppermute | solution.py:16
  2.1 3.1 %copy-start.5 = (s32[128,4]{0,1:T(4,128)S(1)}, s32[128,4]{0,1:T(4,128)}, u32[]{:S(2)}) copy-start(s32[128,4]{0,1:T(4,128)} %param.17) | copy-start | bytes 6148
  2.1 3.1 %copy-start.6 = (s32[128,4]{0,1:T(4,128)S(1)}, s32[128,4]{0,1:T(4,128)}, u32[]{:S(2)}) copy-start(s32[128,4]{0,1:T(4,128)} %param.16) | copy-start | bytes 6148
  2.1 6.9 %collective-permute-start.2 = (f32[4,512]{1,0:T(4,128)S(1)}, f32[4,512]{1,0:T(4,128)S(1)}, u32[]{:S(2)}, u32[]{:S(2)}) collective-permute-start(f32[4,512]{1,0:T(4,128)S(1)} %pad_maximum_fusion.1), channel_id=1, source_target_pairs={{0,8},{2,10},{4,12},{6,14},{8,0},{10,2},{12,4},{14,6},{16,24},{18,... | collective-permute-start | bytes 24584 | tf_op jit(solution)/shard_map/ppermute | solution.py:16
  5.3 3.7 %collective-permute-start.1 = (f32[5,256]{1,0:T(8,128)S(1)}, f32[5,256]{1,0:T(8,128)S(1)}, u32[]{:S(2)}, u32[]{:S(2)}) collective-permute-start(f32[5,256]{1,0:T(8,128)S(1)} %maximum_select_fusion.6), channel_id=1, source_target_pairs={{0,4},{2,6},{4,0},{6,2},{8,12},{10,14},{12,8},{14,10},{16,20},{18,... | collective-permute-start | bytes 15368 | tf_op jit(solution)/shard_map/ppermute | solution.py:16
  9.0 4.9 %collective-permute-start.3 = (f32[4,1024]{1,0:T(4,128)S(1)}, f32[4,1024]{1,0:T(4,128)S(1)}, u32[]{:S(2)}, u32[]{:S(2)}) collective-permute-start(f32[4,1024]{1,0:T(4,128)S(1)} %maximum_select_fusion.5), channel_id=1, source_target_pairs={{0,16},{2,18},{4,20},{6,22},{8,24},{10,26},{12,28},{14,30},{16,0},... | collective-permute-start | bytes 49160 | tf_op jit(solution)/shard_map/ppermute | solution.py:16
  17.8 4.0 %collective-permute-start.4 = (f32[4,512]{1,0:T(4,128)S(1)}, f32[4,512]{1,0:T(4,128)S(1)}, u32[]{:S(2)}, u32[]{:S(2)}) collective-permute-start(f32[4,512]{1,0:T(4,128)S(1)} %fusion.88), channel_id=1, source_target_pairs={{0,1},{1,0},{2,3},{3,2},{4,5},{5,4},{6,7},{7,6},{8,9},{9,8},{10,11... | collective-permute-start | bytes 24584 | tf_op jit(solution)/shard_map/ppermute | solution.py:28
  20.0 2.0 %copy-start.3 = (bf16[128,128]{1,0:T(8,128)(2,1)S(1)}, bf16[128,128]{1,0:T(8,128)(2,1)}, u32[]{:S(2)}) copy-start(bf16[128,128]{1,0:T(8,128)(2,1)} %param.22) | copy-start | bytes 98308
  21.9 1.2 %collective-permute-start.5 = (f32[4,512]{1,0:T(4,128)S(1)}, f32[4,512]{1,0:T(4,128)S(1)}, u32[]{:S(2)}, u32[]{:S(2)}) collective-permute-start(f32[4,512]{1,0:T(4,128)S(1)} %fusion.120), channel_id=1, source_target_pairs={{0,2},{2,0},{4,6},{6,4},{8,10},{10,8},{12,14},{14,12},{16,18},{18,... | collective-permute-start | bytes 24584 | tf_op jit(solution)/shard_map/ppermute | solution.py:28
  22.0 2.8 %copy-start.7 = (bf16[8,128]{1,0:T(8,128)(2,1)S(1)}, bf16[8,128]{1,0:T(8,128)(2,1)}, u32[]{:S(2)}) copy-start(bf16[8,128]{1,0:T(8,128)(2,1)} %param.20) | copy-start | bytes 6148
  23.2 3.7 %collective-permute-start.6 = (f32[4,512]{1,0:T(4,128)S(1)}, f32[4,512]{1,0:T(4,128)S(1)}, u32[]{:S(2)}, u32[]{:S(2)}) collective-permute-start(f32[4,512]{1,0:T(4,128)S(1)} %fusion.122), channel_id=1, source_target_pairs={{0,4},{2,6},{4,0},{6,2},{8,12},{10,14},{12,8},{14,10},{16,20},{18,... | collective-permute-start | bytes 24584 | tf_op jit(solution)/shard_map/ppermute | solution.py:28
  26.9 0.7 %copy-start.9 = (f32[256]{0:T(256)S(1)}, f32[256]{0:T(256)}, u32[]{:S(2)}) copy-start(f32[256]{0:T(256)} %param.24) | copy-start | bytes 3076
  27.0 3.8 %collective-permute-start.7 = (f32[6,512]{1,0:T(8,128)S(1)}, f32[6,512]{1,0:T(8,128)S(1)}, u32[]{:S(2)}, u32[]{:S(2)}) collective-permute-start(f32[6,512]{1,0:T(8,128)S(1)} %pad_maximum_fusion), channel_id=1, source_target_pairs={{0,8},{2,10},{4,12},{6,14},{8,0},{10,2},{12,4},{14,6},{16,24},{18,... | collective-permute-start | bytes 36872 | tf_op jit(solution)/shard_map/ppermute | solution.py:16
  27.6 5.7 %copy-start.11 = (f32[128]{0:T(128)S(1)}, f32[128]{0:T(128)}, u32[]{:S(2)}) copy-start(f32[128]{0:T(128)} %param.21) | copy-start | bytes 1540
  30.8 5.2 %collective-permute-start.8 = (f32[6,1024]{1,0:T(8,128)S(1)}, f32[6,1024]{1,0:T(8,128)S(1)}, u32[]{:S(2)}, u32[]{:S(2)}) collective-permute-start(f32[6,1024]{1,0:T(8,128)S(1)} %maximum_select_fusion.2), channel_id=1, source_target_pairs={{0,16},{2,18},{4,20},{6,22},{8,24},{10,26},{12,28},{14,30},{16,0},... | collective-permute-start | bytes 73736 | tf_op jit(solution)/shard_map/ppermute | solution.py:16
  38.4 1.2 %collective-permute-start.9 = (f32[2048]{0:T(1024)S(1)}, f32[2048]{0:T(1024)S(1)}, u32[]{:S(2)}, u32[]{:S(2)}) collective-permute-start(f32[2048]{0:T(1024)S(1)} %fusion.91), channel_id=1, source_target_pairs={{0,2},{2,0},{4,6},{6,4},{8,10},{10,8},{12,14},{14,12},{16,18},{18,... | collective-permute-start | bytes 24584 | tf_op jit(solution)/shard_map/ppermute | solution.py:28
  39.7 3.7 %collective-permute-start.10 = (f32[2048]{0:T(1024)S(1)}, f32[2048]{0:T(1024)S(1)}, u32[]{:S(2)}, u32[]{:S(2)}) collective-permute-start(f32[2048]{0:T(1024)S(1)} %add.240), channel_id=1, source_target_pairs={{0,4},{2,6},{4,0},{6,2},{8,12},{10,14},{12,8},{14,10},{16,20},{18,... | collective-permute-start | bytes 24584 | tf_op jit(solution)/shard_map/ppermute | solution.py:28
  43.3 3.7 %collective-permute-start.11 = (f32[2048]{0:T(1024)S(1)}, f32[2048]{0:T(1024)S(1)}, u32[]{:S(2)}, u32[]{:S(2)}) collective-permute-start(f32[2048]{0:T(1024)S(1)} %add.241), channel_id=1, source_target_pairs={{0,8},{2,10},{4,12},{6,14},{8,0},{10,2},{12,4},{14,6},{16,24},{18,... | collective-permute-start | bytes 24584 | tf_op jit(solution)/shard_map/ppermute | solution.py:28
  47.0 4.5 %collective-permute-start.12 = (f32[2048]{0:T(1024)S(1)}, f32[2048]{0:T(1024)S(1)}, u32[]{:S(2)}, u32[]{:S(2)}) collective-permute-start(f32[2048]{0:T(1024)S(1)} %add.242), channel_id=1, source_target_pairs={{0,16},{2,18},{4,20},{6,22},{8,24},{10,26},{12,28},{14,30},{16,0},... | collective-permute-start | bytes 24584 | tf_op jit(solution)/shard_map/ppermute | solution.py:162
  (1 other events, 0.7 us)

commit v16 on v14

--- a/solution.py
+++ b/solution.py
@@ -97,10 +97,15 @@
         axis=0,
     )
     near = gather_doubling(own, "blk", 1, low_blocks)
-    mm_some = gather_doubling(
-        jnp.concatenate([mm_pos, mm_charge[None, :]], axis=0), "blk", low_blocks, blocks
-    )
-    partial = potential_pass(near[:3], mm_some)
+    mm_some = jnp.concatenate([mm_pos, mm_charge[None, :]], axis=0)
+    step = low_blocks
+    while step < blocks // 2:
+        mm_some = jnp.concatenate(
+            [mm_some, lax.ppermute(mm_some, "blk", [(i, i ^ step) for i in range(blocks)])], -1
+        )
+        step *= 2
+    arriving = lax.ppermute(mm_some, "blk", [(i, i ^ step) for i in range(blocks)])
+    partial = potential_pass(near[:3], mm_some) + potential_pass(near[:3], arriving)
     total = sum_butterfly(sum_butterfly(partial, "rep"), "blk", low_blocks)
     pull = lax.dynamic_slice_in_dim(total[1:4], (me % low_blocks) * rows, rows, axis=1)
     known = gather_doubling(

time: 55.5 us -> 55.4 us (level)
  starting transfers between devices: 18.1 us -> 16.6 us
  local copies, waits for them, and re-layouts: 0.99 us -> 2.35 us
  waiting for transfers between devices: 22.4 us -> 21.8 us
  other arithmetic: 8.93 us -> 9.5 us
    ppermute x6 -> x4, starting transfers between devices: 11 us -> 4.48 us  [gather_doubling(): other = lax.ppermute(x, axis, [(i, i ^ step) for i in range(n)])]
    ppermute x0 -> x2, starting transfers between devices: none -> 5.68 us  [on_device(): lax.ppermute(mm_some, 'blk', [(i, i ^ step) for i in range(blocks)])]
    squeeze x8 -> x4, local copies, waits for them, and re-layouts: 0.07 us -> 1.45 us  [potential_pass(): lax.scan(body, jnp.zeros((4, qm_some.shape[1]), jnp.float32), stacked)]
    ppermute x6 -> x4, waiting for transfers between devices: 10.1 us -> 8.75 us  [gather_doubling(): other = lax.ppermute(x, axis, [(i, i ^ step) for i in range(n)])]
    ppermute x1, starting transfers between devices: 2.18 us -> 1.31 us  [on_device(): lax.ppermute(part, 'blk', [(i, i ^ blocks // 2) for i in range(blocks)])]
    ppermute x1, waiting for transfers between devices: 2.34 us -> 3.21 us  [on_device(): lax.ppermute(part, 'blk', [(i, i ^ blocks // 2) for i in range(blocks)])]
    concatenate x2, other arithmetic: 0.02 us -> 0.61 us  [the longest x1 0.6 us: on_device(): jnp.concatenate([mm_some, lax.ppermute(mm_some, 'blk', [(i, i ^ step) for...]
  transfers between devices with their start and end apart: 13 -> 13, of which waited for: 10 -> 9; matrix products, arithmetic and copies ran while one was open for 2% -> 8% of each run, Pallas kernels for 0% -> 0%
where the time goes in v16:
time: 55.4 us; the launch traced here: 55 us
  waiting for transfers between devices  21.8 us (39%)
  starting transfers between devices  16.6 us (30%)
  other arithmetic  9.5 us (17%)
  between operations  3.05 us (6%)
  local copies, waits for them, and re-layouts  2.35 us (4%)
  matrix products  1.5 us (3%)
    ppermute x6, waiting for transfers between devices, sum_butterfly(): x = x + lax.ppermute(x, axis, [(i, i ^ step) for i in range(n)])  9.84 us
    ppermute x4, waiting for transfers between devices, gather_doubling(): other = lax.ppermute(x, axis, [(i, i ^ step) for i in range(n)])  8.75 us
    ppermute x2, starting transfers between devices, on_device(): lax.ppermute(mm_some, 'blk', [(i, i ^ step) for i in range(blocks)])  5.68 us
    ppermute x6, starting transfers between devices, sum_butterfly(): x = x + lax.ppermute(x, axis, [(i, i ^ step) for i in range(n)])  5.09 us
    ppermute x4, starting transfers between devices, gather_doubling(): other = lax.ppermute(x, axis, [(i, i ^ step) for i in range(n)])  4.48 us
    reduce_sum x4, other arithmetic, body(): jnp.sum(weighted, axis=0)  3.21 us
    ppermute x1, waiting for transfers between devices, on_device(): lax.ppermute(part, 'blk', [(i, i ^ blocks // 2) for i in range(blocks)])  3.21 us
    reduce_sum x4, other arithmetic, body(): jnp.sum(d[c] * weight, axis=0)  3.19 us
  transfers between devices with their start and end apart: 13, of which 9 were waited for; matrix products, arithmetic and copies ran while one was open for 8% of the time, Pallas kernels for 0%

profile of v16, /device:TPU:0, one launch (start us, length us, event | category | flops | bytes accessed | tf_op | source)
XLA Modules:
  0.0 55.0 jit_solution(3273036680005425606)
XLA Ops:
  2.1 3.1 %collective-permute-start.2 = (f32[4,512]{1,0:T(4,128)S(1)}, f32[4,512]{1,0:T(4,128)S(1)}, u32[]{:S(2)}, u32[]{:S(2)}) collective-permute-start(f32[4,512]{1,0:T(4,128)S(1)} %pad_maximum_fusion.2), channel_id=1, source_target_pairs={{0,8},{2,10},{4,12},{6,14},{8,0},{10,2},{12,4},{14,6},{16,24},{18,... | collective-permute-start | bytes 24584 | tf_op jit(solution)/shard_map/ppermute | solution.py:104
  5.2 1.6 %collective-permute-start.1 = (f32[5,256]{1,0:T(8,128)S(1)}, f32[5,256]{1,0:T(8,128)S(1)}, u32[]{:S(2)}, u32[]{:S(2)}) collective-permute-start(f32[5,256]{1,0:T(8,128)S(1)} %maximum_select_fusion.3), channel_id=1, source_target_pairs={{0,4},{2,6},{4,0},{6,2},{8,12},{10,14},{12,8},{14,10},{16,20},{18,... | collective-permute-start | bytes 15368 | tf_op jit(solution)/shard_map/ppermute | solution.py:16
  6.8 2.1 %collective-permute-done.1 = f32[5,256]{1,0:T(8,128)S(1)} collective-permute-done((f32[5,256]{1,0:T(8,128)S(1)}, f32[5,256]{1,0:T(8,128)S(1)}, u32[]{:S(2)}, u32[]{:S(2)}) %collective-permute-start.1) | collective-permute-done | bytes 5152 | tf_op jit(solution)/shard_map/ppermute | solution.py:16
  9.6 2.6 %collective-permute-start.3 = (f32[4,1024]{1,0:T(4,128)}, f32[4,1024]{1,0:T(4,128)S(1)}, u32[]{:S(2)}, u32[]{:S(2)}) collective-permute-start(f32[4,1024]{1,0:T(4,128)} %pad_maximum_fusion), channel_id=1, source_target_pairs={{0,16},{2,18},{4,20},{6,22},{8,24},{10,26},{12,28},{14,30},{16,0},... | collective-permute-start | bytes 49160 | tf_op jit(solution)/shard_map/ppermute | solution.py:107
  12.2 3.1 %while.33 = (s32[]{:T(128)}, f32[4,512]{1,0:T(4,128)S(1)}, f32[1,512]{1,0:T(1,128)S(1)}, f32[2,512,4]{1,2,0:T(4,128)}, f32[1,512]{1,0:T(1,128)S(1)}, /*index=5*/f32[1,512]{1,0:T(1,128)S(1)}, s32[]{:T(128)}, s32[]{:T(128)}) while((s32[]{:T(128)}, f32[4,512]{1,0:T(4,128)S(1)}, f32[1,512]{1,0:T(1,128)S(1)}, f32[2,512,4]{1,2,0:T(4,128)}, ...), condition=%wide.region_5.6_spmd.clone, body=%wide.region_0.5_spmd.clone.sunk | while | flops 4988931 | bytes 79979 | solution.py:48
  12.9 0.8 %multiply_reduce_fusion.8 = (f32[512]{0:T(512)S(1)}, f32[512]{0:T(512)S(1)}, f32[512]{0:T(512)S(1)}, f32[512]{0:T(512)S(1)}) fusion(f32[512]{0:T(512)S(1)} %bitcast.178, f32[512]{0:T(512)S(1)} %bitcast.179, f32[512]{0:T(512)S(1)} %bitcast.191, f32[512]{0:T(512)S(1)} %bitcast.180, f32[512]{0:T(512)S(1)} %bitcast.193, f32[512]{0:T(512)S(1)} %bitcast.177, ...), kind=kLoop, calls=%fused_computation.1.clone.1 | loop fusion | flops 4978688 | bytes 22528 | tf_op jit(solution)/shard_map/while/body/eval_jaxpr/reduce_sum | solution.py:43
  14.5 0.8 %multiply_reduce_fusion.8 = (f32[512]{0:T(512)S(1)}, f32[512]{0:T(512)S(1)}, f32[512]{0:T(512)S(1)}, f32[512]{0:T(512)S(1)}) fusion(f32[512]{0:T(512)S(1)} %bitcast.178, f32[512]{0:T(512)S(1)} %bitcast.179, f32[512]{0:T(512)S(1)} %bitcast.191, f32[512]{0:T(512)S(1)} %bitcast.180, f32[512]{0:T(512)S(1)} %bitcast.193, f32[512]{0:T(512)S(1)} %bitcast.177, ...), kind=kLoop, calls=%fused_computation.1.clone.1 | loop fusion | flops 4978688 | bytes 22528 | tf_op jit(solution)/shard_map/while/body/eval_jaxpr/reduce_sum | solution.py:43
  15.3 1.8 %while.34 = (s32[]{:T(128)}, f32[4,512]{1,0:T(4,128)S(1)}, f32[1,512]{1,0:T(1,128)S(1)}, f32[2,512,4]{1,2,0:T(4,128)S(1)}, f32[1,512]{1,0:T(1,128)S(1)}, /*index=5*/f32[1,512]{1,0:T(1,128)S(1)}, s32[]{:T(128)}, s32[]{:T(128)}) while((s32[]{:T(128)}, f32[4,512]{1,0:T(4,128)S(1)}, f32[1,512]{1,0:T(1,128)S(1)}, ...), condition=%wide.region_11.12_spmd.clone, body=%wide.region_6.11_spmd.clone.sunk | while | flops 4988931 | bytes 79979 | solution.py:48
  15.4 0.8 %multiply_reduce_fusion.9 = (f32[512]{0:T(512)S(1)}, f32[512]{0:T(512)S(1)}, f32[512]{0:T(512)S(1)}, f32[512]{0:T(512)S(1)}) fusion(f32[512]{0:T(512)S(1)} %bitcast.182, f32[512]{0:T(512)S(1)} %bitcast.183, f32[512]{0:T(512)S(1)} %bitcast.192, f32[512]{0:T(512)S(1)} %bitcast.184, f32[512]{0:T(512)S(1)} %bitcast.194, f32[512]{0:T(512)S(1)} %bitcast.181, ...), kind=kLoop, calls=%fused_computation.18.clone.1 | loop fusion | flops 4978688 | bytes 22528 | tf_op jit(solution)/shard_map/while/body/eval_jaxpr/reduce_sum | solution.py:43
  16.3 0.8 %multiply_reduce_fusion.9 = (f32[512]{0:T(512)S(1)}, f32[512]{0:T(512)S(1)}, f32[512]{0:T(512)S(1)}, f32[512]{0:T(512)S(1)}) fusion(f32[512]{0:T(512)S(1)} %bitcast.182, f32[512]{0:T(512)S(1)} %bitcast.183, f32[512]{0:T(512)S(1)} %bitcast.192, f32[512]{0:T(512)S(1)} %bitcast.184, f32[512]{0:T(512)S(1)} %bitcast.194, f32[512]{0:T(512)S(1)} %bitcast.181, ...), kind=kLoop, calls=%fused_computation.18.clone.1 | loop fusion | flops 4978688 | bytes 22528 | tf_op jit(solution)/shard_map/while/body/eval_jaxpr/reduce_sum | solution.py:43
  17.1 1.6 %collective-permute-start.4 = (f32[4,512]{1,0:T(4,128)S(1)}, f32[4,512]{1,0:T(4,128)S(1)}, u32[]{:S(2)}, u32[]{:S(2)}) collective-permute-start(f32[4,512]{1,0:T(4,128)S(1)} %add.162), channel_id=1, source_target_pairs={{0,1},{1,0},{2,3},{3,2},{4,5},{5,4},{6,7},{7,6},{8,9},{9,8},{10,11... | collective-permute-start | bytes 24584 | tf_op jit(solution)/shard_map/ppermute | solution.py:28
  21.3 1.1 %collective-permute-done.5 = f32[4,512]{1,0:T(4,128)S(1)} collective-permute-done((f32[4,512]{1,0:T(4,128)S(1)}, f32[4,512]{1,0:T(4,128)S(1)}, u32[]{:S(2)}, u32[]{:S(2)}) %collective-permute-start.5) | collective-permute-done | bytes 8224 | tf_op jit(solution)/shard_map/ppermute | solution.py:28
  22.5 1.5 %collective-permute-start.6 = (f32[4,512]{1,0:T(4,128)S(1)}, f32[4,512]{1,0:T(4,128)S(1)}, u32[]{:S(2)}, u32[]{:S(2)}) collective-permute-start(f32[4,512]{1,0:T(4,128)S(1)} %add.164), channel_id=1, source_target_pairs={{0,4},{2,6},{4,0},{6,2},{8,12},{10,14},{12,8},{14,10},{16,20},{18,... | collective-permute-start | bytes 24584 | tf_op jit(solution)/shard_map/ppermute | solution.py:28
  24.0 2.1 %collective-permute-done.6 = f32[4,512]{1,0:T(4,128)S(1)} collective-permute-done((f32[4,512]{1,0:T(4,128)S(1)}, f32[4,512]{1,0:T(4,128)S(1)}, u32[]{:S(2)}, u32[]{:S(2)}) %collective-permute-start.6) | collective-permute-done | bytes 8224 | tf_op jit(solution)/shard_map/ppermute | solution.py:28
  26.8 3.1 %collective-permute-done.7 = f32[6,512]{1,0:T(8,128)S(1)} collective-permute-done((f32[6,512]{1,0:T(8,128)S(1)}, f32[6,512]{1,0:T(8,128)S(1)}, u32[]{:S(2)}, u32[]{:S(2)}) %collective-permute-start.7) | collective-permute-done | bytes 12320 | tf_op jit(solution)/shard_map/ppermute | solution.py:16
  30.0 1.7 %collective-permute-start.8 = (f32[6,1024]{1,0:T(8,128)S(1)}, f32[6,1024]{1,0:T(8,128)S(1)}, u32[]{:S(2)}, u32[]{:S(2)}) collective-permute-start(f32[6,1024]{1,0:T(8,128)S(1)} %maximum_select_fusion.1), channel_id=1, source_target_pairs={{0,16},{2,18},{4,20},{6,22},{8,24},{10,26},{12,28},{14,30},{16,0},... | collective-permute-start | bytes 73736 | tf_op jit(solution)/shard_map/ppermute | solution.py:16
  31.7 3.5 %collective-permute-done.8 = f32[6,1024]{1,0:T(8,128)S(1)} collective-permute-done((f32[6,1024]{1,0:T(8,128)S(1)}, f32[6,1024]{1,0:T(8,128)S(1)}, u32[]{:S(2)}, u32[]{:S(2)}) %collective-permute-start.8) | collective-permute-done | bytes 24608 | tf_op jit(solution)/shard_map/ppermute | solution.py:16
  37.7 1.2 %collective-permute-done.9 = f32[2048]{0:T(1024)S(1)} collective-permute-done((f32[2048]{0:T(1024)S(1)}, f32[2048]{0:T(1024)S(1)}, u32[]{:S(2)}, u32[]{:S(2)}) %collective-permute-start.9) | collective-permute-done | bytes 8224 | tf_op jit(solution)/shard_map/ppermute | solution.py:28
  38.9 1.5 %collective-permute-start.10 = (f32[2048]{0:T(1024)S(1)}, f32[2048]{0:T(1024)S(1)}, u32[]{:S(2)}, u32[]{:S(2)}) collective-permute-start(f32[2048]{0:T(1024)S(1)} %add.182), channel_id=1, source_target_pairs={{0,4},{2,6},{4,0},{6,2},{8,12},{10,14},{12,8},{14,10},{16,20},{18,... | collective-permute-start | bytes 24584 | tf_op jit(solution)/shard_map/ppermute | solution.py:28
  40.4 2.1 %collective-permute-done.10 = f32[2048]{0:T(1024)S(1)} collective-permute-done((f32[2048]{0:T(1024)S(1)}, f32[2048]{0:T(1024)S(1)}, u32[]{:S(2)}, u32[]{:S(2)}) %collective-permute-start.10) | collective-permute-done | bytes 8224 | tf_op jit(solution)/shard_map/ppermute | solution.py:28
  42.9 3.3 %collective-permute-done.11 = f32[2048]{0:T(1024)S(1)} collective-permute-done((f32[2048]{0:T(1024)S(1)}, f32[2048]{0:T(1024)S(1)}, u32[]{:S(2)}, u32[]{:S(2)}) %collective-permute-start.11) | collective-permute-done | bytes 8224 | tf_op jit(solution)/shard_map/ppermute | solution.py:28
  46.2 1.3 %collective-permute-start.12 = (f32[2048]{0:T(1024)S(1)}, f32[2048]{0:T(1024)S(1)}, u32[]{:S(2)}, u32[]{:S(2)}) collective-permute-start(f32[2048]{0:T(1024)S(1)} %add.184), channel_id=1, source_target_pairs={{0,16},{2,18},{4,20},{6,22},{8,24},{10,26},{12,28},{14,30},{16,0},... | collective-permute-start | bytes 24584 | tf_op jit(solution)/shard_map/ppermute | solution.py:167
  47.5 3.2 %collective-permute-done.12 = f32[2048]{0:T(1024)S(1)} collective-permute-done((f32[2048]{0:T(1024)S(1)}, f32[2048]{0:T(1024)S(1)}, u32[]{:S(2)}, u32[]{:S(2)}) %collective-permute-start.12) | collective-permute-done | bytes 8224 | tf_op jit(solution)/shard_map/ppermute | solution.py:167
  50.8 3.6 %while.35 = (s32[]{:T(128)}, f32[3,512]{1,0:T(4,128)S(1)}, f32[4,512,4]{1,2,0:T(4,128)S(1)}, f32[3,512]{1,0:T(4,128)S(1)}, f32[512]{0:T(512)S(1)}, /*index=5*/s32[]{:T(128)}, s32[]{:T(128)}) while((s32[]{:T(128)}, f32[3,512]{1,0:T(4,128)S(1)}, f32[4,512,4]{1,2,0:T(4,128)S(1)}, f32[3,512]{1,0:T(4,128)S(1)}, f32[512]{0:T(512)S(1)}, ...), condition=%wide.region_21.22_spmd.clone, body=%wide.region_17.21_spmd.clone.sunk | while | flops 4985347 | bytes 86115 | solution.py:63
  (116 shorter events, 11.8 us)
Async XLA Ops:
  0.6 35.4 %copy-start = (bf16[128,256]{1,0:T(8,128)(2,1)S(1)}, bf16[128,256]{1,0:T(8,128)(2,1)}, u32[]{:S(2)}) copy-start(bf16[128,256]{1,0:T(8,128)(2,1)} %param.29) | copy-start | bytes 196612
  0.6 0.7 %copy-start.11 = (s32[128]{0:T(128)S(1)}, s32[128]{0:T(128)}, u32[]{:S(2)}) copy-start(s32[128]{0:T(128)} %param.20) | copy-start | bytes 1540
  0.7 0.7 %copy-start.5 = (f32[3,128]{1,0:T(4,128)S(1)}, f32[3,128]{1,0:T(4,128)}, u32[]{:S(2)}) copy-start(f32[3,128]{1,0:T(4,128)} %param.19) | copy-start | bytes 4612
  1.3 0.7 %copy-start.1 = (f32[3,512]{1,0:T(4,128)S(1)}, f32[3,512]{1,0:T(4,128)}, u32[]{:S(2)}) copy-start(f32[3,512]{1,0:T(4,128)} %param.24) | copy-start | bytes 18436
  1.4 3.8 %collective-permute-start = (f32[5,128]{1,0:T(8,128)S(1)}, f32[5,128]{1,0:T(8,128)S(1)}, u32[]{:S(2)}, u32[]{:S(2)}) collective-permute-start(f32[5,128]{1,0:T(8,128)S(1)} %pad_maximum_fusion.3), channel_id=1, source_target_pairs={{0,2},{2,0},{4,6},{6,4},{8,10},{10,8},{12,14},{14,12},{16,18},{18,... | collective-permute-start | bytes 7688 | tf_op jit(solution)/shard_map/ppermute | solution.py:16
  2.1 3.1 %copy-start.6 = (s32[128,4]{0,1:T(4,128)S(1)}, s32[128,4]{0,1:T(4,128)}, u32[]{:S(2)}) copy-start(s32[128,4]{0,1:T(4,128)} %param.23) | copy-start | bytes 6148
  2.1 3.1 %copy-start.7 = (s32[128,4]{0,1:T(4,128)S(1)}, s32[128,4]{0,1:T(4,128)}, u32[]{:S(2)}) copy-start(s32[128,4]{0,1:T(4,128)} %param.22) | copy-start | bytes 6148
  2.1 6.9 %collective-permute-start.2 = (f32[4,512]{1,0:T(4,128)S(1)}, f32[4,512]{1,0:T(4,128)S(1)}, u32[]{:S(2)}, u32[]{:S(2)}) collective-permute-start(f32[4,512]{1,0:T(4,128)S(1)} %pad_maximum_fusion.2), channel_id=1, source_target_pairs={{0,8},{2,10},{4,12},{6,14},{8,0},{10,2},{12,4},{14,6},{16,24},{18,... | collective-permute-start | bytes 24584 | tf_op jit(solution)/shard_map/ppermute | solution.py:104
  5.2 3.7 %collective-permute-start.1 = (f32[5,256]{1,0:T(8,128)S(1)}, f32[5,256]{1,0:T(8,128)S(1)}, u32[]{:S(2)}, u32[]{:S(2)}) collective-permute-start(f32[5,256]{1,0:T(8,128)S(1)} %maximum_select_fusion.3), channel_id=1, source_target_pairs={{0,4},{2,6},{4,0},{6,2},{8,12},{10,14},{12,8},{14,10},{16,20},{18,... | collective-permute-start | bytes 15368 | tf_op jit(solution)/shard_map/ppermute | solution.py:16
  9.6 5.7 %collective-permute-start.3 = (f32[4,1024]{1,0:T(4,128)}, f32[4,1024]{1,0:T(4,128)S(1)}, u32[]{:S(2)}, u32[]{:S(2)}) collective-permute-start(f32[4,1024]{1,0:T(4,128)} %pad_maximum_fusion), channel_id=1, source_target_pairs={{0,16},{2,18},{4,20},{6,22},{8,24},{10,26},{12,28},{14,30},{16,0},... | collective-permute-start | bytes 49160 | tf_op jit(solution)/shard_map/ppermute | solution.py:107
  17.1 4.1 %collective-permute-start.4 = (f32[4,512]{1,0:T(4,128)S(1)}, f32[4,512]{1,0:T(4,128)S(1)}, u32[]{:S(2)}, u32[]{:S(2)}) collective-permute-start(f32[4,512]{1,0:T(4,128)S(1)} %add.162), channel_id=1, source_target_pairs={{0,1},{1,0},{2,3},{3,2},{4,5},{5,4},{6,7},{7,6},{8,9},{9,8},{10,11... | collective-permute-start | bytes 24584 | tf_op jit(solution)/shard_map/ppermute | solution.py:28
  19.3 2.0 %copy-start.3 = (bf16[128,128]{1,0:T(8,128)(2,1)S(1)}, bf16[128,128]{1,0:T(8,128)(2,1)}, u32[]{:S(2)}) copy-start(bf16[128,128]{1,0:T(8,128)(2,1)} %param.28) | copy-start | bytes 98308
  21.2 1.2 %collective-permute-start.5 = (f32[4,512]{1,0:T(4,128)S(1)}, f32[4,512]{1,0:T(4,128)S(1)}, u32[]{:S(2)}, u32[]{:S(2)}) collective-permute-start(f32[4,512]{1,0:T(4,128)S(1)} %add.163), channel_id=1, source_target_pairs={{0,2},{2,0},{4,6},{6,4},{8,10},{10,8},{12,14},{14,12},{16,18},{18,... | collective-permute-start | bytes 24584 | tf_op jit(solution)/shard_map/ppermute | solution.py:28
  21.3 2.7 %copy-start.8 = (bf16[8,128]{1,0:T(8,128)(2,1)S(1)}, bf16[8,128]{1,0:T(8,128)(2,1)}, u32[]{:S(2)}) copy-start(bf16[8,128]{1,0:T(8,128)(2,1)} %param.26) | copy-start | bytes 6148
  22.5 3.7 %collective-permute-start.6 = (f32[4,512]{1,0:T(4,128)S(1)}, f32[4,512]{1,0:T(4,128)S(1)}, u32[]{:S(2)}, u32[]{:S(2)}) collective-permute-start(f32[4,512]{1,0:T(4,128)S(1)} %add.164), channel_id=1, source_target_pairs={{0,4},{2,6},{4,0},{6,2},{8,12},{10,14},{12,8},{14,10},{16,20},{18,... | collective-permute-start | bytes 24584 | tf_op jit(solution)/shard_map/ppermute | solution.py:28
  26.1 0.7 %copy-start.9 = (f32[256]{0:T(256)S(1)}, f32[256]{0:T(256)}, u32[]{:S(2)}) copy-start(f32[256]{0:T(256)} %param.31) | copy-start | bytes 3076
  26.1 0.7 %copy-start.10 = (f32[256]{0:T(256)S(1)}, f32[256]{0:T(256)}, u32[]{:S(2)}) copy-start(f32[256]{0:T(256)} %param.30) | copy-start | bytes 3076
  26.2 3.8 %collective-permute-start.7 = (f32[6,512]{1,0:T(8,128)S(1)}, f32[6,512]{1,0:T(8,128)S(1)}, u32[]{:S(2)}, u32[]{:S(2)}) collective-permute-start(f32[6,512]{1,0:T(8,128)S(1)} %pad_maximum_fusion.1), channel_id=1, source_target_pairs={{0,8},{2,10},{4,12},{6,14},{8,0},{10,2},{12,4},{14,6},{16,24},{18,... | collective-permute-start | bytes 36872 | tf_op jit(solution)/shard_map/ppermute | solution.py:16
  26.8 4.9 %copy-start.12 = (f32[128]{0:T(128)S(1)}, f32[128]{0:T(128)}, u32[]{:S(2)}) copy-start(f32[128]{0:T(128)} %param.27) | copy-start | bytes 1540
  30.0 5.2 %collective-permute-start.8 = (f32[6,1024]{1,0:T(8,128)S(1)}, f32[6,1024]{1,0:T(8,128)S(1)}, u32[]{:S(2)}, u32[]{:S(2)}) collective-permute-start(f32[6,1024]{1,0:T(8,128)S(1)} %maximum_select_fusion.1), channel_id=1, source_target_pairs={{0,16},{2,18},{4,20},{6,22},{8,24},{10,26},{12,28},{14,30},{16,0},... | collective-permute-start | bytes 73736 | tf_op jit(solution)/shard_map/ppermute | solution.py:16
  37.6 1.2 %collective-permute-start.9 = (f32[2048]{0:T(1024)S(1)}, f32[2048]{0:T(1024)S(1)}, u32[]{:S(2)}, u32[]{:S(2)}) collective-permute-start(f32[2048]{0:T(1024)S(1)} %fusion.45), channel_id=1, source_target_pairs={{0,2},{2,0},{4,6},{6,4},{8,10},{10,8},{12,14},{14,12},{16,18},{18,... | collective-permute-start | bytes 24584 | tf_op jit(solution)/shard_map/ppermute | solution.py:28
  38.9 3.7 %collective-permute-start.10 = (f32[2048]{0:T(1024)S(1)}, f32[2048]{0:T(1024)S(1)}, u32[]{:S(2)}, u32[]{:S(2)}) collective-permute-start(f32[2048]{0:T(1024)S(1)} %add.182), channel_id=1, source_target_pairs={{0,4},{2,6},{4,0},{6,2},{8,12},{10,14},{12,8},{14,10},{16,20},{18,... | collective-permute-start | bytes 24584 | tf_op jit(solution)/shard_map/ppermute | solution.py:28
  42.5 3.7 %collective-permute-start.11 = (f32[2048]{0:T(1024)S(1)}, f32[2048]{0:T(1024)S(1)}, u32[]{:S(2)}, u32[]{:S(2)}) collective-permute-start(f32[2048]{0:T(1024)S(1)} %add.183), channel_id=1, source_target_pairs={{0,8},{2,10},{4,12},{6,14},{8,0},{10,2},{12,4},{14,6},{16,24},{18,... | collective-permute-start | bytes 24584 | tf_op jit(solution)/shard_map/ppermute | solution.py:28
  46.2 4.5 %collective-permute-start.12 = (f32[2048]{0:T(1024)S(1)}, f32[2048]{0:T(1024)S(1)}, u32[]{:S(2)}, u32[]{:S(2)}) collective-permute-start(f32[2048]{0:T(1024)S(1)} %add.184), channel_id=1, source_target_pairs={{0,16},{2,18},{4,20},{6,22},{8,24},{10,26},{12,28},{14,30},{16,0},... | collective-permute-start | bytes 24584 | tf_op jit(solution)/shard_map/ppermute | solution.py:167
  (2 other events, 1.4 us)

commit v17 on v16

--- a/solution.py
+++ b/solution.py
@@ -31,21 +31,17 @@
 
 
 def potential_pass(qm_some, mm_some):
-    chunks = mm_some.shape[1] // CHUNK
     cols = [qm_some[c][None, :] for c in range(3)]
-
-    def body(running, block):
+    total = jnp.zeros((4, qm_some.shape[1]), jnp.float32)
+    for lo in range(0, mm_some.shape[1], CHUNK):
+        block = mm_some[:, lo : lo + CHUNK].T
         d = [cols[c] - block[:, c : c + 1] for c in range(3)]
         inverse = lax.rsqrt(d[0] * d[0] + d[1] * d[1] + d[2] * d[2] + SOFTEN)
         weighted = inverse * block[:, 3:4]
         cubed = weighted * inverse * inverse
-        part = jnp.stack(
+        total = total + jnp.stack(
             [jnp.sum(weighted, axis=0)] + [jnp.sum(d[c] * cubed, axis=0) for c in range(3)]
         )
-        return running + part, None
-
-    stacked = jnp.transpose(mm_some.reshape(4, chunks, CHUNK), (1, 2, 0))
-    total, _ = lax.scan(body, jnp.zeros((4, qm_some.shape[1]), jnp.float32), stacked)
     return total
 
 

time: 55.4 us -> 56.5 us (1.020)
  starting transfers between devices: 16.6 us -> 18.3 us
  local copies, waits for them, and re-layouts: 2.35 us -> 1.75 us
    ppermute x2, waiting for transfers between devices: 0.01 us -> 2.04 us  [on_device(): lax.ppermute(mm_some, 'blk', [(i, i ^ step) for i in range(blocks)])]
    squeeze x4 -> x0, local copies, waits for them, and re-layouts: 1.45 us -> none  [potential_pass(): lax.scan(body, jnp.zeros((4, qm_some.shape[1]), jnp.float32), stacked)]
    ppermute x1, starting transfers between devices: 1.31 us -> 2.35 us  [on_device(): lax.ppermute(part, 'blk', [(i, i ^ blocks // 2) for i in range(blocks)])]
    ppermute x1, waiting for transfers between devices: 3.21 us -> 2.17 us  [on_device(): lax.ppermute(part, 'blk', [(i, i ^ blocks // 2) for i in range(blocks)])]
    ppermute x4, waiting for transfers between devices: 8.75 us -> 7.73 us  [gather_doubling(): other = lax.ppermute(x, axis, [(i, i ^ step) for i in range(n)])]
    unnamed x26, local copies, waits for them, and re-layouts: 0.21 us -> 1.06 us
    ppermute x4, starting transfers between devices: 4.48 us -> 5.15 us  [gather_doubling(): other = lax.ppermute(x, axis, [(i, i ^ step) for i in range(n)])]
    reduce_sum x4 -> x1, other arithmetic: 3.21 us -> 3.82 us  [potential_pass(): jnp.sum(weighted, axis=0)]
  transfers between devices with their start and end apart: 13 -> 13, of which waited for: 9 -> 10; matrix products, arithmetic and copies ran while one was open for 8% -> 2% of each run, Pallas kernels for 0% -> 0%
where the time goes in v17:
time: 56.5 us; the launch traced here: 56.2 us
  waiting for transfers between devices  21.9 us (39%)
  starting transfers between devices  18.3 us (32%)
  other arithmetic  9.52 us (17%)
  between operations  3.02 us (5%)
  local copies, waits for them, and re-layouts  1.75 us (3%)
  matrix products  1.5 us (3%)
    ppermute x6, waiting for transfers between devices, sum_butterfly(): x = x + lax.ppermute(x, axis, [(i, i ^ step) for i in range(n)])  9.96 us
    ppermute x4, waiting for transfers between devices, gather_doubling(): other = lax.ppermute(x, axis, [(i, i ^ step) for i in range(n)])  7.73 us
    ppermute x2, starting transfers between devices, on_device(): lax.ppermute(mm_some, 'blk', [(i, i ^ step) for i in range(blocks)])  5.74 us
    ppermute x4, starting transfers between devices, gather_doubling(): other = lax.ppermute(x, axis, [(i, i ^ step) for i in range(n)])  5.15 us
    ppermute x6, starting transfers between devices, sum_butterfly(): x = x + lax.ppermute(x, axis, [(i, i ^ step) for i in range(n)])  5.09 us
    reduce_sum x1, other arithmetic, potential_pass(): jnp.sum(weighted, axis=0)  3.82 us
    reduce_sum x4, other arithmetic, body(): jnp.sum(d[c] * weight, axis=0)  3.19 us
    ppermute x1, starting transfers between devices, on_device(): lax.ppermute(part, 'blk', [(i, i ^ blocks // 2) for i in range(blocks)])  2.35 us
  transfers between devices with their start and end apart: 13, of which 10 were waited for; matrix products, arithmetic and copies ran while one was open for 2% of the time, Pallas kernels for 0%

profile of v17, /device:TPU:0, one launch (start us, length us, event | category | flops | bytes accessed | tf_op | source)
XLA Modules:
  0.0 56.2 jit_solution(13071991354264430209)
XLA Ops:
  2.1 3.1 %collective-permute-start.2 = (f32[4,512]{1,0:T(4,128)S(1)}, f32[4,512]{1,0:T(4,128)S(1)}, u32[]{:S(2)}, u32[]{:S(2)}) collective-permute-start(f32[4,512]{1,0:T(4,128)S(1)} %pad_maximum_fusion.2), channel_id=1, source_target_pairs={{0,8},{2,10},{4,12},{6,14},{8,0},{10,2},{12,4},{14,6},{16,24},{18,... | collective-permute-start | bytes 24584 | tf_op jit(solution)/shard_map/ppermute | solution.py:100
  5.9 1.6 %collective-permute-start.1 = (f32[5,256]{1,0:T(8,128)S(1)}, f32[5,256]{1,0:T(8,128)S(1)}, u32[]{:S(2)}, u32[]{:S(2)}) collective-permute-start(f32[5,256]{1,0:T(8,128)S(1)} %maximum_select_fusion.3), channel_id=1, source_target_pairs={{0,4},{2,6},{4,0},{6,2},{8,12},{10,14},{12,8},{14,10},{16,20},{18,... | collective-permute-start | bytes 15368 | tf_op jit(solution)/shard_map/ppermute | solution.py:16
  7.5 2.1 %collective-permute-done.1 = f32[5,256]{1,0:T(8,128)S(1)} collective-permute-done((f32[5,256]{1,0:T(8,128)S(1)}, f32[5,256]{1,0:T(8,128)S(1)}, u32[]{:S(2)}, u32[]{:S(2)}) %collective-permute-start.1) | collective-permute-done | bytes 5152 | tf_op jit(solution)/shard_map/ppermute | solution.py:16
  9.7 2.7 %collective-permute-start.3 = (f32[4,1024]{1,0:T(4,128)S(1)}, f32[4,1024]{1,0:T(4,128)S(1)}, u32[]{:S(2)}, u32[]{:S(2)}) collective-permute-start(f32[4,1024]{1,0:T(4,128)S(1)} %pad_maximum_fusion), channel_id=1, source_target_pairs={{0,16},{2,18},{4,20},{6,22},{8,24},{10,26},{12,28},{14,30},{16,0},... | collective-permute-start | bytes 49160 | tf_op jit(solution)/shard_map/ppermute | solution.py:103
  12.3 2.0 %collective-permute-done.3 = f32[4,1024]{1,0:T(4,128)S(1)} collective-permute-done((f32[4,1024]{1,0:T(4,128)S(1)}, f32[4,1024]{1,0:T(4,128)S(1)}, u32[]{:S(2)}, u32[]{:S(2)}) %collective-permute-start.3) | collective-permute-done | bytes 16416 | tf_op jit(solution)/shard_map/ppermute | solution.py:103
  14.4 3.8 %multiply_reduce_fusion = (f32[512]{0:T(512)S(1)}, f32[512]{0:T(512)S(1)}, f32[512]{0:T(512)S(1)}, f32[512]{0:T(512)S(1)}, f32[512]{0:T(512)S(1)}, /*index=5*/f3...) fusion(f32[512]{0:T(512)S(1)} %bitcast.192, ...), kind=kLoop, calls=%fused_computation.25 | loop fusion | flops 19914752 | bytes 71680 | tf_op jit(solution)/shard_map/reduce_sum | solution.py:43
  18.3 1.6 %collective-permute-start.4 = (f32[4,512]{1,0:T(4,128)S(1)}, f32[4,512]{1,0:T(4,128)S(1)}, u32[]{:S(2)}, u32[]{:S(2)}) collective-permute-start(f32[4,512]{1,0:T(4,128)S(1)} %fusion.59), channel_id=1, source_target_pairs={{0,1},{1,0},{2,3},{3,2},{4,5},{5,4},{6,7},{7,6},{8,9},{9,8},{10,11... | collective-permute-start | bytes 24584 | tf_op jit(solution)/shard_map/ppermute | solution.py:28
  22.6 1.1 %collective-permute-done.5 = f32[4,512]{1,0:T(4,128)S(1)} collective-permute-done((f32[4,512]{1,0:T(4,128)S(1)}, f32[4,512]{1,0:T(4,128)S(1)}, u32[]{:S(2)}, u32[]{:S(2)}) %collective-permute-start.5) | collective-permute-done | bytes 8224 | tf_op jit(solution)/shard_map/ppermute | solution.py:28
  23.7 1.6 %collective-permute-start.6 = (f32[4,512]{1,0:T(4,128)S(1)}, f32[4,512]{1,0:T(4,128)S(1)}, u32[]{:S(2)}, u32[]{:S(2)}) collective-permute-start(f32[4,512]{1,0:T(4,128)S(1)} %fusion.87), channel_id=1, source_target_pairs={{0,4},{2,6},{4,0},{6,2},{8,12},{10,14},{12,8},{14,10},{16,20},{18,... | collective-permute-start | bytes 24584 | tf_op jit(solution)/shard_map/ppermute | solution.py:28
  25.3 2.1 %collective-permute-done.6 = f32[4,512]{1,0:T(4,128)S(1)} collective-permute-done((f32[4,512]{1,0:T(4,128)S(1)}, f32[4,512]{1,0:T(4,128)S(1)}, u32[]{:S(2)}, u32[]{:S(2)}) %collective-permute-start.6) | collective-permute-done | bytes 8224 | tf_op jit(solution)/shard_map/ppermute | solution.py:28
  28.2 3.1 %collective-permute-done.7 = f32[6,512]{1,0:T(8,128)S(1)} collective-permute-done((f32[6,512]{1,0:T(8,128)S(1)}, f32[6,512]{1,0:T(8,128)S(1)}, u32[]{:S(2)}, u32[]{:S(2)}) %collective-permute-start.7) | collective-permute-done | bytes 12320 | tf_op jit(solution)/shard_map/ppermute | solution.py:16
  31.3 2.6 %collective-permute-start.8 = (f32[6,1024]{1,0:T(8,128)S(1)}, f32[6,1024]{1,0:T(8,128)S(1)}, u32[]{:S(2)}, u32[]{:S(2)}) collective-permute-start(f32[6,1024]{1,0:T(8,128)S(1)} %maximum_select_fusion.1), channel_id=1, source_target_pairs={{0,16},{2,18},{4,20},{6,22},{8,24},{10,26},{12,28},{14,30},{16,0},... | collective-permute-start | bytes 73736 | tf_op jit(solution)/shard_map/ppermute | solution.py:16
  33.9 2.5 %collective-permute-done.8 = f32[6,1024]{1,0:T(8,128)S(1)} collective-permute-done((f32[6,1024]{1,0:T(8,128)S(1)}, f32[6,1024]{1,0:T(8,128)S(1)}, u32[]{:S(2)}, u32[]{:S(2)}) %collective-permute-start.8) | collective-permute-done | bytes 24608 | tf_op jit(solution)/shard_map/ppermute | solution.py:16
  38.9 1.2 %collective-permute-done.9 = f32[2048]{0:T(1024)S(1)} collective-permute-done((f32[2048]{0:T(1024)S(1)}, f32[2048]{0:T(1024)S(1)}, u32[]{:S(2)}, u32[]{:S(2)}) %collective-permute-start.9) | collective-permute-done | bytes 8224 | tf_op jit(solution)/shard_map/ppermute | solution.py:28
  40.1 1.5 %collective-permute-start.10 = (f32[2048]{0:T(1024)S(1)}, f32[2048]{0:T(1024)S(1)}, u32[]{:S(2)}, u32[]{:S(2)}) collective-permute-start(f32[2048]{0:T(1024)S(1)} %add.208), channel_id=1, source_target_pairs={{0,4},{2,6},{4,0},{6,2},{8,12},{10,14},{12,8},{14,10},{16,20},{18,... | collective-permute-start | bytes 24584 | tf_op jit(solution)/shard_map/ppermute | solution.py:28
  41.6 2.1 %collective-permute-done.10 = f32[2048]{0:T(1024)S(1)} collective-permute-done((f32[2048]{0:T(1024)S(1)}, f32[2048]{0:T(1024)S(1)}, u32[]{:S(2)}, u32[]{:S(2)}) %collective-permute-start.10) | collective-permute-done | bytes 8224 | tf_op jit(solution)/shard_map/ppermute | solution.py:28
  44.0 3.4 %collective-permute-done.11 = f32[2048]{0:T(1024)S(1)} collective-permute-done((f32[2048]{0:T(1024)S(1)}, f32[2048]{0:T(1024)S(1)}, u32[]{:S(2)}, u32[]{:S(2)}) %collective-permute-start.11) | collective-permute-done | bytes 8224 | tf_op jit(solution)/shard_map/ppermute | solution.py:28
  47.4 2.3 %collective-permute-start.12 = (f32[2048]{0:T(1024)S(1)}, f32[2048]{0:T(1024)S(1)}, u32[]{:S(2)}, u32[]{:S(2)}) collective-permute-start(f32[2048]{0:T(1024)S(1)} %add.210), channel_id=1, source_target_pairs={{0,16},{2,18},{4,20},{6,22},{8,24},{10,26},{12,28},{14,30},{16,0},... | collective-permute-start | bytes 24584 | tf_op jit(solution)/shard_map/ppermute | solution.py:163
  49.8 2.2 %collective-permute-done.12 = f32[2048]{0:T(1024)S(1)} collective-permute-done((f32[2048]{0:T(1024)S(1)}, f32[2048]{0:T(1024)S(1)}, u32[]{:S(2)}, u32[]{:S(2)}) %collective-permute-start.12) | collective-permute-done | bytes 8224 | tf_op jit(solution)/shard_map/ppermute | solution.py:163
  52.0 3.6 %while.11 = (s32[]{:T(128)}, f32[3,512]{1,0:T(4,128)S(1)}, f32[4,512,4]{1,2,0:T(4,128)S(1)}, f32[3,512]{1,0:T(4,128)S(1)}, f32[512]{0:T(512)S(1)}, /*index=5*/s32[]{:T(128)}, s32[]{:T(128)}) while((s32[]{:T(128)}, f32[3,512]{1,0:T(4,128)S(1)}, f32[4,512,4]{1,2,0:T(4,128)S(1)}, f32[3,512]{1,0:T(4,128)S(1)}, f32[512]{0:T(512)S(1)}, ...), condition=%wide.region_25.26_spmd.clone, body=%wide.region_21.25_spmd.clone.sunk | while | flops 4985347 | bytes 86115 | solution.py:59
  52.0 0.8 %fusion.93 = (f32[512]{0:T(512)S(1)}, f32[512]{0:T(512)S(1)}, f32[512]{0:T(512)S(1)}) fusion(f32[512]{0:T(512)S(1)} %bitcast.125, f32[512]{0:T(512)S(1)} %bitcast.129, f32[512]{0:T(512)S(1)} %get-tuple-element.224, f32[512]{0:T(512)S(1)} %bitcast.127, f32[512]{0:T(512)S(1)} %bitcast.124, f32[512]{0:T(512)S(1)} %bitcast.128, f32[512]{0:T(512)S(1)} %bitcast.123, ...), kind=kLoop, calls=%fused_computation.11.clone.1 | loop fusion | flops 4979200 | bytes 22528 | tf_op jit(solution)/shard_map/while/body/eval_jaxpr/reduce_sum | solution.py:57
  52.9 0.8 %fusion.93 = (f32[512]{0:T(512)S(1)}, f32[512]{0:T(512)S(1)}, f32[512]{0:T(512)S(1)}) fusion(f32[512]{0:T(512)S(1)} %bitcast.125, f32[512]{0:T(512)S(1)} %bitcast.129, f32[512]{0:T(512)S(1)} %get-tuple-element.224, f32[512]{0:T(512)S(1)} %bitcast.127, f32[512]{0:T(512)S(1)} %bitcast.124, f32[512]{0:T(512)S(1)} %bitcast.128, f32[512]{0:T(512)S(1)} %bitcast.123, ...), kind=kLoop, calls=%fused_computation.11.clone.1 | loop fusion | flops 4979200 | bytes 22528 | tf_op jit(solution)/shard_map/while/body/eval_jaxpr/reduce_sum | solution.py:57
  53.8 0.8 %fusion.93 = (f32[512]{0:T(512)S(1)}, f32[512]{0:T(512)S(1)}, f32[512]{0:T(512)S(1)}) fusion(f32[512]{0:T(512)S(1)} %bitcast.125, f32[512]{0:T(512)S(1)} %bitcast.129, f32[512]{0:T(512)S(1)} %get-tuple-element.224, f32[512]{0:T(512)S(1)} %bitcast.127, f32[512]{0:T(512)S(1)} %bitcast.124, f32[512]{0:T(512)S(1)} %bitcast.128, f32[512]{0:T(512)S(1)} %bitcast.123, ...), kind=kLoop, calls=%fused_computation.11.clone.1 | loop fusion | flops 4979200 | bytes 22528 | tf_op jit(solution)/shard_map/while/body/eval_jaxpr/reduce_sum | solution.py:57
  54.7 0.8 %fusion.93 = (f32[512]{0:T(512)S(1)}, f32[512]{0:T(512)S(1)}, f32[512]{0:T(512)S(1)}) fusion(f32[512]{0:T(512)S(1)} %bitcast.125, f32[512]{0:T(512)S(1)} %bitcast.129, f32[512]{0:T(512)S(1)} %get-tuple-element.224, f32[512]{0:T(512)S(1)} %bitcast.127, f32[512]{0:T(512)S(1)} %bitcast.124, f32[512]{0:T(512)S(1)} %bitcast.128, f32[512]{0:T(512)S(1)} %bitcast.123, ...), kind=kLoop, calls=%fused_computation.11.clone.1 | loop fusion | flops 4979200 | bytes 22528 | tf_op jit(solution)/shard_map/while/body/eval_jaxpr/reduce_sum | solution.py:57
  (102 shorter events, 7.1 us)
Async XLA Ops:
  0.6 36.6 %copy-start = (bf16[128,256]{1,0:T(8,128)(2,1)S(1)}, bf16[128,256]{1,0:T(8,128)(2,1)}, u32[]{:S(2)}) copy-start(bf16[128,256]{1,0:T(8,128)(2,1)} %param.25) | copy-start | bytes 196612
  0.6 0.7 %copy-start.11 = (s32[128]{0:T(128)S(1)}, s32[128]{0:T(128)}, u32[]{:S(2)}) copy-start(s32[128]{0:T(128)} %param.16) | copy-start | bytes 1540
  0.7 0.7 %copy-start.5 = (f32[3,128]{1,0:T(4,128)S(1)}, f32[3,128]{1,0:T(4,128)}, u32[]{:S(2)}) copy-start(f32[3,128]{1,0:T(4,128)} %param.15) | copy-start | bytes 4612
  1.3 0.7 %copy-start.1 = (f32[3,512]{1,0:T(4,128)S(1)}, f32[3,512]{1,0:T(4,128)}, u32[]{:S(2)}) copy-start(f32[3,512]{1,0:T(4,128)} %param.20) | copy-start | bytes 18436
  1.4 0.7 %copy-start.3 = (f32[512]{0:T(512)S(1)}, f32[512]{0:T(512)}, u32[]{:S(2)}) copy-start(f32[512]{0:T(512)} %param.21) | copy-start | bytes 6148
  1.4 4.5 %collective-permute-start = (f32[5,128]{1,0:T(8,128)S(1)}, f32[5,128]{1,0:T(8,128)S(1)}, u32[]{:S(2)}, u32[]{:S(2)}) collective-permute-start(f32[5,128]{1,0:T(8,128)S(1)} %pad_maximum_fusion.3), channel_id=1, source_target_pairs={{0,2},{2,0},{4,6},{6,4},{8,10},{10,8},{12,14},{14,12},{16,18},{18,... | collective-permute-start | bytes 7688 | tf_op jit(solution)/shard_map/ppermute | solution.py:16
  2.1 7.5 %collective-permute-start.2 = (f32[4,512]{1,0:T(4,128)S(1)}, f32[4,512]{1,0:T(4,128)S(1)}, u32[]{:S(2)}, u32[]{:S(2)}) collective-permute-start(f32[4,512]{1,0:T(4,128)S(1)} %pad_maximum_fusion.2), channel_id=1, source_target_pairs={{0,8},{2,10},{4,12},{6,14},{8,0},{10,2},{12,4},{14,6},{16,24},{18,... | collective-permute-start | bytes 24584 | tf_op jit(solution)/shard_map/ppermute | solution.py:100
  5.2 0.7 %copy-start.7 = (s32[128,4]{0,1:T(4,128)S(1)}, s32[128,4]{0,1:T(4,128)}, u32[]{:S(2)}) copy-start(s32[128,4]{0,1:T(4,128)} %param.18) | copy-start | bytes 6148
  5.9 3.7 %collective-permute-start.1 = (f32[5,256]{1,0:T(8,128)S(1)}, f32[5,256]{1,0:T(8,128)S(1)}, u32[]{:S(2)}, u32[]{:S(2)}) collective-permute-start(f32[5,256]{1,0:T(8,128)S(1)} %maximum_select_fusion.3), channel_id=1, source_target_pairs={{0,4},{2,6},{4,0},{6,2},{8,12},{10,14},{12,8},{14,10},{16,20},{18,... | collective-permute-start | bytes 15368 | tf_op jit(solution)/shard_map/ppermute | solution.py:16
  9.7 4.7 %collective-permute-start.3 = (f32[4,1024]{1,0:T(4,128)S(1)}, f32[4,1024]{1,0:T(4,128)S(1)}, u32[]{:S(2)}, u32[]{:S(2)}) collective-permute-start(f32[4,1024]{1,0:T(4,128)S(1)} %pad_maximum_fusion), channel_id=1, source_target_pairs={{0,16},{2,18},{4,20},{6,22},{8,24},{10,26},{12,28},{14,30},{16,0},... | collective-permute-start | bytes 49160 | tf_op jit(solution)/shard_map/ppermute | solution.py:103
  18.3 4.1 %collective-permute-start.4 = (f32[4,512]{1,0:T(4,128)S(1)}, f32[4,512]{1,0:T(4,128)S(1)}, u32[]{:S(2)}, u32[]{:S(2)}) collective-permute-start(f32[4,512]{1,0:T(4,128)S(1)} %fusion.59), channel_id=1, source_target_pairs={{0,1},{1,0},{2,3},{3,2},{4,5},{5,4},{6,7},{7,6},{8,9},{9,8},{10,11... | collective-permute-start | bytes 24584 | tf_op jit(solution)/shard_map/ppermute | solution.py:28
  20.6 2.0 %copy-start.4 = (bf16[128,128]{1,0:T(8,128)(2,1)S(1)}, bf16[128,128]{1,0:T(8,128)(2,1)}, u32[]{:S(2)}) copy-start(bf16[128,128]{1,0:T(8,128)(2,1)} %param.24) | copy-start | bytes 98308
  22.5 1.2 %collective-permute-start.5 = (f32[4,512]{1,0:T(4,128)S(1)}, f32[4,512]{1,0:T(4,128)S(1)}, u32[]{:S(2)}, u32[]{:S(2)}) collective-permute-start(f32[4,512]{1,0:T(4,128)S(1)} %fusion.85), channel_id=1, source_target_pairs={{0,2},{2,0},{4,6},{6,4},{8,10},{10,8},{12,14},{14,12},{16,18},{18,... | collective-permute-start | bytes 24584 | tf_op jit(solution)/shard_map/ppermute | solution.py:28
  22.6 2.8 %copy-start.8 = (bf16[8,128]{1,0:T(8,128)(2,1)S(1)}, bf16[8,128]{1,0:T(8,128)(2,1)}, u32[]{:S(2)}) copy-start(bf16[8,128]{1,0:T(8,128)(2,1)} %param.22) | copy-start | bytes 6148
  23.7 3.7 %collective-permute-start.6 = (f32[4,512]{1,0:T(4,128)S(1)}, f32[4,512]{1,0:T(4,128)S(1)}, u32[]{:S(2)}, u32[]{:S(2)}) collective-permute-start(f32[4,512]{1,0:T(4,128)S(1)} %fusion.87), channel_id=1, source_target_pairs={{0,4},{2,6},{4,0},{6,2},{8,12},{10,14},{12,8},{14,10},{16,20},{18,... | collective-permute-start | bytes 24584 | tf_op jit(solution)/shard_map/ppermute | solution.py:28
  27.5 0.7 %copy-start.10 = (f32[256]{0:T(256)S(1)}, f32[256]{0:T(256)}, u32[]{:S(2)}) copy-start(f32[256]{0:T(256)} %param.26) | copy-start | bytes 3076
  27.5 3.8 %collective-permute-start.7 = (f32[6,512]{1,0:T(8,128)S(1)}, f32[6,512]{1,0:T(8,128)S(1)}, u32[]{:S(2)}, u32[]{:S(2)}) collective-permute-start(f32[6,512]{1,0:T(8,128)S(1)} %pad_maximum_fusion.1), channel_id=1, source_target_pairs={{0,8},{2,10},{4,12},{6,14},{8,0},{10,2},{12,4},{14,6},{16,24},{18,... | collective-permute-start | bytes 36872 | tf_op jit(solution)/shard_map/ppermute | solution.py:16
  28.2 5.8 %copy-start.12 = (f32[128]{0:T(128)S(1)}, f32[128]{0:T(128)}, u32[]{:S(2)}) copy-start(f32[128]{0:T(128)} %param.23) | copy-start | bytes 1540
  31.3 5.1 %collective-permute-start.8 = (f32[6,1024]{1,0:T(8,128)S(1)}, f32[6,1024]{1,0:T(8,128)S(1)}, u32[]{:S(2)}, u32[]{:S(2)}) collective-permute-start(f32[6,1024]{1,0:T(8,128)S(1)} %maximum_select_fusion.1), channel_id=1, source_target_pairs={{0,16},{2,18},{4,20},{6,22},{8,24},{10,26},{12,28},{14,30},{16,0},... | collective-permute-start | bytes 73736 | tf_op jit(solution)/shard_map/ppermute | solution.py:16
  38.8 1.2 %collective-permute-start.9 = (f32[2048]{0:T(1024)S(1)}, f32[2048]{0:T(1024)S(1)}, u32[]{:S(2)}, u32[]{:S(2)}) collective-permute-start(f32[2048]{0:T(1024)S(1)} %fusion.60), channel_id=1, source_target_pairs={{0,2},{2,0},{4,6},{6,4},{8,10},{10,8},{12,14},{14,12},{16,18},{18,... | collective-permute-start | bytes 24584 | tf_op jit(solution)/shard_map/ppermute | solution.py:28
  40.1 3.7 %collective-permute-start.10 = (f32[2048]{0:T(1024)S(1)}, f32[2048]{0:T(1024)S(1)}, u32[]{:S(2)}, u32[]{:S(2)}) collective-permute-start(f32[2048]{0:T(1024)S(1)} %add.208), channel_id=1, source_target_pairs={{0,4},{2,6},{4,0},{6,2},{8,12},{10,14},{12,8},{14,10},{16,20},{18,... | collective-permute-start | bytes 24584 | tf_op jit(solution)/shard_map/ppermute | solution.py:28
  43.7 3.7 %collective-permute-start.11 = (f32[2048]{0:T(1024)S(1)}, f32[2048]{0:T(1024)S(1)}, u32[]{:S(2)}, u32[]{:S(2)}) collective-permute-start(f32[2048]{0:T(1024)S(1)} %add.209), channel_id=1, source_target_pairs={{0,8},{2,10},{4,12},{6,14},{8,0},{10,2},{12,4},{14,6},{16,24},{18,... | collective-permute-start | bytes 24584 | tf_op jit(solution)/shard_map/ppermute | solution.py:28
  47.4 4.5 %collective-permute-start.12 = (f32[2048]{0:T(1024)S(1)}, f32[2048]{0:T(1024)S(1)}, u32[]{:S(2)}, u32[]{:S(2)}) collective-permute-start(f32[2048]{0:T(1024)S(1)} %add.210), channel_id=1, source_target_pairs={{0,16},{2,18},{4,20},{6,22},{8,24},{10,26},{12,28},{14,30},{16,0},... | collective-permute-start | bytes 24584 | tf_op jit(solution)/shard_map/ppermute | solution.py:163
  55.5 0.7 %copy-start.2 = (f32[3,512]{1,0:T(4,128)}, f32[3,512]{1,0:T(4,128)S(1)}, u32[]{:S(2)}) copy-start(f32[3,512]{1,0:T(4,128)S(1)} %get-tuple-element.36) | copy-start | bytes 18436
  (2 other events, 1.4 us)

commit v18 on v14

--- a/solution.py
+++ b/solution.py
@@ -97,10 +97,15 @@
         axis=0,
     )
     near = gather_doubling(own, "blk", 1, low_blocks)
-    mm_some = gather_doubling(
-        jnp.concatenate([mm_pos, mm_charge[None, :]], axis=0), "blk", low_blocks, blocks
-    )
+    mm_some = jnp.concatenate([mm_pos, mm_charge[None, :]], axis=0)
     partial = potential_pass(near[:3], mm_some)
+    step = low_blocks
+    while step < blocks:
+        arriving = lax.ppermute(mm_some, "blk", [(i, i ^ step) for i in range(blocks)])
+        partial = partial + potential_pass(near[:3], arriving)
+        if step * 2 < blocks:
+            mm_some = jnp.concatenate([mm_some, arriving], -1)
+        step *= 2
     total = sum_butterfly(sum_butterfly(partial, "rep"), "blk", low_blocks)
     pull = lax.dynamic_slice_in_dim(total[1:4], (me % low_blocks) * rows, rows, axis=1)
     known = gather_doubling(

time: 55.5 us -> 54.3 us (0.978)
  waiting for transfers between devices: 22.4 us -> 20.2 us
  local copies, waits for them, and re-layouts: 0.99 us -> 1.76 us
    ppermute x6 -> x4, starting transfers between devices: 11 us -> 5.15 us  [gather_doubling(): other = lax.ppermute(x, axis, [(i, i ^ step) for i in range(n)])]
    ppermute x0 -> x2, starting transfers between devices: none -> 5.74 us  [on_device(): lax.ppermute(mm_some, 'blk', [(i, i ^ step) for i in range(blocks)])]
    ppermute x6 -> x4, waiting for transfers between devices: 10.1 us -> 7.73 us  [gather_doubling(): other = lax.ppermute(x, axis, [(i, i ^ step) for i in range(n)])]
    unnamed x26, local copies, waits for them, and re-layouts: 0.28 us -> 1.06 us
    reduce_sum x4 -> x3, other arithmetic: 3.21 us -> 3.34 us  [body(): jnp.sum(weighted, axis=0)]
  transfers between devices with their start and end apart: 13 -> 13, of which waited for: 10 -> 10; matrix products, arithmetic and copies ran while one was open for 2% -> 6% of each run, Pallas kernels for 0% -> 0%
where the time goes in v18:
time: 54.3 us; the launch traced here: 54 us
  waiting for transfers between devices  20.2 us (37%)
  starting transfers between devices  18.3 us (34%)
  other arithmetic  9.03 us (17%)
  between operations  3.04 us (6%)
  local copies, waits for them, and re-layouts  1.76 us (3%)
  matrix products  1.51 us (3%)
    ppermute x6, waiting for transfers between devices, sum_butterfly(): x = x + lax.ppermute(x, axis, [(i, i ^ step) for i in range(n)])  9.96 us
    ppermute x4, waiting for transfers between devices, gather_doubling(): other = lax.ppermute(x, axis, [(i, i ^ step) for i in range(n)])  7.73 us
    ppermute x2, starting transfers between devices, on_device(): lax.ppermute(mm_some, 'blk', [(i, i ^ step) for i in range(blocks)])  5.74 us
    ppermute x4, starting transfers between devices, gather_doubling(): other = lax.ppermute(x, axis, [(i, i ^ step) for i in range(n)])  5.15 us
    ppermute x6, starting transfers between devices, sum_butterfly(): x = x + lax.ppermute(x, axis, [(i, i ^ step) for i in range(n)])  5.03 us
    reduce_sum x3, other arithmetic, body(): jnp.sum(weighted, axis=0)  3.34 us
    reduce_sum x4, other arithmetic, body(): jnp.sum(d[c] * weight, axis=0)  3.19 us
    ppermute x1, starting transfers between devices, on_device(): lax.ppermute(part, 'blk', [(i, i ^ blocks // 2) for i in range(blocks)])  2.35 us
  transfers between devices with their start and end apart: 13, of which 10 were waited for; matrix products, arithmetic and copies ran while one was open for 6% of the time, Pallas kernels for 0%

profile of v18, /device:TPU:0, one launch (start us, length us, event | category | flops | bytes accessed | tf_op | source)
XLA Modules:
  0.0 54.0 jit_solution(4026667371765738547)
XLA Ops:
  2.1 3.1 %collective-permute-start.2 = (f32[4,512]{1,0:T(4,128)S(1)}, f32[4,512]{1,0:T(4,128)S(1)}, u32[]{:S(2)}, u32[]{:S(2)}) collective-permute-start(f32[4,512]{1,0:T(4,128)S(1)} %pad_maximum_fusion.2), channel_id=1, source_target_pairs={{0,8},{2,10},{4,12},{6,14},{8,0},{10,2},{12,4},{14,6},{16,24},{18,... | collective-permute-start | bytes 24584 | tf_op jit(solution)/shard_map/ppermute | solution.py:104
  5.9 1.6 %collective-permute-start.1 = (f32[5,256]{1,0:T(8,128)S(1)}, f32[5,256]{1,0:T(8,128)S(1)}, u32[]{:S(2)}, u32[]{:S(2)}) collective-permute-start(f32[5,256]{1,0:T(8,128)S(1)} %maximum_select_fusion.3), channel_id=1, source_target_pairs={{0,4},{2,6},{4,0},{6,2},{8,12},{10,14},{12,8},{14,10},{16,20},{18,... | collective-permute-start | bytes 15368 | tf_op jit(solution)/shard_map/ppermute | solution.py:16
  7.5 2.1 %collective-permute-done.1 = f32[5,256]{1,0:T(8,128)S(1)} collective-permute-done((f32[5,256]{1,0:T(8,128)S(1)}, f32[5,256]{1,0:T(8,128)S(1)}, u32[]{:S(2)}, u32[]{:S(2)}) %collective-permute-start.1) | collective-permute-done | bytes 5152 | tf_op jit(solution)/shard_map/ppermute | solution.py:16
  9.7 2.7 %collective-permute-start.3 = (f32[4,1024]{1,0:T(4,128)S(1)}, f32[4,1024]{1,0:T(4,128)S(1)}, u32[]{:S(2)}, u32[]{:S(2)}) collective-permute-start(f32[4,1024]{1,0:T(4,128)S(1)} %pad_maximum_fusion), channel_id=1, source_target_pairs={{0,16},{2,18},{4,20},{6,22},{8,24},{10,26},{12,28},{14,30},{16,0},... | collective-permute-start | bytes 49160 | tf_op jit(solution)/shard_map/ppermute | solution.py:104
  12.3 1.7 %multiply_reduce_fusion.1 = (f32[512]{0:T(512)S(1)}, f32[512]{0:T(512)S(1)}, f32[512]{0:T(512)S(1)}, f32[512]{0:T(512)S(1)}, f32[512]{0:T(512)S(1)}, /*index=5*/f32[512]{0:T(512)S(1)}, f32[512]{0:T(512)S(1)}, f32[512]{0:T(512)S(1)}) fusion(f32[512]{0:T(512)S(1)} %bitcast.202, f32[512]{0:T(512)S(1)} %bitcast.203, f32[512]{0:T(512)S(1)} %bitcast.204, ...), kind=kLoop, calls=%fused_computation.40 | loop fusion | flops 9957376 | bytes 38912 | tf_op jit(solution)/shard_map/while/body/eval_jaxpr/reduce_sum | solution.py:43
  14.4 1.7 %while.6 = (s32[]{:T(128)}, f32[4,512]{1,0:T(4,128)S(1)}, f32[1,512]{1,0:T(1,128)S(1)}, f32[2,512,4]{1,2,0:T(4,128)S(1)}, f32[1,512]{1,0:T(1,128)S(1)}, /*index=5*/f32[1,512]{1,0:T(1,128)S(1)}, s32[]{:T(128)}, s32[]{:T(128)}) while((s32[]{:T(128)}, f32[4,512]{1,0:T(4,128)S(1)}, f32[1,512]{1,0:T(1,128)S(1)}, ...), condition=%wide.region_13.14_spmd.clone, body=%wide.region_8.13_spmd.clone.sunk | while | flops 4988931 | bytes 79979 | solution.py:48
  14.4 0.8 %multiply_reduce_fusion.8 = (f32[512]{0:T(512)S(1)}, f32[512]{0:T(512)S(1)}, f32[512]{0:T(512)S(1)}, f32[512]{0:T(512)S(1)}) fusion(f32[512]{0:T(512)S(1)} %bitcast.164, f32[512]{0:T(512)S(1)} %bitcast.165, f32[512]{0:T(512)S(1)} %bitcast.192, f32[512]{0:T(512)S(1)} %bitcast.166, f32[512]{0:T(512)S(1)} %bitcast.194, f32[512]{0:T(512)S(1)} %bitcast.163, ...), kind=kLoop, calls=%fused_computation.1.clone.1 | loop fusion | flops 4978688 | bytes 22528 | tf_op jit(solution)/shard_map/while/body/eval_jaxpr/reduce_sum | solution.py:43
  15.3 0.8 %multiply_reduce_fusion.8 = (f32[512]{0:T(512)S(1)}, f32[512]{0:T(512)S(1)}, f32[512]{0:T(512)S(1)}, f32[512]{0:T(512)S(1)}) fusion(f32[512]{0:T(512)S(1)} %bitcast.164, f32[512]{0:T(512)S(1)} %bitcast.165, f32[512]{0:T(512)S(1)} %bitcast.192, f32[512]{0:T(512)S(1)} %bitcast.166, f32[512]{0:T(512)S(1)} %bitcast.194, f32[512]{0:T(512)S(1)} %bitcast.163, ...), kind=kLoop, calls=%fused_computation.1.clone.1 | loop fusion | flops 4978688 | bytes 22528 | tf_op jit(solution)/shard_map/while/body/eval_jaxpr/reduce_sum | solution.py:43
  16.1 1.6 %collective-permute-start.4 = (f32[4,512]{1,0:T(4,128)S(1)}, f32[4,512]{1,0:T(4,128)S(1)}, u32[]{:S(2)}, u32[]{:S(2)}) collective-permute-start(f32[4,512]{1,0:T(4,128)S(1)} %fusion.52), channel_id=1, source_target_pairs={{0,1},{1,0},{2,3},{3,2},{4,5},{5,4},{6,7},{7,6},{8,9},{9,8},{10,11... | collective-permute-start | bytes 24584 | tf_op jit(solution)/shard_map/ppermute | solution.py:28
  20.5 1.1 %collective-permute-done.5 = f32[4,512]{1,0:T(4,128)S(1)} collective-permute-done((f32[4,512]{1,0:T(4,128)S(1)}, f32[4,512]{1,0:T(4,128)S(1)}, u32[]{:S(2)}, u32[]{:S(2)}) %collective-permute-start.5) | collective-permute-done | bytes 8224 | tf_op jit(solution)/shard_map/ppermute | solution.py:28
  21.6 1.5 %collective-permute-start.6 = (f32[4,512]{1,0:T(4,128)S(1)}, f32[4,512]{1,0:T(4,128)S(1)}, u32[]{:S(2)}, u32[]{:S(2)}) collective-permute-start(f32[4,512]{1,0:T(4,128)S(1)} %add.191), channel_id=1, source_target_pairs={{0,4},{2,6},{4,0},{6,2},{8,12},{10,14},{12,8},{14,10},{16,20},{18,... | collective-permute-start | bytes 24584 | tf_op jit(solution)/shard_map/ppermute | solution.py:28
  23.1 2.1 %collective-permute-done.6 = f32[4,512]{1,0:T(4,128)S(1)} collective-permute-done((f32[4,512]{1,0:T(4,128)S(1)}, f32[4,512]{1,0:T(4,128)S(1)}, u32[]{:S(2)}, u32[]{:S(2)}) %collective-permute-start.6) | collective-permute-done | bytes 8224 | tf_op jit(solution)/shard_map/ppermute | solution.py:28
  25.9 3.1 %collective-permute-done.7 = f32[6,512]{1,0:T(8,128)S(1)} collective-permute-done((f32[6,512]{1,0:T(8,128)S(1)}, f32[6,512]{1,0:T(8,128)S(1)}, u32[]{:S(2)}, u32[]{:S(2)}) %collective-permute-start.7) | collective-permute-done | bytes 12320 | tf_op jit(solution)/shard_map/ppermute | solution.py:16
  29.1 2.6 %collective-permute-start.8 = (f32[6,1024]{1,0:T(8,128)S(1)}, f32[6,1024]{1,0:T(8,128)S(1)}, u32[]{:S(2)}, u32[]{:S(2)}) collective-permute-start(f32[6,1024]{1,0:T(8,128)S(1)} %maximum_select_fusion.1), channel_id=1, source_target_pairs={{0,16},{2,18},{4,20},{6,22},{8,24},{10,26},{12,28},{14,30},{16,0},... | collective-permute-start | bytes 73736 | tf_op jit(solution)/shard_map/ppermute | solution.py:16
  31.7 2.5 %collective-permute-done.8 = f32[6,1024]{1,0:T(8,128)S(1)} collective-permute-done((f32[6,1024]{1,0:T(8,128)S(1)}, f32[6,1024]{1,0:T(8,128)S(1)}, u32[]{:S(2)}, u32[]{:S(2)}) %collective-permute-start.8) | collective-permute-done | bytes 24608 | tf_op jit(solution)/shard_map/ppermute | solution.py:16
  36.7 1.2 %collective-permute-done.9 = f32[2048]{0:T(1024)S(1)} collective-permute-done((f32[2048]{0:T(1024)S(1)}, f32[2048]{0:T(1024)S(1)}, u32[]{:S(2)}, u32[]{:S(2)}) %collective-permute-start.9) | collective-permute-done | bytes 8224 | tf_op jit(solution)/shard_map/ppermute | solution.py:28
  37.9 1.5 %collective-permute-start.10 = (f32[2048]{0:T(1024)S(1)}, f32[2048]{0:T(1024)S(1)}, u32[]{:S(2)}, u32[]{:S(2)}) collective-permute-start(f32[2048]{0:T(1024)S(1)} %add.209), channel_id=1, source_target_pairs={{0,4},{2,6},{4,0},{6,2},{8,12},{10,14},{12,8},{14,10},{16,20},{18,... | collective-permute-start | bytes 24584 | tf_op jit(solution)/shard_map/ppermute | solution.py:28
  39.4 2.1 %collective-permute-done.10 = f32[2048]{0:T(1024)S(1)} collective-permute-done((f32[2048]{0:T(1024)S(1)}, f32[2048]{0:T(1024)S(1)}, u32[]{:S(2)}, u32[]{:S(2)}) %collective-permute-start.10) | collective-permute-done | bytes 8224 | tf_op jit(solution)/shard_map/ppermute | solution.py:28
  41.7 3.4 %collective-permute-done.11 = f32[2048]{0:T(1024)S(1)} collective-permute-done((f32[2048]{0:T(1024)S(1)}, f32[2048]{0:T(1024)S(1)}, u32[]{:S(2)}, u32[]{:S(2)}) %collective-permute-start.11) | collective-permute-done | bytes 8224 | tf_op jit(solution)/shard_map/ppermute | solution.py:28
  45.2 2.3 %collective-permute-start.12 = (f32[2048]{0:T(1024)S(1)}, f32[2048]{0:T(1024)S(1)}, u32[]{:S(2)}, u32[]{:S(2)}) collective-permute-start(f32[2048]{0:T(1024)S(1)} %add.211), channel_id=1, source_target_pairs={{0,16},{2,18},{4,20},{6,22},{8,24},{10,26},{12,28},{14,30},{16,0},... | collective-permute-start | bytes 24584 | tf_op jit(solution)/shard_map/ppermute | solution.py:167
  47.5 2.2 %collective-permute-done.12 = f32[2048]{0:T(1024)S(1)} collective-permute-done((f32[2048]{0:T(1024)S(1)}, f32[2048]{0:T(1024)S(1)}, u32[]{:S(2)}, u32[]{:S(2)}) %collective-permute-start.12) | collective-permute-done | bytes 8224 | tf_op jit(solution)/shard_map/ppermute | solution.py:167
  49.7 3.6 %while.7 = (s32[]{:T(128)}, f32[3,512]{1,0:T(4,128)S(1)}, f32[4,512,4]{1,2,0:T(4,128)S(1)}, f32[3,512]{1,0:T(4,128)S(1)}, f32[512]{0:T(512)S(1)}, /*index=5*/s32[]{:T(128)}, s32[]{:T(128)}) while((s32[]{:T(128)}, f32[3,512]{1,0:T(4,128)S(1)}, f32[4,512,4]{1,2,0:T(4,128)S(1)}, f32[3,512]{1,0:T(4,128)S(1)}, f32[512]{0:T(512)S(1)}, ...), condition=%wide.region_23.24_spmd.clone, body=%wide.region_19.23_spmd.clone.sunk | while | flops 4985347 | bytes 86115 | solution.py:63
  49.8 0.8 %fusion.86 = (f32[512]{0:T(512)S(1)}, f32[512]{0:T(512)S(1)}, f32[512]{0:T(512)S(1)}) fusion(f32[512]{0:T(512)S(1)} %bitcast.158, f32[512]{0:T(512)S(1)} %bitcast.162, f32[512]{0:T(512)S(1)} %get-tuple-element.381, f32[512]{0:T(512)S(1)} %bitcast.160, f32[512]{0:T(512)S(1)} %bitcast.157, f32[512]{0:T(512)S(1)} %bitcast.161, f32[512]{0:T(512)S(1)} %bitcast.156, ...), kind=kLoop, calls=%fused_computation.28.clone.1 | loop fusion | flops 4979200 | bytes 22528 | tf_op jit(solution)/shard_map/while/body/eval_jaxpr/reduce_sum | solution.py:61
  50.7 0.8 %fusion.86 = (f32[512]{0:T(512)S(1)}, f32[512]{0:T(512)S(1)}, f32[512]{0:T(512)S(1)}) fusion(f32[512]{0:T(512)S(1)} %bitcast.158, f32[512]{0:T(512)S(1)} %bitcast.162, f32[512]{0:T(512)S(1)} %get-tuple-element.381, f32[512]{0:T(512)S(1)} %bitcast.160, f32[512]{0:T(512)S(1)} %bitcast.157, f32[512]{0:T(512)S(1)} %bitcast.161, f32[512]{0:T(512)S(1)} %bitcast.156, ...), kind=kLoop, calls=%fused_computation.28.clone.1 | loop fusion | flops 4979200 | bytes 22528 | tf_op jit(solution)/shard_map/while/body/eval_jaxpr/reduce_sum | solution.py:61
  (110 shorter events, 9.0 us)
Async XLA Ops:
  0.6 34.4 %copy-start = (bf16[128,256]{1,0:T(8,128)(2,1)S(1)}, bf16[128,256]{1,0:T(8,128)(2,1)}, u32[]{:S(2)}) copy-start(bf16[128,256]{1,0:T(8,128)(2,1)} %param.27) | copy-start | bytes 196612
  0.6 0.7 %copy-start.11 = (s32[128]{0:T(128)S(1)}, s32[128]{0:T(128)}, u32[]{:S(2)}) copy-start(s32[128]{0:T(128)} %param.18) | copy-start | bytes 1540
  0.7 0.7 %copy-start.5 = (f32[3,128]{1,0:T(4,128)S(1)}, f32[3,128]{1,0:T(4,128)}, u32[]{:S(2)}) copy-start(f32[3,128]{1,0:T(4,128)} %param.17) | copy-start | bytes 4612
  1.3 0.7 %copy-start.1 = (f32[3,512]{1,0:T(4,128)S(1)}, f32[3,512]{1,0:T(4,128)}, u32[]{:S(2)}) copy-start(f32[3,512]{1,0:T(4,128)} %param.22) | copy-start | bytes 18436
  1.4 0.7 %copy-start.3 = (f32[512]{0:T(512)S(1)}, f32[512]{0:T(512)}, u32[]{:S(2)}) copy-start(f32[512]{0:T(512)} %param.23) | copy-start | bytes 6148
  1.4 4.5 %collective-permute-start = (f32[5,128]{1,0:T(8,128)S(1)}, f32[5,128]{1,0:T(8,128)S(1)}, u32[]{:S(2)}, u32[]{:S(2)}) collective-permute-start(f32[5,128]{1,0:T(8,128)S(1)} %pad_maximum_fusion.3), channel_id=1, source_target_pairs={{0,2},{2,0},{4,6},{6,4},{8,10},{10,8},{12,14},{14,12},{16,18},{18,... | collective-permute-start | bytes 7688 | tf_op jit(solution)/shard_map/ppermute | solution.py:16
  2.1 7.5 %collective-permute-start.2 = (f32[4,512]{1,0:T(4,128)S(1)}, f32[4,512]{1,0:T(4,128)S(1)}, u32[]{:S(2)}, u32[]{:S(2)}) collective-permute-start(f32[4,512]{1,0:T(4,128)S(1)} %pad_maximum_fusion.2), channel_id=1, source_target_pairs={{0,8},{2,10},{4,12},{6,14},{8,0},{10,2},{12,4},{14,6},{16,24},{18,... | collective-permute-start | bytes 24584 | tf_op jit(solution)/shard_map/ppermute | solution.py:104
  5.2 0.7 %copy-start.7 = (s32[128,4]{0,1:T(4,128)S(1)}, s32[128,4]{0,1:T(4,128)}, u32[]{:S(2)}) copy-start(s32[128,4]{0,1:T(4,128)} %param.20) | copy-start | bytes 6148
  5.9 3.7 %collective-permute-start.1 = (f32[5,256]{1,0:T(8,128)S(1)}, f32[5,256]{1,0:T(8,128)S(1)}, u32[]{:S(2)}, u32[]{:S(2)}) collective-permute-start(f32[5,256]{1,0:T(8,128)S(1)} %maximum_select_fusion.3), channel_id=1, source_target_pairs={{0,4},{2,6},{4,0},{6,2},{8,12},{10,14},{12,8},{14,10},{16,20},{18,... | collective-permute-start | bytes 15368 | tf_op jit(solution)/shard_map/ppermute | solution.py:16
  9.7 4.7 %collective-permute-start.3 = (f32[4,1024]{1,0:T(4,128)S(1)}, f32[4,1024]{1,0:T(4,128)S(1)}, u32[]{:S(2)}, u32[]{:S(2)}) collective-permute-start(f32[4,1024]{1,0:T(4,128)S(1)} %pad_maximum_fusion), channel_id=1, source_target_pairs={{0,16},{2,18},{4,20},{6,22},{8,24},{10,26},{12,28},{14,30},{16,0},... | collective-permute-start | bytes 49160 | tf_op jit(solution)/shard_map/ppermute | solution.py:104
  16.1 4.1 %collective-permute-start.4 = (f32[4,512]{1,0:T(4,128)S(1)}, f32[4,512]{1,0:T(4,128)S(1)}, u32[]{:S(2)}, u32[]{:S(2)}) collective-permute-start(f32[4,512]{1,0:T(4,128)S(1)} %fusion.52), channel_id=1, source_target_pairs={{0,1},{1,0},{2,3},{3,2},{4,5},{5,4},{6,7},{7,6},{8,9},{9,8},{10,11... | collective-permute-start | bytes 24584 | tf_op jit(solution)/shard_map/ppermute | solution.py:28
  18.4 2.0 %copy-start.4 = (bf16[128,128]{1,0:T(8,128)(2,1)S(1)}, bf16[128,128]{1,0:T(8,128)(2,1)}, u32[]{:S(2)}) copy-start(bf16[128,128]{1,0:T(8,128)(2,1)} %param.26) | copy-start | bytes 98308
  20.3 1.2 %collective-permute-start.5 = (f32[4,512]{1,0:T(4,128)S(1)}, f32[4,512]{1,0:T(4,128)S(1)}, u32[]{:S(2)}, u32[]{:S(2)}) collective-permute-start(f32[4,512]{1,0:T(4,128)S(1)} %fusion.77), channel_id=1, source_target_pairs={{0,2},{2,0},{4,6},{6,4},{8,10},{10,8},{12,14},{14,12},{16,18},{18,... | collective-permute-start | bytes 24584 | tf_op jit(solution)/shard_map/ppermute | solution.py:28
  20.4 2.7 %copy-start.8 = (bf16[8,128]{1,0:T(8,128)(2,1)S(1)}, bf16[8,128]{1,0:T(8,128)(2,1)}, u32[]{:S(2)}) copy-start(bf16[8,128]{1,0:T(8,128)(2,1)} %param.24) | copy-start | bytes 6148
  21.6 3.7 %collective-permute-start.6 = (f32[4,512]{1,0:T(4,128)S(1)}, f32[4,512]{1,0:T(4,128)S(1)}, u32[]{:S(2)}, u32[]{:S(2)}) collective-permute-start(f32[4,512]{1,0:T(4,128)S(1)} %add.191), channel_id=1, source_target_pairs={{0,4},{2,6},{4,0},{6,2},{8,12},{10,14},{12,8},{14,10},{16,20},{18,... | collective-permute-start | bytes 24584 | tf_op jit(solution)/shard_map/ppermute | solution.py:28
  25.3 0.7 %copy-start.10 = (f32[256]{0:T(256)S(1)}, f32[256]{0:T(256)}, u32[]{:S(2)}) copy-start(f32[256]{0:T(256)} %param.28) | copy-start | bytes 3076
  25.3 3.8 %collective-permute-start.7 = (f32[6,512]{1,0:T(8,128)S(1)}, f32[6,512]{1,0:T(8,128)S(1)}, u32[]{:S(2)}, u32[]{:S(2)}) collective-permute-start(f32[6,512]{1,0:T(8,128)S(1)} %pad_maximum_fusion.1), channel_id=1, source_target_pairs={{0,8},{2,10},{4,12},{6,14},{8,0},{10,2},{12,4},{14,6},{16,24},{18,... | collective-permute-start | bytes 36872 | tf_op jit(solution)/shard_map/ppermute | solution.py:16
  25.9 5.8 %copy-start.12 = (f32[128]{0:T(128)S(1)}, f32[128]{0:T(128)}, u32[]{:S(2)}) copy-start(f32[128]{0:T(128)} %param.25) | copy-start | bytes 1540
  29.1 5.1 %collective-permute-start.8 = (f32[6,1024]{1,0:T(8,128)S(1)}, f32[6,1024]{1,0:T(8,128)S(1)}, u32[]{:S(2)}, u32[]{:S(2)}) collective-permute-start(f32[6,1024]{1,0:T(8,128)S(1)} %maximum_select_fusion.1), channel_id=1, source_target_pairs={{0,16},{2,18},{4,20},{6,22},{8,24},{10,26},{12,28},{14,30},{16,0},... | collective-permute-start | bytes 73736 | tf_op jit(solution)/shard_map/ppermute | solution.py:16
  36.6 1.2 %collective-permute-start.9 = (f32[2048]{0:T(1024)S(1)}, f32[2048]{0:T(1024)S(1)}, u32[]{:S(2)}, u32[]{:S(2)}) collective-permute-start(f32[2048]{0:T(1024)S(1)} %fusion.53), channel_id=1, source_target_pairs={{0,2},{2,0},{4,6},{6,4},{8,10},{10,8},{12,14},{14,12},{16,18},{18,... | collective-permute-start | bytes 24584 | tf_op jit(solution)/shard_map/ppermute | solution.py:28
  37.9 3.7 %collective-permute-start.10 = (f32[2048]{0:T(1024)S(1)}, f32[2048]{0:T(1024)S(1)}, u32[]{:S(2)}, u32[]{:S(2)}) collective-permute-start(f32[2048]{0:T(1024)S(1)} %add.209), channel_id=1, source_target_pairs={{0,4},{2,6},{4,0},{6,2},{8,12},{10,14},{12,8},{14,10},{16,20},{18,... | collective-permute-start | bytes 24584 | tf_op jit(solution)/shard_map/ppermute | solution.py:28
  41.5 3.7 %collective-permute-start.11 = (f32[2048]{0:T(1024)S(1)}, f32[2048]{0:T(1024)S(1)}, u32[]{:S(2)}, u32[]{:S(2)}) collective-permute-start(f32[2048]{0:T(1024)S(1)} %add.210), channel_id=1, source_target_pairs={{0,8},{2,10},{4,12},{6,14},{8,0},{10,2},{12,4},{14,6},{16,24},{18,... | collective-permute-start | bytes 24584 | tf_op jit(solution)/shard_map/ppermute | solution.py:28
  45.2 4.5 %collective-permute-start.12 = (f32[2048]{0:T(1024)S(1)}, f32[2048]{0:T(1024)S(1)}, u32[]{:S(2)}, u32[]{:S(2)}) collective-permute-start(f32[2048]{0:T(1024)S(1)} %add.211), channel_id=1, source_target_pairs={{0,16},{2,18},{4,20},{6,22},{8,24},{10,26},{12,28},{14,30},{16,0},... | collective-permute-start | bytes 24584 | tf_op jit(solution)/shard_map/ppermute | solution.py:167
  53.3 0.7 %copy-start.2 = (f32[3,512]{1,0:T(4,128)}, f32[3,512]{1,0:T(4,128)S(1)}, u32[]{:S(2)}) copy-start(f32[3,512]{1,0:T(4,128)S(1)} %get-tuple-element.104) | copy-start | bytes 18436
  (2 other events, 1.4 us)
